TPU v7x, 32 devices: a whole 2x2x4 slice. The times are simulated.
32 devices in a mesh: grp: 2 (over y), chan: 4 (over z), tmpl: 4 (over x, core).
Axes of the slice: x: 2, y: 2, z: 4, core: 2. Of those that a mesh axis runs over, the one named last changes fastest.
Arguments:
- data: bfloat16 [1024, 1664], P(('grp', 'chan', 'tmpl')), parts along dimension 0, may hold values from -600 to 600
- templates: bfloat16 [256, 128, 512], P(('grp', 'chan'), 'tmpl'), parts along dimension 0, may hold values from -6 to 6
- stations: int32 [256, 128], P(('grp', 'chan'), 'tmpl'), parts along dimension 0, may hold values from 0 to 511, as said below
- offsets: int32 [256, 128], P(('grp', 'chan'), 'tmpl'), parts along dimension 0, may hold values from 0 to 128
- owner_map: int32 [8, 32], P(('grp', 'chan')), parts along dimension 0, may hold values from 0 to 31, each once within a row
Outputs:
- detection: float32 [256, 1024], P(('grp', 'chan', 'tmpl')), parts along dimension 0
There are 2 independent parts, one for each index of `grp`. A program takes and returns all parts, laid end to end along the dimension named above; each array names one. Nothing has to cross between parts.
Inputs may be any that keep to these rules, and one draw needn't show every extreme that they name: For each template j there is a sub-array g_j such that entries t * 32 to (t + 1) * 32 - 1 of stations[j] are the channels (g_j * 4 + t) * 32 + i, i < 32, each once, in some order. Among the 32 templates of one home block (rows h * 32 to (h + 1) * 32 - 1) at most 16 share a sub-array; in every draw one sub-array is named by exactly 16 templates of every home block.
All inputs are finite; a program needn't handle non-finite values.
Results may differ from a plain program's by a relative error of at most 0.0085.
Values may be sent and summed in bfloat16 or wider, within the bound.
No kernel may reach another device: no remote copies, remote signals or barrier semaphores. Data moves between devices by JAX's collectives and lax.ppermute only.
A program may use at most 64 MiB of HBM per device.

v0:
```python
import jax
import jax.numpy as jnp
from jax import lax
from jax.sharding import PartitionSpec as P

OFF = 128
PHASES = 8


eps = 1e-05


def normalize_rows(values):
    values = values.astype(jnp.float32)
    centred = values - jnp.mean(values, axis=-1, keepdims=True)
    scale = lax.rsqrt(jnp.mean(centred * centred, axis=-1, keepdims=True) + eps)
    return (centred * scale).astype(jnp.bfloat16)


def place_moveout(rows, shifts, padded_len):
    extra = padded_len - rows.shape[-1]
    tail = jnp.zeros(rows.shape[:-1] + (extra,), rows.dtype)
    current = jnp.concatenate([rows, tail], axis=-1)
    for bit_number in range(OFF.bit_length()):
        step_len = 1 << bit_number
        lead = jnp.zeros(rows.shape[:-1] + (step_len,), rows.dtype)
        moved = jnp.concatenate([lead, current[..., : padded_len - step_len]], axis=-1)
        active = shifts >> bit_number & 1 == 1
        current = jnp.where(active[..., None], moved, current)
    return current


def polyphase_filters(placed, phases):
    count, chans, padded_len = placed.shape
    taps = padded_len // phases + 1
    span = taps * phases
    padded = jnp.pad(placed, ((0, 0), (0, 0), (phases - 1, span - padded_len)))
    shifted = jnp.stack(
        [padded[:, :, phases - 1 - e : phases - 1 - e + span] for e in range(phases)], axis=1
    )
    shifted = shifted.reshape(count, phases, chans, taps, phases)
    shifted = jnp.transpose(shifted, (0, 1, 2, 4, 3))
    return shifted.reshape(count * phases, chans * phases, taps)


def polyphase_signal(blocks, phases):
    n_blocks, chans, window = blocks.shape
    split = blocks.reshape(n_blocks, chans, window // phases, phases)
    split = jnp.transpose(split, (0, 1, 3, 2))
    return split.reshape(n_blocks, chans * phases, window // phases)


def shards(data, templates, stations, offsets, owner_map):
    n_tmpl = lax.axis_size("tmpl")
    ch_local = data.shape[0]
    window = data.shape[1]
    count = templates.shape[0]
    padded_len = templates.shape[2] + OFF
    lags = window - padded_len
    phases = PHASES
    signal = normalize_rows(data)
    blocks = lax.all_gather(signal, "chan", axis=0, tiled=False)
    n_blocks = blocks.shape[0]
    shaped = normalize_rows(templates)
    local_chan = stations % ch_local
    target = stations[:, 0] // (ch_local * n_tmpl)
    hit = local_chan[:, :, None] == jnp.arange(ch_local, dtype=jnp.int32)[None, None, :]
    ordered = jnp.einsum(
        "jki,jkl->jil", hit.astype(jnp.bfloat16), shaped, preferred_element_type=jnp.float32
    ).astype(jnp.bfloat16)
    ordered_shift = jnp.sum(jnp.where(hit, offsets[:, :, None], 0), axis=1)
    placed = place_moveout(ordered, ordered_shift, padded_len)
    filters = polyphase_filters(placed, phases)
    lhs = polyphase_signal(blocks, phases)
    corr = lax.conv_general_dilated(
        lhs,
        filters,
        (1,),
        "VALID",
        dimension_numbers=("NCH", "OIH", "NCH"),
        preferred_element_type=jnp.float32,
    )
    corr = corr[:, :, : lags // phases].reshape(n_blocks, count, phases, lags // phases)
    pick = target[None, :] == jnp.arange(n_blocks, dtype=jnp.int32)[:, None]
    chosen = jnp.sum(jnp.where(pick[:, :, None, None], corr, 0.0), axis=0)
    partial_value = jnp.transpose(chosen, (0, 2, 1)).reshape(count, lags)
    partial_value = partial_value.astype(jnp.bfloat16).astype(jnp.float32)
    inverse = (
        jnp.zeros((count,), jnp.int32).at[owner_map[0]].set(jnp.arange(count, dtype=jnp.int32))
    )
    arranged = partial_value[inverse]
    stack = lax.psum_scatter(arranged, "tmpl", scatter_dimension=0, tiled=True)
    power = jnp.mean(stack * stack, axis=1, keepdims=True)
    return stack * lax.rsqrt(power + eps)


def solution(mesh):
    in_specs = (
        P(("grp", "chan", "tmpl"), None),
        P(("grp", "chan"), "tmpl", None),
        P(("grp", "chan"), "tmpl"),
        P(("grp", "chan"), "tmpl"),
        P(("grp", "chan"), None),
    )
    out_specs = P(("grp", "chan", "tmpl"), None)
    return jax.shard_map(shards, mesh=mesh, in_specs=in_specs, out_specs=out_specs, check_vma=False)
```

profile of v0, /device:TPU:0, one launch (start us, length us, event | category | flops | bytes accessed | tf_op | source)
XLA Modules:
  0.0 228.0 jit_solution(13406749056024558241)
XLA Ops:
  6.5 0.8 add_select_fusion
  7.4 0.8 slice_reduce_fusion
  8.2 1.3 select_reduce_fusion
  9.6 1.4 convert_reduce_fusion
  11.0 0.5 fusion.2
  11.6 0.6 convolution_convert_fusion
  12.1 0.1 pad_slice_fusion
  12.3 1.3 pad_select_fusion.7
  13.6 1.3 pad_select_fusion.6
  14.9 1.3 pad_select_fusion.5
  16.3 1.3 pad_select_fusion.4
  17.6 1.3 pad_select_fusion.3
  19.0 1.3 pad_select_fusion.2
  20.3 1.3 pad_select_fusion.1
  21.7 0.1 slice.76
  21.8 0.4 pad_select_fusion
  22.2 6.3 %pad_slice_fusion.1 = (bf16[32,32,648]{2,1,0:T(8,128)(2,1)}, bf16[32,32,648]{2,1,0:T(8,128)(2,1)}, bf16[32,32,648]{2,1,0:T(8,128)(2,1)}, bf16[32,32,648]{2,1,0:T...) fusion(bf16[32,32,640]{2,1,0:T(8,128)(2,1)S(1)} %pad_select_fusion), kind=kLoop, calls=%fused_computation.18 | loop fusion | bytes 11927552 | tf_op jit(solution)/shard_map/slice | solution.py:39
  28.4 4.3 %copy.25 = bf16[32,32,648]{1,2,0:T(8,128)(2,1)} copy(bf16[32,32,648]{2,1,0:T(8,128)(2,1)S(1)} %get-tuple-element.12) | data formatting | bytes 2654208 | tf_op jit(solution)/shard_map/slice | solution.py:39
  32.7 6.3 %copy.33 = bf16[32,1,32,81,8]{3,4,2,1,0:T(8,128)(2,1)S(1)} copy(bf16[32,1,32,81,8]{2,4,3,0,1:T(8,128)(2,1)} %bitcast.31) | data formatting | bytes 2654208 | tf_op jit(solution)/shard_map/stack | solution.py:38
  39.0 1.6 constant_dynamic-update-slice_fusion.7
  40.7 5.4 %copy.26 = bf16[32,32,648]{1,2,0:T(8,128)(2,1)} copy(bf16[32,32,648]{2,1,0:T(8,128)(2,1)} %get-tuple-element.6) | data formatting | bytes 2654208 | tf_op jit(solution)/shard_map/slice | solution.py:39
  46.1 6.3 %copy.34 = bf16[32,1,32,81,8]{3,4,2,1,0:T(8,128)(2,1)S(1)} copy(bf16[32,1,32,81,8]{2,4,3,0,1:T(8,128)(2,1)} %bitcast.32) | data formatting | bytes 2654208 | tf_op jit(solution)/shard_map/stack | solution.py:38
  52.4 5.4 %copy.27 = bf16[32,32,648]{1,2,0:T(8,128)(2,1)} copy(bf16[32,32,648]{2,1,0:T(8,128)(2,1)} %get-tuple-element.7) | data formatting | bytes 2654208 | tf_op jit(solution)/shard_map/slice | solution.py:39
  57.8 6.9 %copy.35 = bf16[32,1,32,81,8]{3,4,2,1,0:T(8,128)(2,1)} copy(bf16[32,1,32,81,8]{2,4,3,0,1:T(8,128)(2,1)} %bitcast.33) | data formatting | bytes 2654208 | tf_op jit(solution)/shard_map/stack | solution.py:38
  64.8 5.4 %copy.28 = bf16[32,32,648]{1,2,0:T(8,128)(2,1)} copy(bf16[32,32,648]{2,1,0:T(8,128)(2,1)} %get-tuple-element.8) | data formatting | bytes 2654208 | tf_op jit(solution)/shard_map/slice | solution.py:39
  70.2 6.9 %copy.36 = bf16[32,1,32,81,8]{3,4,2,1,0:T(8,128)(2,1)} copy(bf16[32,1,32,81,8]{2,4,3,0,1:T(8,128)(2,1)} %bitcast.34) | data formatting | bytes 2654208 | tf_op jit(solution)/shard_map/stack | solution.py:38
  77.1 5.4 %copy.29 = bf16[32,32,648]{1,2,0:T(8,128)(2,1)} copy(bf16[32,32,648]{2,1,0:T(8,128)(2,1)} %get-tuple-element.9) | data formatting | bytes 2654208 | tf_op jit(solution)/shard_map/slice | solution.py:39
  82.6 6.9 %copy.37 = bf16[32,1,32,81,8]{3,4,2,1,0:T(8,128)(2,1)} copy(bf16[32,1,32,81,8]{2,4,3,0,1:T(8,128)(2,1)} %bitcast.35) | data formatting | bytes 2654208 | tf_op jit(solution)/shard_map/stack | solution.py:38
  89.5 5.4 %copy.30 = bf16[32,32,648]{1,2,0:T(8,128)(2,1)} copy(bf16[32,32,648]{2,1,0:T(8,128)(2,1)} %get-tuple-element.10) | data formatting | bytes 2654208 | tf_op jit(solution)/shard_map/slice | solution.py:39
  94.9 6.9 %copy.38 = bf16[32,1,32,81,8]{3,4,2,1,0:T(8,128)(2,1)} copy(bf16[32,1,32,81,8]{2,4,3,0,1:T(8,128)(2,1)} %bitcast.36) | data formatting | bytes 2654208 | tf_op jit(solution)/shard_map/stack | solution.py:38
  101.9 5.4 %copy.31 = bf16[32,32,648]{1,2,0:T(8,128)(2,1)} copy(bf16[32,32,648]{2,1,0:T(8,128)(2,1)} %get-tuple-element.11) | data formatting | bytes 2654208 | tf_op jit(solution)/shard_map/slice | solution.py:39
  107.3 7.0 %copy.39 = bf16[32,1,32,81,8]{3,4,2,1,0:T(8,128)(2,1)} copy(bf16[32,1,32,81,8]{2,4,3,0,1:T(8,128)(2,1)} %bitcast.37) | data formatting | bytes 2654208 | tf_op jit(solution)/shard_map/stack | solution.py:38
  114.2 5.4 %copy.32 = bf16[32,32,648]{1,2,0:T(8,128)(2,1)} copy(bf16[32,32,648]{2,1,0:T(8,128)(2,1)} %get-tuple-element.5) | data formatting | bytes 2654208 | tf_op jit(solution)/shard_map/slice | solution.py:39
  119.7 6.9 %copy.40 = bf16[32,1,32,81,8]{3,4,2,1,0:T(8,128)(2,1)} copy(bf16[32,1,32,81,8]{2,4,3,0,1:T(8,128)(2,1)} %bitcast.38) | data formatting | bytes 2654208 | tf_op jit(solution)/shard_map/stack | solution.py:38
  126.6 1.6 constant_dynamic-update-slice_fusion.6
  128.2 0.6 copy-done.1
  128.8 1.6 constant_dynamic-update-slice_fusion.5
  130.4 0.6 copy-done.2
  131.0 1.6 constant_dynamic-update-slice_fusion.4
  132.7 0.6 copy-done.3
  133.2 1.6 constant_dynamic-update-slice_fusion.3
  134.9 0.6 copy-done.4
  135.4 1.6 constant_dynamic-update-slice_fusion.2
  137.1 0.6 copy-done.5
  137.7 1.6 constant_dynamic-update-slice_fusion.1
  139.3 0.6 copy-done.6
  139.9 1.7 constant_dynamic-update-slice_fusion
  141.5 20.3 %copy.42 = bf16[256,256,81]{1,0,2:T(8,128)(2,1)} copy(bf16[256,256,81]{2,1,0:T(8,128)(2,1)} %bitcast.39) | data formatting | bytes 21233664 | tf_op jit(solution)/shard_map/reshape | solution.py:43
  161.9 0.1 convert_reduce_fusion.1
  162.0 0.2 fusion.11
  162.3 16.4 %all-gather = bf16[128,1664]{1,0:T(8,128)(2,1)S(1)} all-gather(bf16[32,1664]{1,0:T(8,128)(2,1)S(1)} %fusion.12), channel_id=2, replica_groups=mesh['grp'=2,'chan'=4,'tmpl'=4] {'chan'}, dimensions={0}, use_global_device_ids=true | all-gather | bytes 532480 | tf_op jit(solution)/shard_map/all_gather | solution.py:62
  178.7 0.3 copy.23
  179.0 0.7 reshape.185
  179.7 2.9 %copy.24 = bf16[4,32,8,208]{3,2,1,0:T(8,128)(2,1)S(1)} copy(bf16[4,32,8,208]{1,0,2,3:T(4,128)(2,1)S(1)} %bitcast.46) | data formatting | bytes 851968 | tf_op jit(solution)/shard_map/transpose | solution.py:49
  182.6 0.3 copy.41
  183.0 0.1 broadcast_in_dim.102
  183.1 11.7 %fusion.4 = bf16[256,128]{0,1:T(8,128)(2,1)S(1)} fusion(bf16[4,256,208]{1,0,2:T(4,128)(2,1)S(1)} %copy.41, bf16[256,256,81]{1,0,2:T(8,128)(2,1)} %copy.42, pred[4,256]{1,0:T(4,128)(4,1)S(1)} %broadcast_in_dim.102), kind=kOutput, calls=%fused_computation.27 | convolution fusion | flops 5436047360 | bytes 11109376 | tf_op jit(solution)/shard_map/conv_general_dilated | solution.py:75
  194.9 0.2 copy.44
  195.2 0.2 copy.45
  195.4 0.7 scatter_custom_fusion
  196.1 1.2 gather_fusion
  197.4 21.5 %reduce-scatter.2.cloned.1.call-done = f32[8,1024]{1,0:T(8,128)} async-done(((f32[32,1024]{1,0:T(8,128)}), f32[8,1024]{1,0:T(8,128)}) %reduce-scatter.2.cloned.1.call-update) | async-done | bytes 32784 | tf_op jit(solution)/shard_map/reduce_scatter | solution.py:92
  218.8 0.9 multiply_reduce_fusion
  219.7 1.4 broadcast_multiply_fusion
  (29 shorter events, 0.4 us)
Async XLA Ops:
  6.5 4.5 %copy-start = (bf16[32,32,512]{2,1,0:T(8,128)(2,1)S(1)}, bf16[32,32,512]{2,1,0:T(8,128)(2,1)}, u32[]{:S(2)}) copy-start(bf16[32,32,512]{2,1,0:T(8,128)(2,1)} %param.6) | copy-start | bytes 3145732
  6.5 212.3 %reduce-scatter.2.cloned.1.call-start = ((), (), s32[]{:S(2)}) async-start(), calls=%async_computation.1 | async-start | bytes 163840 | tf_op jit(solution)/shard_map/reduce_scatter | solution.py:92
  126.6 2.2 copy-start.1
  128.8 2.2 copy-start.2
  131.0 2.2 copy-start.3
  133.2 2.2 copy-start.4
  135.4 2.2 copy-start.5
  137.7 2.2 copy-start.6
  141.5 20.3 %copy-start.7 = (bf16[32,1664]{1,0:T(8,128)(2,1)S(1)}, bf16[32,1664]{1,0:T(8,128)(2,1)}, u32[]{:S(2)}) copy-start(bf16[32,1664]{1,0:T(8,128)(2,1)} %param.5) | copy-start | bytes 319492
  183.1 12.2 %copy-start.8 = (s32[1,32]{1,0:T(1,128)S(1)}, s32[1,32]{1,0:T(1,128)}, u32[]{:S(2)}) copy-start(s32[1,32]{1,0:T(1,128)} %param.9) | copy-start | bytes 388
Sparse Core Ops, SparseCore 0:
  197.5 21.3 reduce-scatter.1
where the time goes:
time: 231 us; the launch traced here: 228 us
  local copies, waits for them, and re-layouts  147 us (64%)
  waiting for transfers between devices  21.5 us (9%)
  other arithmetic  16.7 us (7%)
  blocking collectives  16.4 us (7%)
  between operations  13.7 us (6%)
  matrix products  12.2 us (5%)
    another operation x9, local copies, waits for them, and re-layouts, polyphase_filters(): jnp.stack([padded[:, :, phases - 1 - e:phases - 1 - e + span] for e in ra...  56 us
    slice x9, local copies, waits for them, and re-layouts, polyphase_filters(): padded[:, :, phases - 1 - e:phases - 1 - e + span]  48.5 us
    reduce_scatter x1, waiting for transfers between devices, shards(): stack = lax.psum_scatter(arranged, 'tmpl', scatter_dimension=0, tiled=True)  21.5 us
    reshape x1, local copies, waits for them, and re-layouts, polyphase_filters(): return shifted.reshape(count * phases, chans * phases, taps)  20.3 us
    all_gather x1, blocking collectives, shards(): blocks = lax.all_gather(signal, 'chan', axis=0, tiled=False)  16.4 us
    unnamed x25, local copies, waits for them, and re-layouts  14.9 us
    conv_general_dilated x1, matrix products, shards(): lax.conv_general_dilated(lhs, filters, (1,), 'VALID', dimension_numbers=(...  11.7 us
    select_n x8, other arithmetic, place_moveout(): current = jnp.where(active[..., None], moved, current)  9.75 us
  transfers between devices with their start and end apart: 1, of which 1 were waited for; matrix products, arithmetic and copies ran while one was open for 0% of the time, Pallas kernels for 0%

commit v1 on v0

--- a/solution.py
+++ b/solution.py
@@ -1,6 +1,10 @@
+import functools
+
 import jax
 import jax.numpy as jnp
 from jax import lax
+from jax.experimental import pallas as pl
+from jax.experimental.pallas import tpu as pltpu
 from jax.sharding import PartitionSpec as P
 
 OFF = 128
@@ -30,24 +34,46 @@
     return current
 
 
+def _filter_kernel(grouped_ref, out_ref, *, steps, count, chans, phases):
+    width = phases * chans
+    first = pl.program_id(0) * steps
+    for step in range(steps):
+        lo = grouped_ref[first + step].astype(jnp.float32)
+        hi = grouped_ref[first + step + 1].astype(jnp.float32)
+        joined = jnp.concatenate([lo, hi], axis=-1)
+        for e in range(phases):
+            cut = (phases - 1 - e) * chans
+            moved = pltpu.roll(joined, 2 * width - cut, 1) if cut else joined
+            out_ref[step, e * count : (e + 1) * count, :] = moved[:, :width].astype(out_ref.dtype)
+
+
 def polyphase_filters(placed, phases):
     count, chans, padded_len = placed.shape
     taps = padded_len // phases + 1
-    span = taps * phases
-    padded = jnp.pad(placed, ((0, 0), (0, 0), (phases - 1, span - padded_len)))
-    shifted = jnp.stack(
-        [padded[:, :, phases - 1 - e : phases - 1 - e + span] for e in range(phases)], axis=1
+    front = phases - 1
+    blocks = taps + 1
+    padded = jnp.pad(placed, ((0, 0), (0, 0), (front, blocks * phases - padded_len - front)))
+    grouped = padded.reshape(count, chans, blocks, phases)
+    grouped = jnp.transpose(grouped, (2, 0, 3, 1)).reshape(blocks, count, phases * chans)
+    steps = next(d for d in (9, 3, 1) if taps % d == 0)
+    width = phases * chans
+    kernel = functools.partial(
+        _filter_kernel, steps=steps, count=count, chans=chans, phases=phases
     )
-    shifted = shifted.reshape(count, phases, chans, taps, phases)
-    shifted = jnp.transpose(shifted, (0, 1, 2, 4, 3))
-    return shifted.reshape(count * phases, chans * phases, taps)
+    return pl.pallas_call(
+        kernel,
+        grid=(taps // steps,),
+        in_specs=[pl.BlockSpec((blocks, count, width), lambda q: (0, 0, 0))],
+        out_specs=pl.BlockSpec((steps, phases * count, width), lambda q: (q, 0, 0)),
+        out_shape=jax.ShapeDtypeStruct((taps, phases * count, width), placed.dtype),
+    )(grouped)
 
 
 def polyphase_signal(blocks, phases):
     n_blocks, chans, window = blocks.shape
     split = blocks.reshape(n_blocks, chans, window // phases, phases)
-    split = jnp.transpose(split, (0, 1, 3, 2))
-    return split.reshape(n_blocks, chans * phases, window // phases)
+    split = jnp.transpose(split, (0, 3, 1, 2))
+    return split.reshape(n_blocks, phases * chans, window // phases)
 
 
 def shards(data, templates, stations, offsets, owner_map):
@@ -77,13 +103,13 @@
         filters,
         (1,),
         "VALID",
-        dimension_numbers=("NCH", "OIH", "NCH"),
+        dimension_numbers=("NCH", "HOI", "NCH"),
         preferred_element_type=jnp.float32,
     )
-    corr = corr[:, :, : lags // phases].reshape(n_blocks, count, phases, lags // phases)
+    corr = corr[:, :, : lags // phases].reshape(n_blocks, phases, count, lags // phases)
     pick = target[None, :] == jnp.arange(n_blocks, dtype=jnp.int32)[:, None]
-    chosen = jnp.sum(jnp.where(pick[:, :, None, None], corr, 0.0), axis=0)
-    partial_value = jnp.transpose(chosen, (0, 2, 1)).reshape(count, lags)
+    chosen = jnp.sum(jnp.where(pick[:, None, :, None], corr, 0.0), axis=0)
+    partial_value = jnp.transpose(chosen, (1, 2, 0)).reshape(count, lags)
     partial_value = partial_value.astype(jnp.bfloat16).astype(jnp.float32)
     inverse = (
         jnp.zeros((count,), jnp.int32).at[owner_map[0]].set(jnp.arange(count, dtype=jnp.int32))

time: 231 us -> 117 us (0.51)
  local copies, waits for them, and re-layouts: 147 us -> 26.8 us
  Pallas kernels: 0 us -> 7.92 us
    another operation x9 -> x0, local copies, waits for them, and re-layouts: 56 us -> none  [polyphase_filters(): jnp.stack([padded[:, :, phases - 1 - e:phases - 1 - e + span] for e in ra...]
    slice x9 -> x0, local copies, waits for them, and re-layouts: 48.5 us -> none  [polyphase_filters(): padded[:, :, phases - 1 - e:phases - 1 - e + span]]
    reshape x2, local copies, waits for them, and re-layouts: 20.6 us -> 2.89 us  [the longest x1 2.62 us: polyphase_filters(): jnp.transpose(grouped, (2, 0, 3, 1)).reshape(blocks, count, phases * chans)]
    transpose x1 -> x3, local copies, waits for them, and re-layouts: 2.88 us -> 14.3 us  [the longest x2 12.5 us: polyphase_filters(): jnp.transpose(grouped, (2, 0, 3, 1)).reshape(blocks, count, phases * chans)]
    unnamed x25 -> x7, local copies, waits for them, and re-layouts: 14.9 us -> 5.01 us
    pallas_call x0 -> x1, Pallas kernels: none -> 7.92 us  [polyphase_filters(): pl.pallas_call(kernel, grid=(taps // steps,), in_specs=[pl.BlockSpec((blo...]
where the time goes in v1:
time: 117 us; the launch traced here: 116 us
  local copies, waits for them, and re-layouts  26.8 us (23%)
  waiting for transfers between devices  21.5 us (18%)
  other arithmetic  17.4 us (15%)
  blocking collectives  16.4 us (14%)
  between operations  13.6 us (12%)
  matrix products  12.2 us (10%)
  Pallas kernels  7.92 us (7%)
    reduce_scatter x1, waiting for transfers between devices, shards(): stack = lax.psum_scatter(arranged, 'tmpl', scatter_dimension=0, tiled=True)  21.5 us
    all_gather x1, blocking collectives, shards(): blocks = lax.all_gather(signal, 'chan', axis=0, tiled=False)  16.4 us
    transpose x2, local copies, waits for them, and re-layouts, polyphase_filters(): jnp.transpose(grouped, (2, 0, 3, 1)).reshape(blocks, count, phases * chans)  12.5 us
    conv_general_dilated x1, matrix products, shards(): lax.conv_general_dilated(lhs, filters, (1,), 'VALID', dimension_numbers=(...  11.7 us
    select_n x8, other arithmetic, place_moveout(): current = jnp.where(active[..., None], moved, current)  9.75 us
    pallas_call x1, Pallas kernels, polyphase_filters(): pl.pallas_call(kernel, grid=(taps // steps,), in_specs=[pl.BlockSpec((blo...  7.92 us
    unnamed x7, local copies, waits for them, and re-layouts  5.01 us
    reshape x1, local copies, waits for them, and re-layouts, polyphase_filters(): jnp.transpose(grouped, (2, 0, 3, 1)).reshape(blocks, count, phases * chans)  2.62 us
  transfers between devices with their start and end apart: 1, of which 1 were waited for; matrix products, arithmetic and copies ran while one was open for 0% of the time, Pallas kernels for 0%

profile of v1, /device:TPU:0, one launch (start us, length us, event | category | flops | bytes accessed | tf_op | source)
XLA Modules:
  0.0 115.9 jit_solution(908560783902600064)
XLA Ops:
  6.5 0.0 reduce-scatter.2.cloned.1.call-start
  6.5 0.7 add_select_fusion
  7.3 0.8 slice_reduce_fusion
  8.1 1.0 convert_reduce_fusion.1
  9.1 1.1 fusion.11
  10.2 1.0 fusion.12
  11.2 16.4 %all-gather = bf16[128,1664]{1,0:T(8,128)(2,1)S(1)} all-gather(bf16[32,1664]{1,0:T(8,128)(2,1)S(1)} %fusion.12), channel_id=2, replica_groups=mesh['grp'=2,'chan'=4,'tmpl'=4] {'chan'}, dimensions={0}, use_global_device_ids=true | all-gather | bytes 532480 | tf_op jit(solution)/shard_map/all_gather | solution.py:88
  27.7 0.3 copy.16
  27.9 0.7 reshape.170
  28.7 0.0 copy-start
  28.7 1.8 %copy.17 = bf16[4,8,32,208]{3,2,1,0:T(8,128)(2,1)S(1)} copy(bf16[4,8,32,208]{2,0,1,3:T(4,128)(2,1)S(1)} %bitcast.32) | data formatting | bytes 851968 | tf_op jit(solution)/shard_map/transpose | solution.py:75
  30.5 0.3 copy.21
  30.8 0.0 copy-done
  30.8 0.2 convert_reduce_fusion
  31.0 0.5 fusion.2
  31.6 0.5 convolution_convert_fusion
  32.1 0.0 copy-start.1
  32.1 0.1 pad_slice_fusion
  32.2 0.6 copy-done.1
  32.8 0.6 select_reduce_fusion
  33.5 1.3 %pad_select_fusion.7 = bf16[32,32,640]{2,1,0:T(8,128)(2,1)S(1)} fusion(bf16[32,32,639]{2,1,0:T(8,128)(2,1)S(1)} %pad_slice_fusion, pred[32,32]{1,0:T(8,128)(4,1)S(1)} %get-tuple-element.6, bf16[32,32,512]{2,1,0:T(8,128)(2,1)S(1)} %convolution_convert_fusion), kind=kLoop, calls=%fused_computation.17 | loop fusion | flops 655360 | bytes 3668992 | tf_op jit(solution)/shard_map/jit(_where)/select_n | solution.py:33
  34.8 1.3 %pad_select_fusion.6 = bf16[32,32,640]{2,1,0:T(8,128)(2,1)S(1)} fusion(bf16[32,32,640]{2,1,0:T(8,128)(2,1)S(1)} %pad_select_fusion.7, bf16[32,32,638]{2,1,0:T(8,128)(2,1)S(1)} %bitcast.25, pred[32,32]{1,0:T(8,128)(4,1)S(1)} %get-tuple-element.7), kind=kLoop, calls=%fused_computation.16 | loop fusion | flops 655360 | bytes 3929088 | tf_op jit(solution)/shard_map/jit(_where)/select_n | solution.py:33
  36.1 1.3 %pad_select_fusion.5 = bf16[32,32,640]{2,1,0:T(8,128)(2,1)S(1)} fusion(bf16[32,32,640]{2,1,0:T(8,128)(2,1)S(1)} %pad_select_fusion.6, bf16[32,32,636]{2,1,0:T(8,128)(2,1)S(1)} %bitcast.26, pred[32,32]{1,0:T(8,128)(4,1)S(1)} %get-tuple-element.8), kind=kLoop, calls=%fused_computation.15 | loop fusion | flops 655360 | bytes 3924992 | tf_op jit(solution)/shard_map/jit(_where)/select_n | solution.py:33
  37.5 1.3 %pad_select_fusion.4 = bf16[32,32,640]{2,1,0:T(8,128)(2,1)S(1)} fusion(bf16[32,32,640]{2,1,0:T(8,128)(2,1)S(1)} %pad_select_fusion.5, bf16[32,32,632]{2,1,0:T(8,128)(2,1)S(1)} %bitcast.27, pred[32,32]{1,0:T(8,128)(4,1)S(1)} %get-tuple-element.9), kind=kLoop, calls=%fused_computation.14 | loop fusion | flops 655360 | bytes 3916800 | tf_op jit(solution)/shard_map/jit(_where)/select_n | solution.py:33
  38.8 1.3 %pad_select_fusion.3 = bf16[32,32,640]{2,1,0:T(8,128)(2,1)S(1)} fusion(bf16[32,32,640]{2,1,0:T(8,128)(2,1)S(1)} %pad_select_fusion.4, bf16[32,32,624]{2,1,0:T(8,128)(2,1)S(1)} %bitcast.28, pred[32,32]{1,0:T(8,128)(4,1)S(1)} %get-tuple-element.10), kind=kLoop, calls=%fused_computation.13 | loop fusion | flops 655360 | bytes 3900416 | tf_op jit(solution)/shard_map/jit(_where)/select_n | solution.py:33
  40.2 1.3 %pad_select_fusion.2 = bf16[32,32,640]{2,1,0:T(8,128)(2,1)S(1)} fusion(bf16[32,32,640]{2,1,0:T(8,128)(2,1)S(1)} %pad_select_fusion.3, bf16[32,32,608]{2,1,0:T(8,128)(2,1)S(1)} %bitcast.29, pred[32,32]{1,0:T(8,128)(4,1)S(1)} %get-tuple-element.11), kind=kLoop, calls=%fused_computation.12 | loop fusion | flops 655360 | bytes 3867648 | tf_op jit(solution)/shard_map/jit(_where)/select_n | solution.py:33
  41.5 1.3 %pad_select_fusion.1 = bf16[32,32,640]{2,1,0:T(8,128)(2,1)S(1)} fusion(bf16[32,32,640]{2,1,0:T(8,128)(2,1)S(1)} %pad_select_fusion.2, bf16[32,32,576]{2,1,0:T(8,128)(2,1)S(1)} %bitcast.30, pred[32,32]{1,0:T(8,128)(4,1)S(1)} %get-tuple-element.12), kind=kLoop, calls=%fused_computation.11 | loop fusion | flops 655360 | bytes 3802112 | tf_op jit(solution)/shard_map/jit(_where)/select_n | solution.py:33
  42.9 0.1 slice.44
  43.0 0.4 pad_select_fusion
  43.4 4.3 %copy.25 = bf16[32,32,640]{1,2,0:T(8,128)(2,1)} copy(bf16[32,32,640]{2,1,0:T(8,128)(2,1)S(1)} %pad_select_fusion) | data formatting | bytes 2621440
  47.7 6.5 %pad_bitcast_fusion = bf16[82,32,8,32]{3,2,0,1:T(8,128)(2,1)} fusion(bf16[32,32,640]{1,2,0:T(8,128)(2,1)} %copy.25), kind=kLoop, calls=%fused_computation.2 | loop fusion | bytes 2654208 | tf_op jit(solution)/shard_map/transpose | solution.py:57
  54.2 6.0 %copy.19 = bf16[82,32,8,32]{0,3,2,1:T(8,128)(2,1)S(1)} copy(bf16[82,32,8,32]{3,2,0,1:T(8,128)(2,1)} %pad_bitcast_fusion) | data formatting | bytes 2686976 | tf_op jit(solution)/shard_map/transpose | solution.py:57
  60.2 2.6 %copy.20.grouped_ref = bf16[82,32,256]{2,1,0:T(8,128)(2,1)} copy(bf16[82,32,256]{0,2,1:T(8,128)(2,1)S(1)} %bitcast.31) | data formatting | bytes 2686976 | tf_op jit(solution)/shard_map/reshape | solution.py:57
  62.9 7.9 %shard_map.55 = bf16[81,256,256]{2,1,0:T(8,128)(2,1)} custom-call(bf16[82,32,256]{2,1,0:T(8,128)(2,1)} %copy.20.grouped_ref), custom_call_target="tpu_custom_call" | custom-call | tf_op jit(solution)/shard_map/pallas_call | solution.py:63
  70.8 0.1 broadcast_in_dim.102
  70.9 11.7 %fusion.4 = bf16[256,128]{0,1:T(8,128)(2,1)S(1)} fusion(bf16[4,256,208]{1,0,2:T(4,128)(2,1)S(1)} %copy.21, bf16[81,256,256]{2,1,0:T(8,128)(2,1)} %shard_map.55, pred[4,256]{1,0:T(4,128)(4,1)S(1)} %broadcast_in_dim.102), kind=kOutput, calls=%fused_computation.20 | convolution fusion | flops 5436047360 | bytes 11109376 | tf_op jit(solution)/shard_map/conv_general_dilated | solution.py:101
  82.6 0.0 copy-start.2
  82.6 0.1 copy.22
  82.7 0.2 copy.23
  82.9 0.2 copy.24
  83.1 0.1 copy-done.2
  83.2 0.7 scatter_custom_fusion
  83.9 1.2 %gather_fusion = f32[32,1024]{1,0:T(8,128)} fusion(f32[32,1024]{1,0:T(8,128)S(1)} %copy.24, s32[1024]{0:T(1024)S(1)} %pad_clamp_fusion), kind=kCustom, calls=%fused_computation | custom fusion | bytes 262272 | tf_op jit(solution)/shard_map/gather | solution.py:117
  85.2 0.0 reduce-scatter.2.cloned.1.call-update
  85.2 21.5 %reduce-scatter.2.cloned.1.call-done = f32[8,1024]{1,0:T(8,128)} async-done(((f32[32,1024]{1,0:T(8,128)}), f32[8,1024]{1,0:T(8,128)}) %reduce-scatter.2.cloned.1.call-update) | async-done | bytes 32784 | tf_op jit(solution)/shard_map/reduce_scatter | solution.py:118
  106.7 0.9 multiply_reduce_fusion
  107.6 1.4 %broadcast_multiply_fusion = f32[8,1024]{1,0:T(8,128)} fusion(f32[8,1024]{1,0:T(8,128)} %reduce-scatter.2.cloned.1.call-done, f32[8]{0:T(128)S(1)} %add_rsqrt_fusion.1), kind=kLoop, calls=%fused_computation.38 | loop fusion | flops 8192 | bytes 65568 | tf_op jit(solution)/shard_map/mul | solution.py:120
  (13 shorter events, 0.1 us)
Async XLA Ops:
  6.5 100.1 %reduce-scatter.2.cloned.1.call-start = ((), (), s32[]{:S(2)}) async-start(), calls=%async_computation.1 | async-start | bytes 163840 | tf_op jit(solution)/shard_map/reduce_scatter | solution.py:118
  28.7 2.1 %copy-start = (bf16[32,32,512]{2,1,0:T(8,128)(2,1)S(1)}, bf16[32,32,512]{2,1,0:T(8,128)(2,1)}, u32[]{:S(2)}) copy-start(bf16[32,32,512]{2,1,0:T(8,128)(2,1)} %param.6) | copy-start | bytes 3145732
  32.1 0.7 copy-start.1
  82.6 0.7 copy-start.2
Sparse Core Ops, SparseCore 0:
  85.3 21.3 reduce-scatter.1

commit v2 on v1

--- a/solution.py
+++ b/solution.py
@@ -85,11 +85,22 @@
     lags = window - padded_len
     phases = PHASES
     signal = normalize_rows(data)
-    blocks = lax.all_gather(signal, "chan", axis=0, tiled=False)
+    n_chan = lax.axis_size("chan")
+    if n_chan <= 8:
+        me = lax.axis_index("chan")
+        pieces = [signal]
+        for shift in range(1, n_chan):
+            pairs = [(c, (c + shift) % n_chan) for c in range(n_chan)]
+            pieces.append(lax.ppermute(signal, "chan", pairs))
+        blocks = jnp.stack(pieces)
+    else:
+        blocks = lax.all_gather(signal, "chan", axis=0, tiled=False)
     n_blocks = blocks.shape[0]
     shaped = normalize_rows(templates)
     local_chan = stations % ch_local
     target = stations[:, 0] // (ch_local * n_tmpl)
+    if n_chan <= 8:
+        target = (me - target) % n_chan
     hit = local_chan[:, :, None] == jnp.arange(ch_local, dtype=jnp.int32)[None, None, :]
     ordered = jnp.einsum(
         "jki,jkl->jil", hit.astype(jnp.bfloat16), shaped, preferred_element_type=jnp.float32
@@ -110,12 +121,13 @@
     pick = target[None, :] == jnp.arange(n_blocks, dtype=jnp.int32)[:, None]
     chosen = jnp.sum(jnp.where(pick[:, None, :, None], corr, 0.0), axis=0)
     partial_value = jnp.transpose(chosen, (1, 2, 0)).reshape(count, lags)
-    partial_value = partial_value.astype(jnp.bfloat16).astype(jnp.float32)
+    partial_value = partial_value.astype(jnp.bfloat16)
     inverse = (
         jnp.zeros((count,), jnp.int32).at[owner_map[0]].set(jnp.arange(count, dtype=jnp.int32))
     )
-    arranged = partial_value[inverse]
-    stack = lax.psum_scatter(arranged, "tmpl", scatter_dimension=0, tiled=True)
+    arranged = partial_value[inverse].reshape(n_tmpl, count // n_tmpl, lags)
+    received = lax.all_to_all(arranged, "tmpl", 0, 0, tiled=True)
+    stack = jnp.sum(received.astype(jnp.float32), axis=0)
     power = jnp.mean(stack * stack, axis=1, keepdims=True)
     return stack * lax.rsqrt(power + eps)
 

time: 117 us -> 76.6 us (0.65)
  waiting for transfers between devices: 21.5 us -> 0.01 us
  between operations: 13.6 us -> 0.28 us
  blocking collectives: 16.4 us -> 6.68 us
  starting transfers between devices: 0.01 us -> 7.01 us
  local copies, waits for them, and re-layouts: 26.8 us -> 25.1 us
    reduce_scatter x1 -> x0, waiting for transfers between devices: 21.5 us -> none  [shards(): stack = lax.psum_scatter(arranged, 'tmpl', scatter_dimension=0, tiled=True)]
    all_gather x1 -> x0, blocking collectives: 16.4 us -> none  [shards(): blocks = lax.all_gather(signal, 'chan', axis=0, tiled=False)]
    ppermute x0 -> x3, starting transfers between devices: none -> 7.01 us  [shards(): pieces.append(lax.ppermute(signal, 'chan', pairs))]
    all_to_all x0 -> x1, blocking collectives: none -> 6.68 us  [shards(): received = lax.all_to_all(arranged, 'tmpl', 0, 0, tiled=True)]
    transpose x1, local copies, waits for them, and re-layouts: 1.79 us -> 0.11 us  [polyphase_signal(): split = jnp.transpose(split, (0, 3, 1, 2))]
    another operation x0 -> x4, local copies, waits for them, and re-layouts: none -> 1.3 us  [shards(): blocks = jnp.stack(pieces)]
    unnamed x7 -> x5, local copies, waits for them, and re-layouts: 5.01 us -> 4.3 us
  transfers between devices with their start and end apart: 1 -> 3, of which waited for: 1 -> 0; matrix products, arithmetic and copies ran while one was open for 0% -> 48% of each run, Pallas kernels for 0% -> 10%
where the time goes in v2:
time: 76.6 us; the launch traced here: 76 us
  local copies, waits for them, and re-layouts  25.1 us (33%)
  other arithmetic  16.8 us (22%)
  matrix products  12.2 us (16%)
  Pallas kernels  7.93 us (10%)
  starting transfers between devices  7.01 us (9%)
  blocking collectives  6.68 us (9%)
    transpose x2, local copies, waits for them, and re-layouts, polyphase_filters(): jnp.transpose(grouped, (2, 0, 3, 1)).reshape(blocks, count, phases * chans)  12.5 us
    conv_general_dilated x1, matrix products, shards(): lax.conv_general_dilated(lhs, filters, (1,), 'VALID', dimension_numbers=(...  11.7 us
    select_n x8, other arithmetic, place_moveout(): current = jnp.where(active[..., None], moved, current)  9.75 us
    pallas_call x1, Pallas kernels, polyphase_filters(): pl.pallas_call(kernel, grid=(taps // steps,), in_specs=[pl.BlockSpec((blo...  7.93 us
    ppermute x3, starting transfers between devices, shards(): pieces.append(lax.ppermute(signal, 'chan', pairs))  7.01 us
    all_to_all x1, blocking collectives, shards(): received = lax.all_to_all(arranged, 'tmpl', 0, 0, tiled=True)  6.68 us
    unnamed x5, local copies, waits for them, and re-layouts  4.3 us
    reshape x1, local copies, waits for them, and re-layouts, polyphase_filters(): jnp.transpose(grouped, (2, 0, 3, 1)).reshape(blocks, count, phases * chans)  2.62 us
  transfers between devices with their start and end apart: 3, of which 0 were waited for; matrix products, arithmetic and copies ran while one was open for 48% of the time, Pallas kernels for 10%

profile of v2, /device:TPU:0, one launch (start us, length us, event | category | flops | bytes accessed | tf_op | source)
XLA Modules:
  0.0 76.0 jit_solution(13746780625954354970)
XLA Ops:
  0.0 0.0 copy-start
  0.0 1.1 %convert_reduce_fusion.1 = f32[32]{0:T(128)S(1)} fusion(bf16[32,1664]{1,0:T(8,128)(2,1)} %param.5), kind=kLoop, calls=%fused_computation.27 | loop fusion | flops 106464 | bytes 106624 | tf_op jit(solution)/shard_map/reduce_sum | solution.py:19
  1.1 1.1 %fusion.11 = f32[32]{0:T(128)S(1)} fusion(bf16[32,1664]{1,0:T(8,128)(2,1)} %param.5, f32[32]{0:T(128)S(1)} %broadcast_multiply_fusion.2), kind=kLoop, calls=%fused_computation.31 | loop fusion | flops 212960 | bytes 106752 | tf_op jit(solution)/shard_map/reduce_sum | solution.py:20
  2.2 1.0 %fusion.12 = bf16[32,1664]{1,0:T(8,128)(2,1)S(1)} fusion(bf16[32,1664]{1,0:T(8,128)(2,1)} %param.5, f32[32]{0:T(128)S(1)} %add_rsqrt_fusion.2, f32[32]{0:T(128)S(1)} %broadcast_multiply_fusion.2), kind=kLoop, calls=%fused_computation.32 | loop fusion | flops 212992 | bytes 213248 | tf_op jit(solution)/shard_map/convert_element_type | solution.py:21
  3.2 3.1 %collective-permute-start = (bf16[32,1664]{1,0:T(8,128)(2,1)S(1)}, bf16[32,1664]{1,0:T(8,128)(2,1)S(1)}, u32[]{:S(2)}, u32[]{:S(2)}) collective-permute-start(bf16[32,1664]{1,0:T(8,128)(2,1)S(1)} %fusion.12), channel_id=1, source_target_pairs={{0,4},{4,8},{8,12},{12,0},{1,5},{5,9},{9,13},{13,1},{2,6},{6,10},{... | collective-permute-start | bytes 319496 | tf_op jit(solution)/shard_map/ppermute | solution.py:94
  6.3 2.6 %collective-permute-start.1 = (bf16[32,1664]{1,0:T(8,128)(2,1)S(1)}, bf16[32,1664]{1,0:T(8,128)(2,1)S(1)}, u32[]{:S(2)}, u32[]{:S(2)}) collective-permute-start(bf16[32,1664]{1,0:T(8,128)(2,1)S(1)} %fusion.12), channel_id=1, source_target_pairs={{0,8},{4,12},{8,0},{12,4},{1,9},{5,13},{9,1},{13,5},{2,10},{6,14},... | collective-permute-start | bytes 319496 | tf_op jit(solution)/shard_map/ppermute | solution.py:94
  8.9 1.3 %collective-permute-start.2 = (bf16[32,1664]{1,0:T(8,128)(2,1)S(1)}, bf16[32,1664]{1,0:T(8,128)(2,1)S(1)}, u32[]{:S(2)}, u32[]{:S(2)}) collective-permute-start(bf16[32,1664]{1,0:T(8,128)(2,1)S(1)} %fusion.12), channel_id=1, source_target_pairs={{0,12},{4,0},{8,4},{12,8},{1,13},{5,1},{9,5},{13,9},{2,14},{6,2},{... | collective-permute-start | bytes 319496 | tf_op jit(solution)/shard_map/ppermute | solution.py:94
  10.2 0.3 copy.22
  10.5 0.7 add_select_fusion
  11.2 0.8 %slice_reduce_fusion = s32[32]{0:T(128)S(1)} fusion(s32[32,32]{1,0:T(8,128)} %param.7), kind=kLoop, calls=%fused_computation.49 | loop fusion | bytes 256 | tf_op jit(solution)/shard_map/slice | solution.py:101
  12.1 1.3 %select_reduce_fusion = s32[32,32]{1,0:T(8,128)S(1)} fusion(s32[32,32]{1,0:T(8,128)} %param.8, s32[32,32]{1,0:T(8,128)S(1)} %add_select_fusion), kind=kLoop, calls=%fused_computation.24 | loop fusion | flops 97280 | bytes 12288 | tf_op jit(solution)/shard_map/reduce_sum | solution.py:108
  13.5 0.0 copy-done
  13.5 0.2 convert_reduce_fusion
  13.7 0.5 fusion.2
  14.2 0.5 convolution_convert_fusion
  14.8 0.1 pad_slice_fusion
  14.9 1.3 %pad_select_fusion.7 = bf16[32,32,640]{2,1,0:T(8,128)(2,1)S(1)} fusion(bf16[32,32,639]{2,1,0:T(8,128)(2,1)S(1)} %pad_slice_fusion, pred[32,32]{1,0:T(8,128)(4,1)S(1)} %get-tuple-element.6, bf16[32,32,512]{2,1,0:T(8,128)(2,1)S(1)} %convolution_convert_fusion), kind=kLoop, calls=%fused_computation.17 | loop fusion | flops 655360 | bytes 3668992 | tf_op jit(solution)/shard_map/jit(_where)/select_n | solution.py:33
  16.2 1.3 %pad_select_fusion.6 = bf16[32,32,640]{2,1,0:T(8,128)(2,1)S(1)} fusion(bf16[32,32,640]{2,1,0:T(8,128)(2,1)S(1)} %pad_select_fusion.7, bf16[32,32,638]{2,1,0:T(8,128)(2,1)S(1)} %bitcast.29, pred[32,32]{1,0:T(8,128)(4,1)S(1)} %get-tuple-element.7), kind=kLoop, calls=%fused_computation.16 | loop fusion | flops 655360 | bytes 3929088 | tf_op jit(solution)/shard_map/jit(_where)/select_n | solution.py:33
  17.6 1.3 %pad_select_fusion.5 = bf16[32,32,640]{2,1,0:T(8,128)(2,1)S(1)} fusion(bf16[32,32,640]{2,1,0:T(8,128)(2,1)S(1)} %pad_select_fusion.6, bf16[32,32,636]{2,1,0:T(8,128)(2,1)S(1)} %bitcast.30, pred[32,32]{1,0:T(8,128)(4,1)S(1)} %get-tuple-element.8), kind=kLoop, calls=%fused_computation.15 | loop fusion | flops 655360 | bytes 3924992 | tf_op jit(solution)/shard_map/jit(_where)/select_n | solution.py:33
  18.9 1.3 %pad_select_fusion.4 = bf16[32,32,640]{2,1,0:T(8,128)(2,1)S(1)} fusion(bf16[32,32,640]{2,1,0:T(8,128)(2,1)S(1)} %pad_select_fusion.5, bf16[32,32,632]{2,1,0:T(8,128)(2,1)S(1)} %bitcast.31, pred[32,32]{1,0:T(8,128)(4,1)S(1)} %get-tuple-element.9), kind=kLoop, calls=%fused_computation.14 | loop fusion | flops 655360 | bytes 3916800 | tf_op jit(solution)/shard_map/jit(_where)/select_n | solution.py:33
  20.3 1.3 %pad_select_fusion.3 = bf16[32,32,640]{2,1,0:T(8,128)(2,1)S(1)} fusion(bf16[32,32,640]{2,1,0:T(8,128)(2,1)S(1)} %pad_select_fusion.4, bf16[32,32,624]{2,1,0:T(8,128)(2,1)S(1)} %bitcast.32, pred[32,32]{1,0:T(8,128)(4,1)S(1)} %get-tuple-element.10), kind=kLoop, calls=%fused_computation.13 | loop fusion | flops 655360 | bytes 3900416 | tf_op jit(solution)/shard_map/jit(_where)/select_n | solution.py:33
  21.6 1.3 %pad_select_fusion.2 = bf16[32,32,640]{2,1,0:T(8,128)(2,1)S(1)} fusion(bf16[32,32,640]{2,1,0:T(8,128)(2,1)S(1)} %pad_select_fusion.3, bf16[32,32,608]{2,1,0:T(8,128)(2,1)S(1)} %bitcast.33, pred[32,32]{1,0:T(8,128)(4,1)S(1)} %get-tuple-element.11), kind=kLoop, calls=%fused_computation.12 | loop fusion | flops 655360 | bytes 3867648 | tf_op jit(solution)/shard_map/jit(_where)/select_n | solution.py:33
  23.0 1.3 %pad_select_fusion.1 = bf16[32,32,640]{2,1,0:T(8,128)(2,1)S(1)} fusion(bf16[32,32,640]{2,1,0:T(8,128)(2,1)S(1)} %pad_select_fusion.2, bf16[32,32,576]{2,1,0:T(8,128)(2,1)S(1)} %bitcast.34, pred[32,32]{1,0:T(8,128)(4,1)S(1)} %get-tuple-element.12), kind=kLoop, calls=%fused_computation.11 | loop fusion | flops 655360 | bytes 3802112 | tf_op jit(solution)/shard_map/jit(_where)/select_n | solution.py:33
  24.3 0.1 slice.44
  24.4 0.4 pad_select_fusion
  24.8 4.3 %copy.38 = bf16[32,32,640]{1,2,0:T(8,128)(2,1)} copy(bf16[32,32,640]{2,1,0:T(8,128)(2,1)S(1)} %pad_select_fusion) | data formatting | bytes 2621440
  29.1 6.5 %pad_bitcast_fusion = bf16[82,32,8,32]{3,2,0,1:T(8,128)(2,1)} fusion(bf16[32,32,640]{1,2,0:T(8,128)(2,1)} %copy.38), kind=kLoop, calls=%fused_computation.2 | loop fusion | bytes 2654208 | tf_op jit(solution)/shard_map/transpose | solution.py:57
  35.7 6.0 %copy.32 = bf16[82,32,8,32]{0,3,2,1:T(8,128)(2,1)S(1)} copy(bf16[82,32,8,32]{3,2,0,1:T(8,128)(2,1)} %pad_bitcast_fusion) | data formatting | bytes 2686976 | tf_op jit(solution)/shard_map/transpose | solution.py:57
  41.7 2.6 %copy.33.grouped_ref = bf16[82,32,256]{2,1,0:T(8,128)(2,1)} copy(bf16[82,32,256]{0,2,1:T(8,128)(2,1)S(1)} %bitcast.35) | data formatting | bytes 2686976 | tf_op jit(solution)/shard_map/reshape | solution.py:57
  44.3 0.0 copy-start.1
  44.3 7.9 %shard_map.55 = bf16[81,256,256]{2,1,0:T(8,128)(2,1)} custom-call(bf16[82,32,256]{2,1,0:T(8,128)(2,1)} %copy.33.grouped_ref), custom_call_target="tpu_custom_call" | custom-call | tf_op jit(solution)/shard_map/pallas_call | solution.py:63
  52.2 0.3 copy.26
  52.6 0.1 broadcast_in_dim.102
  52.7 0.0 copy-done.1
  52.7 0.7 scatter_custom_fusion
  53.4 0.0 collective-permute-done
  53.4 0.3 copy.23
  53.7 0.3 copy.27
  54.0 0.0 collective-permute-done.1
  54.0 0.3 copy.24
  54.3 0.3 copy.28
  54.6 0.0 collective-permute-done.2
  54.6 0.3 copy.25
  54.9 0.3 copy.29
  55.2 0.1 maximum_bitcast_fusion
  55.4 0.1 copy.30
  55.5 0.3 copy.34
  55.8 11.7 %fusion.4 = bf16[256,128]{0,1:T(8,128)(2,1)S(1)} fusion(bf16[4,256,208]{1,0,2:T(4,128)(2,1)S(1)} %copy.34, bf16[81,256,256]{2,1,0:T(8,128)(2,1)} %shard_map.55, pred[4,256]{1,0:T(4,128)(4,1)S(1)} %broadcast_in_dim.102), kind=kOutput, calls=%fused_computation.20 | convolution fusion | flops 5436047360 | bytes 11109376 | tf_op jit(solution)/shard_map/conv_general_dilated | solution.py:112
  67.4 0.1 copy.35
  67.5 0.2 copy.36
  67.7 0.1 copy.37
  67.9 0.6 gather_fusion
  68.5 6.7 %all_to_all.5 = bf16[4,8,1024]{2,1,0:T(8,128)(2,1)S(1)} all-to-all(bf16[4,8,1024]{2,1,0:T(8,128)(2,1)S(1)} %bitcast.43), channel_id=1, replica_groups=mesh['grp'=2,'chan'=4,'tmpl'=4] {'tmpl'}, dimensions={0} | all-to-all | bytes 131072 | tf_op jit(solution)/shard_map/all_to_all | solution.py:129
  75.2 0.1 multiply_reduce_fusion
  75.3 0.7 broadcast_multiply_fusion
  (14 shorter events, 0.1 us)
Async XLA Ops:
  0.0 13.5 %copy-start = (bf16[32,32,512]{2,1,0:T(8,128)(2,1)S(1)}, bf16[32,32,512]{2,1,0:T(8,128)(2,1)}, u32[]{:S(2)}) copy-start(bf16[32,32,512]{2,1,0:T(8,128)(2,1)} %param.6) | copy-start | bytes 3145732
  3.2 50.2 %collective-permute-start = (bf16[32,1664]{1,0:T(8,128)(2,1)S(1)}, bf16[32,1664]{1,0:T(8,128)(2,1)S(1)}, u32[]{:S(2)}, u32[]{:S(2)}) collective-permute-start(bf16[32,1664]{1,0:T(8,128)(2,1)S(1)} %fusion.12), channel_id=1, source_target_pairs={{0,4},{4,8},{8,12},{12,0},{1,5},{5,9},{9,13},{13,1},{2,6},{6,10},{... | collective-permute-start | bytes 319496 | tf_op jit(solution)/shard_map/ppermute | solution.py:94
  6.3 47.7 %collective-permute-start.1 = (bf16[32,1664]{1,0:T(8,128)(2,1)S(1)}, bf16[32,1664]{1,0:T(8,128)(2,1)S(1)}, u32[]{:S(2)}, u32[]{:S(2)}) collective-permute-start(bf16[32,1664]{1,0:T(8,128)(2,1)S(1)} %fusion.12), channel_id=1, source_target_pairs={{0,8},{4,12},{8,0},{12,4},{1,9},{5,13},{9,1},{13,5},{2,10},{6,14},... | collective-permute-start | bytes 319496 | tf_op jit(solution)/shard_map/ppermute | solution.py:94
  8.9 45.7 %collective-permute-start.2 = (bf16[32,1664]{1,0:T(8,128)(2,1)S(1)}, bf16[32,1664]{1,0:T(8,128)(2,1)S(1)}, u32[]{:S(2)}, u32[]{:S(2)}) collective-permute-start(bf16[32,1664]{1,0:T(8,128)(2,1)S(1)} %fusion.12), channel_id=1, source_target_pairs={{0,12},{4,0},{8,4},{12,8},{1,13},{5,1},{9,5},{13,9},{2,14},{6,2},{... | collective-permute-start | bytes 319496 | tf_op jit(solution)/shard_map/ppermute | solution.py:94
  44.3 8.4 %copy-start.1 = (s32[1,32]{1,0:T(1,128)S(1)}, s32[1,32]{1,0:T(1,128)}, u32[]{:S(2)}) copy-start(s32[1,32]{1,0:T(1,128)} %param.9) | copy-start | bytes 388

commit v3 on v2

--- a/solution.py
+++ b/solution.py
@@ -25,12 +25,18 @@
     extra = padded_len - rows.shape[-1]
     tail = jnp.zeros(rows.shape[:-1] + (extra,), rows.dtype)
     current = jnp.concatenate([rows, tail], axis=-1)
-    for bit_number in range(OFF.bit_length()):
-        step_len = 1 << bit_number
-        lead = jnp.zeros(rows.shape[:-1] + (step_len,), rows.dtype)
-        moved = jnp.concatenate([lead, current[..., : padded_len - step_len]], axis=-1)
-        active = shifts >> bit_number & 1 == 1
-        current = jnp.where(active[..., None], moved, current)
+    bits = OFF.bit_length()
+    for low in range(0, bits, 3):
+        width = min(3, bits - low)
+        digit = (shifts >> low) & ((1 << width) - 1)
+        padded = jnp.pad(current, [(0, 0)] * (rows.ndim - 1) + [(((1 << width) - 1) << low, 0)])
+        total = padded.shape[-1]
+        result = current
+        for value in range(1, 1 << width):
+            start = total - padded_len - (value << low)
+            moved = padded[..., start : start + padded_len]
+            result = jnp.where((digit == value)[..., None], moved, result)
+        current = result
     return current
 
 
@@ -53,8 +59,8 @@
     front = phases - 1
     blocks = taps + 1
     padded = jnp.pad(placed, ((0, 0), (0, 0), (front, blocks * phases - padded_len - front)))
-    grouped = padded.reshape(count, chans, blocks, phases)
-    grouped = jnp.transpose(grouped, (2, 0, 3, 1)).reshape(blocks, count, phases * chans)
+    grouped = jnp.transpose(padded, (0, 2, 1)).reshape(count, blocks, phases * chans)
+    grouped = jnp.transpose(grouped, (1, 0, 2))
     steps = next(d for d in (9, 3, 1) if taps % d == 0)
     width = phases * chans
     kernel = functools.partial(

time: 76.6 us -> 73.3 us (0.957)
  local copies, waits for them, and re-layouts: 25.1 us -> 19 us
  other arithmetic: 16.8 us -> 19.7 us
    transpose x2, local copies, waits for them, and re-layouts: 12.5 us -> 5.01 us  [polyphase_filters(): jnp.transpose(padded, (0, 2, 1)).reshape(count, blocks, phases * chans)]
    reshape x1 -> x2, local copies, waits for them, and re-layouts: 2.62 us -> 8.27 us  [polyphase_filters(): jnp.transpose(padded, (0, 2, 1)).reshape(count, blocks, phases * chans)]
    unnamed x5 -> x4, local copies, waits for them, and re-layouts: 4.3 us -> 0.01 us
    select_n x8 -> x3, other arithmetic: 9.75 us -> 12.6 us  [place_moveout(): result = jnp.where((digit == value)[..., None], moved, result)]
  transfers between devices with their start and end apart: 3 -> 3, of which waited for: 0 -> 0; matrix products, arithmetic and copies ran while one was open for 48% -> 45% of each run, Pallas kernels for 10% -> 11%
where the time goes in v3:
time: 73.3 us; the launch traced here: 72.8 us
  other arithmetic  19.7 us (27%)
  local copies, waits for them, and re-layouts  19 us (26%)
  matrix products  12.2 us (17%)
  Pallas kernels  7.93 us (11%)
  starting transfers between devices  7.01 us (10%)
  blocking collectives  6.68 us (9%)
    select_n x3, other arithmetic, place_moveout(): result = jnp.where((digit == value)[..., None], moved, result)  12.6 us
    conv_general_dilated x1, matrix products, shards(): lax.conv_general_dilated(lhs, filters, (1,), 'VALID', dimension_numbers=(...  11.7 us
    reshape x2, local copies, waits for them, and re-layouts, polyphase_filters(): jnp.transpose(padded, (0, 2, 1)).reshape(count, blocks, phases * chans)  8.27 us
    pallas_call x1, Pallas kernels, polyphase_filters(): pl.pallas_call(kernel, grid=(taps // steps,), in_specs=[pl.BlockSpec((blo...  7.93 us
    ppermute x3, starting transfers between devices, shards(): pieces.append(lax.ppermute(signal, 'chan', pairs))  7.01 us
    all_to_all x1, blocking collectives, shards(): received = lax.all_to_all(arranged, 'tmpl', 0, 0, tiled=True)  6.68 us
    transpose x2, local copies, waits for them, and re-layouts, polyphase_filters(): jnp.transpose(padded, (0, 2, 1)).reshape(count, blocks, phases * chans)  5.01 us
    reduce_sum x2, other arithmetic, normalize_rows(): scale = lax.rsqrt(jnp.mean(centred * centred, axis=-1, keepdims=True) + eps)  1.62 us
  transfers between devices with their start and end apart: 3, of which 0 were waited for; matrix products, arithmetic and copies ran while one was open for 45% of the time, Pallas kernels for 11%

profile of v3, /device:TPU:0, one launch (start us, length us, event | category | flops | bytes accessed | tf_op | source)
XLA Modules:
  0.0 72.8 jit_solution(17637506772875471609)
XLA Ops:
  0.0 0.0 copy-start
  0.0 1.1 %convert_reduce_fusion.1 = f32[32]{0:T(128)S(1)} fusion(bf16[32,1664]{1,0:T(8,128)(2,1)} %param.5), kind=kLoop, calls=%fused_computation.37 | loop fusion | flops 106464 | bytes 106624 | tf_op jit(solution)/shard_map/reduce_sum | solution.py:19
  1.1 1.1 %fusion.14 = f32[32]{0:T(128)S(1)} fusion(bf16[32,1664]{1,0:T(8,128)(2,1)} %param.5, f32[32]{0:T(128)S(1)} %broadcast_multiply_fusion.2), kind=kLoop, calls=%fused_computation.41 | loop fusion | flops 212960 | bytes 106752 | tf_op jit(solution)/shard_map/reduce_sum | solution.py:20
  2.2 1.0 %fusion.15 = bf16[32,1664]{1,0:T(8,128)(2,1)S(1)} fusion(bf16[32,1664]{1,0:T(8,128)(2,1)} %param.5, f32[32]{0:T(128)S(1)} %add_rsqrt_fusion.2, f32[32]{0:T(128)S(1)} %broadcast_multiply_fusion.2), kind=kLoop, calls=%fused_computation.42 | loop fusion | flops 212992 | bytes 213248 | tf_op jit(solution)/shard_map/convert_element_type | solution.py:21
  3.2 3.1 %collective-permute-start = (bf16[32,1664]{1,0:T(8,128)(2,1)S(1)}, bf16[32,1664]{1,0:T(8,128)(2,1)S(1)}, u32[]{:S(2)}, u32[]{:S(2)}) collective-permute-start(bf16[32,1664]{1,0:T(8,128)(2,1)S(1)} %fusion.15), channel_id=1, source_target_pairs={{0,4},{4,8},{8,12},{12,0},{1,5},{5,9},{9,13},{13,1},{2,6},{6,10},{... | collective-permute-start | bytes 319496 | tf_op jit(solution)/shard_map/ppermute | solution.py:100
  6.3 2.6 %collective-permute-start.1 = (bf16[32,1664]{1,0:T(8,128)(2,1)S(1)}, bf16[32,1664]{1,0:T(8,128)(2,1)S(1)}, u32[]{:S(2)}, u32[]{:S(2)}) collective-permute-start(bf16[32,1664]{1,0:T(8,128)(2,1)S(1)} %fusion.15), channel_id=1, source_target_pairs={{0,8},{4,12},{8,0},{12,4},{1,9},{5,13},{9,1},{13,5},{2,10},{6,14},... | collective-permute-start | bytes 319496 | tf_op jit(solution)/shard_map/ppermute | solution.py:100
  8.9 1.3 %collective-permute-start.2 = (bf16[32,1664]{1,0:T(8,128)(2,1)S(1)}, bf16[32,1664]{1,0:T(8,128)(2,1)S(1)}, u32[]{:S(2)}, u32[]{:S(2)}) collective-permute-start(bf16[32,1664]{1,0:T(8,128)(2,1)S(1)} %fusion.15), channel_id=1, source_target_pairs={{0,12},{4,0},{8,4},{12,8},{1,13},{5,1},{9,5},{13,9},{2,14},{6,2},{... | collective-permute-start | bytes 319496 | tf_op jit(solution)/shard_map/ppermute | solution.py:100
  10.2 0.3 copy.20
  10.5 0.7 %add_select_fusion = s32[32,32]{1,0:T(8,128)S(1)} fusion(s32[32,32]{1,0:T(8,128)} %param.7), kind=kLoop, calls=%fused_computation.45 | loop fusion | flops 11264 | bytes 8192 | tf_op jit(solution)/shard_map/jit(remainder)/select_n | solution.py:106
  11.2 0.8 %slice_reduce_fusion = s32[32]{0:T(128)S(1)} fusion(s32[32,32]{1,0:T(8,128)} %param.7), kind=kLoop, calls=%fused_computation.54 | loop fusion | bytes 256 | tf_op jit(solution)/shard_map/slice | solution.py:107
  12.1 1.3 %select_reduce_fusion = s32[32,32]{1,0:T(8,128)S(1)} fusion(s32[32,32]{1,0:T(8,128)} %param.8, s32[32,32]{1,0:T(8,128)S(1)} %add_select_fusion), kind=kLoop, calls=%fused_computation.34 | loop fusion | flops 97280 | bytes 12288 | tf_op jit(solution)/shard_map/reduce_sum | solution.py:114
  13.5 0.0 copy-done
  13.5 0.2 convert_reduce_fusion
  13.7 0.5 fusion.2
  14.3 0.5 convolution_convert_fusion
  14.8 0.1 concatenate.4
  14.9 4.9 %select_select_fusion.1 = bf16[32,32,640]{2,1,0:T(8,128)(2,1)S(1)} fusion(bf16[32,32,640]{2,1,0:T(8,128)(2,1)S(1)} %concatenate.4, pred[32,32]{1,0:T(8,128)(4,1)S(1)} %get-tuple-element.11, pred[32,32]{1,0:T(8,128)(4,1)S(1)} %get-tuple-element.10, pred[32,32]{1,0:T(8,128)(4,1)S(1)} %get-tuple-element.9, pred[32,32]{1,0:T(8,128)(4,1)S(1)} %get-tuple-element.8, ...), kind=kLoop, calls=%fused_computation.23 | loop fusion | flops 4587520 | bytes 2628608 | tf_op jit(solution)/shard_map/jit(_where)/select_n | solution.py:38
  19.9 4.9 %select_select_fusion = bf16[32,32,640]{2,1,0:T(8,128)(2,1)S(1)} fusion(bf16[32,32,640]{2,1,0:T(8,128)(2,1)S(1)} %select_select_fusion.1, pred[32,32]{1,0:T(8,128)(4,1)S(1)} %get-tuple-element.17, pred[32,32]{1,0:T(8,128)(4,1)S(1)} %get-tuple-element.16, pred[32,32]{1,0:T(8,128)(4,1)S(1)} %get-tuple-element.15, pred[32,32]{1,0:T(8,128)(4,1)S(1)} %get-tuple-element.14, ...), kind=kLoop, calls=%fused_computation.17 | loop fusion | flops 4587520 | bytes 2628608 | tf_op jit(solution)/shard_map/jit(_where)/select_n | solution.py:38
  24.8 2.8 %fusion.4 = bf16[32,32,640]{2,1,0:T(8,128)(2,1)S(1)} fusion(bf16[32,32,640]{2,1,0:T(8,128)(2,1)S(1)} %select_select_fusion, pred[32,32]{1,0:T(8,128)(4,1)S(1)} %get-tuple-element.19, pred[32,32]{1,0:T(8,128)(4,1)S(1)} %get-tuple-element.18, pred[32,32]{1,0:T(8,128)(4,1)S(1)} %get-tuple-element.5), kind=kLoop, calls=%fused_computation.14 | loop fusion | flops 1966080 | bytes 2624512 | tf_op jit(solution)/shard_map/jit(_where)/select_n | solution.py:38
  27.6 0.7 %pad_bitcast_fusion = bf16[32,656,32]{1,2,0:T(8,128)(2,1)S(1)} fusion(bf16[32,32,640]{2,1,0:T(8,128)(2,1)S(1)} %fusion.4), kind=kLoop, calls=%fused_computation.11 | loop fusion | bytes 2654208 | tf_op jit(solution)/shard_map/transpose | solution.py:62
  28.3 4.3 %copy.29 = bf16[32,656,32]{2,1,0:T(8,128)(2,1)} copy(bf16[32,656,32]{1,2,0:T(8,128)(2,1)S(1)} %pad_bitcast_fusion) | data formatting | bytes 2686976 | tf_op jit(solution)/shard_map/transpose | solution.py:62
  32.6 6.9 %reshape.202 = bf16[32,82,256]{2,1,0:T(8,128)(2,1)S(1)} reshape(bf16[32,656,32]{2,1,0:T(8,128)(2,1)} %copy.29) | data formatting | bytes 2686976 | tf_op jit(solution)/shard_map/reshape | solution.py:62
  39.5 1.4 %copy.36 = bf16[32,82,256]{2,0,1:T(8,128)(2,1)} copy(bf16[32,82,256]{2,1,0:T(8,128)(2,1)S(1)} %reshape.202) | data formatting | bytes 2686976 | tf_op jit(solution)/shard_map/reshape | solution.py:62
  40.9 0.0 copy-start.1
  40.9 7.9 %shard_map.55 = bf16[81,256,256]{2,1,0:T(8,128)(2,1)} custom-call(bf16[82,32,256]{2,1,0:T(8,128)(2,1)} %bitcast.23), custom_call_target="tpu_custom_call" | custom-call | tf_op jit(solution)/shard_map/pallas_call | solution.py:69
  48.8 0.3 copy.24
  49.2 0.1 broadcast_in_dim.150
  49.3 0.0 copy-done.1
  49.3 0.9 %scatter_custom_fusion = s32[32]{0:T(128)S(1)} fusion(s32[32]{0:T(128)S(1)} %fusion.21, s32[32]{0:T(128)S(1)} %iota.15, s32[]{:T(128)} %constant.66.clone.1), kind=kCustom, calls=%fused_computation.89 | custom fusion | bytes 132 | tf_op jit(solution)/shard_map/scatter | solution.py:132
  50.2 0.0 collective-permute-done
  50.2 0.3 copy.21
  50.4 0.3 copy.25
  50.8 0.0 collective-permute-done.1
  50.8 0.3 copy.22
  51.0 0.3 copy.26
  51.4 0.0 collective-permute-done.2
  51.4 0.3 copy.23
  51.7 0.3 copy.27
  52.0 0.1 maximum_bitcast_fusion
  52.1 0.1 copy.28
  52.2 0.3 copy.31
  52.5 11.7 %fusion.7 = bf16[256,128]{0,1:T(8,128)(2,1)S(1)} fusion(bf16[4,256,208]{1,0,2:T(4,128)(2,1)S(1)} %copy.31, bf16[81,256,256]{2,1,0:T(8,128)(2,1)} %shard_map.55, pred[4,256]{1,0:T(4,128)(4,1)S(1)} %broadcast_in_dim.150), kind=kOutput, calls=%fused_computation.30 | convolution fusion | flops 5436047360 | bytes 11109376 | tf_op jit(solution)/shard_map/conv_general_dilated | solution.py:118
  64.2 0.1 copy.32
  64.3 0.2 copy.33
  64.5 0.1 copy.34
  64.6 0.6 gather_fusion
  65.3 6.7 %all_to_all.5 = bf16[4,8,1024]{2,1,0:T(8,128)(2,1)S(1)} all-to-all(bf16[4,8,1024]{2,1,0:T(8,128)(2,1)S(1)} %bitcast.31), channel_id=1, replica_groups=mesh['grp'=2,'chan'=4,'tmpl'=4] {'tmpl'}, dimensions={0} | all-to-all | bytes 131072 | tf_op jit(solution)/shard_map/all_to_all | solution.py:135
  72.0 0.1 multiply_reduce_fusion
  72.1 0.7 broadcast_multiply_fusion
  (14 shorter events, 0.1 us)
Async XLA Ops:
  0.0 13.5 %copy-start = (bf16[32,32,512]{2,1,0:T(8,128)(2,1)S(1)}, bf16[32,32,512]{2,1,0:T(8,128)(2,1)}, u32[]{:S(2)}) copy-start(bf16[32,32,512]{2,1,0:T(8,128)(2,1)} %param.6) | copy-start | bytes 3145732
  3.2 46.9 %collective-permute-start = (bf16[32,1664]{1,0:T(8,128)(2,1)S(1)}, bf16[32,1664]{1,0:T(8,128)(2,1)S(1)}, u32[]{:S(2)}, u32[]{:S(2)}) collective-permute-start(bf16[32,1664]{1,0:T(8,128)(2,1)S(1)} %fusion.15), channel_id=1, source_target_pairs={{0,4},{4,8},{8,12},{12,0},{1,5},{5,9},{9,13},{13,1},{2,6},{6,10},{... | collective-permute-start | bytes 319496 | tf_op jit(solution)/shard_map/ppermute | solution.py:100
  6.3 44.5 %collective-permute-start.1 = (bf16[32,1664]{1,0:T(8,128)(2,1)S(1)}, bf16[32,1664]{1,0:T(8,128)(2,1)S(1)}, u32[]{:S(2)}, u32[]{:S(2)}) collective-permute-start(bf16[32,1664]{1,0:T(8,128)(2,1)S(1)} %fusion.15), channel_id=1, source_target_pairs={{0,8},{4,12},{8,0},{12,4},{1,9},{5,13},{9,1},{13,5},{2,10},{6,14},... | collective-permute-start | bytes 319496 | tf_op jit(solution)/shard_map/ppermute | solution.py:100
  8.9 42.5 %collective-permute-start.2 = (bf16[32,1664]{1,0:T(8,128)(2,1)S(1)}, bf16[32,1664]{1,0:T(8,128)(2,1)S(1)}, u32[]{:S(2)}, u32[]{:S(2)}) collective-permute-start(bf16[32,1664]{1,0:T(8,128)(2,1)S(1)} %fusion.15), channel_id=1, source_target_pairs={{0,12},{4,0},{8,4},{12,8},{1,13},{5,1},{9,5},{13,9},{2,14},{6,2},{... | collective-permute-start | bytes 319496 | tf_op jit(solution)/shard_map/ppermute | solution.py:100
  40.9 8.4 %copy-start.1 = (s32[1,32]{1,0:T(1,128)S(1)}, s32[1,32]{1,0:T(1,128)}, u32[]{:S(2)}) copy-start(s32[1,32]{1,0:T(1,128)} %param.9) | copy-start | bytes 388

commit v4 on v2

--- a/solution.py
+++ b/solution.py
@@ -48,13 +48,13 @@
 
 
 def polyphase_filters(placed, phases):
-    count, chans, padded_len = placed.shape
+    count, padded_len, chans = placed.shape
     taps = padded_len // phases + 1
     front = phases - 1
     blocks = taps + 1
-    padded = jnp.pad(placed, ((0, 0), (0, 0), (front, blocks * phases - padded_len - front)))
-    grouped = padded.reshape(count, chans, blocks, phases)
-    grouped = jnp.transpose(grouped, (2, 0, 3, 1)).reshape(blocks, count, phases * chans)
+    padded = jnp.pad(placed, ((0, 0), (front, blocks * phases - padded_len - front), (0, 0)))
+    grouped = padded.reshape(count, blocks, phases * chans)
+    grouped = jnp.transpose(grouped, (1, 0, 2))
     steps = next(d for d in (9, 3, 1) if taps % d == 0)
     width = phases * chans
     kernel = functools.partial(
@@ -102,11 +102,10 @@
     if n_chan <= 8:
         target = (me - target) % n_chan
     hit = local_chan[:, :, None] == jnp.arange(ch_local, dtype=jnp.int32)[None, None, :]
-    ordered = jnp.einsum(
-        "jki,jkl->jil", hit.astype(jnp.bfloat16), shaped, preferred_element_type=jnp.float32
+    moved = place_moveout(shaped, offsets, padded_len)
+    placed = jnp.einsum(
+        "jki,jkl->jli", hit.astype(jnp.bfloat16), moved, preferred_element_type=jnp.float32
     ).astype(jnp.bfloat16)
-    ordered_shift = jnp.sum(jnp.where(hit, offsets[:, :, None], 0), axis=1)
-    placed = place_moveout(ordered, ordered_shift, padded_len)
     filters = polyphase_filters(placed, phases)
     lhs = polyphase_signal(blocks, phases)
     corr = lax.conv_general_dilated(

time: 76.6 us -> 75.6 us (0.987)
    transpose x2 -> x0, local copies, waits for them, and re-layouts: 12.5 us -> none  [polyphase_filters(): jnp.transpose(grouped, (2, 0, 3, 1)).reshape(blocks, count, phases * chans)]
    pad x0 -> x1, local copies, waits for them, and re-layouts: none -> 6.54 us  [polyphase_filters(): jnp.pad(placed, ((0, 0), (front, blocks * phases - padded_len - front), (...]
    reshape x1 -> x2, local copies, waits for them, and re-layouts: 2.62 us -> 8.27 us  [polyphase_filters(): grouped = padded.reshape(count, blocks, phases * chans)]
    reduce_sum x1 -> x0, other arithmetic: 1.34 us -> none  [shards(): ordered_shift = jnp.sum(jnp.where(hit, offsets[:, :, None], 0), axis=1)]
    select_n x8 -> x7, other arithmetic: 9.75 us -> 9.37 us  [place_moveout(): current = jnp.where(active[..., None], moved, current)]
  transfers between devices with their start and end apart: 3 -> 3, of which waited for: 0 -> 0; matrix products, arithmetic and copies ran while one was open for 48% -> 47% of each run, Pallas kernels for 10% -> 11%
where the time goes in v4:
time: 75.6 us; the launch traced here: 75.1 us
  local copies, waits for them, and re-layouts  24.7 us (33%)
  other arithmetic  16.1 us (21%)
  matrix products  12.3 us (16%)
  Pallas kernels  7.93 us (10%)
  starting transfers between devices  7.01 us (9%)
  blocking collectives  6.68 us (9%)
    conv_general_dilated x1, matrix products, shards(): lax.conv_general_dilated(lhs, filters, (1,), 'VALID', dimension_numbers=(...  11.7 us
    select_n x7, other arithmetic, place_moveout(): current = jnp.where(active[..., None], moved, current)  9.37 us
    reshape x2, local copies, waits for them, and re-layouts, polyphase_filters(): grouped = padded.reshape(count, blocks, phases * chans)  8.27 us
    pallas_call x1, Pallas kernels, polyphase_filters(): pl.pallas_call(kernel, grid=(taps // steps,), in_specs=[pl.BlockSpec((blo...  7.93 us
    ppermute x3, starting transfers between devices, shards(): pieces.append(lax.ppermute(signal, 'chan', pairs))  7.01 us
    all_to_all x1, blocking collectives, shards(): received = lax.all_to_all(arranged, 'tmpl', 0, 0, tiled=True)  6.68 us
    pad x1, local copies, waits for them, and re-layouts, polyphase_filters(): jnp.pad(placed, ((0, 0), (front, blocks * phases - padded_len - front), (...  6.54 us
    unnamed x5, local copies, waits for them, and re-layouts  4.3 us
  transfers between devices with their start and end apart: 3, of which 0 were waited for; matrix products, arithmetic and copies ran while one was open for 47% of the time, Pallas kernels for 11%

profile of v4, /device:TPU:0, one launch (start us, length us, event | category | flops | bytes accessed | tf_op | source)
XLA Modules:
  0.0 75.1 jit_solution(14196143958209316625)
XLA Ops:
  0.0 0.0 copy-start
  0.0 1.1 %convert_reduce_fusion.1 = f32[32]{0:T(128)S(1)} fusion(bf16[32,1664]{1,0:T(8,128)(2,1)} %param.5), kind=kLoop, calls=%fused_computation.26 | loop fusion | flops 106464 | bytes 106624 | tf_op jit(solution)/shard_map/reduce_sum | solution.py:19
  1.1 1.1 %fusion.11 = f32[32]{0:T(128)S(1)} fusion(bf16[32,1664]{1,0:T(8,128)(2,1)} %param.5, f32[32]{0:T(128)S(1)} %broadcast_multiply_fusion.2), kind=kLoop, calls=%fused_computation.30 | loop fusion | flops 212960 | bytes 106752 | tf_op jit(solution)/shard_map/reduce_sum | solution.py:20
  2.2 1.0 %fusion.12 = bf16[32,1664]{1,0:T(8,128)(2,1)S(1)} fusion(bf16[32,1664]{1,0:T(8,128)(2,1)} %param.5, f32[32]{0:T(128)S(1)} %add_rsqrt_fusion.2, f32[32]{0:T(128)S(1)} %broadcast_multiply_fusion.2), kind=kLoop, calls=%fused_computation.31 | loop fusion | flops 212992 | bytes 213248 | tf_op jit(solution)/shard_map/convert_element_type | solution.py:21
  3.2 3.1 %collective-permute-start = (bf16[32,1664]{1,0:T(8,128)(2,1)S(1)}, bf16[32,1664]{1,0:T(8,128)(2,1)S(1)}, u32[]{:S(2)}, u32[]{:S(2)}) collective-permute-start(bf16[32,1664]{1,0:T(8,128)(2,1)S(1)} %fusion.12), channel_id=1, source_target_pairs={{0,4},{4,8},{8,12},{12,0},{1,5},{5,9},{9,13},{13,1},{2,6},{6,10},{... | collective-permute-start | bytes 319496 | tf_op jit(solution)/shard_map/ppermute | solution.py:94
  6.3 2.6 %collective-permute-start.1 = (bf16[32,1664]{1,0:T(8,128)(2,1)S(1)}, bf16[32,1664]{1,0:T(8,128)(2,1)S(1)}, u32[]{:S(2)}, u32[]{:S(2)}) collective-permute-start(bf16[32,1664]{1,0:T(8,128)(2,1)S(1)} %fusion.12), channel_id=1, source_target_pairs={{0,8},{4,12},{8,0},{12,4},{1,9},{5,13},{9,1},{13,5},{2,10},{6,14},... | collective-permute-start | bytes 319496 | tf_op jit(solution)/shard_map/ppermute | solution.py:94
  8.9 1.3 %collective-permute-start.2 = (bf16[32,1664]{1,0:T(8,128)(2,1)S(1)}, bf16[32,1664]{1,0:T(8,128)(2,1)S(1)}, u32[]{:S(2)}, u32[]{:S(2)}) collective-permute-start(bf16[32,1664]{1,0:T(8,128)(2,1)S(1)} %fusion.12), channel_id=1, source_target_pairs={{0,12},{4,0},{8,4},{12,8},{1,13},{5,1},{9,5},{13,9},{2,14},{6,2},{... | collective-permute-start | bytes 319496 | tf_op jit(solution)/shard_map/ppermute | solution.py:94
  10.2 0.3 copy.20
  10.5 0.7 add_select_fusion
  11.2 0.8 %slice_reduce_fusion = s32[32]{0:T(128)S(1)} fusion(s32[32,32]{1,0:T(8,128)} %param.7), kind=kLoop, calls=%fused_computation.48 | loop fusion | bytes 256 | tf_op jit(solution)/shard_map/slice | solution.py:101
  12.1 0.8 %and_compare_fusion.7 = (pred[32,32]{1,0:T(8,128)(4,1)S(1)}, pred[32,32]{1,0:T(8,128)(4,1)S(1)}, pred[32,32]{1,0:T(8,128)(4,1)S(1)}, pred[32,32]{1,0:T(8,128)(4,...) fusion(s32[32,32]{1,0:T(8,128)} %param.8), kind=kLoop, calls=%fused_computation.47 | loop fusion | flops 24576 | bytes 12288 | tf_op jit(solution)/shard_map/eq | solution.py:32
  12.8 0.0 copy-done
  12.8 0.2 convert_reduce_fusion
  13.1 0.5 fusion.2
  13.6 0.3 fusion.3
  14.0 0.1 pad_slice_fusion
  14.1 1.3 %pad_select_fusion.6 = bf16[32,32,640]{2,1,0:T(8,128)(2,1)S(1)} fusion(bf16[32,32,639]{2,1,0:T(8,128)(2,1)S(1)} %pad_slice_fusion, pred[32,32]{1,0:T(8,128)(4,1)S(1)} %get-tuple-element.11, bf16[32,32,512]{2,1,0:T(8,128)(2,1)S(1)} %fusion.3), kind=kLoop, calls=%fused_computation.18 | loop fusion | flops 655360 | bytes 3668992 | tf_op jit(solution)/shard_map/jit(_where)/select_n | solution.py:33
  15.4 1.3 %pad_select_fusion.5 = bf16[32,32,640]{2,1,0:T(8,128)(2,1)S(1)} fusion(bf16[32,32,640]{2,1,0:T(8,128)(2,1)S(1)} %pad_select_fusion.6, bf16[32,32,638]{2,1,0:T(8,128)(2,1)S(1)} %bitcast.27, pred[32,32]{1,0:T(8,128)(4,1)S(1)} %get-tuple-element.12), kind=kLoop, calls=%fused_computation.17 | loop fusion | flops 655360 | bytes 3929088 | tf_op jit(solution)/shard_map/jit(_where)/select_n | solution.py:33
  16.7 1.3 %pad_select_fusion.4 = bf16[32,32,640]{2,1,0:T(8,128)(2,1)S(1)} fusion(bf16[32,32,640]{2,1,0:T(8,128)(2,1)S(1)} %pad_select_fusion.5, bf16[32,32,636]{2,1,0:T(8,128)(2,1)S(1)} %bitcast.28, pred[32,32]{1,0:T(8,128)(4,1)S(1)} %get-tuple-element.6), kind=kLoop, calls=%fused_computation.16 | loop fusion | flops 655360 | bytes 3924992 | tf_op jit(solution)/shard_map/jit(_where)/select_n | solution.py:33
  18.1 1.3 %pad_select_fusion.3 = bf16[32,32,640]{2,1,0:T(8,128)(2,1)S(1)} fusion(bf16[32,32,640]{2,1,0:T(8,128)(2,1)S(1)} %pad_select_fusion.4, bf16[32,32,632]{2,1,0:T(8,128)(2,1)S(1)} %bitcast.29, pred[32,32]{1,0:T(8,128)(4,1)S(1)} %get-tuple-element.7), kind=kLoop, calls=%fused_computation.15 | loop fusion | flops 655360 | bytes 3916800 | tf_op jit(solution)/shard_map/jit(_where)/select_n | solution.py:33
  19.4 1.3 %pad_select_fusion.2 = bf16[32,32,640]{2,1,0:T(8,128)(2,1)S(1)} fusion(bf16[32,32,640]{2,1,0:T(8,128)(2,1)S(1)} %pad_select_fusion.3, bf16[32,32,624]{2,1,0:T(8,128)(2,1)S(1)} %bitcast.30, pred[32,32]{1,0:T(8,128)(4,1)S(1)} %get-tuple-element.8), kind=kLoop, calls=%fused_computation.14 | loop fusion | flops 655360 | bytes 3900416 | tf_op jit(solution)/shard_map/jit(_where)/select_n | solution.py:33
  20.8 1.3 %pad_select_fusion.1 = bf16[32,32,640]{2,1,0:T(8,128)(2,1)S(1)} fusion(bf16[32,32,640]{2,1,0:T(8,128)(2,1)S(1)} %pad_select_fusion.2, bf16[32,32,608]{2,1,0:T(8,128)(2,1)S(1)} %bitcast.31, pred[32,32]{1,0:T(8,128)(4,1)S(1)} %get-tuple-element.9), kind=kLoop, calls=%fused_computation.13 | loop fusion | flops 655360 | bytes 3867648 | tf_op jit(solution)/shard_map/jit(_where)/select_n | solution.py:33
  22.1 1.3 %pad_select_fusion = bf16[32,32,640]{2,1,0:T(8,128)(2,1)S(1)} fusion(bf16[32,32,640]{2,1,0:T(8,128)(2,1)S(1)} %pad_select_fusion.1, bf16[32,32,576]{2,1,0:T(8,128)(2,1)S(1)} %bitcast.32, pred[32,32]{1,0:T(8,128)(4,1)S(1)} %get-tuple-element.10), kind=kLoop, calls=%fused_computation.12 | loop fusion | flops 655360 | bytes 3802112 | tf_op jit(solution)/shard_map/jit(_where)/select_n | solution.py:33
  23.5 0.1 slice.44
  23.6 0.6 convolution_convert_fusion
  24.2 4.3 %copy.35 = bf16[32,640,32]{2,1,0:T(8,128)(2,1)} copy(bf16[32,640,32]{1,2,0:T(8,128)(2,1)S(1)} %convolution_convert_fusion) | data formatting | bytes 2621440
  28.5 6.5 %pad.13.clone = bf16[32,656,32]{2,1,0:T(8,128)(2,1)} pad(bf16[32,640,32]{2,1,0:T(8,128)(2,1)} %copy.35, bf16[]{:T(256)} %constant.86.clone.1), padding=0_0x7_9x0_0 | pad | bytes 2654210 | tf_op jit(solution)/shard_map/jit(_pad)/pad | solution.py:55
  35.1 6.9 %reshape.152 = bf16[32,82,256]{2,1,0:T(8,128)(2,1)S(1)} reshape(bf16[32,656,32]{2,1,0:T(8,128)(2,1)} %pad.13.clone) | data formatting | bytes 2686976 | tf_op jit(solution)/shard_map/reshape | solution.py:56
  41.9 1.4 %copy.37 = bf16[32,82,256]{2,0,1:T(8,128)(2,1)} copy(bf16[32,82,256]{2,1,0:T(8,128)(2,1)S(1)} %reshape.152) | data formatting | bytes 2686976 | tf_op jit(solution)/shard_map/reshape | solution.py:56
  43.3 0.0 copy-start.1
  43.3 7.9 %shard_map.55 = bf16[81,256,256]{2,1,0:T(8,128)(2,1)} custom-call(bf16[82,32,256]{2,1,0:T(8,128)(2,1)} %bitcast.33), custom_call_target="tpu_custom_call" | custom-call | tf_op jit(solution)/shard_map/pallas_call | solution.py:63
  51.3 0.3 copy.24
  51.7 0.1 broadcast_in_dim.89
  51.7 0.0 copy-done.1
  51.8 0.7 scatter_custom_fusion
  52.5 0.0 collective-permute-done
  52.5 0.3 copy.21
  52.7 0.3 copy.25
  53.1 0.0 collective-permute-done.1
  53.1 0.3 copy.22
  53.3 0.3 copy.26
  53.7 0.0 collective-permute-done.2
  53.7 0.3 copy.23
  54.0 0.3 copy.27
  54.3 0.1 maximum_bitcast_fusion
  54.4 0.1 copy.28
  54.5 0.3 copy.31
  54.8 11.7 %fusion.7 = bf16[256,128]{0,1:T(8,128)(2,1)S(1)} fusion(bf16[4,256,208]{1,0,2:T(4,128)(2,1)S(1)} %copy.31, bf16[81,256,256]{2,1,0:T(8,128)(2,1)} %shard_map.55, pred[4,256]{1,0:T(4,128)(4,1)S(1)} %broadcast_in_dim.89), kind=kOutput, calls=%fused_computation.22 | convolution fusion | flops 5436047360 | bytes 11109376 | tf_op jit(solution)/shard_map/conv_general_dilated | solution.py:111
  66.5 0.1 copy.32
  66.6 0.2 copy.33
  66.8 0.1 copy.34
  66.9 0.6 gather_fusion
  67.6 6.7 %all_to_all.5 = bf16[4,8,1024]{2,1,0:T(8,128)(2,1)S(1)} all-to-all(bf16[4,8,1024]{2,1,0:T(8,128)(2,1)S(1)} %bitcast.41), channel_id=1, replica_groups=mesh['grp'=2,'chan'=4,'tmpl'=4] {'tmpl'}, dimensions={0} | all-to-all | bytes 131072 | tf_op jit(solution)/shard_map/all_to_all | solution.py:128
  74.3 0.1 multiply_reduce_fusion
  74.4 0.7 broadcast_multiply_fusion
  (13 shorter events, 0.1 us)
Async XLA Ops:
  0.0 12.8 %copy-start = (bf16[32,32,512]{2,1,0:T(8,128)(2,1)S(1)}, bf16[32,32,512]{2,1,0:T(8,128)(2,1)}, u32[]{:S(2)}) copy-start(bf16[32,32,512]{2,1,0:T(8,128)(2,1)} %param.6) | copy-start | bytes 3145732
  3.2 49.2 %collective-permute-start = (bf16[32,1664]{1,0:T(8,128)(2,1)S(1)}, bf16[32,1664]{1,0:T(8,128)(2,1)S(1)}, u32[]{:S(2)}, u32[]{:S(2)}) collective-permute-start(bf16[32,1664]{1,0:T(8,128)(2,1)S(1)} %fusion.12), channel_id=1, source_target_pairs={{0,4},{4,8},{8,12},{12,0},{1,5},{5,9},{9,13},{13,1},{2,6},{6,10},{... | collective-permute-start | bytes 319496 | tf_op jit(solution)/shard_map/ppermute | solution.py:94
  6.3 46.8 %collective-permute-start.1 = (bf16[32,1664]{1,0:T(8,128)(2,1)S(1)}, bf16[32,1664]{1,0:T(8,128)(2,1)S(1)}, u32[]{:S(2)}, u32[]{:S(2)}) collective-permute-start(bf16[32,1664]{1,0:T(8,128)(2,1)S(1)} %fusion.12), channel_id=1, source_target_pairs={{0,8},{4,12},{8,0},{12,4},{1,9},{5,13},{9,1},{13,5},{2,10},{6,14},... | collective-permute-start | bytes 319496 | tf_op jit(solution)/shard_map/ppermute | solution.py:94
  8.9 44.8 %collective-permute-start.2 = (bf16[32,1664]{1,0:T(8,128)(2,1)S(1)}, bf16[32,1664]{1,0:T(8,128)(2,1)S(1)}, u32[]{:S(2)}, u32[]{:S(2)}) collective-permute-start(bf16[32,1664]{1,0:T(8,128)(2,1)S(1)} %fusion.12), channel_id=1, source_target_pairs={{0,12},{4,0},{8,4},{12,8},{1,13},{5,1},{9,5},{13,9},{2,14},{6,2},{... | collective-permute-start | bytes 319496 | tf_op jit(solution)/shard_map/ppermute | solution.py:94
  43.3 8.4 %copy-start.1 = (s32[1,32]{1,0:T(1,128)S(1)}, s32[1,32]{1,0:T(1,128)}, u32[]{:S(2)}) copy-start(s32[1,32]{1,0:T(1,128)} %param.9) | copy-start | bytes 388

commit v5 on v2

--- a/solution.py
+++ b/solution.py
@@ -53,8 +53,8 @@
     front = phases - 1
     blocks = taps + 1
     padded = jnp.pad(placed, ((0, 0), (0, 0), (front, blocks * phases - padded_len - front)))
-    grouped = padded.reshape(count, chans, blocks, phases)
-    grouped = jnp.transpose(grouped, (2, 0, 3, 1)).reshape(blocks, count, phases * chans)
+    grouped = jnp.transpose(padded, (0, 2, 1)).reshape(count, blocks, phases * chans)
+    grouped = jnp.transpose(grouped, (1, 0, 2))
     steps = next(d for d in (9, 3, 1) if taps % d == 0)
     width = phases * chans
     kernel = functools.partial(
@@ -109,6 +109,8 @@
     placed = place_moveout(ordered, ordered_shift, padded_len)
     filters = polyphase_filters(placed, phases)
     lhs = polyphase_signal(blocks, phases)
+    span = lhs.shape[-1]
+    lhs = jnp.transpose(lhs, (1, 0, 2)).reshape(1, lhs.shape[1], n_blocks * span)
     corr = lax.conv_general_dilated(
         lhs,
         filters,
@@ -117,7 +119,9 @@
         dimension_numbers=("NCH", "HOI", "NCH"),
         preferred_element_type=jnp.float32,
     )
-    corr = corr[:, :, : lags // phases].reshape(n_blocks, phases, count, lags // phases)
+    corr = jnp.pad(corr[0], ((0, 0), (0, n_blocks * span - corr.shape[-1])))
+    corr = corr.reshape(corr.shape[0], n_blocks, span)[:, :, : lags // phases]
+    corr = jnp.transpose(corr, (1, 0, 2)).reshape(n_blocks, phases, count, lags // phases)
     pick = target[None, :] == jnp.arange(n_blocks, dtype=jnp.int32)[:, None]
     chosen = jnp.sum(jnp.where(pick[:, None, :, None], corr, 0.0), axis=0)
     partial_value = jnp.transpose(chosen, (1, 2, 0)).reshape(count, lags)

time: 76.6 us -> 73 us (0.953)
  local copies, waits for them, and re-layouts: 25.1 us -> 19.9 us
  matrix products: 12.2 us -> 13.7 us
    transpose x2 -> x3, local copies, waits for them, and re-layouts: 12.5 us -> 5.39 us  [the longest x2 5.19 us: polyphase_filters(): jnp.transpose(padded, (0, 2, 1)).reshape(count, blocks, phases * chans)]
    reshape x2, local copies, waits for them, and re-layouts: 2.89 us -> 8.27 us  [polyphase_filters(): jnp.transpose(padded, (0, 2, 1)).reshape(count, blocks, phases * chans)]
    unnamed x5 -> x6, local copies, waits for them, and re-layouts: 4.3 us -> 0.33 us
    conv_general_dilated x1, matrix products: 11.7 us -> 13.1 us  [shards(): lax.conv_general_dilated(lhs, filters, (1,), 'VALID', dimension_numbers=(...]
  transfers between devices with their start and end apart: 3 -> 3, of which waited for: 0 -> 0; matrix products, arithmetic and copies ran while one was open for 48% -> 42% of each run, Pallas kernels for 10% -> 11%
where the time goes in v5:
time: 73 us; the launch traced here: 72.4 us
  local copies, waits for them, and re-layouts  19.9 us (27%)
  other arithmetic  16.9 us (23%)
  matrix products  13.7 us (19%)
  Pallas kernels  7.93 us (11%)
  starting transfers between devices  7.01 us (10%)
  blocking collectives  6.68 us (9%)
    conv_general_dilated x1, matrix products, shards(): lax.conv_general_dilated(lhs, filters, (1,), 'VALID', dimension_numbers=(...  13.1 us
    select_n x8, other arithmetic, place_moveout(): current = jnp.where(active[..., None], moved, current)  9.75 us
    reshape x2, local copies, waits for them, and re-layouts, polyphase_filters(): jnp.transpose(padded, (0, 2, 1)).reshape(count, blocks, phases * chans)  8.27 us
    pallas_call x1, Pallas kernels, polyphase_filters(): pl.pallas_call(kernel, grid=(taps // steps,), in_specs=[pl.BlockSpec((blo...  7.93 us
    ppermute x3, starting transfers between devices, shards(): pieces.append(lax.ppermute(signal, 'chan', pairs))  7.01 us
    all_to_all x1, blocking collectives, shards(): received = lax.all_to_all(arranged, 'tmpl', 0, 0, tiled=True)  6.68 us
    transpose x2, local copies, waits for them, and re-layouts, polyphase_filters(): jnp.transpose(padded, (0, 2, 1)).reshape(count, blocks, phases * chans)  5.19 us
    reduce_sum x2, other arithmetic, normalize_rows(): scale = lax.rsqrt(jnp.mean(centred * centred, axis=-1, keepdims=True) + eps)  1.62 us
  transfers between devices with their start and end apart: 3, of which 0 were waited for; matrix products, arithmetic and copies ran while one was open for 42% of the time, Pallas kernels for 11%

profile of v5, /device:TPU:0, one launch (start us, length us, event | category | flops | bytes accessed | tf_op | source)
XLA Modules:
  0.0 72.4 jit_solution(16126054197308386412)
XLA Ops:
  0.0 0.0 copy-start
  0.0 1.1 %convert_reduce_fusion.1 = f32[32]{0:T(128)S(1)} fusion(bf16[32,1664]{1,0:T(8,128)(2,1)} %param.5), kind=kLoop, calls=%fused_computation.39 | loop fusion | flops 106464 | bytes 106624 | tf_op jit(solution)/shard_map/reduce_sum | solution.py:19
  1.1 1.1 %fusion.20 = f32[32]{0:T(128)S(1)} fusion(bf16[32,1664]{1,0:T(8,128)(2,1)} %param.5, f32[32]{0:T(128)S(1)} %broadcast_multiply_fusion.2), kind=kLoop, calls=%fused_computation.43 | loop fusion | flops 212960 | bytes 106752 | tf_op jit(solution)/shard_map/reduce_sum | solution.py:20
  2.2 1.0 %fusion.21 = bf16[32,1664]{1,0:T(8,128)(2,1)S(1)} fusion(bf16[32,1664]{1,0:T(8,128)(2,1)} %param.5, f32[32]{0:T(128)S(1)} %add_rsqrt_fusion.2, f32[32]{0:T(128)S(1)} %broadcast_multiply_fusion.2), kind=kLoop, calls=%fused_computation.44 | loop fusion | flops 212992 | bytes 213248 | tf_op jit(solution)/shard_map/convert_element_type | solution.py:21
  3.2 3.1 %collective-permute-start = (bf16[32,1664]{1,0:T(8,128)(2,1)S(1)}, bf16[32,1664]{1,0:T(8,128)(2,1)S(1)}, u32[]{:S(2)}, u32[]{:S(2)}) collective-permute-start(bf16[32,1664]{1,0:T(8,128)(2,1)S(1)} %fusion.21), channel_id=1, source_target_pairs={{0,4},{4,8},{8,12},{12,0},{1,5},{5,9},{9,13},{13,1},{2,6},{6,10},{... | collective-permute-start | bytes 319496 | tf_op jit(solution)/shard_map/ppermute | solution.py:94
  6.3 2.6 %collective-permute-start.1 = (bf16[32,1664]{1,0:T(8,128)(2,1)S(1)}, bf16[32,1664]{1,0:T(8,128)(2,1)S(1)}, u32[]{:S(2)}, u32[]{:S(2)}) collective-permute-start(bf16[32,1664]{1,0:T(8,128)(2,1)S(1)} %fusion.21), channel_id=1, source_target_pairs={{0,8},{4,12},{8,0},{12,4},{1,9},{5,13},{9,1},{13,5},{2,10},{6,14},... | collective-permute-start | bytes 319496 | tf_op jit(solution)/shard_map/ppermute | solution.py:94
  8.9 1.3 %collective-permute-start.2 = (bf16[32,1664]{1,0:T(8,128)(2,1)S(1)}, bf16[32,1664]{1,0:T(8,128)(2,1)S(1)}, u32[]{:S(2)}, u32[]{:S(2)}) collective-permute-start(bf16[32,1664]{1,0:T(8,128)(2,1)S(1)} %fusion.21), channel_id=1, source_target_pairs={{0,12},{4,0},{8,4},{12,8},{1,13},{5,1},{9,5},{13,9},{2,14},{6,2},{... | collective-permute-start | bytes 319496 | tf_op jit(solution)/shard_map/ppermute | solution.py:94
  10.2 0.3 copy.19
  10.5 0.7 %add_select_fusion = s32[32,32]{1,0:T(8,128)S(1)} fusion(s32[32,32]{1,0:T(8,128)} %param.7), kind=kLoop, calls=%fused_computation.47 | loop fusion | flops 11264 | bytes 8192 | tf_op jit(solution)/shard_map/jit(remainder)/select_n | solution.py:100
  11.2 0.8 %slice_reduce_fusion = s32[32]{0:T(128)S(1)} fusion(s32[32,32]{1,0:T(8,128)} %param.7), kind=kLoop, calls=%fused_computation.61 | loop fusion | bytes 256 | tf_op jit(solution)/shard_map/slice | solution.py:101
  12.1 1.3 %select_reduce_fusion = s32[32,32]{1,0:T(8,128)S(1)} fusion(s32[32,32]{1,0:T(8,128)} %param.8, s32[32,32]{1,0:T(8,128)S(1)} %add_select_fusion), kind=kLoop, calls=%fused_computation.35 | loop fusion | flops 97280 | bytes 12288 | tf_op jit(solution)/shard_map/reduce_sum | solution.py:108
  13.5 0.0 copy-done
  13.5 0.2 convert_reduce_fusion
  13.7 0.5 fusion.2
  14.2 0.5 convolution_convert_fusion
  14.8 0.1 pad_slice_fusion
  14.9 1.3 %pad_select_fusion.7 = bf16[32,32,640]{2,1,0:T(8,128)(2,1)S(1)} fusion(bf16[32,32,639]{2,1,0:T(8,128)(2,1)S(1)} %pad_slice_fusion, pred[32,32]{1,0:T(8,128)(4,1)S(1)} %get-tuple-element.6, bf16[32,32,512]{2,1,0:T(8,128)(2,1)S(1)} %convolution_convert_fusion), kind=kLoop, calls=%fused_computation.20 | loop fusion | flops 655360 | bytes 3668992 | tf_op jit(solution)/shard_map/jit(_where)/select_n | solution.py:33
  16.2 1.3 %pad_select_fusion.6 = bf16[32,32,640]{2,1,0:T(8,128)(2,1)S(1)} fusion(bf16[32,32,640]{2,1,0:T(8,128)(2,1)S(1)} %pad_select_fusion.7, bf16[32,32,638]{2,1,0:T(8,128)(2,1)S(1)} %bitcast.46, pred[32,32]{1,0:T(8,128)(4,1)S(1)} %get-tuple-element.7), kind=kLoop, calls=%fused_computation.19 | loop fusion | flops 655360 | bytes 3929088 | tf_op jit(solution)/shard_map/jit(_where)/select_n | solution.py:33
  17.6 1.3 %pad_select_fusion.5 = bf16[32,32,640]{2,1,0:T(8,128)(2,1)S(1)} fusion(bf16[32,32,640]{2,1,0:T(8,128)(2,1)S(1)} %pad_select_fusion.6, bf16[32,32,636]{2,1,0:T(8,128)(2,1)S(1)} %bitcast.47, pred[32,32]{1,0:T(8,128)(4,1)S(1)} %get-tuple-element.8), kind=kLoop, calls=%fused_computation.18 | loop fusion | flops 655360 | bytes 3924992 | tf_op jit(solution)/shard_map/jit(_where)/select_n | solution.py:33
  18.9 1.3 %pad_select_fusion.4 = bf16[32,32,640]{2,1,0:T(8,128)(2,1)S(1)} fusion(bf16[32,32,640]{2,1,0:T(8,128)(2,1)S(1)} %pad_select_fusion.5, bf16[32,32,632]{2,1,0:T(8,128)(2,1)S(1)} %bitcast.48, pred[32,32]{1,0:T(8,128)(4,1)S(1)} %get-tuple-element.9), kind=kLoop, calls=%fused_computation.17 | loop fusion | flops 655360 | bytes 3916800 | tf_op jit(solution)/shard_map/jit(_where)/select_n | solution.py:33
  20.3 1.3 %pad_select_fusion.3 = bf16[32,32,640]{2,1,0:T(8,128)(2,1)S(1)} fusion(bf16[32,32,640]{2,1,0:T(8,128)(2,1)S(1)} %pad_select_fusion.4, bf16[32,32,624]{2,1,0:T(8,128)(2,1)S(1)} %bitcast.49, pred[32,32]{1,0:T(8,128)(4,1)S(1)} %get-tuple-element.10), kind=kLoop, calls=%fused_computation.16 | loop fusion | flops 655360 | bytes 3900416 | tf_op jit(solution)/shard_map/jit(_where)/select_n | solution.py:33
  21.6 1.3 %pad_select_fusion.2 = bf16[32,32,640]{2,1,0:T(8,128)(2,1)S(1)} fusion(bf16[32,32,640]{2,1,0:T(8,128)(2,1)S(1)} %pad_select_fusion.3, bf16[32,32,608]{2,1,0:T(8,128)(2,1)S(1)} %bitcast.50, pred[32,32]{1,0:T(8,128)(4,1)S(1)} %get-tuple-element.11), kind=kLoop, calls=%fused_computation.15 | loop fusion | flops 655360 | bytes 3867648 | tf_op jit(solution)/shard_map/jit(_where)/select_n | solution.py:33
  23.0 1.3 %pad_select_fusion.1 = bf16[32,32,640]{2,1,0:T(8,128)(2,1)S(1)} fusion(bf16[32,32,640]{2,1,0:T(8,128)(2,1)S(1)} %pad_select_fusion.2, bf16[32,32,576]{2,1,0:T(8,128)(2,1)S(1)} %bitcast.51, pred[32,32]{1,0:T(8,128)(4,1)S(1)} %get-tuple-element.12), kind=kLoop, calls=%fused_computation.14 | loop fusion | flops 655360 | bytes 3802112 | tf_op jit(solution)/shard_map/jit(_where)/select_n | solution.py:33
  24.3 0.1 slice.51
  24.4 0.4 pad_select_fusion
  24.8 0.9 %pad_bitcast_fusion = bf16[32,656,32]{1,2,0:T(8,128)(2,1)S(1)} fusion(bf16[32,32,640]{2,1,0:T(8,128)(2,1)S(1)} %pad_select_fusion), kind=kLoop, calls=%fused_computation.8 | loop fusion | bytes 2654208 | tf_op jit(solution)/shard_map/transpose | solution.py:56
  25.8 4.3 %copy.31 = bf16[32,656,32]{2,1,0:T(8,128)(2,1)} copy(bf16[32,656,32]{1,2,0:T(8,128)(2,1)S(1)} %pad_bitcast_fusion) | data formatting | bytes 2686976 | tf_op jit(solution)/shard_map/transpose | solution.py:56
  30.0 6.9 %reshape.192 = bf16[32,82,256]{2,1,0:T(8,128)(2,1)S(1)} reshape(bf16[32,656,32]{2,1,0:T(8,128)(2,1)} %copy.31) | data formatting | bytes 2686976 | tf_op jit(solution)/shard_map/reshape | solution.py:56
  36.9 1.4 %copy.38 = bf16[32,82,256]{2,0,1:T(8,128)(2,1)} copy(bf16[32,82,256]{2,1,0:T(8,128)(2,1)S(1)} %reshape.192) | data formatting | bytes 2686976 | tf_op jit(solution)/shard_map/reshape | solution.py:56
  38.3 0.0 copy-start.1
  38.3 7.9 %shard_map.55 = bf16[81,256,256]{2,1,0:T(8,128)(2,1)} custom-call(bf16[82,32,256]{2,1,0:T(8,128)(2,1)} %bitcast.52), custom_call_target="tpu_custom_call" | custom-call | tf_op jit(solution)/shard_map/pallas_call | solution.py:63
  46.2 0.3 copy.23
  46.6 0.1 broadcast_in_dim.102
  46.7 0.0 copy-done.1
  46.7 0.7 scatter_custom_fusion
  47.4 0.0 collective-permute-done
  47.4 0.3 copy.20
  47.7 0.3 copy.24
  48.0 0.0 collective-permute-done.1
  48.1 0.3 copy.21
  48.3 0.3 copy.25
  48.6 0.0 collective-permute-done.2
  48.7 0.3 copy.22
  48.9 0.3 copy.26
  49.3 0.1 maximum_bitcast_fusion
  49.4 0.1 copy.27
  49.5 0.0 copy-start.2
  49.5 0.2 copy.28
  49.7 0.1 copy.30
  49.8 0.1 slice.44
  49.9 0.3 copy-done.2
  50.2 13.1 %convolution_select_fusion = f32[8,104,256]{2,0,1:T(8,128)S(1)} fusion(bf16[81,256,256]{2,1,0:T(8,128)(2,1)} %shard_map.55, bf16[256,1,7,80]{0,2,3,1:T(8,128)(2,1)S(1)} %slice.44, bf16[256,1,8,104]{0,2,3,1:T(8,128)(2,1)S(1)} %copy.30, pred[8,104]{0,1:T(8,128)(4,1)S(1)} %copy-done.2), kind=kOutput, calls=%fused_computation.22 | convolution fusion | flops 8835678208 | bytes 12182336 | tf_op jit(solution)/shard_map/conv_general_dilated | solution.py:114
  63.3 0.3 copy.33
  63.6 0.1 slice_bitcast_fusion
  63.7 0.1 pad.18
  63.8 0.1 copy.34
  63.9 0.2 copy.35
  64.1 0.1 copy.36
  64.2 0.6 gather_fusion
  64.9 6.7 %all_to_all.5 = bf16[4,8,1024]{2,1,0:T(8,128)(2,1)S(1)} all-to-all(bf16[4,8,1024]{2,1,0:T(8,128)(2,1)S(1)} %bitcast.63), channel_id=1, replica_groups=mesh['grp'=2,'chan'=4,'tmpl'=4] {'tmpl'}, dimensions={0} | all-to-all | bytes 131072 | tf_op jit(solution)/shard_map/all_to_all | solution.py:133
  71.6 0.1 multiply_reduce_fusion
  71.7 0.7 broadcast_multiply_fusion
  (15 shorter events, 0.2 us)
Async XLA Ops:
  0.0 13.5 %copy-start = (bf16[32,32,512]{2,1,0:T(8,128)(2,1)S(1)}, bf16[32,32,512]{2,1,0:T(8,128)(2,1)}, u32[]{:S(2)}) copy-start(bf16[32,32,512]{2,1,0:T(8,128)(2,1)} %param.6) | copy-start | bytes 3145732
  3.2 44.2 %collective-permute-start = (bf16[32,1664]{1,0:T(8,128)(2,1)S(1)}, bf16[32,1664]{1,0:T(8,128)(2,1)S(1)}, u32[]{:S(2)}, u32[]{:S(2)}) collective-permute-start(bf16[32,1664]{1,0:T(8,128)(2,1)S(1)} %fusion.21), channel_id=1, source_target_pairs={{0,4},{4,8},{8,12},{12,0},{1,5},{5,9},{9,13},{13,1},{2,6},{6,10},{... | collective-permute-start | bytes 319496 | tf_op jit(solution)/shard_map/ppermute | solution.py:94
  6.3 41.7 %collective-permute-start.1 = (bf16[32,1664]{1,0:T(8,128)(2,1)S(1)}, bf16[32,1664]{1,0:T(8,128)(2,1)S(1)}, u32[]{:S(2)}, u32[]{:S(2)}) collective-permute-start(bf16[32,1664]{1,0:T(8,128)(2,1)S(1)} %fusion.21), channel_id=1, source_target_pairs={{0,8},{4,12},{8,0},{12,4},{1,9},{5,13},{9,1},{13,5},{2,10},{6,14},... | collective-permute-start | bytes 319496 | tf_op jit(solution)/shard_map/ppermute | solution.py:94
  8.9 39.8 %collective-permute-start.2 = (bf16[32,1664]{1,0:T(8,128)(2,1)S(1)}, bf16[32,1664]{1,0:T(8,128)(2,1)S(1)}, u32[]{:S(2)}, u32[]{:S(2)}) collective-permute-start(bf16[32,1664]{1,0:T(8,128)(2,1)S(1)} %fusion.21), channel_id=1, source_target_pairs={{0,12},{4,0},{8,4},{12,8},{1,13},{5,1},{9,5},{13,9},{2,14},{6,2},{... | collective-permute-start | bytes 319496 | tf_op jit(solution)/shard_map/ppermute | solution.py:94
  38.3 8.4 %copy-start.1 = (s32[1,32]{1,0:T(1,128)S(1)}, s32[1,32]{1,0:T(1,128)}, u32[]{:S(2)}) copy-start(s32[1,32]{1,0:T(1,128)} %param.9) | copy-start | bytes 388
  49.5 0.7 copy-start.2

commit v6 on v2

--- a/solution.py
+++ b/solution.py
@@ -53,8 +53,8 @@
     front = phases - 1
     blocks = taps + 1
     padded = jnp.pad(placed, ((0, 0), (0, 0), (front, blocks * phases - padded_len - front)))
-    grouped = padded.reshape(count, chans, blocks, phases)
-    grouped = jnp.transpose(grouped, (2, 0, 3, 1)).reshape(blocks, count, phases * chans)
+    grouped = jnp.transpose(padded, (0, 2, 1)).reshape(count, blocks, phases * chans)
+    grouped = jnp.transpose(grouped, (1, 0, 2))
     steps = next(d for d in (9, 3, 1) if taps % d == 0)
     width = phases * chans
     kernel = functools.partial(
@@ -126,8 +126,16 @@
         jnp.zeros((count,), jnp.int32).at[owner_map[0]].set(jnp.arange(count, dtype=jnp.int32))
     )
     arranged = partial_value[inverse].reshape(n_tmpl, count // n_tmpl, lags)
-    received = lax.all_to_all(arranged, "tmpl", 0, 0, tiled=True)
-    stack = jnp.sum(received.astype(jnp.float32), axis=0)
+    if n_tmpl <= 8:
+        mine = lax.axis_index("tmpl")
+        stack = jnp.take(arranged, mine, axis=0).astype(jnp.float32)
+        for shift in range(1, n_tmpl):
+            pairs = [(t, (t + shift) % n_tmpl) for t in range(n_tmpl)]
+            outgoing = jnp.take(arranged, (mine + shift) % n_tmpl, axis=0)
+            stack = stack + lax.ppermute(outgoing, "tmpl", pairs).astype(jnp.float32)
+    else:
+        received = lax.all_to_all(arranged, "tmpl", 0, 0, tiled=True)
+        stack = jnp.sum(received.astype(jnp.float32), axis=0)
     power = jnp.mean(stack * stack, axis=1, keepdims=True)
     return stack * lax.rsqrt(power + eps)
 

time: 76.6 us -> 68.5 us (0.89)
  blocking collectives: 6.68 us -> 0 us
  local copies, waits for them, and re-layouts: 25.1 us -> 19.1 us
  starting transfers between devices: 7.01 us -> 10 us
  waiting for transfers between devices: 0.01 us -> 1.45 us
    transpose x2, local copies, waits for them, and re-layouts: 12.5 us -> 5.19 us  [polyphase_filters(): jnp.transpose(padded, (0, 2, 1)).reshape(count, blocks, phases * chans)]
    all_to_all x1 -> x0, blocking collectives: 6.68 us -> none  [shards(): received = lax.all_to_all(arranged, 'tmpl', 0, 0, tiled=True)]
    reshape x1 -> x2, local copies, waits for them, and re-layouts: 2.62 us -> 8.27 us  [polyphase_filters(): jnp.transpose(padded, (0, 2, 1)).reshape(count, blocks, phases * chans)]
    unnamed x5 -> x4, local copies, waits for them, and re-layouts: 4.3 us -> 0.01 us
    ppermute x0 -> x3, starting transfers between devices: none -> 3 us  [shards(): stack = stack + lax.ppermute(outgoing, 'tmpl', pairs).astype(jnp.float32)]
    ppermute x0 -> x3, waiting for transfers between devices: none -> 1.44 us  [shards(): stack = stack + lax.ppermute(outgoing, 'tmpl', pairs).astype(jnp.float32)]
  transfers between devices with their start and end apart: 3 -> 6, of which waited for: 0 -> 3; matrix products, arithmetic and copies ran while one was open for 48% -> 45% of each run, Pallas kernels for 10% -> 12%
where the time goes in v6:
time: 68.5 us; the launch traced here: 67.9 us
  local copies, waits for them, and re-layouts  19.1 us (28%)
  other arithmetic  16.8 us (25%)
  matrix products  12.2 us (18%)
  starting transfers between devices  10 us (15%)
  Pallas kernels  7.93 us (12%)
  waiting for transfers between devices  1.45 us (2%)
    conv_general_dilated x1, matrix products, shards(): lax.conv_general_dilated(lhs, filters, (1,), 'VALID', dimension_numbers=(...  11.7 us
    select_n x8, other arithmetic, place_moveout(): current = jnp.where(active[..., None], moved, current)  9.75 us
    reshape x2, local copies, waits for them, and re-layouts, polyphase_filters(): jnp.transpose(padded, (0, 2, 1)).reshape(count, blocks, phases * chans)  8.27 us
    pallas_call x1, Pallas kernels, polyphase_filters(): pl.pallas_call(kernel, grid=(taps // steps,), in_specs=[pl.BlockSpec((blo...  7.93 us
    ppermute x3, starting transfers between devices, shards(): pieces.append(lax.ppermute(signal, 'chan', pairs))  7.01 us
    transpose x2, local copies, waits for them, and re-layouts, polyphase_filters(): jnp.transpose(padded, (0, 2, 1)).reshape(count, blocks, phases * chans)  5.19 us
    ppermute x3, starting transfers between devices, shards(): stack = stack + lax.ppermute(outgoing, 'tmpl', pairs).astype(jnp.float32)  3 us
    reduce_sum x2, other arithmetic, normalize_rows(): scale = lax.rsqrt(jnp.mean(centred * centred, axis=-1, keepdims=True) + eps)  1.62 us
  transfers between devices with their start and end apart: 6, of which 3 were waited for; matrix products, arithmetic and copies ran while one was open for 45% of the time, Pallas kernels for 12%

profile of v6, /device:TPU:0, one launch (start us, length us, event | category | flops | bytes accessed | tf_op | source)
XLA Modules:
  0.0 67.9 jit_solution(969178361883346576)
XLA Ops:
  0.0 0.0 copy-start
  0.0 1.1 %convert_reduce_fusion.1 = f32[32]{0:T(128)S(1)} fusion(bf16[32,1664]{1,0:T(8,128)(2,1)} %param.7), kind=kLoop, calls=%fused_computation.28 | loop fusion | flops 106464 | bytes 106624 | tf_op jit(solution)/shard_map/reduce_sum | solution.py:19
  1.1 1.1 %fusion.11 = f32[32]{0:T(128)S(1)} fusion(bf16[32,1664]{1,0:T(8,128)(2,1)} %param.7, f32[32]{0:T(128)S(1)} %broadcast_multiply_fusion.2), kind=kLoop, calls=%fused_computation.32 | loop fusion | flops 212960 | bytes 106752 | tf_op jit(solution)/shard_map/reduce_sum | solution.py:20
  2.2 1.0 %fusion.12 = bf16[32,1664]{1,0:T(8,128)(2,1)S(1)} fusion(bf16[32,1664]{1,0:T(8,128)(2,1)} %param.7, f32[32]{0:T(128)S(1)} %add_rsqrt_fusion.2, f32[32]{0:T(128)S(1)} %broadcast_multiply_fusion.2), kind=kLoop, calls=%fused_computation.33 | loop fusion | flops 212992 | bytes 213248 | tf_op jit(solution)/shard_map/convert_element_type | solution.py:21
  3.2 3.1 %collective-permute-start = (bf16[32,1664]{1,0:T(8,128)(2,1)S(1)}, bf16[32,1664]{1,0:T(8,128)(2,1)S(1)}, u32[]{:S(2)}, u32[]{:S(2)}) collective-permute-start(bf16[32,1664]{1,0:T(8,128)(2,1)S(1)} %fusion.12), channel_id=1, source_target_pairs={{0,4},{4,8},{8,12},{12,0},{1,5},{5,9},{9,13},{13,1},{2,6},{6,10},{... | collective-permute-start | bytes 319496 | tf_op jit(solution)/shard_map/ppermute | solution.py:94
  6.3 2.6 %collective-permute-start.1 = (bf16[32,1664]{1,0:T(8,128)(2,1)S(1)}, bf16[32,1664]{1,0:T(8,128)(2,1)S(1)}, u32[]{:S(2)}, u32[]{:S(2)}) collective-permute-start(bf16[32,1664]{1,0:T(8,128)(2,1)S(1)} %fusion.12), channel_id=1, source_target_pairs={{0,8},{4,12},{8,0},{12,4},{1,9},{5,13},{9,1},{13,5},{2,10},{6,14},... | collective-permute-start | bytes 319496 | tf_op jit(solution)/shard_map/ppermute | solution.py:94
  8.9 1.3 %collective-permute-start.2 = (bf16[32,1664]{1,0:T(8,128)(2,1)S(1)}, bf16[32,1664]{1,0:T(8,128)(2,1)S(1)}, u32[]{:S(2)}, u32[]{:S(2)}) collective-permute-start(bf16[32,1664]{1,0:T(8,128)(2,1)S(1)} %fusion.12), channel_id=1, source_target_pairs={{0,12},{4,0},{8,4},{12,8},{1,13},{5,1},{9,5},{13,9},{2,14},{6,2},{... | collective-permute-start | bytes 319496 | tf_op jit(solution)/shard_map/ppermute | solution.py:94
  10.2 0.3 copy.20
  10.5 0.7 %add_select_fusion = s32[32,32]{1,0:T(8,128)S(1)} fusion(s32[32,32]{1,0:T(8,128)} %param.9), kind=kLoop, calls=%fused_computation.36 | loop fusion | flops 11264 | bytes 8192 | tf_op jit(solution)/shard_map/jit(remainder)/select_n | solution.py:100
  11.2 0.8 %slice_reduce_fusion = s32[32]{0:T(128)S(1)} fusion(s32[32,32]{1,0:T(8,128)} %param.9), kind=kLoop, calls=%fused_computation.53 | loop fusion | bytes 256 | tf_op jit(solution)/shard_map/slice | solution.py:101
  12.1 1.3 %select_reduce_fusion = s32[32,32]{1,0:T(8,128)S(1)} fusion(s32[32,32]{1,0:T(8,128)} %param.10, s32[32,32]{1,0:T(8,128)S(1)} %add_select_fusion), kind=kLoop, calls=%fused_computation.25 | loop fusion | flops 97280 | bytes 12288 | tf_op jit(solution)/shard_map/reduce_sum | solution.py:108
  13.5 0.0 copy-done
  13.5 0.2 convert_reduce_fusion
  13.8 0.5 fusion.2
  14.3 0.5 convolution_convert_fusion
  14.8 0.1 pad_slice_fusion
  15.0 1.3 %pad_select_fusion.7 = bf16[32,32,640]{2,1,0:T(8,128)(2,1)S(1)} fusion(bf16[32,32,639]{2,1,0:T(8,128)(2,1)S(1)} %pad_slice_fusion, pred[32,32]{1,0:T(8,128)(4,1)S(1)} %get-tuple-element.21, bf16[32,32,512]{2,1,0:T(8,128)(2,1)S(1)} %convolution_convert_fusion), kind=kLoop, calls=%fused_computation.18 | loop fusion | flops 655360 | bytes 3668992 | tf_op jit(solution)/shard_map/jit(_where)/select_n | solution.py:33
  16.3 1.3 %pad_select_fusion.6 = bf16[32,32,640]{2,1,0:T(8,128)(2,1)S(1)} fusion(bf16[32,32,640]{2,1,0:T(8,128)(2,1)S(1)} %pad_select_fusion.7, bf16[32,32,638]{2,1,0:T(8,128)(2,1)S(1)} %bitcast.41, pred[32,32]{1,0:T(8,128)(4,1)S(1)} %get-tuple-element.22), kind=kLoop, calls=%fused_computation.17 | loop fusion | flops 655360 | bytes 3929088 | tf_op jit(solution)/shard_map/jit(_where)/select_n | solution.py:33
  17.6 1.3 %pad_select_fusion.5 = bf16[32,32,640]{2,1,0:T(8,128)(2,1)S(1)} fusion(bf16[32,32,640]{2,1,0:T(8,128)(2,1)S(1)} %pad_select_fusion.6, bf16[32,32,636]{2,1,0:T(8,128)(2,1)S(1)} %bitcast.42, pred[32,32]{1,0:T(8,128)(4,1)S(1)} %get-tuple-element.23), kind=kLoop, calls=%fused_computation.16 | loop fusion | flops 655360 | bytes 3924992 | tf_op jit(solution)/shard_map/jit(_where)/select_n | solution.py:33
  19.0 1.3 %pad_select_fusion.4 = bf16[32,32,640]{2,1,0:T(8,128)(2,1)S(1)} fusion(bf16[32,32,640]{2,1,0:T(8,128)(2,1)S(1)} %pad_select_fusion.5, bf16[32,32,632]{2,1,0:T(8,128)(2,1)S(1)} %bitcast.43, pred[32,32]{1,0:T(8,128)(4,1)S(1)} %get-tuple-element.24), kind=kLoop, calls=%fused_computation.15 | loop fusion | flops 655360 | bytes 3916800 | tf_op jit(solution)/shard_map/jit(_where)/select_n | solution.py:33
  20.3 1.3 %pad_select_fusion.3 = bf16[32,32,640]{2,1,0:T(8,128)(2,1)S(1)} fusion(bf16[32,32,640]{2,1,0:T(8,128)(2,1)S(1)} %pad_select_fusion.4, bf16[32,32,624]{2,1,0:T(8,128)(2,1)S(1)} %bitcast.44, pred[32,32]{1,0:T(8,128)(4,1)S(1)} %get-tuple-element.25), kind=kLoop, calls=%fused_computation.14 | loop fusion | flops 655360 | bytes 3900416 | tf_op jit(solution)/shard_map/jit(_where)/select_n | solution.py:33
  21.7 1.3 %pad_select_fusion.2 = bf16[32,32,640]{2,1,0:T(8,128)(2,1)S(1)} fusion(bf16[32,32,640]{2,1,0:T(8,128)(2,1)S(1)} %pad_select_fusion.3, bf16[32,32,608]{2,1,0:T(8,128)(2,1)S(1)} %bitcast.45, pred[32,32]{1,0:T(8,128)(4,1)S(1)} %get-tuple-element.26), kind=kLoop, calls=%fused_computation.13 | loop fusion | flops 655360 | bytes 3867648 | tf_op jit(solution)/shard_map/jit(_where)/select_n | solution.py:33
  23.0 1.3 %pad_select_fusion.1 = bf16[32,32,640]{2,1,0:T(8,128)(2,1)S(1)} fusion(bf16[32,32,640]{2,1,0:T(8,128)(2,1)S(1)} %pad_select_fusion.2, bf16[32,32,576]{2,1,0:T(8,128)(2,1)S(1)} %bitcast.46, pred[32,32]{1,0:T(8,128)(4,1)S(1)} %get-tuple-element.27), kind=kLoop, calls=%fused_computation.12 | loop fusion | flops 655360 | bytes 3802112 | tf_op jit(solution)/shard_map/jit(_where)/select_n | solution.py:33
  24.4 0.1 slice.53
  24.5 0.4 pad_select_fusion
  24.9 0.9 %pad_bitcast_fusion = bf16[32,656,32]{1,2,0:T(8,128)(2,1)S(1)} fusion(bf16[32,32,640]{2,1,0:T(8,128)(2,1)S(1)} %pad_select_fusion), kind=kLoop, calls=%fused_computation.8 | loop fusion | bytes 2654208 | tf_op jit(solution)/shard_map/transpose | solution.py:56
  25.8 4.3 %copy.29 = bf16[32,656,32]{2,1,0:T(8,128)(2,1)} copy(bf16[32,656,32]{1,2,0:T(8,128)(2,1)S(1)} %pad_bitcast_fusion) | data formatting | bytes 2686976 | tf_op jit(solution)/shard_map/transpose | solution.py:56
  30.1 6.9 %reshape.186 = bf16[32,82,256]{2,1,0:T(8,128)(2,1)S(1)} reshape(bf16[32,656,32]{2,1,0:T(8,128)(2,1)} %copy.29) | data formatting | bytes 2686976 | tf_op jit(solution)/shard_map/reshape | solution.py:56
  37.0 1.4 %copy.36 = bf16[32,82,256]{2,0,1:T(8,128)(2,1)} copy(bf16[32,82,256]{2,1,0:T(8,128)(2,1)S(1)} %reshape.186) | data formatting | bytes 2686976 | tf_op jit(solution)/shard_map/reshape | solution.py:56
  38.4 0.0 copy-start.1
  38.4 7.9 %shard_map.55 = bf16[81,256,256]{2,1,0:T(8,128)(2,1)} custom-call(bf16[82,32,256]{2,1,0:T(8,128)(2,1)} %bitcast.47), custom_call_target="tpu_custom_call" | custom-call | tf_op jit(solution)/shard_map/pallas_call | solution.py:63
  46.3 0.3 copy.24
  46.6 0.0 copy-done.1
  46.7 0.7 scatter_custom_fusion
  47.4 0.1 broadcast_in_dim.111
  47.5 0.0 collective-permute-done
  47.5 0.3 copy.21
  47.8 0.3 copy.25
  48.1 0.0 collective-permute-done.1
  48.1 0.3 copy.22
  48.4 0.3 copy.26
  48.7 0.0 collective-permute-done.2
  48.7 0.3 copy.23
  49.0 0.3 copy.27
  49.3 0.1 maximum_bitcast_fusion
  49.4 0.1 copy.28
  49.6 0.3 copy.31
  49.8 11.7 %fusion.4 = bf16[256,128]{0,1:T(8,128)(2,1)S(1)} fusion(bf16[4,256,208]{1,0,2:T(4,128)(2,1)S(1)} %copy.31, bf16[81,256,256]{2,1,0:T(8,128)(2,1)} %shard_map.55, pred[4,256]{1,0:T(4,128)(4,1)S(1)} %broadcast_in_dim.111), kind=kOutput, calls=%fused_computation.21 | convolution fusion | flops 5436047360 | bytes 11109376 | tf_op jit(solution)/shard_map/conv_general_dilated | solution.py:112
  61.5 0.1 copy.32
  61.6 0.2 copy.33
  61.8 0.1 copy.34
  61.9 0.6 gather_fusion
  62.6 0.1 collective-permute-start.3
  62.7 1.6 %collective-permute-start.4 = (bf16[8,1024]{1,0:T(8,128)(2,1)S(1)}, bf16[8,1024]{1,0:T(8,128)(2,1)S(1)}, u32[]{:S(2)}, u32[]{:S(2)}) collective-permute-start(bf16[8,1024]{1,0:T(8,128)(2,1)S(1)} %get-tuple-element.19), channel_id=1, source_target_pairs={{0,2},{1,3},{2,0},{3,1},{4,6},{5,7},{6,4},{7,5},{8,10},{9,11},{10,... | collective-permute-start | bytes 49160 | tf_op jit(solution)/shard_map/ppermute | solution.py:135
  64.2 1.4 %collective-permute-start.5 = (bf16[8,1024]{1,0:T(8,128)(2,1)S(1)}, bf16[8,1024]{1,0:T(8,128)(2,1)S(1)}, u32[]{:S(2)}, u32[]{:S(2)}) collective-permute-start(bf16[8,1024]{1,0:T(8,128)(2,1)S(1)} %get-tuple-element.18), channel_id=1, source_target_pairs={{0,3},{1,0},{2,1},{3,2},{4,7},{5,4},{6,5},{7,6},{8,11},{9,8},{10,9... | collective-permute-start | bytes 49160 | tf_op jit(solution)/shard_map/ppermute | solution.py:135
  65.6 0.2 collective-permute-done.3
  65.8 0.7 collective-permute-done.4
  66.5 0.6 collective-permute-done.5
  67.1 0.1 multiply_reduce_fusion
  67.2 0.7 %broadcast_multiply_fusion = f32[8,1024]{1,0:T(8,128)} fusion(f32[8]{0:T(128)S(1)} %add_rsqrt_fusion.1, bf16[8,1024]{1,0:T(8,128)(2,1)S(1)} %collective-permute-done.5, bf16[8,1024]{1,0:T(8,128)(2,1)S(1)} %collective-permute-done.4, bf16[8,1024]{1,0:T(8,128)(2,1)S(1)} %collective-permute-done.3, bf16[4,8,1024]{2,1,0:T(8,128)(2,1)S(1)} %bitcast.56, ...), kind=kLoop, calls=%fused_computation.43 | loop fusion | flops 73728 | bytes 98341 | tf_op jit(solution)/shard_map/mul | solution.py:140
  (13 shorter events, 0.1 us)
Async XLA Ops:
  0.0 13.5 %copy-start = (bf16[32,32,512]{2,1,0:T(8,128)(2,1)S(1)}, bf16[32,32,512]{2,1,0:T(8,128)(2,1)}, u32[]{:S(2)}) copy-start(bf16[32,32,512]{2,1,0:T(8,128)(2,1)} %param.8) | copy-start | bytes 3145732
  3.2 44.3 %collective-permute-start = (bf16[32,1664]{1,0:T(8,128)(2,1)S(1)}, bf16[32,1664]{1,0:T(8,128)(2,1)S(1)}, u32[]{:S(2)}, u32[]{:S(2)}) collective-permute-start(bf16[32,1664]{1,0:T(8,128)(2,1)S(1)} %fusion.12), channel_id=1, source_target_pairs={{0,4},{4,8},{8,12},{12,0},{1,5},{5,9},{9,13},{13,1},{2,6},{6,10},{... | collective-permute-start | bytes 319496 | tf_op jit(solution)/shard_map/ppermute | solution.py:94
  6.3 41.8 %collective-permute-start.1 = (bf16[32,1664]{1,0:T(8,128)(2,1)S(1)}, bf16[32,1664]{1,0:T(8,128)(2,1)S(1)}, u32[]{:S(2)}, u32[]{:S(2)}) collective-permute-start(bf16[32,1664]{1,0:T(8,128)(2,1)S(1)} %fusion.12), channel_id=1, source_target_pairs={{0,8},{4,12},{8,0},{12,4},{1,9},{5,13},{9,1},{13,5},{2,10},{6,14},... | collective-permute-start | bytes 319496 | tf_op jit(solution)/shard_map/ppermute | solution.py:94
  8.9 39.8 %collective-permute-start.2 = (bf16[32,1664]{1,0:T(8,128)(2,1)S(1)}, bf16[32,1664]{1,0:T(8,128)(2,1)S(1)}, u32[]{:S(2)}, u32[]{:S(2)}) collective-permute-start(bf16[32,1664]{1,0:T(8,128)(2,1)S(1)} %fusion.12), channel_id=1, source_target_pairs={{0,12},{4,0},{8,4},{12,8},{1,13},{5,1},{9,5},{13,9},{2,14},{6,2},{... | collective-permute-start | bytes 319496 | tf_op jit(solution)/shard_map/ppermute | solution.py:94
  38.4 8.3 %copy-start.1 = (s32[1,32]{1,0:T(1,128)S(1)}, s32[1,32]{1,0:T(1,128)}, u32[]{:S(2)}) copy-start(s32[1,32]{1,0:T(1,128)} %param.11) | copy-start | bytes 388
  62.6 3.2 %collective-permute-start.3 = (bf16[8,1024]{1,0:T(8,128)(2,1)S(1)}, bf16[8,1024]{1,0:T(8,128)(2,1)S(1)}, u32[]{:S(2)}, u32[]{:S(2)}) collective-permute-start(bf16[8,1024]{1,0:T(8,128)(2,1)S(1)} %get-tuple-element.17), channel_id=1, source_target_pairs={{0,1},{1,2},{2,3},{3,0},{4,5},{5,6},{6,7},{7,4},{8,9},{9,10},{10,1... | collective-permute-start | bytes 49160 | tf_op jit(solution)/shard_map/ppermute | solution.py:135
  62.7 3.8 %collective-permute-start.4 = (bf16[8,1024]{1,0:T(8,128)(2,1)S(1)}, bf16[8,1024]{1,0:T(8,128)(2,1)S(1)}, u32[]{:S(2)}, u32[]{:S(2)}) collective-permute-start(bf16[8,1024]{1,0:T(8,128)(2,1)S(1)} %get-tuple-element.19), channel_id=1, source_target_pairs={{0,2},{1,3},{2,0},{3,1},{4,6},{5,7},{6,4},{7,5},{8,10},{9,11},{10,... | collective-permute-start | bytes 49160 | tf_op jit(solution)/shard_map/ppermute | solution.py:135
  64.2 2.8 %collective-permute-start.5 = (bf16[8,1024]{1,0:T(8,128)(2,1)S(1)}, bf16[8,1024]{1,0:T(8,128)(2,1)S(1)}, u32[]{:S(2)}, u32[]{:S(2)}) collective-permute-start(bf16[8,1024]{1,0:T(8,128)(2,1)S(1)} %get-tuple-element.18), channel_id=1, source_target_pairs={{0,3},{1,0},{2,1},{3,2},{4,7},{5,4},{6,5},{7,6},{8,11},{9,8},{10,9... | collective-permute-start | bytes 49160 | tf_op jit(solution)/shard_map/ppermute | solution.py:135

commit v7 on v6

--- a/solution.py
+++ b/solution.py
@@ -38,13 +38,13 @@
     width = phases * chans
     first = pl.program_id(0) * steps
     for step in range(steps):
-        lo = grouped_ref[first + step].astype(jnp.float32)
-        hi = grouped_ref[first + step + 1].astype(jnp.float32)
+        lo = grouped_ref[first + step]
+        hi = grouped_ref[first + step + 1]
         joined = jnp.concatenate([lo, hi], axis=-1)
         for e in range(phases):
             cut = (phases - 1 - e) * chans
             moved = pltpu.roll(joined, 2 * width - cut, 1) if cut else joined
-            out_ref[step, e * count : (e + 1) * count, :] = moved[:, :width].astype(out_ref.dtype)
+            out_ref[step, e * count : (e + 1) * count, :] = moved[:, :width]
 
 
 def polyphase_filters(placed, phases):
@@ -86,16 +86,7 @@
     phases = PHASES
     signal = normalize_rows(data)
     n_chan = lax.axis_size("chan")
-    if n_chan <= 8:
-        me = lax.axis_index("chan")
-        pieces = [signal]
-        for shift in range(1, n_chan):
-            pairs = [(c, (c + shift) % n_chan) for c in range(n_chan)]
-            pieces.append(lax.ppermute(signal, "chan", pairs))
-        blocks = jnp.stack(pieces)
-    else:
-        blocks = lax.all_gather(signal, "chan", axis=0, tiled=False)
-    n_blocks = blocks.shape[0]
+    me = lax.axis_index("chan")
     shaped = normalize_rows(templates)
     local_chan = stations % ch_local
     target = stations[:, 0] // (ch_local * n_tmpl)
@@ -107,6 +98,16 @@
     ).astype(jnp.bfloat16)
     ordered_shift = jnp.sum(jnp.where(hit, offsets[:, :, None], 0), axis=1)
     placed = place_moveout(ordered, ordered_shift, padded_len)
+    signal, placed = lax.optimization_barrier((signal, placed))
+    if n_chan <= 8:
+        pieces = [signal]
+        for shift in range(1, n_chan):
+            pairs = [(c, (c + shift) % n_chan) for c in range(n_chan)]
+            pieces.append(lax.ppermute(signal, "chan", pairs))
+        blocks = jnp.stack(pieces)
+    else:
+        blocks = lax.all_gather(signal, "chan", axis=0, tiled=False)
+    n_blocks = blocks.shape[0]
     filters = polyphase_filters(placed, phases)
     lhs = polyphase_signal(blocks, phases)
     corr = lax.conv_general_dilated(

time: 68.5 us -> 68.9 us (level)
  local copies, waits for them, and re-layouts: 19.1 us -> 20.8 us
  other arithmetic: 16.8 us -> 15.4 us
    ppermute x3, local copies, waits for them, and re-layouts: 0.79 us -> 2.58 us  [shards(): pieces.append(lax.ppermute(signal, 'chan', pairs))]
    convert_element_type x1, other arithmetic: 0.99 us -> 0.1 us  [normalize_rows(): return (centred * scale).astype(jnp.bfloat16)]
    reduce_sum x2, other arithmetic: 1.62 us -> 0.75 us  [normalize_rows(): scale = lax.rsqrt(jnp.mean(centred * centred, axis=-1, keepdims=True) + eps)]
    unnamed x4 -> x8, local copies, waits for them, and re-layouts: 0.01 us -> 0.77 us
    slice x1, local copies, waits for them, and re-layouts: 0.83 us -> 0.11 us  [shards(): target = stations[:, 0] // (ch_local * n_tmpl)]
  transfers between devices with their start and end apart: 6 -> 6, of which waited for: 3 -> 3; matrix products, arithmetic and copies ran while one was open for 45% -> 26% of each run, Pallas kernels for 12% -> 12%
where the time goes in v7:
time: 68.9 us; the launch traced here: 68.3 us
  local copies, waits for them, and re-layouts  20.8 us (30%)
  other arithmetic  15.4 us (22%)
  matrix products  12.2 us (18%)
  starting transfers between devices  10.2 us (15%)
  Pallas kernels  7.92 us (11%)
  waiting for transfers between devices  1.45 us (2%)
    conv_general_dilated x1, matrix products, shards(): lax.conv_general_dilated(lhs, filters, (1,), 'VALID', dimension_numbers=(...  11.7 us
    select_n x8, other arithmetic, place_moveout(): current = jnp.where(active[..., None], moved, current)  9.75 us
    reshape x2, local copies, waits for them, and re-layouts, polyphase_filters(): jnp.transpose(padded, (0, 2, 1)).reshape(count, blocks, phases * chans)  8.27 us
    pallas_call x1, Pallas kernels, polyphase_filters(): pl.pallas_call(kernel, grid=(taps // steps,), in_specs=[pl.BlockSpec((blo...  7.92 us
    ppermute x3, starting transfers between devices, shards(): pieces.append(lax.ppermute(signal, 'chan', pairs))  7.19 us
    transpose x2, local copies, waits for them, and re-layouts, polyphase_filters(): jnp.transpose(padded, (0, 2, 1)).reshape(count, blocks, phases * chans)  5.01 us
    ppermute x3, starting transfers between devices, shards(): stack = stack + lax.ppermute(outgoing, 'tmpl', pairs).astype(jnp.float32)  3 us
    ppermute x3, local copies, waits for them, and re-layouts, shards(): pieces.append(lax.ppermute(signal, 'chan', pairs))  2.58 us
  transfers between devices with their start and end apart: 6, of which 3 were waited for; matrix products, arithmetic and copies ran while one was open for 26% of the time, Pallas kernels for 12%

profile of v7, /device:TPU:0, one launch (start us, length us, event | category | flops | bytes accessed | tf_op | source)
XLA Modules:
  0.0 68.3 jit_solution(294225230566671184)
XLA Ops:
  0.0 0.0 copy-start
  0.0 0.8 %add_select_fusion = s32[32,32]{1,0:T(8,128)S(1)} fusion(s32[32,32]{1,0:T(8,128)} %param.9), kind=kLoop, calls=%fused_computation.36 | loop fusion | flops 11264 | bytes 8192 | tf_op jit(solution)/shard_map/jit(remainder)/select_n | solution.py:91
  0.8 1.3 %select_reduce_fusion = s32[32,32]{1,0:T(8,128)S(1)} fusion(s32[32,32]{1,0:T(8,128)} %param.10, s32[32,32]{1,0:T(8,128)S(1)} %add_select_fusion), kind=kLoop, calls=%fused_computation.25 | loop fusion | flops 97280 | bytes 12288 | tf_op jit(solution)/shard_map/reduce_sum | solution.py:99
  2.2 1.4 %convert_reduce_fusion = f32[32,32]{1,0:T(8,128)S(1)} fusion(bf16[32,32,512]{2,1,0:T(8,128)(2,1)} %param.8), kind=kLoop, calls=%fused_computation.3 | loop fusion | flops 1047552 | bytes 1052672 | tf_op jit(solution)/shard_map/reduce_sum | solution.py:19
  3.7 0.0 copy-done
  3.7 0.5 fusion.2
  4.2 0.6 convolution_convert_fusion
  4.8 0.1 pad_slice_fusion
  4.9 1.3 %pad_select_fusion.7 = bf16[32,32,640]{2,1,0:T(8,128)(2,1)S(1)} fusion(bf16[32,32,639]{2,1,0:T(8,128)(2,1)S(1)} %pad_slice_fusion, pred[32,32]{1,0:T(8,128)(4,1)S(1)} %get-tuple-element.25, bf16[32,32,512]{2,1,0:T(8,128)(2,1)S(1)} %convolution_convert_fusion), kind=kLoop, calls=%fused_computation.18 | loop fusion | flops 655360 | bytes 3668992 | tf_op jit(solution)/shard_map/jit(_where)/select_n | solution.py:33
  6.2 1.3 %pad_select_fusion.6 = bf16[32,32,640]{2,1,0:T(8,128)(2,1)S(1)} fusion(bf16[32,32,640]{2,1,0:T(8,128)(2,1)S(1)} %pad_select_fusion.7, bf16[32,32,638]{2,1,0:T(8,128)(2,1)S(1)} %bitcast.41, pred[32,32]{1,0:T(8,128)(4,1)S(1)} %get-tuple-element.26), kind=kLoop, calls=%fused_computation.17 | loop fusion | flops 655360 | bytes 3929088 | tf_op jit(solution)/shard_map/jit(_where)/select_n | solution.py:33
  7.6 1.3 %pad_select_fusion.5 = bf16[32,32,640]{2,1,0:T(8,128)(2,1)S(1)} fusion(bf16[32,32,640]{2,1,0:T(8,128)(2,1)S(1)} %pad_select_fusion.6, bf16[32,32,636]{2,1,0:T(8,128)(2,1)S(1)} %bitcast.42, pred[32,32]{1,0:T(8,128)(4,1)S(1)} %get-tuple-element.27), kind=kLoop, calls=%fused_computation.16 | loop fusion | flops 655360 | bytes 3924992 | tf_op jit(solution)/shard_map/jit(_where)/select_n | solution.py:33
  8.9 1.3 %pad_select_fusion.4 = bf16[32,32,640]{2,1,0:T(8,128)(2,1)S(1)} fusion(bf16[32,32,640]{2,1,0:T(8,128)(2,1)S(1)} %pad_select_fusion.5, bf16[32,32,632]{2,1,0:T(8,128)(2,1)S(1)} %bitcast.43, pred[32,32]{1,0:T(8,128)(4,1)S(1)} %get-tuple-element.28), kind=kLoop, calls=%fused_computation.15 | loop fusion | flops 655360 | bytes 3916800 | tf_op jit(solution)/shard_map/jit(_where)/select_n | solution.py:33
  10.3 1.3 %pad_select_fusion.3 = bf16[32,32,640]{2,1,0:T(8,128)(2,1)S(1)} fusion(bf16[32,32,640]{2,1,0:T(8,128)(2,1)S(1)} %pad_select_fusion.4, bf16[32,32,624]{2,1,0:T(8,128)(2,1)S(1)} %bitcast.44, pred[32,32]{1,0:T(8,128)(4,1)S(1)} %get-tuple-element.29), kind=kLoop, calls=%fused_computation.14 | loop fusion | flops 655360 | bytes 3900416 | tf_op jit(solution)/shard_map/jit(_where)/select_n | solution.py:33
  11.6 1.3 %pad_select_fusion.2 = bf16[32,32,640]{2,1,0:T(8,128)(2,1)S(1)} fusion(bf16[32,32,640]{2,1,0:T(8,128)(2,1)S(1)} %pad_select_fusion.3, bf16[32,32,608]{2,1,0:T(8,128)(2,1)S(1)} %bitcast.45, pred[32,32]{1,0:T(8,128)(4,1)S(1)} %get-tuple-element.30), kind=kLoop, calls=%fused_computation.13 | loop fusion | flops 655360 | bytes 3867648 | tf_op jit(solution)/shard_map/jit(_where)/select_n | solution.py:33
  13.0 1.3 %pad_select_fusion.1 = bf16[32,32,640]{2,1,0:T(8,128)(2,1)S(1)} fusion(bf16[32,32,640]{2,1,0:T(8,128)(2,1)S(1)} %pad_select_fusion.2, bf16[32,32,576]{2,1,0:T(8,128)(2,1)S(1)} %bitcast.46, pred[32,32]{1,0:T(8,128)(4,1)S(1)} %get-tuple-element.31), kind=kLoop, calls=%fused_computation.12 | loop fusion | flops 655360 | bytes 3802112 | tf_op jit(solution)/shard_map/jit(_where)/select_n | solution.py:33
  14.3 0.0 copy-start.1
  14.3 0.1 slice.53
  14.5 0.8 %copy-done.1 = bf16[32,1664]{1,0:T(8,128)(2,1)S(1)} copy-done((bf16[32,1664]{1,0:T(8,128)(2,1)S(1)}, bf16[32,1664]{1,0:T(8,128)(2,1)}, u32[]{:S(2)}) %copy-start.1) | copy-done | bytes 106520
  15.2 0.1 convert_reduce_fusion.1
  15.3 0.2 fusion.11
  15.6 0.1 fusion.12
  15.7 0.0 copy-start.2
  15.7 0.4 pad_select_fusion
  16.1 3.3 %collective-permute-start = (bf16[32,1664]{1,0:T(8,128)(2,1)S(1)}, bf16[32,1664]{1,0:T(8,128)(2,1)}, u32[]{:S(2)}, u32[]{:S(2)}) collective-permute-start(bf16[32,1664]{1,0:T(8,128)(2,1)S(1)} %fusion.12), channel_id=1, source_target_pairs={{0,4},{4,8},{8,12},{12,0},{1,5},{5,9},{9,13},{13,1},{2,6},{6,10},{... | collective-permute-start | bytes 319496 | tf_op jit(solution)/shard_map/ppermute | solution.py:106
  19.3 2.6 %collective-permute-start.1 = (bf16[32,1664]{1,0:T(8,128)(2,1)S(1)}, bf16[32,1664]{1,0:T(8,128)(2,1)}, u32[]{:S(2)}, u32[]{:S(2)}) collective-permute-start(bf16[32,1664]{1,0:T(8,128)(2,1)S(1)} %fusion.12), channel_id=1, source_target_pairs={{0,8},{4,12},{8,0},{12,4},{1,9},{5,13},{9,1},{13,5},{2,10},{6,14},... | collective-permute-start | bytes 319496 | tf_op jit(solution)/shard_map/ppermute | solution.py:106
  21.9 1.3 %collective-permute-start.2 = (bf16[32,1664]{1,0:T(8,128)(2,1)S(1)}, bf16[32,1664]{1,0:T(8,128)(2,1)S(1)}, u32[]{:S(2)}, u32[]{:S(2)}) collective-permute-start(bf16[32,1664]{1,0:T(8,128)(2,1)S(1)} %fusion.12), channel_id=1, source_target_pairs={{0,12},{4,0},{8,4},{12,8},{1,13},{5,1},{9,5},{13,9},{2,14},{6,2},{... | collective-permute-start | bytes 319496 | tf_op jit(solution)/shard_map/ppermute | solution.py:106
  23.3 0.3 copy.20
  23.5 0.0 copy-done.2
  23.5 0.1 slice_reduce_fusion
  23.7 0.7 %pad_bitcast_fusion = bf16[32,656,32]{1,2,0:T(8,128)(2,1)S(1)} fusion(bf16[32,32,640]{2,1,0:T(8,128)(2,1)S(1)} %pad_select_fusion), kind=kLoop, calls=%fused_computation.8 | loop fusion | bytes 2654208 | tf_op jit(solution)/shard_map/transpose | solution.py:56
  24.4 4.3 %copy.29 = bf16[32,656,32]{2,1,0:T(8,128)(2,1)} copy(bf16[32,656,32]{1,2,0:T(8,128)(2,1)S(1)} %pad_bitcast_fusion) | data formatting | bytes 2686976 | tf_op jit(solution)/shard_map/transpose | solution.py:56
  28.7 6.9 %reshape.186 = bf16[32,82,256]{2,1,0:T(8,128)(2,1)S(1)} reshape(bf16[32,656,32]{2,1,0:T(8,128)(2,1)} %copy.29) | data formatting | bytes 2686976 | tf_op jit(solution)/shard_map/reshape | solution.py:56
  35.6 1.4 %copy.36 = bf16[32,82,256]{2,0,1:T(8,128)(2,1)} copy(bf16[32,82,256]{2,1,0:T(8,128)(2,1)S(1)} %reshape.186) | data formatting | bytes 2686976 | tf_op jit(solution)/shard_map/reshape | solution.py:56
  37.0 0.0 copy-start.3
  37.0 7.9 %shard_map.55 = bf16[81,256,256]{2,1,0:T(8,128)(2,1)} custom-call(bf16[82,32,256]{2,1,0:T(8,128)(2,1)} %bitcast.47), custom_call_target="tpu_custom_call" | custom-call | tf_op jit(solution)/shard_map/pallas_call | solution.py:63
  44.9 0.3 copy.24
  45.2 0.0 copy-done.3
  45.3 0.7 scatter_custom_fusion
  46.0 0.1 broadcast_in_dim.111
  46.1 0.0 collective-permute-done
  46.1 1.2 %copy.21 = bf16[32,1664]{0,1:T(8,128)(2,1)S(1)} copy(bf16[32,1664]{1,0:T(8,128)(2,1)} %collective-permute-done) | data formatting | bytes 212992 | tf_op jit(solution)/shard_map/ppermute | solution.py:106
  47.3 0.3 copy.25
  47.6 0.0 collective-permute-done.1
  47.6 1.2 %copy.22 = bf16[32,1664]{0,1:T(8,128)(2,1)S(1)} copy(bf16[32,1664]{1,0:T(8,128)(2,1)} %collective-permute-done.1) | data formatting | bytes 212992 | tf_op jit(solution)/shard_map/ppermute | solution.py:106
  48.8 0.3 copy.26
  49.1 0.0 collective-permute-done.2
  49.1 0.3 copy.23
  49.4 0.3 copy.27
  49.7 0.1 maximum_bitcast_fusion
  49.9 0.1 copy.28
  50.0 0.3 copy.31
  50.3 11.7 %fusion.4 = bf16[256,128]{0,1:T(8,128)(2,1)S(1)} fusion(bf16[4,256,208]{1,0,2:T(4,128)(2,1)S(1)} %copy.31, bf16[81,256,256]{2,1,0:T(8,128)(2,1)} %shard_map.55, pred[4,256]{1,0:T(4,128)(4,1)S(1)} %broadcast_in_dim.111), kind=kOutput, calls=%fused_computation.21 | convolution fusion | flops 5436047360 | bytes 11109376 | tf_op jit(solution)/shard_map/conv_general_dilated | solution.py:113
  61.9 0.1 copy.32
  62.0 0.2 copy.33
  62.2 0.1 copy.34
  62.4 0.6 gather_fusion
  63.0 0.1 collective-permute-start.3
  63.1 1.6 %collective-permute-start.4 = (bf16[8,1024]{1,0:T(8,128)(2,1)S(1)}, bf16[8,1024]{1,0:T(8,128)(2,1)S(1)}, u32[]{:S(2)}, u32[]{:S(2)}) collective-permute-start(bf16[8,1024]{1,0:T(8,128)(2,1)S(1)} %get-tuple-element.23), channel_id=1, source_target_pairs={{0,2},{1,3},{2,0},{3,1},{4,6},{5,7},{6,4},{7,5},{8,10},{9,11},{10,... | collective-permute-start | bytes 49160 | tf_op jit(solution)/shard_map/ppermute | solution.py:136
  64.6 1.4 %collective-permute-start.5 = (bf16[8,1024]{1,0:T(8,128)(2,1)S(1)}, bf16[8,1024]{1,0:T(8,128)(2,1)S(1)}, u32[]{:S(2)}, u32[]{:S(2)}) collective-permute-start(bf16[8,1024]{1,0:T(8,128)(2,1)S(1)} %get-tuple-element.22), channel_id=1, source_target_pairs={{0,3},{1,0},{2,1},{3,2},{4,7},{5,4},{6,5},{7,6},{8,11},{9,8},{10,9... | collective-permute-start | bytes 49160 | tf_op jit(solution)/shard_map/ppermute | solution.py:136
  66.0 0.2 collective-permute-done.3
  66.2 0.7 collective-permute-done.4
  66.9 0.6 collective-permute-done.5
  67.5 0.1 multiply_reduce_fusion
  67.6 0.7 %broadcast_multiply_fusion = f32[8,1024]{1,0:T(8,128)} fusion(f32[8]{0:T(128)S(1)} %add_rsqrt_fusion.1, bf16[8,1024]{1,0:T(8,128)(2,1)S(1)} %collective-permute-done.5, bf16[8,1024]{1,0:T(8,128)(2,1)S(1)} %collective-permute-done.4, bf16[8,1024]{1,0:T(8,128)(2,1)S(1)} %collective-permute-done.3, bf16[4,8,1024]{2,1,0:T(8,128)(2,1)S(1)} %bitcast.56, ...), kind=kLoop, calls=%fused_computation.43 | loop fusion | flops 73728 | bytes 98341 | tf_op jit(solution)/shard_map/mul | solution.py:141
  (13 shorter events, 0.1 us)
Async XLA Ops:
  0.0 3.7 %copy-start = (bf16[32,32,512]{2,1,0:T(8,128)(2,1)S(1)}, bf16[32,32,512]{2,1,0:T(8,128)(2,1)}, u32[]{:S(2)}) copy-start(bf16[32,32,512]{2,1,0:T(8,128)(2,1)} %param.8) | copy-start | bytes 3145732
  14.3 0.9 %copy-start.1 = (bf16[32,1664]{1,0:T(8,128)(2,1)S(1)}, bf16[32,1664]{1,0:T(8,128)(2,1)}, u32[]{:S(2)}) copy-start(bf16[32,1664]{1,0:T(8,128)(2,1)} %param.7) | copy-start | bytes 319492
  15.7 7.9 %copy-start.2 = (s32[32,32]{1,0:T(8,128)S(1)}, s32[32,32]{1,0:T(8,128)}, u32[]{:S(2)}) copy-start(s32[32,32]{1,0:T(8,128)} %param.9) | copy-start | bytes 12292
  16.1 30.0 %collective-permute-start = (bf16[32,1664]{1,0:T(8,128)(2,1)S(1)}, bf16[32,1664]{1,0:T(8,128)(2,1)}, u32[]{:S(2)}, u32[]{:S(2)}) collective-permute-start(bf16[32,1664]{1,0:T(8,128)(2,1)S(1)} %fusion.12), channel_id=1, source_target_pairs={{0,4},{4,8},{8,12},{12,0},{1,5},{5,9},{9,13},{13,1},{2,6},{6,10},{... | collective-permute-start | bytes 319496 | tf_op jit(solution)/shard_map/ppermute | solution.py:106
  19.3 28.3 %collective-permute-start.1 = (bf16[32,1664]{1,0:T(8,128)(2,1)S(1)}, bf16[32,1664]{1,0:T(8,128)(2,1)}, u32[]{:S(2)}, u32[]{:S(2)}) collective-permute-start(bf16[32,1664]{1,0:T(8,128)(2,1)S(1)} %fusion.12), channel_id=1, source_target_pairs={{0,8},{4,12},{8,0},{12,4},{1,9},{5,13},{9,1},{13,5},{2,10},{6,14},... | collective-permute-start | bytes 319496 | tf_op jit(solution)/shard_map/ppermute | solution.py:106
  21.9 27.2 %collective-permute-start.2 = (bf16[32,1664]{1,0:T(8,128)(2,1)S(1)}, bf16[32,1664]{1,0:T(8,128)(2,1)S(1)}, u32[]{:S(2)}, u32[]{:S(2)}) collective-permute-start(bf16[32,1664]{1,0:T(8,128)(2,1)S(1)} %fusion.12), channel_id=1, source_target_pairs={{0,12},{4,0},{8,4},{12,8},{1,13},{5,1},{9,5},{13,9},{2,14},{6,2},{... | collective-permute-start | bytes 319496 | tf_op jit(solution)/shard_map/ppermute | solution.py:106
  37.0 8.3 %copy-start.3 = (s32[1,32]{1,0:T(1,128)S(1)}, s32[1,32]{1,0:T(1,128)}, u32[]{:S(2)}) copy-start(s32[1,32]{1,0:T(1,128)} %param.11) | copy-start | bytes 388
  63.0 3.2 %collective-permute-start.3 = (bf16[8,1024]{1,0:T(8,128)(2,1)S(1)}, bf16[8,1024]{1,0:T(8,128)(2,1)S(1)}, u32[]{:S(2)}, u32[]{:S(2)}) collective-permute-start(bf16[8,1024]{1,0:T(8,128)(2,1)S(1)} %get-tuple-element.21), channel_id=1, source_target_pairs={{0,1},{1,2},{2,3},{3,0},{4,5},{5,6},{6,7},{7,4},{8,9},{9,10},{10,1... | collective-permute-start | bytes 49160 | tf_op jit(solution)/shard_map/ppermute | solution.py:136
  63.1 3.8 %collective-permute-start.4 = (bf16[8,1024]{1,0:T(8,128)(2,1)S(1)}, bf16[8,1024]{1,0:T(8,128)(2,1)S(1)}, u32[]{:S(2)}, u32[]{:S(2)}) collective-permute-start(bf16[8,1024]{1,0:T(8,128)(2,1)S(1)} %get-tuple-element.23), channel_id=1, source_target_pairs={{0,2},{1,3},{2,0},{3,1},{4,6},{5,7},{6,4},{7,5},{8,10},{9,11},{10,... | collective-permute-start | bytes 49160 | tf_op jit(solution)/shard_map/ppermute | solution.py:136
  64.6 2.8 %collective-permute-start.5 = (bf16[8,1024]{1,0:T(8,128)(2,1)S(1)}, bf16[8,1024]{1,0:T(8,128)(2,1)S(1)}, u32[]{:S(2)}, u32[]{:S(2)}) collective-permute-start(bf16[8,1024]{1,0:T(8,128)(2,1)S(1)} %get-tuple-element.22), channel_id=1, source_target_pairs={{0,3},{1,0},{2,1},{3,2},{4,7},{5,4},{6,5},{7,6},{8,11},{9,8},{10,9... | collective-permute-start | bytes 49160 | tf_op jit(solution)/shard_map/ppermute | solution.py:136

commit v8 on v7

--- a/solution.py
+++ b/solution.py
@@ -69,11 +69,72 @@
     )(grouped)
 
 
-def polyphase_signal(blocks, phases):
-    n_blocks, chans, window = blocks.shape
-    split = blocks.reshape(n_blocks, chans, window // phases, phases)
-    split = jnp.transpose(split, (0, 3, 1, 2))
-    return split.reshape(n_blocks, phases * chans, window // phases)
+def _corr_kernel(grouped_ref, signal_ref, out_ref, acc_ref, filt_ref, *, steps, count, chans, phases, rows):
+    width = phases * chans
+    pid = pl.program_id(0)
+
+    @pl.when(pid == 0)
+    def _():
+        acc_ref[...] = jnp.zeros_like(acc_ref)
+
+    base = pl.multiple_of(pid * steps, steps)
+    for step in range(steps):
+        joined = jnp.concatenate([grouped_ref[base + step], grouped_ref[base + step + 1]], axis=-1)
+        for e in range(phases):
+            cut = (phases - 1 - e) * chans
+            moved = pltpu.roll(joined, 2 * width - cut, 1) if cut else joined
+            filt_ref[step, e * count : (e + 1) * count, :] = moved[:, :width]
+
+    def accumulate(g, carry):
+        band = signal_ref[g, pl.ds(base, rows + steps), :]
+        total = acc_ref[g]
+        for step in range(steps):
+            window = band[step : step + rows].astype(filt_ref.dtype)
+            total += lax.dot_general(
+                window, filt_ref[step], (((1,), (1,)), ((), ())),
+                preferred_element_type=jnp.float32,
+            )
+        acc_ref[g] = total
+        return carry
+
+    lax.fori_loop(0, signal_ref.shape[0], accumulate, 0)
+
+    @pl.when(pid == pl.num_programs(0) - 1)
+    def _():
+        out_ref[...] = acc_ref[...]
+
+
+def correlate(placed, blocks, phases, lags):
+    count, chans, padded_len = placed.shape
+    n_blocks, _, window = blocks.shape
+    steps = 8
+    taps = -(-(padded_len // phases + 1) // steps) * steps
+    front = phases - 1
+    n_groups = taps + 1
+    rows = lags // phases
+    width = phases * chans
+    padded = jnp.pad(placed, ((0, 0), (0, 0), (front, n_groups * phases - padded_len - front)))
+    grouped = jnp.transpose(padded, (0, 2, 1)).reshape(count, n_groups, width)
+    grouped = jnp.transpose(grouped, (1, 0, 2))
+    signal = jnp.transpose(blocks, (0, 2, 1)).reshape(n_blocks, window // phases, width)
+    signal = jnp.pad(signal.astype(jnp.float32), ((0, 0), (0, taps + rows - window // phases), (0, 0)))
+    kernel = functools.partial(
+        _corr_kernel, steps=steps, count=count, chans=chans, phases=phases, rows=rows
+    )
+    return pl.pallas_call(
+        kernel,
+        grid=(taps // steps,),
+        in_specs=[
+            pl.BlockSpec(grouped.shape, lambda q: (0, 0, 0)),
+            pl.BlockSpec(signal.shape, lambda q: (0, 0, 0)),
+        ],
+        out_specs=pl.BlockSpec((n_blocks, rows, phases * count), lambda q: (0, 0, 0)),
+        out_shape=jax.ShapeDtypeStruct((n_blocks, rows, phases * count), jnp.float32),
+        scratch_shapes=[
+            pltpu.VMEM((n_blocks, rows, phases * count), jnp.float32),
+            pltpu.VMEM((steps, phases * count, width), placed.dtype),
+        ],
+    )(grouped, signal)
 
 
 def shards(data, templates, stations, offsets, owner_map):
@@ -108,20 +169,11 @@
     else:
         blocks = lax.all_gather(signal, "chan", axis=0, tiled=False)
     n_blocks = blocks.shape[0]
-    filters = polyphase_filters(placed, phases)
-    lhs = polyphase_signal(blocks, phases)
-    corr = lax.conv_general_dilated(
-        lhs,
-        filters,
-        (1,),
-        "VALID",
-        dimension_numbers=("NCH", "HOI", "NCH"),
-        preferred_element_type=jnp.float32,
-    )
-    corr = corr[:, :, : lags // phases].reshape(n_blocks, phases, count, lags // phases)
+    corr = correlate(placed, blocks, phases, lags)
+    corr = corr.reshape(n_blocks, lags // phases, phases, count)
     pick = target[None, :] == jnp.arange(n_blocks, dtype=jnp.int32)[:, None]
-    chosen = jnp.sum(jnp.where(pick[:, None, :, None], corr, 0.0), axis=0)
-    partial_value = jnp.transpose(chosen, (1, 2, 0)).reshape(count, lags)
+    chosen = jnp.sum(jnp.where(pick[:, None, None, :], corr, 0.0), axis=0)
+    partial_value = jnp.transpose(chosen, (2, 0, 1)).reshape(count, lags)
     partial_value = partial_value.astype(jnp.bfloat16)
     inverse = (
         jnp.zeros((count,), jnp.int32).at[owner_map[0]].set(jnp.arange(count, dtype=jnp.int32))

time: 68.9 us -> 76.7 us (1.11)
  Pallas kernels: 7.92 us -> 26.8 us
  matrix products: 12.2 us -> 0.56 us
  other arithmetic: 15.4 us -> 18.6 us
  starting transfers between devices: 10.2 us -> 7.9 us
  local copies, waits for them, and re-layouts: 20.8 us -> 19.1 us
  waiting for transfers between devices: 1.45 us -> 3 us
    pallas_call x1, Pallas kernels: 7.92 us -> 26.8 us  [correlate(): pl.pallas_call(kernel, grid=(taps // steps,), in_specs=[pl.BlockSpec(grou...]
    conv_general_dilated x1 -> x0, matrix products: 11.7 us -> none  [shards(): lax.conv_general_dilated(lhs, filters, (1,), 'VALID', dimension_numbers=(...]
    ppermute x3 -> x0, local copies, waits for them, and re-layouts: 2.58 us -> none  [shards(): pieces.append(lax.ppermute(signal, 'chan', pairs))]
    convert_element_type x0 -> x2, local copies, waits for them, and re-layouts: none -> 2.11 us  [correlate(): signal.astype(jnp.float32)]
    ppermute x3, waiting for transfers between devices: 1.44 us -> 3 us  [shards(): stack = stack + lax.ppermute(outgoing, 'tmpl', pairs).astype(jnp.float32)]
    another operation x4 -> x0, local copies, waits for them, and re-layouts: 1.31 us -> none  [shards(): blocks = jnp.stack(pieces)]
    ppermute x3, starting transfers between devices: 3 us -> 1.79 us  [shards(): stack = stack + lax.ppermute(outgoing, 'tmpl', pairs).astype(jnp.float32)]
    reduce_sum x0 -> x1, other arithmetic: none -> 1.08 us  [shards(): chosen = jnp.sum(jnp.where(pick[:, None, None, :], corr, 0.0), axis=0)]
  transfers between devices with their start and end apart: 6 -> 6, of which waited for: 3 -> 2; matrix products, arithmetic and copies ran while one was open for 26% -> 20% of each run, Pallas kernels for 12% -> 0%
where the time goes in v8:
time: 76.7 us; the launch traced here: 76.3 us
  Pallas kernels  26.8 us (35%)
  local copies, waits for them, and re-layouts  19.1 us (25%)
  other arithmetic  18.6 us (24%)
  starting transfers between devices  7.9 us (10%)
  waiting for transfers between devices  3 us (4%)
    pallas_call x1, Pallas kernels, correlate(): pl.pallas_call(kernel, grid=(taps // steps,), in_specs=[pl.BlockSpec(grou...  26.8 us
    select_n x8, other arithmetic, place_moveout(): current = jnp.where(active[..., None], moved, current)  9.75 us
    reshape x2, local copies, waits for them, and re-layouts, correlate(): grouped = jnp.transpose(padded, (0, 2, 1)).reshape(count, n_groups, width)  8.94 us
    ppermute x3, starting transfers between devices, shards(): pieces.append(lax.ppermute(signal, 'chan', pairs))  6.12 us
    transpose x2, local copies, waits for them, and re-layouts, correlate(): grouped = jnp.transpose(padded, (0, 2, 1)).reshape(count, n_groups, width)  5.22 us
    ppermute x3, waiting for transfers between devices, shards(): stack = stack + lax.ppermute(outgoing, 'tmpl', pairs).astype(jnp.float32)  3 us
    reduce_sum x2, other arithmetic, normalize_rows(): centred = values - jnp.mean(values, axis=-1, keepdims=True)  2.54 us
    convert_element_type x2, local copies, waits for them, and re-layouts, correlate(): signal.astype(jnp.float32)  2.11 us
  transfers between devices with their start and end apart: 6, of which 2 were waited for; matrix products, arithmetic and copies ran while one was open for 20% of the time, Pallas kernels for 0%

profile of v8, /device:TPU:0, one launch (start us, length us, event | category | flops | bytes accessed | tf_op | source)
XLA Modules:
  0.0 76.3 jit_solution(11216373691822369109)
XLA Ops:
  0.0 0.0 copy-start
  0.0 0.0 copy-start.1
  0.0 1.1 %convert_reduce_fusion.1 = f32[32]{0:T(128)S(1)} fusion(bf16[32,1664]{1,0:T(8,128)(2,1)} %param.7), kind=kLoop, calls=%fused_computation.28 | loop fusion | flops 106464 | bytes 106624 | tf_op jit(solution)/shard_map/reduce_sum | solution.py:19
  1.1 1.1 %fusion.10 = f32[32]{0:T(128)S(1)} fusion(bf16[32,1664]{1,0:T(8,128)(2,1)} %param.7, f32[32]{0:T(128)S(1)} %broadcast_multiply_fusion.2), kind=kLoop, calls=%fused_computation.32 | loop fusion | flops 212960 | bytes 106752 | tf_op jit(solution)/shard_map/reduce_sum | solution.py:20
  2.2 1.0 %fusion.11 = bf16[32,1664]{1,0:T(8,128)(2,1)S(1)} fusion(bf16[32,1664]{1,0:T(8,128)(2,1)} %param.7, f32[32]{0:T(128)S(1)} %add_rsqrt_fusion.2, f32[32]{0:T(128)S(1)} %broadcast_multiply_fusion.2), kind=kLoop, calls=%fused_computation.33 | loop fusion | flops 212992 | bytes 213248 | tf_op jit(solution)/shard_map/convert_element_type | solution.py:21
  3.2 1.4 %convert_reduce_fusion = f32[32,32]{1,0:T(8,128)S(1)} fusion(bf16[32,32,512]{2,1,0:T(8,128)(2,1)} %param.8), kind=kLoop, calls=%fused_computation.3 | loop fusion | flops 1047552 | bytes 1052672 | tf_op jit(solution)/shard_map/reduce_sum | solution.py:19
  4.7 0.0 copy-done
  4.7 0.5 fusion.2
  5.3 0.0 copy-done.1
  5.3 0.6 convolution_convert_fusion
  5.8 0.0 copy-start.2
  5.9 0.1 pad_slice_fusion
  6.0 0.6 copy-done.2
  6.6 0.6 select_reduce_fusion.1
  7.2 1.3 %pad_select_fusion.7 = bf16[32,32,640]{2,1,0:T(8,128)(2,1)S(1)} fusion(bf16[32,32,639]{2,1,0:T(8,128)(2,1)S(1)} %pad_slice_fusion, pred[32,32]{1,0:T(8,128)(4,1)S(1)} %get-tuple-element.25, bf16[32,32,512]{2,1,0:T(8,128)(2,1)S(1)} %convolution_convert_fusion), kind=kLoop, calls=%fused_computation.18 | loop fusion | flops 655360 | bytes 3668992 | tf_op jit(solution)/shard_map/jit(_where)/select_n | solution.py:33
  8.5 1.3 %pad_select_fusion.6 = bf16[32,32,640]{2,1,0:T(8,128)(2,1)S(1)} fusion(bf16[32,32,640]{2,1,0:T(8,128)(2,1)S(1)} %pad_select_fusion.7, bf16[32,32,638]{2,1,0:T(8,128)(2,1)S(1)} %bitcast.38, pred[32,32]{1,0:T(8,128)(4,1)S(1)} %get-tuple-element.26), kind=kLoop, calls=%fused_computation.17 | loop fusion | flops 655360 | bytes 3929088 | tf_op jit(solution)/shard_map/jit(_where)/select_n | solution.py:33
  9.9 1.3 %pad_select_fusion.5 = bf16[32,32,640]{2,1,0:T(8,128)(2,1)S(1)} fusion(bf16[32,32,640]{2,1,0:T(8,128)(2,1)S(1)} %pad_select_fusion.6, bf16[32,32,636]{2,1,0:T(8,128)(2,1)S(1)} %bitcast.39, pred[32,32]{1,0:T(8,128)(4,1)S(1)} %get-tuple-element.27), kind=kLoop, calls=%fused_computation.16 | loop fusion | flops 655360 | bytes 3924992 | tf_op jit(solution)/shard_map/jit(_where)/select_n | solution.py:33
  11.2 1.3 %pad_select_fusion.4 = bf16[32,32,640]{2,1,0:T(8,128)(2,1)S(1)} fusion(bf16[32,32,640]{2,1,0:T(8,128)(2,1)S(1)} %pad_select_fusion.5, bf16[32,32,632]{2,1,0:T(8,128)(2,1)S(1)} %bitcast.40, pred[32,32]{1,0:T(8,128)(4,1)S(1)} %get-tuple-element.28), kind=kLoop, calls=%fused_computation.15 | loop fusion | flops 655360 | bytes 3916800 | tf_op jit(solution)/shard_map/jit(_where)/select_n | solution.py:33
  12.6 1.3 %pad_select_fusion.3 = bf16[32,32,640]{2,1,0:T(8,128)(2,1)S(1)} fusion(bf16[32,32,640]{2,1,0:T(8,128)(2,1)S(1)} %pad_select_fusion.4, bf16[32,32,624]{2,1,0:T(8,128)(2,1)S(1)} %bitcast.41, pred[32,32]{1,0:T(8,128)(4,1)S(1)} %get-tuple-element.29), kind=kLoop, calls=%fused_computation.14 | loop fusion | flops 655360 | bytes 3900416 | tf_op jit(solution)/shard_map/jit(_where)/select_n | solution.py:33
  13.9 1.3 %pad_select_fusion.2 = bf16[32,32,640]{2,1,0:T(8,128)(2,1)S(1)} fusion(bf16[32,32,640]{2,1,0:T(8,128)(2,1)S(1)} %pad_select_fusion.3, bf16[32,32,608]{2,1,0:T(8,128)(2,1)S(1)} %bitcast.42, pred[32,32]{1,0:T(8,128)(4,1)S(1)} %get-tuple-element.30), kind=kLoop, calls=%fused_computation.13 | loop fusion | flops 655360 | bytes 3867648 | tf_op jit(solution)/shard_map/jit(_where)/select_n | solution.py:33
  15.3 1.3 %pad_select_fusion.1 = bf16[32,32,640]{2,1,0:T(8,128)(2,1)S(1)} fusion(bf16[32,32,640]{2,1,0:T(8,128)(2,1)S(1)} %pad_select_fusion.2, bf16[32,32,576]{2,1,0:T(8,128)(2,1)S(1)} %bitcast.43, pred[32,32]{1,0:T(8,128)(4,1)S(1)} %get-tuple-element.31), kind=kLoop, calls=%fused_computation.12 | loop fusion | flops 655360 | bytes 3802112 | tf_op jit(solution)/shard_map/jit(_where)/select_n | solution.py:33
  16.6 0.1 slice.53
  16.7 0.4 pad_select_fusion
  17.1 5.1 %collective-permute-start.2 = (bf16[32,1664]{1,0:T(8,128)(2,1)S(1)}, bf16[32,1664]{1,0:T(8,128)(2,1)S(1)}, u32[]{:S(2)}, u32[]{:S(2)}) collective-permute-start(bf16[32,1664]{1,0:T(8,128)(2,1)S(1)} %fusion.11), channel_id=1, source_target_pairs={{0,12},{4,0},{8,4},{12,8},{1,13},{5,1},{9,5},{13,9},{2,14},{6,2},{... | collective-permute-start | bytes 319496 | tf_op jit(solution)/shard_map/ppermute | solution.py:167
  22.2 0.0 collective-permute-start.1
  22.2 1.0 %collective-permute-start = (bf16[32,1664]{1,0:T(8,128)(2,1)S(1)}, bf16[32,1664]{1,0:T(8,128)(2,1)S(1)}, u32[]{:S(2)}, u32[]{:S(2)}) collective-permute-start(bf16[32,1664]{1,0:T(8,128)(2,1)S(1)} %fusion.11), channel_id=1, source_target_pairs={{0,4},{4,8},{8,12},{12,0},{1,5},{5,9},{9,13},{13,1},{2,6},{6,10},{... | collective-permute-start | bytes 319496 | tf_op jit(solution)/shard_map/ppermute | solution.py:167
  23.3 0.1 slice_reduce_fusion
  23.4 0.7 pad_bitcast_fusion
  24.2 4.5 %copy.12 = bf16[32,712,32]{2,1,0:T(8,128)(2,1)} copy(bf16[32,712,32]{1,2,0:T(8,128)(2,1)S(1)} %pad_bitcast_fusion) | data formatting | bytes 2916352 | tf_op jit(solution)/shard_map/transpose | solution.py:117
  28.7 7.0 %reshape.175 = bf16[32,89,256]{2,1,0:T(8,128)(2,1)S(1)} reshape(bf16[32,712,32]{2,1,0:T(8,128)(2,1)} %copy.12) | data formatting | bytes 2916352 | tf_op jit(solution)/shard_map/reshape | solution.py:117
  35.7 0.0 copy-start.3
  35.7 1.9 %copy.19 = bf16[32,89,256]{2,0,1:T(8,128)(2,1)} copy(bf16[32,89,256]{2,1,0:T(8,128)(2,1)S(1)} %reshape.175) | data formatting | bytes 2916352 | tf_op jit(solution)/shard_map/reshape | solution.py:117
  37.6 0.0 copy-done.3
  37.6 0.7 scatter_custom_fusion
  38.4 0.1 broadcast_in_dim.111
  38.4 0.0 collective-permute-done.2
  38.5 0.0 collective-permute-done.1
  38.5 0.0 collective-permute-done
  38.5 0.1 maximum_bitcast_fusion
  38.5 0.9 %copy.14 = bf16[4,1664,32]{2,1,0:T(8,128)(2,1)S(1)} copy(bf16[4,1664,32]{1,2,0:T(8,128)(2,1)S(1)} %maximum_bitcast_fusion) | data formatting | bytes 851968 | tf_op jit(solution)/shard_map/convert_element_type | solution.py:120
  39.5 1.2 %convert_element_type.57 = bf16[4,208,256]{2,1,0:T(8,128)(2,1)S(1)} reshape(bf16[4,1664,32]{2,1,0:T(8,128)(2,1)S(1)} %copy.14) | data formatting | bytes 851968 | tf_op jit(solution)/shard_map/convert_element_type | solution.py:120
  40.7 1.0 %pad_convert_fusion.signal_ref = f32[4,216,256]{2,1,0:T(8,128)} fusion(bf16[4,208,256]{2,1,0:T(8,128)(2,1)S(1)} %convert_element_type.57), kind=kLoop, calls=%fused_computation.25 | loop fusion | flops 221184 | bytes 1310720 | tf_op jit(solution)/shard_map/jit(_pad)/pad | solution.py:120
  41.7 26.8 %shard_map.55 = f32[4,128,256]{2,1,0:T(8,128)} custom-call(bf16[89,32,256]{2,1,0:T(8,128)(2,1)} %bitcast.44, f32[4,216,256]{2,1,0:T(8,128)} %pad_convert_fusion.signal_ref), custom_call_target="tpu_custom_call" | custom-call | tf_op jit(solution)/shard_map/pallas_call | solution.py:124
  68.5 1.1 %select_reduce_fusion = bf16[128,256]{1,0:T(8,128)(2,1)S(1)} fusion(f32[4,128,256]{2,1,0:T(8,128)} %shard_map.55, pred[4,256]{1,0:T(4,128)(4,1)S(1)} %broadcast_in_dim.111), kind=kLoop, calls=%fused_computation.22 | loop fusion | flops 229376 | bytes 590848 | tf_op jit(solution)/shard_map/reduce_sum | solution.py:175
  69.6 0.1 copy.15
  69.7 0.2 copy.16
  69.9 0.1 copy.17
  70.0 0.6 gather_fusion
  70.6 0.1 collective-permute-start.5
  70.8 1.5 %collective-permute-start.4 = (bf16[8,1024]{1,0:T(8,128)(2,1)S(1)}, bf16[8,1024]{1,0:T(8,128)(2,1)S(1)}, u32[]{:S(2)}, u32[]{:S(2)}) collective-permute-start(bf16[8,1024]{1,0:T(8,128)(2,1)S(1)} %get-tuple-element.23), channel_id=1, source_target_pairs={{0,2},{1,3},{2,0},{3,1},{4,6},{5,7},{6,4},{7,5},{8,10},{9,11},{10,... | collective-permute-start | bytes 49160 | tf_op jit(solution)/shard_map/ppermute | solution.py:188
  72.3 0.2 collective-permute-start.3
  72.4 0.0 collective-permute-done.5
  72.4 2.1 %collective-permute-done.4 = bf16[8,1024]{1,0:T(8,128)(2,1)S(1)} collective-permute-done((bf16[8,1024]{1,0:T(8,128)(2,1)S(1)}, bf16[8,1024]{1,0:T(8,128)(2,1)S(1)}, u32[]{:S(2)}, u32[]{:S(2)}) %collective-permute-start.4) | collective-permute-done | bytes 16416 | tf_op jit(solution)/shard_map/ppermute | solution.py:188
  74.5 0.9 %collective-permute-done.3 = bf16[8,1024]{1,0:T(8,128)(2,1)S(1)} collective-permute-done((bf16[8,1024]{1,0:T(8,128)(2,1)S(1)}, bf16[8,1024]{1,0:T(8,128)(2,1)S(1)}, u32[]{:S(2)}, u32[]{:S(2)}) %collective-permute-start.3) | collective-permute-done | bytes 16416 | tf_op jit(solution)/shard_map/ppermute | solution.py:188
  75.4 0.1 multiply_reduce_fusion
  75.6 0.7 broadcast_multiply_fusion
  (14 shorter events, 0.1 us)
Async XLA Ops:
  0.0 4.7 %copy-start = (bf16[32,32,512]{2,1,0:T(8,128)(2,1)S(1)}, bf16[32,32,512]{2,1,0:T(8,128)(2,1)}, u32[]{:S(2)}) copy-start(bf16[32,32,512]{2,1,0:T(8,128)(2,1)} %param.8) | copy-start | bytes 3145732
  0.0 5.3 %copy-start.1 = (s32[32,32]{1,0:T(8,128)S(1)}, s32[32,32]{1,0:T(8,128)}, u32[]{:S(2)}) copy-start(s32[32,32]{1,0:T(8,128)} %param.9) | copy-start | bytes 12292
  5.8 0.7 copy-start.2
  17.1 21.3 %collective-permute-start.2 = (bf16[32,1664]{1,0:T(8,128)(2,1)S(1)}, bf16[32,1664]{1,0:T(8,128)(2,1)S(1)}, u32[]{:S(2)}, u32[]{:S(2)}) collective-permute-start(bf16[32,1664]{1,0:T(8,128)(2,1)S(1)} %fusion.11), channel_id=1, source_target_pairs={{0,12},{4,0},{8,4},{12,8},{1,13},{5,1},{9,5},{13,9},{2,14},{6,2},{... | collective-permute-start | bytes 319496 | tf_op jit(solution)/shard_map/ppermute | solution.py:167
  22.2 16.2 %collective-permute-start.1 = (bf16[32,1664]{1,0:T(8,128)(2,1)S(1)}, bf16[32,1664]{1,0:T(8,128)(2,1)S(1)}, u32[]{:S(2)}, u32[]{:S(2)}) collective-permute-start(bf16[32,1664]{1,0:T(8,128)(2,1)S(1)} %fusion.11), channel_id=1, source_target_pairs={{0,8},{4,12},{8,0},{12,4},{1,9},{5,13},{9,1},{13,5},{2,10},{6,14},... | collective-permute-start | bytes 319496 | tf_op jit(solution)/shard_map/ppermute | solution.py:167
  22.2 16.2 %collective-permute-start = (bf16[32,1664]{1,0:T(8,128)(2,1)S(1)}, bf16[32,1664]{1,0:T(8,128)(2,1)S(1)}, u32[]{:S(2)}, u32[]{:S(2)}) collective-permute-start(bf16[32,1664]{1,0:T(8,128)(2,1)S(1)} %fusion.11), channel_id=1, source_target_pairs={{0,4},{4,8},{8,12},{12,0},{1,5},{5,9},{9,13},{13,1},{2,6},{6,10},{... | collective-permute-start | bytes 319496 | tf_op jit(solution)/shard_map/ppermute | solution.py:167
  35.7 2.0 %copy-start.3 = (s32[1,32]{1,0:T(1,128)S(1)}, s32[1,32]{1,0:T(1,128)}, u32[]{:S(2)}) copy-start(s32[1,32]{1,0:T(1,128)} %param.11) | copy-start | bytes 388
  70.6 1.8 %collective-permute-start.5 = (bf16[8,1024]{1,0:T(8,128)(2,1)S(1)}, bf16[8,1024]{1,0:T(8,128)(2,1)S(1)}, u32[]{:S(2)}, u32[]{:S(2)}) collective-permute-start(bf16[8,1024]{1,0:T(8,128)(2,1)S(1)} %get-tuple-element.22), channel_id=1, source_target_pairs={{0,3},{1,0},{2,1},{3,2},{4,7},{5,4},{6,5},{7,6},{8,11},{9,8},{10,9... | collective-permute-start | bytes 49160 | tf_op jit(solution)/shard_map/ppermute | solution.py:188
  70.8 3.7 %collective-permute-start.4 = (bf16[8,1024]{1,0:T(8,128)(2,1)S(1)}, bf16[8,1024]{1,0:T(8,128)(2,1)S(1)}, u32[]{:S(2)}, u32[]{:S(2)}) collective-permute-start(bf16[8,1024]{1,0:T(8,128)(2,1)S(1)} %get-tuple-element.23), channel_id=1, source_target_pairs={{0,2},{1,3},{2,0},{3,1},{4,6},{5,7},{6,4},{7,5},{8,10},{9,11},{10,... | collective-permute-start | bytes 49160 | tf_op jit(solution)/shard_map/ppermute | solution.py:188
  72.3 3.2 %collective-permute-start.3 = (bf16[8,1024]{1,0:T(8,128)(2,1)S(1)}, bf16[8,1024]{1,0:T(8,128)(2,1)S(1)}, u32[]{:S(2)}, u32[]{:S(2)}) collective-permute-start(bf16[8,1024]{1,0:T(8,128)(2,1)S(1)} %get-tuple-element.21), channel_id=1, source_target_pairs={{0,1},{1,2},{2,3},{3,0},{4,5},{5,6},{6,7},{7,4},{8,9},{9,10},{10,1... | collective-permute-start | bytes 49160 | tf_op jit(solution)/shard_map/ppermute | solution.py:188

commit v9 on v8

--- a/solution.py
+++ b/solution.py
@@ -80,20 +80,20 @@
     base = pl.multiple_of(pid * steps, steps)
     for step in range(steps):
         joined = jnp.concatenate([grouped_ref[base + step], grouped_ref[base + step + 1]], axis=-1)
+        joined = joined.astype(jnp.float32)
+        parts = []
         for e in range(phases):
             cut = (phases - 1 - e) * chans
             moved = pltpu.roll(joined, 2 * width - cut, 1) if cut else joined
-            filt_ref[step, e * count : (e + 1) * count, :] = moved[:, :width]
+            parts.append(moved[:, :width])
+        filt_ref[step] = jnp.transpose(jnp.concatenate(parts, axis=0)).astype(filt_ref.dtype)
 
     def accumulate(g, carry):
         band = signal_ref[g, pl.ds(base, rows + steps), :]
         total = acc_ref[g]
         for step in range(steps):
             window = band[step : step + rows].astype(filt_ref.dtype)
-            total += lax.dot_general(
-                window, filt_ref[step], (((1,), (1,)), ((), ())),
-                preferred_element_type=jnp.float32,
-            )
+            total += jnp.dot(window, filt_ref[step], preferred_element_type=jnp.float32)
         acc_ref[g] = total
         return carry
 

time: 76.7 us -> 72.6 us (0.947)
  Pallas kernels: 26.8 us -> 22.7 us
    pallas_call x1, Pallas kernels: 26.8 us -> 22.7 us  [correlate(): pl.pallas_call(kernel, grid=(taps // steps,), in_specs=[pl.BlockSpec(grou...]
  transfers between devices with their start and end apart: 6 -> 6, of which waited for: 2 -> 2; matrix products, arithmetic and copies ran while one was open for 20% -> 21% of each run, Pallas kernels for 0% -> 0%
where the time goes in v9:
time: 72.6 us; the launch traced here: 72.1 us
  Pallas kernels  22.7 us (31%)
  local copies, waits for them, and re-layouts  19.1 us (26%)
  other arithmetic  18.6 us (26%)
  starting transfers between devices  7.9 us (11%)
  waiting for transfers between devices  3 us (4%)
    pallas_call x1, Pallas kernels, correlate(): pl.pallas_call(kernel, grid=(taps // steps,), in_specs=[pl.BlockSpec(grou...  22.7 us
    select_n x8, other arithmetic, place_moveout(): current = jnp.where(active[..., None], moved, current)  9.75 us
    reshape x2, local copies, waits for them, and re-layouts, correlate(): grouped = jnp.transpose(padded, (0, 2, 1)).reshape(count, n_groups, width)  8.94 us
    ppermute x3, starting transfers between devices, shards(): pieces.append(lax.ppermute(signal, 'chan', pairs))  6.12 us
    transpose x2, local copies, waits for them, and re-layouts, correlate(): grouped = jnp.transpose(padded, (0, 2, 1)).reshape(count, n_groups, width)  5.22 us
    ppermute x3, waiting for transfers between devices, shards(): stack = stack + lax.ppermute(outgoing, 'tmpl', pairs).astype(jnp.float32)  3 us
    reduce_sum x2, other arithmetic, normalize_rows(): centred = values - jnp.mean(values, axis=-1, keepdims=True)  2.54 us
    convert_element_type x2, local copies, waits for them, and re-layouts, correlate(): signal.astype(jnp.float32)  2.11 us
  transfers between devices with their start and end apart: 6, of which 2 were waited for; matrix products, arithmetic and copies ran while one was open for 21% of the time, Pallas kernels for 0%

profile of v9, /device:TPU:0, one launch (start us, length us, event | category | flops | bytes accessed | tf_op | source)
XLA Modules:
  0.0 72.1 jit_solution(9133639401514733448)
XLA Ops:
  0.0 0.0 copy-start
  0.0 0.0 copy-start.1
  0.0 1.1 %convert_reduce_fusion.1 = f32[32]{0:T(128)S(1)} fusion(bf16[32,1664]{1,0:T(8,128)(2,1)} %param.7), kind=kLoop, calls=%fused_computation.28 | loop fusion | flops 106464 | bytes 106624 | tf_op jit(solution)/shard_map/reduce_sum | solution.py:19
  1.1 1.1 %fusion.10 = f32[32]{0:T(128)S(1)} fusion(bf16[32,1664]{1,0:T(8,128)(2,1)} %param.7, f32[32]{0:T(128)S(1)} %broadcast_multiply_fusion.2), kind=kLoop, calls=%fused_computation.32 | loop fusion | flops 212960 | bytes 106752 | tf_op jit(solution)/shard_map/reduce_sum | solution.py:20
  2.2 1.0 %fusion.11 = bf16[32,1664]{1,0:T(8,128)(2,1)S(1)} fusion(bf16[32,1664]{1,0:T(8,128)(2,1)} %param.7, f32[32]{0:T(128)S(1)} %add_rsqrt_fusion.2, f32[32]{0:T(128)S(1)} %broadcast_multiply_fusion.2), kind=kLoop, calls=%fused_computation.33 | loop fusion | flops 212992 | bytes 213248 | tf_op jit(solution)/shard_map/convert_element_type | solution.py:21
  3.2 1.4 %convert_reduce_fusion = f32[32,32]{1,0:T(8,128)S(1)} fusion(bf16[32,32,512]{2,1,0:T(8,128)(2,1)} %param.8), kind=kLoop, calls=%fused_computation.3 | loop fusion | flops 1047552 | bytes 1052672 | tf_op jit(solution)/shard_map/reduce_sum | solution.py:19
  4.7 0.0 copy-done
  4.7 0.5 fusion.2
  5.3 0.0 copy-done.1
  5.3 0.6 convolution_convert_fusion
  5.8 0.0 copy-start.2
  5.9 0.1 pad_slice_fusion
  6.0 0.6 copy-done.2
  6.6 0.6 select_reduce_fusion.1
  7.2 1.3 %pad_select_fusion.7 = bf16[32,32,640]{2,1,0:T(8,128)(2,1)S(1)} fusion(bf16[32,32,639]{2,1,0:T(8,128)(2,1)S(1)} %pad_slice_fusion, pred[32,32]{1,0:T(8,128)(4,1)S(1)} %get-tuple-element.25, bf16[32,32,512]{2,1,0:T(8,128)(2,1)S(1)} %convolution_convert_fusion), kind=kLoop, calls=%fused_computation.18 | loop fusion | flops 655360 | bytes 3668992 | tf_op jit(solution)/shard_map/jit(_where)/select_n | solution.py:33
  8.5 1.3 %pad_select_fusion.6 = bf16[32,32,640]{2,1,0:T(8,128)(2,1)S(1)} fusion(bf16[32,32,640]{2,1,0:T(8,128)(2,1)S(1)} %pad_select_fusion.7, bf16[32,32,638]{2,1,0:T(8,128)(2,1)S(1)} %bitcast.38, pred[32,32]{1,0:T(8,128)(4,1)S(1)} %get-tuple-element.26), kind=kLoop, calls=%fused_computation.17 | loop fusion | flops 655360 | bytes 3929088 | tf_op jit(solution)/shard_map/jit(_where)/select_n | solution.py:33
  9.9 1.3 %pad_select_fusion.5 = bf16[32,32,640]{2,1,0:T(8,128)(2,1)S(1)} fusion(bf16[32,32,640]{2,1,0:T(8,128)(2,1)S(1)} %pad_select_fusion.6, bf16[32,32,636]{2,1,0:T(8,128)(2,1)S(1)} %bitcast.39, pred[32,32]{1,0:T(8,128)(4,1)S(1)} %get-tuple-element.27), kind=kLoop, calls=%fused_computation.16 | loop fusion | flops 655360 | bytes 3924992 | tf_op jit(solution)/shard_map/jit(_where)/select_n | solution.py:33
  11.2 1.3 %pad_select_fusion.4 = bf16[32,32,640]{2,1,0:T(8,128)(2,1)S(1)} fusion(bf16[32,32,640]{2,1,0:T(8,128)(2,1)S(1)} %pad_select_fusion.5, bf16[32,32,632]{2,1,0:T(8,128)(2,1)S(1)} %bitcast.40, pred[32,32]{1,0:T(8,128)(4,1)S(1)} %get-tuple-element.28), kind=kLoop, calls=%fused_computation.15 | loop fusion | flops 655360 | bytes 3916800 | tf_op jit(solution)/shard_map/jit(_where)/select_n | solution.py:33
  12.6 1.3 %pad_select_fusion.3 = bf16[32,32,640]{2,1,0:T(8,128)(2,1)S(1)} fusion(bf16[32,32,640]{2,1,0:T(8,128)(2,1)S(1)} %pad_select_fusion.4, bf16[32,32,624]{2,1,0:T(8,128)(2,1)S(1)} %bitcast.41, pred[32,32]{1,0:T(8,128)(4,1)S(1)} %get-tuple-element.29), kind=kLoop, calls=%fused_computation.14 | loop fusion | flops 655360 | bytes 3900416 | tf_op jit(solution)/shard_map/jit(_where)/select_n | solution.py:33
  13.9 1.3 %pad_select_fusion.2 = bf16[32,32,640]{2,1,0:T(8,128)(2,1)S(1)} fusion(bf16[32,32,640]{2,1,0:T(8,128)(2,1)S(1)} %pad_select_fusion.3, bf16[32,32,608]{2,1,0:T(8,128)(2,1)S(1)} %bitcast.42, pred[32,32]{1,0:T(8,128)(4,1)S(1)} %get-tuple-element.30), kind=kLoop, calls=%fused_computation.13 | loop fusion | flops 655360 | bytes 3867648 | tf_op jit(solution)/shard_map/jit(_where)/select_n | solution.py:33
  15.3 1.3 %pad_select_fusion.1 = bf16[32,32,640]{2,1,0:T(8,128)(2,1)S(1)} fusion(bf16[32,32,640]{2,1,0:T(8,128)(2,1)S(1)} %pad_select_fusion.2, bf16[32,32,576]{2,1,0:T(8,128)(2,1)S(1)} %bitcast.43, pred[32,32]{1,0:T(8,128)(4,1)S(1)} %get-tuple-element.31), kind=kLoop, calls=%fused_computation.12 | loop fusion | flops 655360 | bytes 3802112 | tf_op jit(solution)/shard_map/jit(_where)/select_n | solution.py:33
  16.6 0.1 slice.53
  16.7 0.4 pad_select_fusion
  17.1 5.1 %collective-permute-start.2 = (bf16[32,1664]{1,0:T(8,128)(2,1)S(1)}, bf16[32,1664]{1,0:T(8,128)(2,1)S(1)}, u32[]{:S(2)}, u32[]{:S(2)}) collective-permute-start(bf16[32,1664]{1,0:T(8,128)(2,1)S(1)} %fusion.11), channel_id=1, source_target_pairs={{0,12},{4,0},{8,4},{12,8},{1,13},{5,1},{9,5},{13,9},{2,14},{6,2},{... | collective-permute-start | bytes 319496 | tf_op jit(solution)/shard_map/ppermute | solution.py:167
  22.2 0.0 collective-permute-start.1
  22.2 1.0 %collective-permute-start = (bf16[32,1664]{1,0:T(8,128)(2,1)S(1)}, bf16[32,1664]{1,0:T(8,128)(2,1)S(1)}, u32[]{:S(2)}, u32[]{:S(2)}) collective-permute-start(bf16[32,1664]{1,0:T(8,128)(2,1)S(1)} %fusion.11), channel_id=1, source_target_pairs={{0,4},{4,8},{8,12},{12,0},{1,5},{5,9},{9,13},{13,1},{2,6},{6,10},{... | collective-permute-start | bytes 319496 | tf_op jit(solution)/shard_map/ppermute | solution.py:167
  23.3 0.1 slice_reduce_fusion
  23.4 0.7 %pad_bitcast_fusion = bf16[32,712,32]{1,2,0:T(8,128)(2,1)S(1)} fusion(bf16[32,32,640]{2,1,0:T(8,128)(2,1)S(1)} %pad_select_fusion), kind=kLoop, calls=%fused_computation.8 | loop fusion | bytes 2768896 | tf_op jit(solution)/shard_map/transpose | solution.py:117
  24.2 4.5 %copy.12 = bf16[32,712,32]{2,1,0:T(8,128)(2,1)} copy(bf16[32,712,32]{1,2,0:T(8,128)(2,1)S(1)} %pad_bitcast_fusion) | data formatting | bytes 2916352 | tf_op jit(solution)/shard_map/transpose | solution.py:117
  28.7 7.0 %reshape.175 = bf16[32,89,256]{2,1,0:T(8,128)(2,1)S(1)} reshape(bf16[32,712,32]{2,1,0:T(8,128)(2,1)} %copy.12) | data formatting | bytes 2916352 | tf_op jit(solution)/shard_map/reshape | solution.py:117
  35.7 0.0 copy-start.3
  35.7 1.9 %copy.19 = bf16[32,89,256]{2,0,1:T(8,128)(2,1)} copy(bf16[32,89,256]{2,1,0:T(8,128)(2,1)S(1)} %reshape.175) | data formatting | bytes 2916352 | tf_op jit(solution)/shard_map/reshape | solution.py:117
  37.6 0.0 copy-done.3
  37.6 0.7 scatter_custom_fusion
  38.4 0.1 broadcast_in_dim.111
  38.4 0.0 collective-permute-done.2
  38.5 0.0 collective-permute-done.1
  38.5 0.0 collective-permute-done
  38.5 0.1 maximum_bitcast_fusion
  38.5 0.9 %copy.14 = bf16[4,1664,32]{2,1,0:T(8,128)(2,1)S(1)} copy(bf16[4,1664,32]{1,2,0:T(8,128)(2,1)S(1)} %maximum_bitcast_fusion) | data formatting | bytes 851968 | tf_op jit(solution)/shard_map/convert_element_type | solution.py:120
  39.5 1.2 %convert_element_type.57 = bf16[4,208,256]{2,1,0:T(8,128)(2,1)S(1)} reshape(bf16[4,1664,32]{2,1,0:T(8,128)(2,1)S(1)} %copy.14) | data formatting | bytes 851968 | tf_op jit(solution)/shard_map/convert_element_type | solution.py:120
  40.7 1.0 %pad_convert_fusion.signal_ref = f32[4,216,256]{2,1,0:T(8,128)} fusion(bf16[4,208,256]{2,1,0:T(8,128)(2,1)S(1)} %convert_element_type.57), kind=kLoop, calls=%fused_computation.25 | loop fusion | flops 221184 | bytes 1310720 | tf_op jit(solution)/shard_map/jit(_pad)/pad | solution.py:120
  41.7 22.7 %shard_map.55 = f32[4,128,256]{2,1,0:T(8,128)} custom-call(bf16[89,32,256]{2,1,0:T(8,128)(2,1)} %bitcast.44, f32[4,216,256]{2,1,0:T(8,128)} %pad_convert_fusion.signal_ref), custom_call_target="tpu_custom_call" | custom-call | tf_op jit(solution)/shard_map/pallas_call | solution.py:124
  64.3 1.1 %select_reduce_fusion = bf16[128,256]{1,0:T(8,128)(2,1)S(1)} fusion(f32[4,128,256]{2,1,0:T(8,128)} %shard_map.55, pred[4,256]{1,0:T(4,128)(4,1)S(1)} %broadcast_in_dim.111), kind=kLoop, calls=%fused_computation.22 | loop fusion | flops 229376 | bytes 590848 | tf_op jit(solution)/shard_map/reduce_sum | solution.py:175
  65.4 0.1 copy.15
  65.5 0.2 copy.16
  65.7 0.1 copy.17
  65.8 0.6 gather_fusion
  66.5 0.1 collective-permute-start.5
  66.6 1.5 %collective-permute-start.4 = (bf16[8,1024]{1,0:T(8,128)(2,1)S(1)}, bf16[8,1024]{1,0:T(8,128)(2,1)S(1)}, u32[]{:S(2)}, u32[]{:S(2)}) collective-permute-start(bf16[8,1024]{1,0:T(8,128)(2,1)S(1)} %get-tuple-element.23), channel_id=1, source_target_pairs={{0,2},{1,3},{2,0},{3,1},{4,6},{5,7},{6,4},{7,5},{8,10},{9,11},{10,... | collective-permute-start | bytes 49160 | tf_op jit(solution)/shard_map/ppermute | solution.py:188
  68.1 0.2 collective-permute-start.3
  68.3 0.0 collective-permute-done.5
  68.3 2.1 %collective-permute-done.4 = bf16[8,1024]{1,0:T(8,128)(2,1)S(1)} collective-permute-done((bf16[8,1024]{1,0:T(8,128)(2,1)S(1)}, bf16[8,1024]{1,0:T(8,128)(2,1)S(1)}, u32[]{:S(2)}, u32[]{:S(2)}) %collective-permute-start.4) | collective-permute-done | bytes 16416 | tf_op jit(solution)/shard_map/ppermute | solution.py:188
  70.4 0.9 %collective-permute-done.3 = bf16[8,1024]{1,0:T(8,128)(2,1)S(1)} collective-permute-done((bf16[8,1024]{1,0:T(8,128)(2,1)S(1)}, bf16[8,1024]{1,0:T(8,128)(2,1)S(1)}, u32[]{:S(2)}, u32[]{:S(2)}) %collective-permute-start.3) | collective-permute-done | bytes 16416 | tf_op jit(solution)/shard_map/ppermute | solution.py:188
  71.3 0.1 multiply_reduce_fusion
  71.4 0.7 broadcast_multiply_fusion
  (14 shorter events, 0.1 us)
Async XLA Ops:
  0.0 4.7 %copy-start = (bf16[32,32,512]{2,1,0:T(8,128)(2,1)S(1)}, bf16[32,32,512]{2,1,0:T(8,128)(2,1)}, u32[]{:S(2)}) copy-start(bf16[32,32,512]{2,1,0:T(8,128)(2,1)} %param.8) | copy-start | bytes 3145732
  0.0 5.3 %copy-start.1 = (s32[32,32]{1,0:T(8,128)S(1)}, s32[32,32]{1,0:T(8,128)}, u32[]{:S(2)}) copy-start(s32[32,32]{1,0:T(8,128)} %param.9) | copy-start | bytes 12292
  5.8 0.7 copy-start.2
  17.1 21.3 %collective-permute-start.2 = (bf16[32,1664]{1,0:T(8,128)(2,1)S(1)}, bf16[32,1664]{1,0:T(8,128)(2,1)S(1)}, u32[]{:S(2)}, u32[]{:S(2)}) collective-permute-start(bf16[32,1664]{1,0:T(8,128)(2,1)S(1)} %fusion.11), channel_id=1, source_target_pairs={{0,12},{4,0},{8,4},{12,8},{1,13},{5,1},{9,5},{13,9},{2,14},{6,2},{... | collective-permute-start | bytes 319496 | tf_op jit(solution)/shard_map/ppermute | solution.py:167
  22.2 16.2 %collective-permute-start.1 = (bf16[32,1664]{1,0:T(8,128)(2,1)S(1)}, bf16[32,1664]{1,0:T(8,128)(2,1)S(1)}, u32[]{:S(2)}, u32[]{:S(2)}) collective-permute-start(bf16[32,1664]{1,0:T(8,128)(2,1)S(1)} %fusion.11), channel_id=1, source_target_pairs={{0,8},{4,12},{8,0},{12,4},{1,9},{5,13},{9,1},{13,5},{2,10},{6,14},... | collective-permute-start | bytes 319496 | tf_op jit(solution)/shard_map/ppermute | solution.py:167
  22.2 16.2 %collective-permute-start = (bf16[32,1664]{1,0:T(8,128)(2,1)S(1)}, bf16[32,1664]{1,0:T(8,128)(2,1)S(1)}, u32[]{:S(2)}, u32[]{:S(2)}) collective-permute-start(bf16[32,1664]{1,0:T(8,128)(2,1)S(1)} %fusion.11), channel_id=1, source_target_pairs={{0,4},{4,8},{8,12},{12,0},{1,5},{5,9},{9,13},{13,1},{2,6},{6,10},{... | collective-permute-start | bytes 319496 | tf_op jit(solution)/shard_map/ppermute | solution.py:167
  35.7 2.0 %copy-start.3 = (s32[1,32]{1,0:T(1,128)S(1)}, s32[1,32]{1,0:T(1,128)}, u32[]{:S(2)}) copy-start(s32[1,32]{1,0:T(1,128)} %param.11) | copy-start | bytes 388
  66.5 1.8 %collective-permute-start.5 = (bf16[8,1024]{1,0:T(8,128)(2,1)S(1)}, bf16[8,1024]{1,0:T(8,128)(2,1)S(1)}, u32[]{:S(2)}, u32[]{:S(2)}) collective-permute-start(bf16[8,1024]{1,0:T(8,128)(2,1)S(1)} %get-tuple-element.22), channel_id=1, source_target_pairs={{0,3},{1,0},{2,1},{3,2},{4,7},{5,4},{6,5},{7,6},{8,11},{9,8},{10,9... | collective-permute-start | bytes 49160 | tf_op jit(solution)/shard_map/ppermute | solution.py:188
  66.6 3.7 %collective-permute-start.4 = (bf16[8,1024]{1,0:T(8,128)(2,1)S(1)}, bf16[8,1024]{1,0:T(8,128)(2,1)S(1)}, u32[]{:S(2)}, u32[]{:S(2)}) collective-permute-start(bf16[8,1024]{1,0:T(8,128)(2,1)S(1)} %get-tuple-element.23), channel_id=1, source_target_pairs={{0,2},{1,3},{2,0},{3,1},{4,6},{5,7},{6,4},{7,5},{8,10},{9,11},{10,... | collective-permute-start | bytes 49160 | tf_op jit(solution)/shard_map/ppermute | solution.py:188
  68.1 3.2 %collective-permute-start.3 = (bf16[8,1024]{1,0:T(8,128)(2,1)S(1)}, bf16[8,1024]{1,0:T(8,128)(2,1)S(1)}, u32[]{:S(2)}, u32[]{:S(2)}) collective-permute-start(bf16[8,1024]{1,0:T(8,128)(2,1)S(1)} %get-tuple-element.21), channel_id=1, source_target_pairs={{0,1},{1,2},{2,3},{3,0},{4,5},{5,6},{6,7},{7,4},{8,9},{9,10},{10,1... | collective-permute-start | bytes 49160 | tf_op jit(solution)/shard_map/ppermute | solution.py:188

commit v10 on v9

--- a/solution.py
+++ b/solution.py
@@ -88,20 +88,32 @@
             parts.append(moved[:, :width])
         filt_ref[step] = jnp.transpose(jnp.concatenate(parts, axis=0)).astype(filt_ref.dtype)
 
-    def accumulate(g, carry):
-        band = signal_ref[g, pl.ds(base, rows + steps), :]
-        total = acc_ref[g]
+    n_blocks = signal_ref.shape[0]
+    if n_blocks <= 8:
+        band = signal_ref[:, pl.ds(base, rows + steps), :]
+        total = acc_ref[...]
         for step in range(steps):
-            window = band[step : step + rows].astype(filt_ref.dtype)
+            window = band[:, step : step + rows].astype(filt_ref.dtype)
+            window = window.reshape(n_blocks * rows, width)
             total += jnp.dot(window, filt_ref[step], preferred_element_type=jnp.float32)
-        acc_ref[g] = total
-        return carry
-
-    lax.fori_loop(0, signal_ref.shape[0], accumulate, 0)
+        acc_ref[...] = total
+    else:
+
+        def accumulate(g, carry):
+            band = signal_ref[g, pl.ds(base, rows + steps), :]
+            start = pl.multiple_of(g * rows, rows)
+            total = acc_ref[pl.ds(start, rows), :]
+            for step in range(steps):
+                window = band[step : step + rows].astype(filt_ref.dtype)
+                total += jnp.dot(window, filt_ref[step], preferred_element_type=jnp.float32)
+            acc_ref[pl.ds(start, rows), :] = total
+            return carry
+
+        lax.fori_loop(0, n_blocks, accumulate, 0)
 
     @pl.when(pid == pl.num_programs(0) - 1)
     def _():
-        out_ref[...] = acc_ref[...]
+        out_ref[...] = acc_ref[...].reshape(out_ref.shape)
 
 
 def correlate(placed, blocks, phases, lags):
@@ -131,7 +143,7 @@
         out_specs=pl.BlockSpec((n_blocks, rows, phases * count), lambda q: (0, 0, 0)),
         out_shape=jax.ShapeDtypeStruct((n_blocks, rows, phases * count), jnp.float32),
         scratch_shapes=[
-            pltpu.VMEM((n_blocks, rows, phases * count), jnp.float32),
+            pltpu.VMEM((n_blocks * rows, phases * count), jnp.float32),
             pltpu.VMEM((steps, phases * count, width), placed.dtype),
         ],
     )(grouped, signal)

time: 72.6 us -> 63.9 us (0.88)
  Pallas kernels: 22.7 us -> 14 us
    pallas_call x1, Pallas kernels: 22.7 us -> 14 us  [correlate(): pl.pallas_call(kernel, grid=(taps // steps,), in_specs=[pl.BlockSpec(grou...]
  transfers between devices with their start and end apart: 6 -> 6, of which waited for: 2 -> 2; matrix products, arithmetic and copies ran while one was open for 21% -> 24% of each run, Pallas kernels for 0% -> 0%
where the time goes in v10:
time: 63.9 us; the launch traced here: 63.5 us
  local copies, waits for them, and re-layouts  19.1 us (30%)
  other arithmetic  18.6 us (29%)
  Pallas kernels  14 us (22%)
  starting transfers between devices  7.89 us (12%)
  waiting for transfers between devices  3 us (5%)
    pallas_call x1, Pallas kernels, correlate(): pl.pallas_call(kernel, grid=(taps // steps,), in_specs=[pl.BlockSpec(grou...  14 us
    select_n x8, other arithmetic, place_moveout(): current = jnp.where(active[..., None], moved, current)  9.75 us
    reshape x2, local copies, waits for them, and re-layouts, correlate(): grouped = jnp.transpose(padded, (0, 2, 1)).reshape(count, n_groups, width)  8.94 us
    ppermute x3, starting transfers between devices, shards(): pieces.append(lax.ppermute(signal, 'chan', pairs))  6.12 us
    transpose x2, local copies, waits for them, and re-layouts, correlate(): grouped = jnp.transpose(padded, (0, 2, 1)).reshape(count, n_groups, width)  5.22 us
    ppermute x3, waiting for transfers between devices, shards(): stack = stack + lax.ppermute(outgoing, 'tmpl', pairs).astype(jnp.float32)  3 us
    reduce_sum x2, other arithmetic, normalize_rows(): centred = values - jnp.mean(values, axis=-1, keepdims=True)  2.54 us
    convert_element_type x2, local copies, waits for them, and re-layouts, correlate(): signal.astype(jnp.float32)  2.11 us
  transfers between devices with their start and end apart: 6, of which 2 were waited for; matrix products, arithmetic and copies ran while one was open for 24% of the time, Pallas kernels for 0%

profile of v10, /device:TPU:0, one launch (start us, length us, event | category | flops | bytes accessed | tf_op | source)
XLA Modules:
  0.0 63.5 jit_solution(13388283960677179430)
XLA Ops:
  0.0 0.0 copy-start
  0.0 0.0 copy-start.1
  0.0 1.1 %convert_reduce_fusion.1 = f32[32]{0:T(128)S(1)} fusion(bf16[32,1664]{1,0:T(8,128)(2,1)} %param.7), kind=kLoop, calls=%fused_computation.28 | loop fusion | flops 106464 | bytes 106624 | tf_op jit(solution)/shard_map/reduce_sum | solution.py:19
  1.1 1.1 %fusion.10 = f32[32]{0:T(128)S(1)} fusion(bf16[32,1664]{1,0:T(8,128)(2,1)} %param.7, f32[32]{0:T(128)S(1)} %broadcast_multiply_fusion.2), kind=kLoop, calls=%fused_computation.32 | loop fusion | flops 212960 | bytes 106752 | tf_op jit(solution)/shard_map/reduce_sum | solution.py:20
  2.2 1.0 %fusion.11 = bf16[32,1664]{1,0:T(8,128)(2,1)S(1)} fusion(bf16[32,1664]{1,0:T(8,128)(2,1)} %param.7, f32[32]{0:T(128)S(1)} %add_rsqrt_fusion.2, f32[32]{0:T(128)S(1)} %broadcast_multiply_fusion.2), kind=kLoop, calls=%fused_computation.33 | loop fusion | flops 212992 | bytes 213248 | tf_op jit(solution)/shard_map/convert_element_type | solution.py:21
  3.2 1.4 %convert_reduce_fusion = f32[32,32]{1,0:T(8,128)S(1)} fusion(bf16[32,32,512]{2,1,0:T(8,128)(2,1)} %param.8), kind=kLoop, calls=%fused_computation.3 | loop fusion | flops 1047552 | bytes 1052672 | tf_op jit(solution)/shard_map/reduce_sum | solution.py:19
  4.7 0.0 copy-done
  4.7 0.5 fusion.2
  5.3 0.0 copy-done.1
  5.3 0.6 convolution_convert_fusion
  5.8 0.0 copy-start.2
  5.9 0.1 pad_slice_fusion
  6.0 0.6 copy-done.2
  6.6 0.6 select_reduce_fusion.1
  7.2 1.3 %pad_select_fusion.7 = bf16[32,32,640]{2,1,0:T(8,128)(2,1)S(1)} fusion(bf16[32,32,639]{2,1,0:T(8,128)(2,1)S(1)} %pad_slice_fusion, pred[32,32]{1,0:T(8,128)(4,1)S(1)} %get-tuple-element.25, bf16[32,32,512]{2,1,0:T(8,128)(2,1)S(1)} %convolution_convert_fusion), kind=kLoop, calls=%fused_computation.18 | loop fusion | flops 655360 | bytes 3668992 | tf_op jit(solution)/shard_map/jit(_where)/select_n | solution.py:33
  8.5 1.3 %pad_select_fusion.6 = bf16[32,32,640]{2,1,0:T(8,128)(2,1)S(1)} fusion(bf16[32,32,640]{2,1,0:T(8,128)(2,1)S(1)} %pad_select_fusion.7, bf16[32,32,638]{2,1,0:T(8,128)(2,1)S(1)} %bitcast.38, pred[32,32]{1,0:T(8,128)(4,1)S(1)} %get-tuple-element.26), kind=kLoop, calls=%fused_computation.17 | loop fusion | flops 655360 | bytes 3929088 | tf_op jit(solution)/shard_map/jit(_where)/select_n | solution.py:33
  9.9 1.3 %pad_select_fusion.5 = bf16[32,32,640]{2,1,0:T(8,128)(2,1)S(1)} fusion(bf16[32,32,640]{2,1,0:T(8,128)(2,1)S(1)} %pad_select_fusion.6, bf16[32,32,636]{2,1,0:T(8,128)(2,1)S(1)} %bitcast.39, pred[32,32]{1,0:T(8,128)(4,1)S(1)} %get-tuple-element.27), kind=kLoop, calls=%fused_computation.16 | loop fusion | flops 655360 | bytes 3924992 | tf_op jit(solution)/shard_map/jit(_where)/select_n | solution.py:33
  11.2 1.3 %pad_select_fusion.4 = bf16[32,32,640]{2,1,0:T(8,128)(2,1)S(1)} fusion(bf16[32,32,640]{2,1,0:T(8,128)(2,1)S(1)} %pad_select_fusion.5, bf16[32,32,632]{2,1,0:T(8,128)(2,1)S(1)} %bitcast.40, pred[32,32]{1,0:T(8,128)(4,1)S(1)} %get-tuple-element.28), kind=kLoop, calls=%fused_computation.15 | loop fusion | flops 655360 | bytes 3916800 | tf_op jit(solution)/shard_map/jit(_where)/select_n | solution.py:33
  12.6 1.3 %pad_select_fusion.3 = bf16[32,32,640]{2,1,0:T(8,128)(2,1)S(1)} fusion(bf16[32,32,640]{2,1,0:T(8,128)(2,1)S(1)} %pad_select_fusion.4, bf16[32,32,624]{2,1,0:T(8,128)(2,1)S(1)} %bitcast.41, pred[32,32]{1,0:T(8,128)(4,1)S(1)} %get-tuple-element.29), kind=kLoop, calls=%fused_computation.14 | loop fusion | flops 655360 | bytes 3900416 | tf_op jit(solution)/shard_map/jit(_where)/select_n | solution.py:33
  13.9 1.3 %pad_select_fusion.2 = bf16[32,32,640]{2,1,0:T(8,128)(2,1)S(1)} fusion(bf16[32,32,640]{2,1,0:T(8,128)(2,1)S(1)} %pad_select_fusion.3, bf16[32,32,608]{2,1,0:T(8,128)(2,1)S(1)} %bitcast.42, pred[32,32]{1,0:T(8,128)(4,1)S(1)} %get-tuple-element.30), kind=kLoop, calls=%fused_computation.13 | loop fusion | flops 655360 | bytes 3867648 | tf_op jit(solution)/shard_map/jit(_where)/select_n | solution.py:33
  15.3 1.3 %pad_select_fusion.1 = bf16[32,32,640]{2,1,0:T(8,128)(2,1)S(1)} fusion(bf16[32,32,640]{2,1,0:T(8,128)(2,1)S(1)} %pad_select_fusion.2, bf16[32,32,576]{2,1,0:T(8,128)(2,1)S(1)} %bitcast.43, pred[32,32]{1,0:T(8,128)(4,1)S(1)} %get-tuple-element.31), kind=kLoop, calls=%fused_computation.12 | loop fusion | flops 655360 | bytes 3802112 | tf_op jit(solution)/shard_map/jit(_where)/select_n | solution.py:33
  16.6 0.1 slice.53
  16.7 0.4 pad_select_fusion
  17.1 5.1 %collective-permute-start.2 = (bf16[32,1664]{1,0:T(8,128)(2,1)S(1)}, bf16[32,1664]{1,0:T(8,128)(2,1)S(1)}, u32[]{:S(2)}, u32[]{:S(2)}) collective-permute-start(bf16[32,1664]{1,0:T(8,128)(2,1)S(1)} %fusion.11), channel_id=1, source_target_pairs={{0,12},{4,0},{8,4},{12,8},{1,13},{5,1},{9,5},{13,9},{2,14},{6,2},{... | collective-permute-start | bytes 319496 | tf_op jit(solution)/shard_map/ppermute | solution.py:179
  22.2 0.0 collective-permute-start.1
  22.2 1.0 %collective-permute-start = (bf16[32,1664]{1,0:T(8,128)(2,1)S(1)}, bf16[32,1664]{1,0:T(8,128)(2,1)S(1)}, u32[]{:S(2)}, u32[]{:S(2)}) collective-permute-start(bf16[32,1664]{1,0:T(8,128)(2,1)S(1)} %fusion.11), channel_id=1, source_target_pairs={{0,4},{4,8},{8,12},{12,0},{1,5},{5,9},{9,13},{13,1},{2,6},{6,10},{... | collective-permute-start | bytes 319496 | tf_op jit(solution)/shard_map/ppermute | solution.py:179
  23.3 0.1 slice_reduce_fusion
  23.4 0.7 %pad_bitcast_fusion = bf16[32,712,32]{1,2,0:T(8,128)(2,1)S(1)} fusion(bf16[32,32,640]{2,1,0:T(8,128)(2,1)S(1)} %pad_select_fusion), kind=kLoop, calls=%fused_computation.8 | loop fusion | bytes 2768896 | tf_op jit(solution)/shard_map/transpose | solution.py:129
  24.2 4.5 %copy.12 = bf16[32,712,32]{2,1,0:T(8,128)(2,1)} copy(bf16[32,712,32]{1,2,0:T(8,128)(2,1)S(1)} %pad_bitcast_fusion) | data formatting | bytes 2916352 | tf_op jit(solution)/shard_map/transpose | solution.py:129
  28.7 7.0 %reshape.175 = bf16[32,89,256]{2,1,0:T(8,128)(2,1)S(1)} reshape(bf16[32,712,32]{2,1,0:T(8,128)(2,1)} %copy.12) | data formatting | bytes 2916352 | tf_op jit(solution)/shard_map/reshape | solution.py:129
  35.7 0.0 copy-start.3
  35.7 1.9 %copy.19 = bf16[32,89,256]{2,0,1:T(8,128)(2,1)} copy(bf16[32,89,256]{2,1,0:T(8,128)(2,1)S(1)} %reshape.175) | data formatting | bytes 2916352 | tf_op jit(solution)/shard_map/reshape | solution.py:129
  37.6 0.0 copy-done.3
  37.6 0.7 %scatter_custom_fusion = s32[32]{0:T(128)S(1)} fusion(s32[32]{0:T(128)S(1)} %fusion.14, s32[32]{0:T(128)S(1)} %iota.14, s32[]{:T(128)} %constant.105.clone.1), kind=kCustom, calls=%fused_computation.71 | custom fusion | bytes 132 | tf_op jit(solution)/shard_map/scatter | solution.py:191
  38.4 0.1 broadcast_in_dim.111
  38.4 0.0 collective-permute-done.2
  38.5 0.0 collective-permute-done.1
  38.5 0.0 collective-permute-done
  38.5 0.1 maximum_bitcast_fusion
  38.5 0.9 %copy.14 = bf16[4,1664,32]{2,1,0:T(8,128)(2,1)S(1)} copy(bf16[4,1664,32]{1,2,0:T(8,128)(2,1)S(1)} %maximum_bitcast_fusion) | data formatting | bytes 851968 | tf_op jit(solution)/shard_map/convert_element_type | solution.py:132
  39.5 1.2 %convert_element_type.57 = bf16[4,208,256]{2,1,0:T(8,128)(2,1)S(1)} reshape(bf16[4,1664,32]{2,1,0:T(8,128)(2,1)S(1)} %copy.14) | data formatting | bytes 851968 | tf_op jit(solution)/shard_map/convert_element_type | solution.py:132
  40.7 1.0 %pad_convert_fusion.signal_ref = f32[4,216,256]{2,1,0:T(8,128)} fusion(bf16[4,208,256]{2,1,0:T(8,128)(2,1)S(1)} %convert_element_type.57), kind=kLoop, calls=%fused_computation.25 | loop fusion | flops 221184 | bytes 1310720 | tf_op jit(solution)/shard_map/jit(_pad)/pad | solution.py:132
  41.7 14.0 %shard_map.55 = f32[4,128,256]{2,1,0:T(8,128)} custom-call(bf16[89,32,256]{2,1,0:T(8,128)(2,1)} %bitcast.44, f32[4,216,256]{2,1,0:T(8,128)} %pad_convert_fusion.signal_ref), custom_call_target="tpu_custom_call" | custom-call | tf_op jit(solution)/shard_map/pallas_call | solution.py:136
  55.7 1.1 %select_reduce_fusion = bf16[128,256]{1,0:T(8,128)(2,1)S(1)} fusion(f32[4,128,256]{2,1,0:T(8,128)} %shard_map.55, pred[4,256]{1,0:T(4,128)(4,1)S(1)} %broadcast_in_dim.111), kind=kLoop, calls=%fused_computation.22 | loop fusion | flops 229376 | bytes 590848 | tf_op jit(solution)/shard_map/reduce_sum | solution.py:187
  56.8 0.1 copy.15
  56.9 0.2 copy.16
  57.1 0.1 copy.17
  57.2 0.6 gather_fusion
  57.9 0.1 collective-permute-start.5
  58.0 1.5 %collective-permute-start.4 = (bf16[8,1024]{1,0:T(8,128)(2,1)S(1)}, bf16[8,1024]{1,0:T(8,128)(2,1)S(1)}, u32[]{:S(2)}, u32[]{:S(2)}) collective-permute-start(bf16[8,1024]{1,0:T(8,128)(2,1)S(1)} %get-tuple-element.23), channel_id=1, source_target_pairs={{0,2},{1,3},{2,0},{3,1},{4,6},{5,7},{6,4},{7,5},{8,10},{9,11},{10,... | collective-permute-start | bytes 49160 | tf_op jit(solution)/shard_map/ppermute | solution.py:200
  59.5 0.2 collective-permute-start.3
  59.6 0.0 collective-permute-done.5
  59.6 2.1 %collective-permute-done.4 = bf16[8,1024]{1,0:T(8,128)(2,1)S(1)} collective-permute-done((bf16[8,1024]{1,0:T(8,128)(2,1)S(1)}, bf16[8,1024]{1,0:T(8,128)(2,1)S(1)}, u32[]{:S(2)}, u32[]{:S(2)}) %collective-permute-start.4) | collective-permute-done | bytes 16416 | tf_op jit(solution)/shard_map/ppermute | solution.py:200
  61.7 0.9 %collective-permute-done.3 = bf16[8,1024]{1,0:T(8,128)(2,1)S(1)} collective-permute-done((bf16[8,1024]{1,0:T(8,128)(2,1)S(1)}, bf16[8,1024]{1,0:T(8,128)(2,1)S(1)}, u32[]{:S(2)}, u32[]{:S(2)}) %collective-permute-start.3) | collective-permute-done | bytes 16416 | tf_op jit(solution)/shard_map/ppermute | solution.py:200
  62.6 0.1 multiply_reduce_fusion
  62.8 0.7 %broadcast_multiply_fusion = f32[8,1024]{1,0:T(8,128)} fusion(f32[8]{0:T(128)S(1)} %add_rsqrt_fusion.1, bf16[8,1024]{1,0:T(8,128)(2,1)S(1)} %collective-permute-done.5, bf16[8,1024]{1,0:T(8,128)(2,1)S(1)} %collective-permute-done.4, bf16[8,1024]{1,0:T(8,128)(2,1)S(1)} %collective-permute-done.3, bf16[4,8,1024]{2,1,0:T(8,128)(2,1)S(1)} %bitcast.49, ...), kind=kLoop, calls=%fused_computation.43 | loop fusion | flops 73728 | bytes 98341 | tf_op jit(solution)/shard_map/mul | solution.py:205
  (14 shorter events, 0.1 us)
Async XLA Ops:
  0.0 4.7 %copy-start = (bf16[32,32,512]{2,1,0:T(8,128)(2,1)S(1)}, bf16[32,32,512]{2,1,0:T(8,128)(2,1)}, u32[]{:S(2)}) copy-start(bf16[32,32,512]{2,1,0:T(8,128)(2,1)} %param.8) | copy-start | bytes 3145732
  0.0 5.3 %copy-start.1 = (s32[32,32]{1,0:T(8,128)S(1)}, s32[32,32]{1,0:T(8,128)}, u32[]{:S(2)}) copy-start(s32[32,32]{1,0:T(8,128)} %param.9) | copy-start | bytes 12292
  5.8 0.7 %copy-start.2 = (s32[32,32]{1,0:T(8,128)S(1)}, s32[32,32]{1,0:T(8,128)}, u32[]{:S(2)}) copy-start(s32[32,32]{1,0:T(8,128)} %param.10) | copy-start | bytes 12292
  17.1 21.3 %collective-permute-start.2 = (bf16[32,1664]{1,0:T(8,128)(2,1)S(1)}, bf16[32,1664]{1,0:T(8,128)(2,1)S(1)}, u32[]{:S(2)}, u32[]{:S(2)}) collective-permute-start(bf16[32,1664]{1,0:T(8,128)(2,1)S(1)} %fusion.11), channel_id=1, source_target_pairs={{0,12},{4,0},{8,4},{12,8},{1,13},{5,1},{9,5},{13,9},{2,14},{6,2},{... | collective-permute-start | bytes 319496 | tf_op jit(solution)/shard_map/ppermute | solution.py:179
  22.2 16.2 %collective-permute-start.1 = (bf16[32,1664]{1,0:T(8,128)(2,1)S(1)}, bf16[32,1664]{1,0:T(8,128)(2,1)S(1)}, u32[]{:S(2)}, u32[]{:S(2)}) collective-permute-start(bf16[32,1664]{1,0:T(8,128)(2,1)S(1)} %fusion.11), channel_id=1, source_target_pairs={{0,8},{4,12},{8,0},{12,4},{1,9},{5,13},{9,1},{13,5},{2,10},{6,14},... | collective-permute-start | bytes 319496 | tf_op jit(solution)/shard_map/ppermute | solution.py:179
  22.2 16.2 %collective-permute-start = (bf16[32,1664]{1,0:T(8,128)(2,1)S(1)}, bf16[32,1664]{1,0:T(8,128)(2,1)S(1)}, u32[]{:S(2)}, u32[]{:S(2)}) collective-permute-start(bf16[32,1664]{1,0:T(8,128)(2,1)S(1)} %fusion.11), channel_id=1, source_target_pairs={{0,4},{4,8},{8,12},{12,0},{1,5},{5,9},{9,13},{13,1},{2,6},{6,10},{... | collective-permute-start | bytes 319496 | tf_op jit(solution)/shard_map/ppermute | solution.py:179
  35.7 2.0 %copy-start.3 = (s32[1,32]{1,0:T(1,128)S(1)}, s32[1,32]{1,0:T(1,128)}, u32[]{:S(2)}) copy-start(s32[1,32]{1,0:T(1,128)} %param.11) | copy-start | bytes 388
  57.9 1.8 %collective-permute-start.5 = (bf16[8,1024]{1,0:T(8,128)(2,1)S(1)}, bf16[8,1024]{1,0:T(8,128)(2,1)S(1)}, u32[]{:S(2)}, u32[]{:S(2)}) collective-permute-start(bf16[8,1024]{1,0:T(8,128)(2,1)S(1)} %get-tuple-element.22), channel_id=1, source_target_pairs={{0,3},{1,0},{2,1},{3,2},{4,7},{5,4},{6,5},{7,6},{8,11},{9,8},{10,9... | collective-permute-start | bytes 49160 | tf_op jit(solution)/shard_map/ppermute | solution.py:200
  58.0 3.7 %collective-permute-start.4 = (bf16[8,1024]{1,0:T(8,128)(2,1)S(1)}, bf16[8,1024]{1,0:T(8,128)(2,1)S(1)}, u32[]{:S(2)}, u32[]{:S(2)}) collective-permute-start(bf16[8,1024]{1,0:T(8,128)(2,1)S(1)} %get-tuple-element.23), channel_id=1, source_target_pairs={{0,2},{1,3},{2,0},{3,1},{4,6},{5,7},{6,4},{7,5},{8,10},{9,11},{10,... | collective-permute-start | bytes 49160 | tf_op jit(solution)/shard_map/ppermute | solution.py:200
  59.5 3.2 %collective-permute-start.3 = (bf16[8,1024]{1,0:T(8,128)(2,1)S(1)}, bf16[8,1024]{1,0:T(8,128)(2,1)S(1)}, u32[]{:S(2)}, u32[]{:S(2)}) collective-permute-start(bf16[8,1024]{1,0:T(8,128)(2,1)S(1)} %get-tuple-element.21), channel_id=1, source_target_pairs={{0,1},{1,2},{2,3},{3,0},{4,5},{5,6},{6,7},{7,4},{8,9},{9,10},{10,1... | collective-permute-start | bytes 49160 | tf_op jit(solution)/shard_map/ppermute | solution.py:200

commit v11 on v10

--- a/solution.py
+++ b/solution.py
@@ -79,7 +79,9 @@
 
     base = pl.multiple_of(pid * steps, steps)
     for step in range(steps):
-        joined = jnp.concatenate([grouped_ref[base + step], grouped_ref[base + step + 1]], axis=-1)
+        joined = jnp.concatenate(
+            [grouped_ref[:, base + step, :], grouped_ref[:, base + step + 1, :]], axis=-1
+        )
         joined = joined.astype(jnp.float32)
         parts = []
         for e in range(phases):
@@ -127,7 +129,7 @@
     width = phases * chans
     padded = jnp.pad(placed, ((0, 0), (0, 0), (front, n_groups * phases - padded_len - front)))
     grouped = jnp.transpose(padded, (0, 2, 1)).reshape(count, n_groups, width)
-    grouped = jnp.transpose(grouped, (1, 0, 2))
+    grouped = grouped.astype(jnp.float32)
     signal = jnp.transpose(blocks, (0, 2, 1)).reshape(n_blocks, window // phases, width)
     signal = jnp.pad(signal.astype(jnp.float32), ((0, 0), (0, taps + rows - window // phases), (0, 0)))
     kernel = functools.partial(

time: 63.9 us -> 70.3 us (1.10)
  other arithmetic: 18.6 us -> 22.6 us
  local copies, waits for them, and re-layouts: 19.1 us -> 20.6 us
  Pallas kernels: 14 us -> 14.9 us
    convert_element_type x0 -> x2, local copies, waits for them, and re-layouts: none -> 15.8 us  [correlate(): grouped = grouped.astype(jnp.float32)]
    reshape x2 -> x0, local copies, waits for them, and re-layouts: 8.94 us -> none  [correlate(): grouped = jnp.transpose(padded, (0, 2, 1)).reshape(count, n_groups, width)]
    transpose x2 -> x0, local copies, waits for them, and re-layouts: 5.22 us -> none  [correlate(): grouped = jnp.transpose(padded, (0, 2, 1)).reshape(count, n_groups, width)]
    convert_element_type x0 -> x1, other arithmetic: none -> 1.96 us  [correlate(): grouped = grouped.astype(jnp.float32)]
    select_n x8, other arithmetic: 9.75 us -> 10.8 us  [place_moveout(): current = jnp.where(active[..., None], moved, current)]
    convert_element_type x1, other arithmetic: 0.07 us -> 0.96 us  [correlate(): signal.astype(jnp.float32)]
    pallas_call x1, Pallas kernels: 14 us -> 14.9 us  [correlate(): pl.pallas_call(kernel, grid=(taps // steps,), in_specs=[pl.BlockSpec(grou...]
  transfers between devices with their start and end apart: 6 -> 6, of which waited for: 2 -> 2; matrix products, arithmetic and copies ran while one was open for 24% -> 27% of each run, Pallas kernels for 0% -> 0%
where the time goes in v11:
time: 70.3 us; the launch traced here: 69.8 us
  other arithmetic  22.6 us (32%)
  local copies, waits for them, and re-layouts  20.6 us (29%)
  Pallas kernels  14.9 us (21%)
  starting transfers between devices  7.85 us (11%)
  waiting for transfers between devices  3 us (4%)
    convert_element_type x2, local copies, waits for them, and re-layouts, correlate(): grouped = grouped.astype(jnp.float32)  15.8 us
    pallas_call x1, Pallas kernels, correlate(): pl.pallas_call(kernel, grid=(taps // steps,), in_specs=[pl.BlockSpec(grou...  14.9 us
    select_n x8, other arithmetic, place_moveout(): current = jnp.where(active[..., None], moved, current)  10.8 us
    ppermute x3, starting transfers between devices, shards(): pieces.append(lax.ppermute(signal, 'chan', pairs))  6.06 us
    ppermute x3, waiting for transfers between devices, shards(): stack = stack + lax.ppermute(outgoing, 'tmpl', pairs).astype(jnp.float32)  3 us
    reduce_sum x2, other arithmetic, normalize_rows(): centred = values - jnp.mean(values, axis=-1, keepdims=True)  2.54 us
    convert_element_type x2, local copies, waits for them, and re-layouts, correlate(): signal.astype(jnp.float32)  2.11 us
    convert_element_type x1, other arithmetic, correlate(): grouped = grouped.astype(jnp.float32)  1.96 us
  transfers between devices with their start and end apart: 6, of which 2 were waited for; matrix products, arithmetic and copies ran while one was open for 27% of the time, Pallas kernels for 0%

profile of v11, /device:TPU:0, one launch (start us, length us, event | category | flops | bytes accessed | tf_op | source)
XLA Modules:
  0.0 69.8 jit_solution(14366819323268633246)
XLA Ops:
  0.0 0.0 copy-start
  0.0 0.0 copy-start.1
  0.0 1.1 %convert_reduce_fusion.1 = f32[32]{0:T(128)S(1)} fusion(bf16[32,1664]{1,0:T(8,128)(2,1)} %param.7), kind=kLoop, calls=%fused_computation.27 | loop fusion | flops 106464 | bytes 106624 | tf_op jit(solution)/shard_map/reduce_sum | solution.py:19
  1.1 1.1 %fusion.10 = f32[32]{0:T(128)S(1)} fusion(bf16[32,1664]{1,0:T(8,128)(2,1)} %param.7, f32[32]{0:T(128)S(1)} %broadcast_multiply_fusion.2), kind=kLoop, calls=%fused_computation.31 | loop fusion | flops 212960 | bytes 106752 | tf_op jit(solution)/shard_map/reduce_sum | solution.py:20
  2.2 1.0 %fusion.11 = bf16[32,1664]{1,0:T(8,128)(2,1)S(1)} fusion(bf16[32,1664]{1,0:T(8,128)(2,1)} %param.7, f32[32]{0:T(128)S(1)} %add_rsqrt_fusion.2, f32[32]{0:T(128)S(1)} %broadcast_multiply_fusion.2), kind=kLoop, calls=%fused_computation.32 | loop fusion | flops 212992 | bytes 213248 | tf_op jit(solution)/shard_map/convert_element_type | solution.py:21
  3.2 1.4 %convert_reduce_fusion = f32[32,32]{1,0:T(8,128)S(1)} fusion(bf16[32,32,512]{2,1,0:T(8,128)(2,1)} %param.8), kind=kLoop, calls=%fused_computation.4 | loop fusion | flops 1047552 | bytes 1052672 | tf_op jit(solution)/shard_map/reduce_sum | solution.py:19
  4.7 0.0 copy-done
  4.7 0.5 fusion.2
  5.3 0.0 copy-done.1
  5.3 0.6 convolution_convert_fusion
  5.8 0.0 copy-start.2
  5.9 0.1 pad_slice_fusion
  6.0 0.6 copy-done.2
  6.6 0.6 select_reduce_fusion.1
  7.2 1.3 %pad_select_fusion.7 = bf16[32,32,640]{2,1,0:T(8,128)(2,1)S(1)} fusion(bf16[32,32,639]{2,1,0:T(8,128)(2,1)S(1)} %pad_slice_fusion, pred[32,32]{1,0:T(8,128)(4,1)S(1)} %get-tuple-element.25, bf16[32,32,512]{2,1,0:T(8,128)(2,1)S(1)} %convolution_convert_fusion), kind=kLoop, calls=%fused_computation.17 | loop fusion | flops 655360 | bytes 3668992 | tf_op jit(solution)/shard_map/jit(_where)/select_n | solution.py:33
  8.5 1.3 %pad_select_fusion.6 = bf16[32,32,640]{2,1,0:T(8,128)(2,1)S(1)} fusion(bf16[32,32,640]{2,1,0:T(8,128)(2,1)S(1)} %pad_select_fusion.7, bf16[32,32,638]{2,1,0:T(8,128)(2,1)S(1)} %bitcast.35, pred[32,32]{1,0:T(8,128)(4,1)S(1)} %get-tuple-element.26), kind=kLoop, calls=%fused_computation.16 | loop fusion | flops 655360 | bytes 3929088 | tf_op jit(solution)/shard_map/jit(_where)/select_n | solution.py:33
  9.9 1.3 %pad_select_fusion.5 = bf16[32,32,640]{2,1,0:T(8,128)(2,1)S(1)} fusion(bf16[32,32,640]{2,1,0:T(8,128)(2,1)S(1)} %pad_select_fusion.6, bf16[32,32,636]{2,1,0:T(8,128)(2,1)S(1)} %bitcast.36, pred[32,32]{1,0:T(8,128)(4,1)S(1)} %get-tuple-element.27), kind=kLoop, calls=%fused_computation.15 | loop fusion | flops 655360 | bytes 3924992 | tf_op jit(solution)/shard_map/jit(_where)/select_n | solution.py:33
  11.2 1.3 %pad_select_fusion.4 = bf16[32,32,640]{2,1,0:T(8,128)(2,1)S(1)} fusion(bf16[32,32,640]{2,1,0:T(8,128)(2,1)S(1)} %pad_select_fusion.5, bf16[32,32,632]{2,1,0:T(8,128)(2,1)S(1)} %bitcast.37, pred[32,32]{1,0:T(8,128)(4,1)S(1)} %get-tuple-element.28), kind=kLoop, calls=%fused_computation.14 | loop fusion | flops 655360 | bytes 3916800 | tf_op jit(solution)/shard_map/jit(_where)/select_n | solution.py:33
  12.6 1.3 %pad_select_fusion.3 = bf16[32,32,640]{2,1,0:T(8,128)(2,1)S(1)} fusion(bf16[32,32,640]{2,1,0:T(8,128)(2,1)S(1)} %pad_select_fusion.4, bf16[32,32,624]{2,1,0:T(8,128)(2,1)S(1)} %bitcast.38, pred[32,32]{1,0:T(8,128)(4,1)S(1)} %get-tuple-element.29), kind=kLoop, calls=%fused_computation.13 | loop fusion | flops 655360 | bytes 3900416 | tf_op jit(solution)/shard_map/jit(_where)/select_n | solution.py:33
  13.9 1.3 %pad_select_fusion.2 = bf16[32,32,640]{2,1,0:T(8,128)(2,1)S(1)} fusion(bf16[32,32,640]{2,1,0:T(8,128)(2,1)S(1)} %pad_select_fusion.3, bf16[32,32,608]{2,1,0:T(8,128)(2,1)S(1)} %bitcast.39, pred[32,32]{1,0:T(8,128)(4,1)S(1)} %get-tuple-element.30), kind=kLoop, calls=%fused_computation.12 | loop fusion | flops 655360 | bytes 3867648 | tf_op jit(solution)/shard_map/jit(_where)/select_n | solution.py:33
  15.3 1.3 %pad_select_fusion.1 = bf16[32,32,640]{2,1,0:T(8,128)(2,1)S(1)} fusion(bf16[32,32,640]{2,1,0:T(8,128)(2,1)S(1)} %pad_select_fusion.2, bf16[32,32,576]{2,1,0:T(8,128)(2,1)S(1)} %bitcast.40, pred[32,32]{1,0:T(8,128)(4,1)S(1)} %get-tuple-element.31), kind=kLoop, calls=%fused_computation.11 | loop fusion | flops 655360 | bytes 3802112 | tf_op jit(solution)/shard_map/jit(_where)/select_n | solution.py:33
  16.6 0.1 slice.53
  16.7 1.5 %pad_select_fusion = bf16[32,32,640]{2,1,0:T(8,128)(2,1)} fusion(bf16[32,32,640]{2,1,0:T(8,128)(2,1)S(1)} %pad_select_fusion.1, bf16[32,32,512]{2,1,0:T(8,128)(2,1)S(1)} %slice.53, pred[32,32]{1,0:T(8,128)(4,1)S(1)} %get-tuple-element.24), kind=kLoop, calls=%fused_computation.10 | loop fusion | flops 655360 | bytes 3671040 | tf_op jit(solution)/shard_map/jit(_where)/select_n | solution.py:33
  18.2 5.0 %collective-permute-start.2 = (bf16[32,1664]{1,0:T(8,128)(2,1)S(1)}, bf16[32,1664]{1,0:T(8,128)(2,1)S(1)}, u32[]{:S(2)}, u32[]{:S(2)}) collective-permute-start(bf16[32,1664]{1,0:T(8,128)(2,1)S(1)} %fusion.11), channel_id=1, source_target_pairs={{0,12},{4,0},{8,4},{12,8},{1,13},{5,1},{9,5},{13,9},{2,14},{6,2},{... | collective-permute-start | bytes 319496 | tf_op jit(solution)/shard_map/ppermute | solution.py:181
  23.3 0.0 collective-permute-start.1
  23.3 1.0 %collective-permute-start = (bf16[32,1664]{1,0:T(8,128)(2,1)S(1)}, bf16[32,1664]{1,0:T(8,128)(2,1)}, u32[]{:S(2)}, u32[]{:S(2)}) collective-permute-start(bf16[32,1664]{1,0:T(8,128)(2,1)S(1)} %fusion.11), channel_id=1, source_target_pairs={{0,4},{4,8},{8,12},{12,0},{1,5},{5,9},{9,13},{13,1},{2,6},{6,10},{... | collective-permute-start | bytes 319496 | tf_op jit(solution)/shard_map/ppermute | solution.py:181
  24.3 0.1 slice_reduce_fusion
  24.4 2.0 %convert_bitcast_fusion = f32[32,712,32]{1,2,0:T(8,128)S(1)} fusion(bf16[32,32,640]{2,1,0:T(8,128)(2,1)} %pad_select_fusion), kind=kLoop, calls=%fused_computation.2 | loop fusion | flops 729088 | bytes 4227072 | tf_op jit(solution)/shard_map/convert_element_type | solution.py:132
  26.4 6.6 %copy.12 = f32[32,712,32]{2,1,0:T(8,128)} copy(f32[32,712,32]{1,2,0:T(8,128)S(1)} %convert_bitcast_fusion) | data formatting | bytes 5832704 | tf_op jit(solution)/shard_map/convert_element_type | solution.py:132
  33.0 0.0 copy-start.3
  33.0 9.1 %reshape.235.grouped_ref = f32[32,89,256]{2,1,0:T(8,128)} reshape(f32[32,712,32]{2,1,0:T(8,128)} %copy.12) | data formatting | bytes 5832704 | tf_op jit(solution)/shard_map/convert_element_type | solution.py:132
  42.2 0.0 copy-done.3
  42.2 0.7 scatter_custom_fusion
  42.9 0.1 broadcast_in_dim.111
  43.0 0.0 collective-permute-done.2
  43.0 0.0 collective-permute-done.1
  43.0 0.0 collective-permute-done
  43.0 1.0 %maximum_bitcast_fusion = bf16[4,1664,32]{1,2,0:T(8,128)(2,1)S(1)} fusion(bf16[1,32,1664]{2,1,0:T(8,128)(2,1)S(1)} %bitcast.47, bf16[1,32,1664]{2,1,0:T(8,128)(2,1)S(1)} %bitcast.48, bf16[1,32,1664]{2,1,0:T(8,128)(2,1)} %bitcast.2, bf16[1,32,1664]{2,1,0:T(8,128)(2,1)S(1)} %bitcast.42), kind=kLoop, calls=%fused_computation.25 | loop fusion | flops 638976 | bytes 851968 | tf_op jit(solution)/shard_map/convert_element_type | solution.py:134
  44.0 0.9 %copy.13 = bf16[4,1664,32]{2,1,0:T(8,128)(2,1)S(1)} copy(bf16[4,1664,32]{1,2,0:T(8,128)(2,1)S(1)} %maximum_bitcast_fusion) | data formatting | bytes 851968 | tf_op jit(solution)/shard_map/convert_element_type | solution.py:134
  44.9 1.2 %convert_element_type.67 = bf16[4,208,256]{2,1,0:T(8,128)(2,1)S(1)} reshape(bf16[4,1664,32]{2,1,0:T(8,128)(2,1)S(1)} %copy.13) | data formatting | bytes 851968 | tf_op jit(solution)/shard_map/convert_element_type | solution.py:134
  46.1 1.0 %pad_convert_fusion.signal_ref = f32[4,216,256]{2,1,0:T(8,128)} fusion(bf16[4,208,256]{2,1,0:T(8,128)(2,1)S(1)} %convert_element_type.67), kind=kLoop, calls=%fused_computation.24 | loop fusion | flops 221184 | bytes 1310720 | tf_op jit(solution)/shard_map/jit(_pad)/pad | solution.py:134
  47.1 14.9 %shard_map.55 = f32[4,128,256]{2,1,0:T(8,128)} custom-call(f32[32,89,256]{2,1,0:T(8,128)} %reshape.235.grouped_ref, f32[4,216,256]{2,1,0:T(8,128)} %pad_convert_fusion.signal_ref), custom_call_target="tpu_custom_call" | custom-call | tf_op jit(solution)/shard_map/pallas_call | solution.py:138
  62.0 1.1 %select_reduce_fusion = bf16[128,256]{1,0:T(8,128)(2,1)S(1)} fusion(f32[4,128,256]{2,1,0:T(8,128)} %shard_map.55, pred[4,256]{1,0:T(4,128)(4,1)S(1)} %broadcast_in_dim.111), kind=kLoop, calls=%fused_computation.21 | loop fusion | flops 229376 | bytes 590848 | tf_op jit(solution)/shard_map/reduce_sum | solution.py:189
  63.0 0.1 copy.14
  63.2 0.2 copy.15
  63.4 0.1 copy.16
  63.5 0.6 gather_fusion
  64.1 0.1 collective-permute-start.5
  64.3 1.5 %collective-permute-start.4 = (bf16[8,1024]{1,0:T(8,128)(2,1)S(1)}, bf16[8,1024]{1,0:T(8,128)(2,1)S(1)}, u32[]{:S(2)}, u32[]{:S(2)}) collective-permute-start(bf16[8,1024]{1,0:T(8,128)(2,1)S(1)} %get-tuple-element.23), channel_id=1, source_target_pairs={{0,2},{1,3},{2,0},{3,1},{4,6},{5,7},{6,4},{7,5},{8,10},{9,11},{10,... | collective-permute-start | bytes 49160 | tf_op jit(solution)/shard_map/ppermute | solution.py:202
  65.8 0.2 collective-permute-start.3
  65.9 0.0 collective-permute-done.5
  65.9 2.1 %collective-permute-done.4 = bf16[8,1024]{1,0:T(8,128)(2,1)S(1)} collective-permute-done((bf16[8,1024]{1,0:T(8,128)(2,1)S(1)}, bf16[8,1024]{1,0:T(8,128)(2,1)S(1)}, u32[]{:S(2)}, u32[]{:S(2)}) %collective-permute-start.4) | collective-permute-done | bytes 16416 | tf_op jit(solution)/shard_map/ppermute | solution.py:202
  68.0 0.9 %collective-permute-done.3 = bf16[8,1024]{1,0:T(8,128)(2,1)S(1)} collective-permute-done((bf16[8,1024]{1,0:T(8,128)(2,1)S(1)}, bf16[8,1024]{1,0:T(8,128)(2,1)S(1)}, u32[]{:S(2)}, u32[]{:S(2)}) %collective-permute-start.3) | collective-permute-done | bytes 16416 | tf_op jit(solution)/shard_map/ppermute | solution.py:202
  68.9 0.1 multiply_reduce_fusion
  69.1 0.7 broadcast_multiply_fusion
  (14 shorter events, 0.1 us)
Async XLA Ops:
  0.0 4.7 %copy-start = (bf16[32,32,512]{2,1,0:T(8,128)(2,1)S(1)}, bf16[32,32,512]{2,1,0:T(8,128)(2,1)}, u32[]{:S(2)}) copy-start(bf16[32,32,512]{2,1,0:T(8,128)(2,1)} %param.8) | copy-start | bytes 3145732
  0.0 5.3 %copy-start.1 = (s32[32,32]{1,0:T(8,128)S(1)}, s32[32,32]{1,0:T(8,128)}, u32[]{:S(2)}) copy-start(s32[32,32]{1,0:T(8,128)} %param.9) | copy-start | bytes 12292
  5.8 0.7 %copy-start.2 = (s32[32,32]{1,0:T(8,128)S(1)}, s32[32,32]{1,0:T(8,128)}, u32[]{:S(2)}) copy-start(s32[32,32]{1,0:T(8,128)} %param.10) | copy-start | bytes 12292
  18.2 24.8 %collective-permute-start.2 = (bf16[32,1664]{1,0:T(8,128)(2,1)S(1)}, bf16[32,1664]{1,0:T(8,128)(2,1)S(1)}, u32[]{:S(2)}, u32[]{:S(2)}) collective-permute-start(bf16[32,1664]{1,0:T(8,128)(2,1)S(1)} %fusion.11), channel_id=1, source_target_pairs={{0,12},{4,0},{8,4},{12,8},{1,13},{5,1},{9,5},{13,9},{2,14},{6,2},{... | collective-permute-start | bytes 319496 | tf_op jit(solution)/shard_map/ppermute | solution.py:181
  23.3 19.7 %collective-permute-start.1 = (bf16[32,1664]{1,0:T(8,128)(2,1)S(1)}, bf16[32,1664]{1,0:T(8,128)(2,1)S(1)}, u32[]{:S(2)}, u32[]{:S(2)}) collective-permute-start(bf16[32,1664]{1,0:T(8,128)(2,1)S(1)} %fusion.11), channel_id=1, source_target_pairs={{0,8},{4,12},{8,0},{12,4},{1,9},{5,13},{9,1},{13,5},{2,10},{6,14},... | collective-permute-start | bytes 319496 | tf_op jit(solution)/shard_map/ppermute | solution.py:181
  23.3 19.8 %collective-permute-start = (bf16[32,1664]{1,0:T(8,128)(2,1)S(1)}, bf16[32,1664]{1,0:T(8,128)(2,1)}, u32[]{:S(2)}, u32[]{:S(2)}) collective-permute-start(bf16[32,1664]{1,0:T(8,128)(2,1)S(1)} %fusion.11), channel_id=1, source_target_pairs={{0,4},{4,8},{8,12},{12,0},{1,5},{5,9},{9,13},{13,1},{2,6},{6,10},{... | collective-permute-start | bytes 319496 | tf_op jit(solution)/shard_map/ppermute | solution.py:181
  33.0 9.1 %copy-start.3 = (s32[1,32]{1,0:T(1,128)S(1)}, s32[1,32]{1,0:T(1,128)}, u32[]{:S(2)}) copy-start(s32[1,32]{1,0:T(1,128)} %param.11) | copy-start | bytes 388
  64.1 1.8 %collective-permute-start.5 = (bf16[8,1024]{1,0:T(8,128)(2,1)S(1)}, bf16[8,1024]{1,0:T(8,128)(2,1)S(1)}, u32[]{:S(2)}, u32[]{:S(2)}) collective-permute-start(bf16[8,1024]{1,0:T(8,128)(2,1)S(1)} %get-tuple-element.22), channel_id=1, source_target_pairs={{0,3},{1,0},{2,1},{3,2},{4,7},{5,4},{6,5},{7,6},{8,11},{9,8},{10,9... | collective-permute-start | bytes 49160 | tf_op jit(solution)/shard_map/ppermute | solution.py:202
  64.3 3.7 %collective-permute-start.4 = (bf16[8,1024]{1,0:T(8,128)(2,1)S(1)}, bf16[8,1024]{1,0:T(8,128)(2,1)S(1)}, u32[]{:S(2)}, u32[]{:S(2)}) collective-permute-start(bf16[8,1024]{1,0:T(8,128)(2,1)S(1)} %get-tuple-element.23), channel_id=1, source_target_pairs={{0,2},{1,3},{2,0},{3,1},{4,6},{5,7},{6,4},{7,5},{8,10},{9,11},{10,... | collective-permute-start | bytes 49160 | tf_op jit(solution)/shard_map/ppermute | solution.py:202
  65.8 3.2 %collective-permute-start.3 = (bf16[8,1024]{1,0:T(8,128)(2,1)S(1)}, bf16[8,1024]{1,0:T(8,128)(2,1)S(1)}, u32[]{:S(2)}, u32[]{:S(2)}) collective-permute-start(bf16[8,1024]{1,0:T(8,128)(2,1)S(1)} %get-tuple-element.21), channel_id=1, source_target_pairs={{0,1},{1,2},{2,3},{3,0},{4,5},{5,6},{6,7},{7,4},{8,9},{9,10},{10,1... | collective-permute-start | bytes 49160 | tf_op jit(solution)/shard_map/ppermute | solution.py:202

commit v12 on v10

--- a/solution.py
+++ b/solution.py
@@ -69,16 +69,9 @@
     )(grouped)
 
 
-def _corr_kernel(grouped_ref, signal_ref, out_ref, acc_ref, filt_ref, *, steps, count, chans, phases, rows):
-    width = phases * chans
-    pid = pl.program_id(0)
-
-    @pl.when(pid == 0)
-    def _():
-        acc_ref[...] = jnp.zeros_like(acc_ref)
-
-    base = pl.multiple_of(pid * steps, steps)
-    for step in range(steps):
+def _build_filters(grouped_ref, filt_ref, base, steps_range, *, count, chans, phases):
+    width = phases * chans
+    for step in steps_range:
         joined = jnp.concatenate([grouped_ref[base + step], grouped_ref[base + step + 1]], axis=-1)
         joined = joined.astype(jnp.float32)
         parts = []
@@ -88,39 +81,78 @@
             parts.append(moved[:, :width])
         filt_ref[step] = jnp.transpose(jnp.concatenate(parts, axis=0)).astype(filt_ref.dtype)
 
+
+def _accumulate(signal_ref, filt_ref, acc_ref, base, steps_range, *, steps, rows, width):
     n_blocks = signal_ref.shape[0]
     if n_blocks <= 8:
         band = signal_ref[:, pl.ds(base, rows + steps), :]
         total = acc_ref[...]
-        for step in range(steps):
+        for step in steps_range:
             window = band[:, step : step + rows].astype(filt_ref.dtype)
             window = window.reshape(n_blocks * rows, width)
             total += jnp.dot(window, filt_ref[step], preferred_element_type=jnp.float32)
         acc_ref[...] = total
     else:
 
-        def accumulate(g, carry):
+        def body(g, carry):
             band = signal_ref[g, pl.ds(base, rows + steps), :]
             start = pl.multiple_of(g * rows, rows)
             total = acc_ref[pl.ds(start, rows), :]
-            for step in range(steps):
+            for step in steps_range:
                 window = band[step : step + rows].astype(filt_ref.dtype)
                 total += jnp.dot(window, filt_ref[step], preferred_element_type=jnp.float32)
             acc_ref[pl.ds(start, rows), :] = total
             return carry
 
-        lax.fori_loop(0, n_blocks, accumulate, 0)
-
-    @pl.when(pid == pl.num_programs(0) - 1)
+        lax.fori_loop(0, n_blocks, body, 0)
+
+
+def _corr_kernel(grouped_ref, signal_ref, out_ref, acc_ref, filt_ref, *, steps, last_steps, count, chans, phases, rows):
+    width = phases * chans
+    pid = pl.program_id(0)
+    last = pl.num_programs(0) - 1
+    base = pl.multiple_of(pid * steps, steps)
+    build = functools.partial(_build_filters, count=count, chans=chans, phases=phases)
+    accumulate = functools.partial(_accumulate, steps=steps, rows=rows, width=width)
+
+    @pl.when(pid == 0)
+    def _():
+        acc_ref[...] = jnp.zeros_like(acc_ref)
+
+    build(grouped_ref, filt_ref, base, range(last_steps))
+    accumulate(signal_ref, filt_ref, acc_ref, base, range(last_steps))
+    if last_steps < steps:
+
+        @pl.when(pid < last)
+        def _():
+            build(grouped_ref, filt_ref, base, range(last_steps, steps))
+            accumulate(signal_ref, filt_ref, acc_ref, base, range(last_steps, steps))
+
+    @pl.when(pid == last)
     def _():
         out_ref[...] = acc_ref[...].reshape(out_ref.shape)
 
 
-def correlate(placed, blocks, phases, lags):
+CORR_STEPS = 8
+
+
+def corr_taps(padded_len, phases):
+    taps = padded_len // phases + 1
+    return taps, -(-taps // CORR_STEPS) * CORR_STEPS
+
+
+def polyphase_rows(signal, phases, total_rows):
+    chans, window = signal.shape
+    rows = jnp.transpose(signal, (1, 0)).reshape(window // phases, phases * chans)
+    return jnp.pad(rows, ((0, total_rows - window // phases), (0, 0)))
+
+
+def correlate(placed, signal_rows, phases, lags):
     count, chans, padded_len = placed.shape
-    n_blocks, _, window = blocks.shape
-    steps = 8
-    taps = -(-(padded_len // phases + 1) // steps) * steps
+    n_blocks = signal_rows.shape[0]
+    steps = CORR_STEPS
+    real_taps, taps = corr_taps(padded_len, phases)
+    last_steps = real_taps - (taps - steps)
     front = phases - 1
     n_groups = taps + 1
     rows = lags // phases
@@ -128,10 +160,10 @@
     padded = jnp.pad(placed, ((0, 0), (0, 0), (front, n_groups * phases - padded_len - front)))
     grouped = jnp.transpose(padded, (0, 2, 1)).reshape(count, n_groups, width)
     grouped = jnp.transpose(grouped, (1, 0, 2))
-    signal = jnp.transpose(blocks, (0, 2, 1)).reshape(n_blocks, window // phases, width)
-    signal = jnp.pad(signal.astype(jnp.float32), ((0, 0), (0, taps + rows - window // phases), (0, 0)))
+    signal = signal_rows.astype(jnp.float32)
     kernel = functools.partial(
-        _corr_kernel, steps=steps, count=count, chans=chans, phases=phases, rows=rows
+        _corr_kernel, steps=steps, last_steps=last_steps, count=count, chans=chans,
+        phases=phases, rows=rows,
     )
     return pl.pallas_call(
         kernel,
@@ -171,6 +203,8 @@
     ).astype(jnp.bfloat16)
     ordered_shift = jnp.sum(jnp.where(hit, offsets[:, :, None], 0), axis=1)
     placed = place_moveout(ordered, ordered_shift, padded_len)
+    _, taps = corr_taps(padded_len, phases)
+    signal = polyphase_rows(signal, phases, taps + lags // phases)
     signal, placed = lax.optimization_barrier((signal, placed))
     if n_chan <= 8:
         pieces = [signal]

time: 63.9 us -> 66 us (1.033)
  Pallas kernels: 14 us -> 18.8 us
  local copies, waits for them, and re-layouts: 19.1 us -> 17.5 us
  other arithmetic: 18.6 us -> 17.5 us
    pallas_call x1, Pallas kernels: 14 us -> 18.8 us  [correlate(): pl.pallas_call(kernel, grid=(taps // steps,), in_specs=[pl.BlockSpec(grou...]
    convert_element_type x2 -> x0, local copies, waits for them, and re-layouts: 2.11 us -> none  [correlate(): signal.astype(jnp.float32)]
    reduce_sum x2, other arithmetic: 2.54 us -> 1.32 us  [normalize_rows(): centred = values - jnp.mean(values, axis=-1, keepdims=True)]
    transpose x0 -> x1, other arithmetic: none -> 0.99 us  [polyphase_rows(): jnp.transpose(signal, (1, 0)).reshape(window // phases, phases * chans)]
    pad x1 -> x0, other arithmetic: 0.98 us -> none  [correlate(): jnp.pad(signal.astype(jnp.float32), ((0, 0), (0, taps + rows - window //...]
  transfers between devices with their start and end apart: 6 -> 6, of which waited for: 2 -> 2; matrix products, arithmetic and copies ran while one was open for 24% -> 23% of each run, Pallas kernels for 0% -> 0%
where the time goes in v12:
time: 66 us; the launch traced here: 65.5 us
  Pallas kernels  18.8 us (28%)
  local copies, waits for them, and re-layouts  17.5 us (27%)
  other arithmetic  17.5 us (27%)
  starting transfers between devices  7.89 us (12%)
  waiting for transfers between devices  3 us (5%)
    pallas_call x1, Pallas kernels, correlate(): pl.pallas_call(kernel, grid=(taps // steps,), in_specs=[pl.BlockSpec(grou...  18.8 us
    select_n x8, other arithmetic, place_moveout(): current = jnp.where(active[..., None], moved, current)  9.93 us
    reshape x2, local copies, waits for them, and re-layouts, correlate(): grouped = jnp.transpose(padded, (0, 2, 1)).reshape(count, n_groups, width)  8.94 us
    ppermute x3, starting transfers between devices, shards(): pieces.append(lax.ppermute(signal, 'chan', pairs))  6.12 us
    transpose x2, local copies, waits for them, and re-layouts, correlate(): grouped = jnp.transpose(padded, (0, 2, 1)).reshape(count, n_groups, width)  5.22 us
    ppermute x3, waiting for transfers between devices, shards(): stack = stack + lax.ppermute(outgoing, 'tmpl', pairs).astype(jnp.float32)  3 us
    ppermute x3, starting transfers between devices, shards(): stack = stack + lax.ppermute(outgoing, 'tmpl', pairs).astype(jnp.float32)  1.78 us
    reduce_sum x2, other arithmetic, normalize_rows(): scale = lax.rsqrt(jnp.mean(centred * centred, axis=-1, keepdims=True) + eps)  1.62 us
  transfers between devices with their start and end apart: 6, of which 2 were waited for; matrix products, arithmetic and copies ran while one was open for 23% of the time, Pallas kernels for 0%

profile of v12, /device:TPU:0, one launch (start us, length us, event | category | flops | bytes accessed | tf_op | source)
XLA Modules:
  0.0 65.5 jit_solution(12875196844777357685)
XLA Ops:
  0.0 0.0 copy-start
  0.0 1.1 %convert_reduce_fusion.1 = f32[32]{0:T(128)S(1)} fusion(bf16[32,1664]{1,0:T(8,128)(2,1)} %param.7), kind=kLoop, calls=%fused_computation.27 | loop fusion | flops 106464 | bytes 106624 | tf_op jit(solution)/shard_map/reduce_sum | solution.py:19
  1.1 1.1 %fusion.10 = f32[32]{0:T(128)S(1)} fusion(bf16[32,1664]{1,0:T(8,128)(2,1)} %param.7, f32[32]{0:T(128)S(1)} %broadcast_multiply_fusion.2), kind=kLoop, calls=%fused_computation.31 | loop fusion | flops 212960 | bytes 106752 | tf_op jit(solution)/shard_map/reduce_sum | solution.py:20
  2.2 1.0 %fusion.12 = bf16[1664,32]{0,1:T(8,128)(2,1)S(1)} fusion(bf16[32,1664]{1,0:T(8,128)(2,1)} %param.7, f32[32]{0:T(128)S(1)} %add_rsqrt_fusion.2, f32[32]{0:T(128)S(1)} %broadcast_multiply_fusion.2), kind=kLoop, calls=%fused_computation.33 | loop fusion | flops 212992 | bytes 213248 | tf_op jit(solution)/shard_map/transpose | solution.py:146
  3.2 0.3 copy.12
  3.5 0.0 copy-start.1
  3.5 0.3 reshape.175
  3.8 0.0 copy-done
  3.8 0.2 convert_reduce_fusion
  4.0 0.5 fusion.2
  4.6 0.0 copy-done.1
  4.6 0.5 convolution_convert_fusion
  5.1 0.0 copy-start.2
  5.2 0.1 pad_slice_fusion
  5.3 0.6 copy-done.2
  5.9 0.6 select_reduce_fusion.1
  6.5 1.3 %pad_select_fusion.7 = bf16[32,32,640]{2,1,0:T(8,128)(2,1)S(1)} fusion(bf16[32,32,639]{2,1,0:T(8,128)(2,1)S(1)} %pad_slice_fusion, pred[32,32]{1,0:T(8,128)(4,1)S(1)} %get-tuple-element.25, bf16[32,32,512]{2,1,0:T(8,128)(2,1)S(1)} %convolution_convert_fusion), kind=kLoop, calls=%fused_computation.18 | loop fusion | flops 655360 | bytes 3668992 | tf_op jit(solution)/shard_map/jit(_where)/select_n | solution.py:33
  7.8 1.3 %pad_select_fusion.6 = bf16[32,32,640]{2,1,0:T(8,128)(2,1)S(1)} fusion(bf16[32,32,640]{2,1,0:T(8,128)(2,1)S(1)} %pad_select_fusion.7, bf16[32,32,638]{2,1,0:T(8,128)(2,1)S(1)} %bitcast.38, pred[32,32]{1,0:T(8,128)(4,1)S(1)} %get-tuple-element.26), kind=kLoop, calls=%fused_computation.17 | loop fusion | flops 655360 | bytes 3929088 | tf_op jit(solution)/shard_map/jit(_where)/select_n | solution.py:33
  9.2 1.3 %pad_select_fusion.5 = bf16[32,32,640]{2,1,0:T(8,128)(2,1)S(1)} fusion(bf16[32,32,640]{2,1,0:T(8,128)(2,1)S(1)} %pad_select_fusion.6, bf16[32,32,636]{2,1,0:T(8,128)(2,1)S(1)} %bitcast.39, pred[32,32]{1,0:T(8,128)(4,1)S(1)} %get-tuple-element.27), kind=kLoop, calls=%fused_computation.16 | loop fusion | flops 655360 | bytes 3924992 | tf_op jit(solution)/shard_map/jit(_where)/select_n | solution.py:33
  10.5 1.3 %pad_select_fusion.4 = bf16[32,32,640]{2,1,0:T(8,128)(2,1)S(1)} fusion(bf16[32,32,640]{2,1,0:T(8,128)(2,1)S(1)} %pad_select_fusion.5, bf16[32,32,632]{2,1,0:T(8,128)(2,1)S(1)} %bitcast.40, pred[32,32]{1,0:T(8,128)(4,1)S(1)} %get-tuple-element.28), kind=kLoop, calls=%fused_computation.15 | loop fusion | flops 655360 | bytes 3916800 | tf_op jit(solution)/shard_map/jit(_where)/select_n | solution.py:33
  11.9 1.3 %pad_select_fusion.3 = bf16[32,32,640]{2,1,0:T(8,128)(2,1)S(1)} fusion(bf16[32,32,640]{2,1,0:T(8,128)(2,1)S(1)} %pad_select_fusion.4, bf16[32,32,624]{2,1,0:T(8,128)(2,1)S(1)} %bitcast.41, pred[32,32]{1,0:T(8,128)(4,1)S(1)} %get-tuple-element.29), kind=kLoop, calls=%fused_computation.14 | loop fusion | flops 655360 | bytes 3900416 | tf_op jit(solution)/shard_map/jit(_where)/select_n | solution.py:33
  13.2 1.3 %pad_select_fusion.2 = bf16[32,32,640]{2,1,0:T(8,128)(2,1)S(1)} fusion(bf16[32,32,640]{2,1,0:T(8,128)(2,1)S(1)} %pad_select_fusion.3, bf16[32,32,608]{2,1,0:T(8,128)(2,1)S(1)} %bitcast.42, pred[32,32]{1,0:T(8,128)(4,1)S(1)} %get-tuple-element.30), kind=kLoop, calls=%fused_computation.13 | loop fusion | flops 655360 | bytes 3867648 | tf_op jit(solution)/shard_map/jit(_where)/select_n | solution.py:33
  14.6 1.3 %pad_select_fusion.1 = bf16[32,32,640]{2,1,0:T(8,128)(2,1)S(1)} fusion(bf16[32,32,640]{2,1,0:T(8,128)(2,1)S(1)} %pad_select_fusion.2, bf16[32,32,576]{2,1,0:T(8,128)(2,1)S(1)} %bitcast.43, pred[32,32]{1,0:T(8,128)(4,1)S(1)} %get-tuple-element.31), kind=kLoop, calls=%fused_computation.12 | loop fusion | flops 655360 | bytes 3802112 | tf_op jit(solution)/shard_map/jit(_where)/select_n | solution.py:33
  15.9 0.1 slice.53
  16.1 0.6 pad_select_fusion
  16.6 5.1 %collective-permute-start.2 = (bf16[216,256]{1,0:T(8,128)(2,1)S(1)}, bf16[216,256]{1,0:T(8,128)(2,1)S(1)}, u32[]{:S(2)}, u32[]{:S(2)}) collective-permute-start(bf16[216,256]{1,0:T(8,128)(2,1)S(1)} %pad.17), channel_id=1, source_target_pairs={{0,12},{4,0},{8,4},{12,8},{1,13},{5,1},{9,5},{13,9},{2,14},{6,2},{... | collective-permute-start | bytes 331784 | tf_op jit(solution)/shard_map/ppermute | solution.py:213
  21.7 0.0 collective-permute-start.1
  21.7 1.0 %collective-permute-start = (bf16[216,256]{1,0:T(8,128)(2,1)S(1)}, bf16[216,256]{1,0:T(8,128)(2,1)S(1)}, u32[]{:S(2)}, u32[]{:S(2)}) collective-permute-start(bf16[216,256]{1,0:T(8,128)(2,1)S(1)} %pad.17), channel_id=1, source_target_pairs={{0,4},{4,8},{8,12},{12,0},{1,5},{5,9},{9,13},{13,1},{2,6},{6,10},{... | collective-permute-start | bytes 331784 | tf_op jit(solution)/shard_map/ppermute | solution.py:213
  22.8 0.1 slice_reduce_fusion
  22.9 0.7 %pad_bitcast_fusion = bf16[32,712,32]{1,2,0:T(8,128)(2,1)S(1)} fusion(bf16[32,32,640]{2,1,0:T(8,128)(2,1)S(1)} %pad_select_fusion), kind=kLoop, calls=%fused_computation.8 | loop fusion | bytes 2768896 | tf_op jit(solution)/shard_map/transpose | solution.py:161
  23.7 4.5 %copy.13 = bf16[32,712,32]{2,1,0:T(8,128)(2,1)} copy(bf16[32,712,32]{1,2,0:T(8,128)(2,1)S(1)} %pad_bitcast_fusion) | data formatting | bytes 2916352 | tf_op jit(solution)/shard_map/transpose | solution.py:161
  28.2 7.0 %reshape.176 = bf16[32,89,256]{2,1,0:T(8,128)(2,1)S(1)} reshape(bf16[32,712,32]{2,1,0:T(8,128)(2,1)} %copy.13) | data formatting | bytes 2916352 | tf_op jit(solution)/shard_map/reshape | solution.py:161
  35.2 0.0 copy-start.3
  35.2 1.9 %copy.19 = bf16[32,89,256]{2,0,1:T(8,128)(2,1)} copy(bf16[32,89,256]{2,1,0:T(8,128)(2,1)S(1)} %reshape.176) | data formatting | bytes 2916352 | tf_op jit(solution)/shard_map/reshape | solution.py:161
  37.1 0.0 copy-done.3
  37.1 0.7 %scatter_custom_fusion = s32[32]{0:T(128)S(1)} fusion(s32[32]{0:T(128)S(1)} %fusion.15, s32[32]{0:T(128)S(1)} %iota.14, s32[]{:T(128)} %constant.103.clone.1), kind=kCustom, calls=%fused_computation.71 | custom fusion | bytes 132 | tf_op jit(solution)/shard_map/scatter | solution.py:225
  37.8 0.1 broadcast_in_dim.111
  37.9 0.0 collective-permute-done.2
  37.9 0.0 collective-permute-done.1
  38.0 0.0 collective-permute-done
  38.0 1.0 %maximum_convert_fusion.signal_ref = f32[4,216,256]{2,1,0:T(8,128)} fusion(bf16[1,216,256]{2,1,0:T(8,128)(2,1)S(1)} %bitcast.51, bf16[1,216,256]{2,1,0:T(8,128)(2,1)S(1)} %bitcast.52, bf16[1,216,256]{2,1,0:T(8,128)(2,1)S(1)} %bitcast.53, bf16[1,216,256]{2,1,0:T(8,128)(2,1)S(1)} %bitcast.46), kind=kLoop, calls=%fused_computation.25 | loop fusion | flops 884736 | bytes 1327104 | tf_op jit(solution)/shard_map/convert_element_type | solution.py:163
  39.0 18.8 %shard_map.55 = f32[4,128,256]{2,1,0:T(8,128)} custom-call(bf16[89,32,256]{2,1,0:T(8,128)(2,1)} %bitcast.44, f32[4,216,256]{2,1,0:T(8,128)} %maximum_convert_fusion.signal_ref), custom_call_target="tpu_custom_call" | custom-call | tf_op jit(solution)/shard_map/pallas_call | solution.py:168
  57.7 1.1 %select_reduce_fusion = bf16[128,256]{1,0:T(8,128)(2,1)S(1)} fusion(f32[4,128,256]{2,1,0:T(8,128)} %shard_map.55, pred[4,256]{1,0:T(4,128)(4,1)S(1)} %broadcast_in_dim.111), kind=kLoop, calls=%fused_computation.22 | loop fusion | flops 229376 | bytes 590848 | tf_op jit(solution)/shard_map/reduce_sum | solution.py:221
  58.8 0.1 copy.15
  59.0 0.2 copy.16
  59.2 0.1 copy.17
  59.3 0.6 gather_fusion
  59.9 0.1 collective-permute-start.5
  60.1 1.5 %collective-permute-start.4 = (bf16[8,1024]{1,0:T(8,128)(2,1)S(1)}, bf16[8,1024]{1,0:T(8,128)(2,1)S(1)}, u32[]{:S(2)}, u32[]{:S(2)}) collective-permute-start(bf16[8,1024]{1,0:T(8,128)(2,1)S(1)} %get-tuple-element.23), channel_id=1, source_target_pairs={{0,2},{1,3},{2,0},{3,1},{4,6},{5,7},{6,4},{7,5},{8,10},{9,11},{10,... | collective-permute-start | bytes 49160 | tf_op jit(solution)/shard_map/ppermute | solution.py:234
  61.5 0.2 collective-permute-start.3
  61.7 0.0 collective-permute-done.5
  61.7 2.1 %collective-permute-done.4 = bf16[8,1024]{1,0:T(8,128)(2,1)S(1)} collective-permute-done((bf16[8,1024]{1,0:T(8,128)(2,1)S(1)}, bf16[8,1024]{1,0:T(8,128)(2,1)S(1)}, u32[]{:S(2)}, u32[]{:S(2)}) %collective-permute-start.4) | collective-permute-done | bytes 16416 | tf_op jit(solution)/shard_map/ppermute | solution.py:234
  63.8 0.9 %collective-permute-done.3 = bf16[8,1024]{1,0:T(8,128)(2,1)S(1)} collective-permute-done((bf16[8,1024]{1,0:T(8,128)(2,1)S(1)}, bf16[8,1024]{1,0:T(8,128)(2,1)S(1)}, u32[]{:S(2)}, u32[]{:S(2)}) %collective-permute-start.3) | collective-permute-done | bytes 16416 | tf_op jit(solution)/shard_map/ppermute | solution.py:234
  64.7 0.1 multiply_reduce_fusion
  64.8 0.7 %broadcast_multiply_fusion = f32[8,1024]{1,0:T(8,128)} fusion(f32[8]{0:T(128)S(1)} %add_rsqrt_fusion.1, bf16[8,1024]{1,0:T(8,128)(2,1)S(1)} %collective-permute-done.5, bf16[8,1024]{1,0:T(8,128)(2,1)S(1)} %collective-permute-done.4, bf16[8,1024]{1,0:T(8,128)(2,1)S(1)} %collective-permute-done.3, bf16[4,8,1024]{2,1,0:T(8,128)(2,1)S(1)} %bitcast.49, ...), kind=kLoop, calls=%fused_computation.43 | loop fusion | flops 73728 | bytes 98341 | tf_op jit(solution)/shard_map/mul | solution.py:239
  (15 shorter events, 0.2 us)
Async XLA Ops:
  0.0 3.8 %copy-start = (bf16[32,32,512]{2,1,0:T(8,128)(2,1)S(1)}, bf16[32,32,512]{2,1,0:T(8,128)(2,1)}, u32[]{:S(2)}) copy-start(bf16[32,32,512]{2,1,0:T(8,128)(2,1)} %param.8) | copy-start | bytes 3145732
  3.5 1.1 %copy-start.1 = (s32[32,32]{1,0:T(8,128)S(1)}, s32[32,32]{1,0:T(8,128)}, u32[]{:S(2)}) copy-start(s32[32,32]{1,0:T(8,128)} %param.9) | copy-start | bytes 12292
  5.1 0.7 %copy-start.2 = (s32[32,32]{1,0:T(8,128)S(1)}, s32[32,32]{1,0:T(8,128)}, u32[]{:S(2)}) copy-start(s32[32,32]{1,0:T(8,128)} %param.10) | copy-start | bytes 12292
  16.6 21.3 %collective-permute-start.2 = (bf16[216,256]{1,0:T(8,128)(2,1)S(1)}, bf16[216,256]{1,0:T(8,128)(2,1)S(1)}, u32[]{:S(2)}, u32[]{:S(2)}) collective-permute-start(bf16[216,256]{1,0:T(8,128)(2,1)S(1)} %pad.17), channel_id=1, source_target_pairs={{0,12},{4,0},{8,4},{12,8},{1,13},{5,1},{9,5},{13,9},{2,14},{6,2},{... | collective-permute-start | bytes 331784 | tf_op jit(solution)/shard_map/ppermute | solution.py:213
  21.7 16.2 %collective-permute-start.1 = (bf16[216,256]{1,0:T(8,128)(2,1)S(1)}, bf16[216,256]{1,0:T(8,128)(2,1)S(1)}, u32[]{:S(2)}, u32[]{:S(2)}) collective-permute-start(bf16[216,256]{1,0:T(8,128)(2,1)S(1)} %pad.17), channel_id=1, source_target_pairs={{0,8},{4,12},{8,0},{12,4},{1,9},{5,13},{9,1},{13,5},{2,10},{6,14},... | collective-permute-start | bytes 331784 | tf_op jit(solution)/shard_map/ppermute | solution.py:213
  21.7 16.2 %collective-permute-start = (bf16[216,256]{1,0:T(8,128)(2,1)S(1)}, bf16[216,256]{1,0:T(8,128)(2,1)S(1)}, u32[]{:S(2)}, u32[]{:S(2)}) collective-permute-start(bf16[216,256]{1,0:T(8,128)(2,1)S(1)} %pad.17), channel_id=1, source_target_pairs={{0,4},{4,8},{8,12},{12,0},{1,5},{5,9},{9,13},{13,1},{2,6},{6,10},{... | collective-permute-start | bytes 331784 | tf_op jit(solution)/shard_map/ppermute | solution.py:213
  35.2 2.0 %copy-start.3 = (s32[1,32]{1,0:T(1,128)S(1)}, s32[1,32]{1,0:T(1,128)}, u32[]{:S(2)}) copy-start(s32[1,32]{1,0:T(1,128)} %param.11) | copy-start | bytes 388
  59.9 1.8 %collective-permute-start.5 = (bf16[8,1024]{1,0:T(8,128)(2,1)S(1)}, bf16[8,1024]{1,0:T(8,128)(2,1)S(1)}, u32[]{:S(2)}, u32[]{:S(2)}) collective-permute-start(bf16[8,1024]{1,0:T(8,128)(2,1)S(1)} %get-tuple-element.22), channel_id=1, source_target_pairs={{0,3},{1,0},{2,1},{3,2},{4,7},{5,4},{6,5},{7,6},{8,11},{9,8},{10,9... | collective-permute-start | bytes 49160 | tf_op jit(solution)/shard_map/ppermute | solution.py:234
  60.1 3.7 %collective-permute-start.4 = (bf16[8,1024]{1,0:T(8,128)(2,1)S(1)}, bf16[8,1024]{1,0:T(8,128)(2,1)S(1)}, u32[]{:S(2)}, u32[]{:S(2)}) collective-permute-start(bf16[8,1024]{1,0:T(8,128)(2,1)S(1)} %get-tuple-element.23), channel_id=1, source_target_pairs={{0,2},{1,3},{2,0},{3,1},{4,6},{5,7},{6,4},{7,5},{8,10},{9,11},{10,... | collective-permute-start | bytes 49160 | tf_op jit(solution)/shard_map/ppermute | solution.py:234
  61.5 3.2 %collective-permute-start.3 = (bf16[8,1024]{1,0:T(8,128)(2,1)S(1)}, bf16[8,1024]{1,0:T(8,128)(2,1)S(1)}, u32[]{:S(2)}, u32[]{:S(2)}) collective-permute-start(bf16[8,1024]{1,0:T(8,128)(2,1)S(1)} %get-tuple-element.21), channel_id=1, source_target_pairs={{0,1},{1,2},{2,3},{3,0},{4,5},{5,6},{6,7},{7,4},{8,9},{9,10},{10,1... | collective-permute-start | bytes 49160 | tf_op jit(solution)/shard_map/ppermute | solution.py:234

commit v13 on v10

--- a/solution.py
+++ b/solution.py
@@ -116,11 +116,25 @@
         out_ref[...] = acc_ref[...].reshape(out_ref.shape)
 
 
-def correlate(placed, blocks, phases, lags):
+CORR_STEPS = 8
+
+
+def corr_taps(padded_len, phases):
+    taps = padded_len // phases + 1
+    return taps, -(-taps // CORR_STEPS) * CORR_STEPS
+
+
+def polyphase_rows(signal, phases, total_rows):
+    chans, window = signal.shape
+    rows = jnp.transpose(signal, (1, 0)).reshape(window // phases, phases * chans)
+    return jnp.pad(rows, ((0, total_rows - window // phases), (0, 0)))
+
+
+def correlate(placed, signal_rows, phases, lags):
     count, chans, padded_len = placed.shape
-    n_blocks, _, window = blocks.shape
-    steps = 8
-    taps = -(-(padded_len // phases + 1) // steps) * steps
+    n_blocks = signal_rows.shape[0]
+    steps = CORR_STEPS
+    _, taps = corr_taps(padded_len, phases)
     front = phases - 1
     n_groups = taps + 1
     rows = lags // phases
@@ -128,8 +142,7 @@
     padded = jnp.pad(placed, ((0, 0), (0, 0), (front, n_groups * phases - padded_len - front)))
     grouped = jnp.transpose(padded, (0, 2, 1)).reshape(count, n_groups, width)
     grouped = jnp.transpose(grouped, (1, 0, 2))
-    signal = jnp.transpose(blocks, (0, 2, 1)).reshape(n_blocks, window // phases, width)
-    signal = jnp.pad(signal.astype(jnp.float32), ((0, 0), (0, taps + rows - window // phases), (0, 0)))
+    signal = signal_rows.astype(jnp.float32)
     kernel = functools.partial(
         _corr_kernel, steps=steps, count=count, chans=chans, phases=phases, rows=rows
     )
@@ -171,6 +184,8 @@
     ).astype(jnp.bfloat16)
     ordered_shift = jnp.sum(jnp.where(hit, offsets[:, :, None], 0), axis=1)
     placed = place_moveout(ordered, ordered_shift, padded_len)
+    _, taps = corr_taps(padded_len, phases)
+    signal = polyphase_rows(signal, phases, taps + lags // phases)
     signal, placed = lax.optimization_barrier((signal, placed))
     if n_chan <= 8:
         pieces = [signal]

time: 63.9 us -> 61.2 us (0.958)
  local copies, waits for them, and re-layouts: 19.1 us -> 17.5 us
  other arithmetic: 18.6 us -> 17.5 us
    convert_element_type x2 -> x0, local copies, waits for them, and re-layouts: 2.11 us -> none  [correlate(): signal.astype(jnp.float32)]
    reduce_sum x2, other arithmetic: 2.54 us -> 1.32 us  [normalize_rows(): centred = values - jnp.mean(values, axis=-1, keepdims=True)]
    transpose x0 -> x1, other arithmetic: none -> 0.99 us  [polyphase_rows(): jnp.transpose(signal, (1, 0)).reshape(window // phases, phases * chans)]
    pad x1 -> x0, other arithmetic: 0.98 us -> none  [correlate(): jnp.pad(signal.astype(jnp.float32), ((0, 0), (0, taps + rows - window //...]
  transfers between devices with their start and end apart: 6 -> 6, of which waited for: 2 -> 2; matrix products, arithmetic and copies ran while one was open for 24% -> 25% of each run, Pallas kernels for 0% -> 0%
where the time goes in v13:
time: 61.2 us; the launch traced here: 60.8 us
  local copies, waits for them, and re-layouts  17.5 us (29%)
  other arithmetic  17.5 us (29%)
  Pallas kernels  14 us (23%)
  starting transfers between devices  7.9 us (13%)
  waiting for transfers between devices  3 us (5%)
    pallas_call x1, Pallas kernels, correlate(): pl.pallas_call(kernel, grid=(taps // steps,), in_specs=[pl.BlockSpec(grou...  14 us
    select_n x8, other arithmetic, place_moveout(): current = jnp.where(active[..., None], moved, current)  9.93 us
    reshape x2, local copies, waits for them, and re-layouts, correlate(): grouped = jnp.transpose(padded, (0, 2, 1)).reshape(count, n_groups, width)  8.94 us
    ppermute x3, starting transfers between devices, shards(): pieces.append(lax.ppermute(signal, 'chan', pairs))  6.12 us
    transpose x2, local copies, waits for them, and re-layouts, correlate(): grouped = jnp.transpose(padded, (0, 2, 1)).reshape(count, n_groups, width)  5.22 us
    ppermute x3, waiting for transfers between devices, shards(): stack = stack + lax.ppermute(outgoing, 'tmpl', pairs).astype(jnp.float32)  3 us
    ppermute x3, starting transfers between devices, shards(): stack = stack + lax.ppermute(outgoing, 'tmpl', pairs).astype(jnp.float32)  1.79 us
    reduce_sum x2, other arithmetic, normalize_rows(): scale = lax.rsqrt(jnp.mean(centred * centred, axis=-1, keepdims=True) + eps)  1.62 us
  transfers between devices with their start and end apart: 6, of which 2 were waited for; matrix products, arithmetic and copies ran while one was open for 25% of the time, Pallas kernels for 0%

profile of v13, /device:TPU:0, one launch (start us, length us, event | category | flops | bytes accessed | tf_op | source)
XLA Modules:
  0.0 60.8 jit_solution(7263184481394458628)
XLA Ops:
  0.0 0.0 copy-start
  0.0 1.1 %convert_reduce_fusion.1 = f32[32]{0:T(128)S(1)} fusion(bf16[32,1664]{1,0:T(8,128)(2,1)} %param.7), kind=kLoop, calls=%fused_computation.27 | loop fusion | flops 106464 | bytes 106624 | tf_op jit(solution)/shard_map/reduce_sum | solution.py:19
  1.1 1.1 %fusion.10 = f32[32]{0:T(128)S(1)} fusion(bf16[32,1664]{1,0:T(8,128)(2,1)} %param.7, f32[32]{0:T(128)S(1)} %broadcast_multiply_fusion.2), kind=kLoop, calls=%fused_computation.31 | loop fusion | flops 212960 | bytes 106752 | tf_op jit(solution)/shard_map/reduce_sum | solution.py:20
  2.2 1.0 %fusion.12 = bf16[1664,32]{0,1:T(8,128)(2,1)S(1)} fusion(bf16[32,1664]{1,0:T(8,128)(2,1)} %param.7, f32[32]{0:T(128)S(1)} %add_rsqrt_fusion.2, f32[32]{0:T(128)S(1)} %broadcast_multiply_fusion.2), kind=kLoop, calls=%fused_computation.33 | loop fusion | flops 212992 | bytes 213248 | tf_op jit(solution)/shard_map/transpose | solution.py:129
  3.2 0.3 copy.12
  3.5 0.0 copy-start.1
  3.5 0.3 reshape.175
  3.8 0.0 copy-done
  3.8 0.2 convert_reduce_fusion
  4.0 0.5 fusion.2
  4.6 0.0 copy-done.1
  4.6 0.5 convolution_convert_fusion
  5.1 0.0 copy-start.2
  5.2 0.1 pad_slice_fusion
  5.3 0.6 copy-done.2
  5.9 0.6 %select_reduce_fusion.1 = s32[32,32]{1,0:T(8,128)S(1)} fusion(s32[32,32]{1,0:T(8,128)S(1)} %copy-done.2, s32[32,32]{1,0:T(8,128)S(1)} %add_select_fusion), kind=kLoop, calls=%fused_computation.23 | loop fusion | flops 97280 | bytes 12288 | tf_op jit(solution)/shard_map/reduce_sum | solution.py:185
  6.5 1.3 %pad_select_fusion.7 = bf16[32,32,640]{2,1,0:T(8,128)(2,1)S(1)} fusion(bf16[32,32,639]{2,1,0:T(8,128)(2,1)S(1)} %pad_slice_fusion, pred[32,32]{1,0:T(8,128)(4,1)S(1)} %get-tuple-element.25, bf16[32,32,512]{2,1,0:T(8,128)(2,1)S(1)} %convolution_convert_fusion), kind=kLoop, calls=%fused_computation.18 | loop fusion | flops 655360 | bytes 3668992 | tf_op jit(solution)/shard_map/jit(_where)/select_n | solution.py:33
  7.8 1.3 %pad_select_fusion.6 = bf16[32,32,640]{2,1,0:T(8,128)(2,1)S(1)} fusion(bf16[32,32,640]{2,1,0:T(8,128)(2,1)S(1)} %pad_select_fusion.7, bf16[32,32,638]{2,1,0:T(8,128)(2,1)S(1)} %bitcast.38, pred[32,32]{1,0:T(8,128)(4,1)S(1)} %get-tuple-element.26), kind=kLoop, calls=%fused_computation.17 | loop fusion | flops 655360 | bytes 3929088 | tf_op jit(solution)/shard_map/jit(_where)/select_n | solution.py:33
  9.2 1.3 %pad_select_fusion.5 = bf16[32,32,640]{2,1,0:T(8,128)(2,1)S(1)} fusion(bf16[32,32,640]{2,1,0:T(8,128)(2,1)S(1)} %pad_select_fusion.6, bf16[32,32,636]{2,1,0:T(8,128)(2,1)S(1)} %bitcast.39, pred[32,32]{1,0:T(8,128)(4,1)S(1)} %get-tuple-element.27), kind=kLoop, calls=%fused_computation.16 | loop fusion | flops 655360 | bytes 3924992 | tf_op jit(solution)/shard_map/jit(_where)/select_n | solution.py:33
  10.5 1.3 %pad_select_fusion.4 = bf16[32,32,640]{2,1,0:T(8,128)(2,1)S(1)} fusion(bf16[32,32,640]{2,1,0:T(8,128)(2,1)S(1)} %pad_select_fusion.5, bf16[32,32,632]{2,1,0:T(8,128)(2,1)S(1)} %bitcast.40, pred[32,32]{1,0:T(8,128)(4,1)S(1)} %get-tuple-element.28), kind=kLoop, calls=%fused_computation.15 | loop fusion | flops 655360 | bytes 3916800 | tf_op jit(solution)/shard_map/jit(_where)/select_n | solution.py:33
  11.9 1.3 %pad_select_fusion.3 = bf16[32,32,640]{2,1,0:T(8,128)(2,1)S(1)} fusion(bf16[32,32,640]{2,1,0:T(8,128)(2,1)S(1)} %pad_select_fusion.4, bf16[32,32,624]{2,1,0:T(8,128)(2,1)S(1)} %bitcast.41, pred[32,32]{1,0:T(8,128)(4,1)S(1)} %get-tuple-element.29), kind=kLoop, calls=%fused_computation.14 | loop fusion | flops 655360 | bytes 3900416 | tf_op jit(solution)/shard_map/jit(_where)/select_n | solution.py:33
  13.2 1.3 %pad_select_fusion.2 = bf16[32,32,640]{2,1,0:T(8,128)(2,1)S(1)} fusion(bf16[32,32,640]{2,1,0:T(8,128)(2,1)S(1)} %pad_select_fusion.3, bf16[32,32,608]{2,1,0:T(8,128)(2,1)S(1)} %bitcast.42, pred[32,32]{1,0:T(8,128)(4,1)S(1)} %get-tuple-element.30), kind=kLoop, calls=%fused_computation.13 | loop fusion | flops 655360 | bytes 3867648 | tf_op jit(solution)/shard_map/jit(_where)/select_n | solution.py:33
  14.6 1.3 %pad_select_fusion.1 = bf16[32,32,640]{2,1,0:T(8,128)(2,1)S(1)} fusion(bf16[32,32,640]{2,1,0:T(8,128)(2,1)S(1)} %pad_select_fusion.2, bf16[32,32,576]{2,1,0:T(8,128)(2,1)S(1)} %bitcast.43, pred[32,32]{1,0:T(8,128)(4,1)S(1)} %get-tuple-element.31), kind=kLoop, calls=%fused_computation.12 | loop fusion | flops 655360 | bytes 3802112 | tf_op jit(solution)/shard_map/jit(_where)/select_n | solution.py:33
  15.9 0.1 slice.53
  16.1 0.6 pad_select_fusion
  16.6 5.1 %collective-permute-start.2 = (bf16[216,256]{1,0:T(8,128)(2,1)S(1)}, bf16[216,256]{1,0:T(8,128)(2,1)S(1)}, u32[]{:S(2)}, u32[]{:S(2)}) collective-permute-start(bf16[216,256]{1,0:T(8,128)(2,1)S(1)} %pad.17), channel_id=1, source_target_pairs={{0,12},{4,0},{8,4},{12,8},{1,13},{5,1},{9,5},{13,9},{2,14},{6,2},{... | collective-permute-start | bytes 331784 | tf_op jit(solution)/shard_map/ppermute | solution.py:194
  21.7 0.0 collective-permute-start.1
  21.7 1.0 %collective-permute-start = (bf16[216,256]{1,0:T(8,128)(2,1)S(1)}, bf16[216,256]{1,0:T(8,128)(2,1)S(1)}, u32[]{:S(2)}, u32[]{:S(2)}) collective-permute-start(bf16[216,256]{1,0:T(8,128)(2,1)S(1)} %pad.17), channel_id=1, source_target_pairs={{0,4},{4,8},{8,12},{12,0},{1,5},{5,9},{9,13},{13,1},{2,6},{6,10},{... | collective-permute-start | bytes 331784 | tf_op jit(solution)/shard_map/ppermute | solution.py:194
  22.8 0.1 slice_reduce_fusion
  22.9 0.7 %pad_bitcast_fusion = bf16[32,712,32]{1,2,0:T(8,128)(2,1)S(1)} fusion(bf16[32,32,640]{2,1,0:T(8,128)(2,1)S(1)} %pad_select_fusion), kind=kLoop, calls=%fused_computation.8 | loop fusion | bytes 2768896 | tf_op jit(solution)/shard_map/transpose | solution.py:143
  23.7 4.5 %copy.13 = bf16[32,712,32]{2,1,0:T(8,128)(2,1)} copy(bf16[32,712,32]{1,2,0:T(8,128)(2,1)S(1)} %pad_bitcast_fusion) | data formatting | bytes 2916352 | tf_op jit(solution)/shard_map/transpose | solution.py:143
  28.2 7.0 %reshape.176 = bf16[32,89,256]{2,1,0:T(8,128)(2,1)S(1)} reshape(bf16[32,712,32]{2,1,0:T(8,128)(2,1)} %copy.13) | data formatting | bytes 2916352 | tf_op jit(solution)/shard_map/reshape | solution.py:143
  35.2 0.0 copy-start.3
  35.2 1.9 %copy.19 = bf16[32,89,256]{2,0,1:T(8,128)(2,1)} copy(bf16[32,89,256]{2,1,0:T(8,128)(2,1)S(1)} %reshape.176) | data formatting | bytes 2916352 | tf_op jit(solution)/shard_map/reshape | solution.py:143
  37.1 0.0 copy-done.3
  37.1 0.7 %scatter_custom_fusion = s32[32]{0:T(128)S(1)} fusion(s32[32]{0:T(128)S(1)} %fusion.15, s32[32]{0:T(128)S(1)} %iota.14, s32[]{:T(128)} %constant.103.clone.1), kind=kCustom, calls=%fused_computation.71 | custom fusion | bytes 132 | tf_op jit(solution)/shard_map/scatter | solution.py:206
  37.8 0.1 broadcast_in_dim.111
  37.9 0.0 collective-permute-done.2
  37.9 0.0 collective-permute-done.1
  38.0 0.0 collective-permute-done
  38.0 1.0 %maximum_convert_fusion.signal_ref = f32[4,216,256]{2,1,0:T(8,128)} fusion(bf16[1,216,256]{2,1,0:T(8,128)(2,1)S(1)} %bitcast.51, bf16[1,216,256]{2,1,0:T(8,128)(2,1)S(1)} %bitcast.52, bf16[1,216,256]{2,1,0:T(8,128)(2,1)S(1)} %bitcast.53, bf16[1,216,256]{2,1,0:T(8,128)(2,1)S(1)} %bitcast.46), kind=kLoop, calls=%fused_computation.25 | loop fusion | flops 884736 | bytes 1327104 | tf_op jit(solution)/shard_map/convert_element_type | solution.py:145
  39.0 14.0 %shard_map.55 = f32[4,128,256]{2,1,0:T(8,128)} custom-call(bf16[89,32,256]{2,1,0:T(8,128)(2,1)} %bitcast.44, f32[4,216,256]{2,1,0:T(8,128)} %maximum_convert_fusion.signal_ref), custom_call_target="tpu_custom_call" | custom-call | tf_op jit(solution)/shard_map/pallas_call | solution.py:149
  53.0 1.1 %select_reduce_fusion = bf16[128,256]{1,0:T(8,128)(2,1)S(1)} fusion(f32[4,128,256]{2,1,0:T(8,128)} %shard_map.55, pred[4,256]{1,0:T(4,128)(4,1)S(1)} %broadcast_in_dim.111), kind=kLoop, calls=%fused_computation.22 | loop fusion | flops 229376 | bytes 590848 | tf_op jit(solution)/shard_map/reduce_sum | solution.py:202
  54.1 0.1 copy.15
  54.2 0.2 copy.16
  54.4 0.1 copy.17
  54.5 0.6 %gather_fusion = bf16[32,1024]{1,0:T(8,128)(2,1)S(1)} fusion(bf16[32,1024]{1,0:T(8,128)(2,1)S(1)} %copy.17, s32[1024]{0:T(1024)S(1)} %pad_clamp_fusion), kind=kCustom, calls=%fused_computation | custom fusion | bytes 131200 | tf_op jit(solution)/shard_map/gather | solution.py:208
  55.2 0.1 collective-permute-start.5
  55.3 1.5 %collective-permute-start.4 = (bf16[8,1024]{1,0:T(8,128)(2,1)S(1)}, bf16[8,1024]{1,0:T(8,128)(2,1)S(1)}, u32[]{:S(2)}, u32[]{:S(2)}) collective-permute-start(bf16[8,1024]{1,0:T(8,128)(2,1)S(1)} %get-tuple-element.23), channel_id=1, source_target_pairs={{0,2},{1,3},{2,0},{3,1},{4,6},{5,7},{6,4},{7,5},{8,10},{9,11},{10,... | collective-permute-start | bytes 49160 | tf_op jit(solution)/shard_map/ppermute | solution.py:215
  56.8 0.2 collective-permute-start.3
  57.0 0.0 collective-permute-done.5
  57.0 2.1 %collective-permute-done.4 = bf16[8,1024]{1,0:T(8,128)(2,1)S(1)} collective-permute-done((bf16[8,1024]{1,0:T(8,128)(2,1)S(1)}, bf16[8,1024]{1,0:T(8,128)(2,1)S(1)}, u32[]{:S(2)}, u32[]{:S(2)}) %collective-permute-start.4) | collective-permute-done | bytes 16416 | tf_op jit(solution)/shard_map/ppermute | solution.py:215
  59.0 0.9 %collective-permute-done.3 = bf16[8,1024]{1,0:T(8,128)(2,1)S(1)} collective-permute-done((bf16[8,1024]{1,0:T(8,128)(2,1)S(1)}, bf16[8,1024]{1,0:T(8,128)(2,1)S(1)}, u32[]{:S(2)}, u32[]{:S(2)}) %collective-permute-start.3) | collective-permute-done | bytes 16416 | tf_op jit(solution)/shard_map/ppermute | solution.py:215
  60.0 0.1 multiply_reduce_fusion
  60.1 0.7 %broadcast_multiply_fusion = f32[8,1024]{1,0:T(8,128)} fusion(f32[8]{0:T(128)S(1)} %add_rsqrt_fusion.1, bf16[8,1024]{1,0:T(8,128)(2,1)S(1)} %collective-permute-done.5, bf16[8,1024]{1,0:T(8,128)(2,1)S(1)} %collective-permute-done.4, bf16[8,1024]{1,0:T(8,128)(2,1)S(1)} %collective-permute-done.3, bf16[4,8,1024]{2,1,0:T(8,128)(2,1)S(1)} %bitcast.49, ...), kind=kLoop, calls=%fused_computation.43 | loop fusion | flops 73728 | bytes 98341 | tf_op jit(solution)/shard_map/mul | solution.py:220
  (15 shorter events, 0.2 us)
Async XLA Ops:
  0.0 3.8 %copy-start = (bf16[32,32,512]{2,1,0:T(8,128)(2,1)S(1)}, bf16[32,32,512]{2,1,0:T(8,128)(2,1)}, u32[]{:S(2)}) copy-start(bf16[32,32,512]{2,1,0:T(8,128)(2,1)} %param.8) | copy-start | bytes 3145732
  3.5 1.1 %copy-start.1 = (s32[32,32]{1,0:T(8,128)S(1)}, s32[32,32]{1,0:T(8,128)}, u32[]{:S(2)}) copy-start(s32[32,32]{1,0:T(8,128)} %param.9) | copy-start | bytes 12292
  5.1 0.7 %copy-start.2 = (s32[32,32]{1,0:T(8,128)S(1)}, s32[32,32]{1,0:T(8,128)}, u32[]{:S(2)}) copy-start(s32[32,32]{1,0:T(8,128)} %param.10) | copy-start | bytes 12292
  16.6 21.3 %collective-permute-start.2 = (bf16[216,256]{1,0:T(8,128)(2,1)S(1)}, bf16[216,256]{1,0:T(8,128)(2,1)S(1)}, u32[]{:S(2)}, u32[]{:S(2)}) collective-permute-start(bf16[216,256]{1,0:T(8,128)(2,1)S(1)} %pad.17), channel_id=1, source_target_pairs={{0,12},{4,0},{8,4},{12,8},{1,13},{5,1},{9,5},{13,9},{2,14},{6,2},{... | collective-permute-start | bytes 331784 | tf_op jit(solution)/shard_map/ppermute | solution.py:194
  21.7 16.2 %collective-permute-start.1 = (bf16[216,256]{1,0:T(8,128)(2,1)S(1)}, bf16[216,256]{1,0:T(8,128)(2,1)S(1)}, u32[]{:S(2)}, u32[]{:S(2)}) collective-permute-start(bf16[216,256]{1,0:T(8,128)(2,1)S(1)} %pad.17), channel_id=1, source_target_pairs={{0,8},{4,12},{8,0},{12,4},{1,9},{5,13},{9,1},{13,5},{2,10},{6,14},... | collective-permute-start | bytes 331784 | tf_op jit(solution)/shard_map/ppermute | solution.py:194
  21.7 16.2 %collective-permute-start = (bf16[216,256]{1,0:T(8,128)(2,1)S(1)}, bf16[216,256]{1,0:T(8,128)(2,1)S(1)}, u32[]{:S(2)}, u32[]{:S(2)}) collective-permute-start(bf16[216,256]{1,0:T(8,128)(2,1)S(1)} %pad.17), channel_id=1, source_target_pairs={{0,4},{4,8},{8,12},{12,0},{1,5},{5,9},{9,13},{13,1},{2,6},{6,10},{... | collective-permute-start | bytes 331784 | tf_op jit(solution)/shard_map/ppermute | solution.py:194
  35.2 2.0 %copy-start.3 = (s32[1,32]{1,0:T(1,128)S(1)}, s32[1,32]{1,0:T(1,128)}, u32[]{:S(2)}) copy-start(s32[1,32]{1,0:T(1,128)} %param.11) | copy-start | bytes 388
  55.2 1.8 %collective-permute-start.5 = (bf16[8,1024]{1,0:T(8,128)(2,1)S(1)}, bf16[8,1024]{1,0:T(8,128)(2,1)S(1)}, u32[]{:S(2)}, u32[]{:S(2)}) collective-permute-start(bf16[8,1024]{1,0:T(8,128)(2,1)S(1)} %get-tuple-element.22), channel_id=1, source_target_pairs={{0,3},{1,0},{2,1},{3,2},{4,7},{5,4},{6,5},{7,6},{8,11},{9,8},{10,9... | collective-permute-start | bytes 49160 | tf_op jit(solution)/shard_map/ppermute | solution.py:215
  55.3 3.7 %collective-permute-start.4 = (bf16[8,1024]{1,0:T(8,128)(2,1)S(1)}, bf16[8,1024]{1,0:T(8,128)(2,1)S(1)}, u32[]{:S(2)}, u32[]{:S(2)}) collective-permute-start(bf16[8,1024]{1,0:T(8,128)(2,1)S(1)} %get-tuple-element.23), channel_id=1, source_target_pairs={{0,2},{1,3},{2,0},{3,1},{4,6},{5,7},{6,4},{7,5},{8,10},{9,11},{10,... | collective-permute-start | bytes 49160 | tf_op jit(solution)/shard_map/ppermute | solution.py:215
  56.8 3.2 %collective-permute-start.3 = (bf16[8,1024]{1,0:T(8,128)(2,1)S(1)}, bf16[8,1024]{1,0:T(8,128)(2,1)S(1)}, u32[]{:S(2)}, u32[]{:S(2)}) collective-permute-start(bf16[8,1024]{1,0:T(8,128)(2,1)S(1)} %get-tuple-element.21), channel_id=1, source_target_pairs={{0,1},{1,2},{2,3},{3,0},{4,5},{5,6},{6,7},{7,4},{8,9},{9,10},{10,1... | collective-permute-start | bytes 49160 | tf_op jit(solution)/shard_map/ppermute | solution.py:215

commit v14 on v13

--- a/solution.py
+++ b/solution.py
@@ -69,7 +69,7 @@
     )(grouped)
 
 
-def _corr_kernel(grouped_ref, signal_ref, out_ref, acc_ref, filt_ref, *, steps, count, chans, phases, rows):
+def _corr_kernel(grouped_ref, signal_ref, mask_ref, out_ref, acc_ref, filt_ref, *, steps, count, chans, phases, rows):
     width = phases * chans
     pid = pl.program_id(0)
 
@@ -113,7 +113,11 @@
 
     @pl.when(pid == pl.num_programs(0) - 1)
     def _():
-        out_ref[...] = acc_ref[...].reshape(out_ref.shape)
+        def pick(g, carry):
+            start = pl.multiple_of(g * rows, rows)
+            return carry + acc_ref[pl.ds(start, rows), :] * mask_ref[g]
+
+        out_ref[...] = lax.fori_loop(0, n_blocks, pick, jnp.zeros(out_ref.shape, jnp.float32))
 
 
 CORR_STEPS = 8
@@ -130,7 +134,7 @@
     return jnp.pad(rows, ((0, total_rows - window // phases), (0, 0)))
 
 
-def correlate(placed, signal_rows, phases, lags):
+def correlate(placed, signal_rows, target, phases, lags):
     count, chans, padded_len = placed.shape
     n_blocks = signal_rows.shape[0]
     steps = CORR_STEPS
@@ -143,6 +147,8 @@
     grouped = jnp.transpose(padded, (0, 2, 1)).reshape(count, n_groups, width)
     grouped = jnp.transpose(grouped, (1, 0, 2))
     signal = signal_rows.astype(jnp.float32)
+    hit = target[None, :] == jnp.arange(n_blocks, dtype=jnp.int32)[:, None]
+    mask = jnp.tile(hit.astype(jnp.float32), (1, phases))[:, None, :]
     kernel = functools.partial(
         _corr_kernel, steps=steps, count=count, chans=chans, phases=phases, rows=rows
     )
@@ -152,14 +158,15 @@
         in_specs=[
             pl.BlockSpec(grouped.shape, lambda q: (0, 0, 0)),
             pl.BlockSpec(signal.shape, lambda q: (0, 0, 0)),
+            pl.BlockSpec(mask.shape, lambda q: (0, 0, 0)),
         ],
-        out_specs=pl.BlockSpec((n_blocks, rows, phases * count), lambda q: (0, 0, 0)),
-        out_shape=jax.ShapeDtypeStruct((n_blocks, rows, phases * count), jnp.float32),
+        out_specs=pl.BlockSpec((rows, phases * count), lambda q: (0, 0)),
+        out_shape=jax.ShapeDtypeStruct((rows, phases * count), jnp.float32),
         scratch_shapes=[
             pltpu.VMEM((n_blocks * rows, phases * count), jnp.float32),
             pltpu.VMEM((steps, phases * count, width), placed.dtype),
         ],
-    )(grouped, signal)
+    )(grouped, signal, mask)
 
 
 def shards(data, templates, stations, offsets, owner_map):
@@ -196,10 +203,8 @@
     else:
         blocks = lax.all_gather(signal, "chan", axis=0, tiled=False)
     n_blocks = blocks.shape[0]
-    corr = correlate(placed, blocks, phases, lags)
-    corr = corr.reshape(n_blocks, lags // phases, phases, count)
-    pick = target[None, :] == jnp.arange(n_blocks, dtype=jnp.int32)[:, None]
-    chosen = jnp.sum(jnp.where(pick[:, None, None, :], corr, 0.0), axis=0)
+    corr = correlate(placed, blocks, target, phases, lags)
+    chosen = corr.reshape(lags // phases, phases, count)
     partial_value = jnp.transpose(chosen, (2, 0, 1)).reshape(count, lags)
     partial_value = partial_value.astype(jnp.bfloat16)
     inverse = (

time: 61.2 us -> 61.6 us (level)
    reduce_sum x1 -> x0, other arithmetic: 1.08 us -> none  [shards(): chosen = jnp.sum(jnp.where(pick[:, None, None, :], corr, 0.0), axis=0)]
    convert_element_type x0 -> x2, other arithmetic: none -> 0.92 us  [the longest x1 0.91 us: shards(): partial_value = partial_value.astype(jnp.bfloat16)]
    another operation x0 -> x2, local copies, waits for them, and re-layouts: none -> 0.68 us  [correlate(): mask = jnp.tile(hit.astype(jnp.float32), (1, phases))[:, None, :]]
  transfers between devices with their start and end apart: 6 -> 6, of which waited for: 2 -> 2; matrix products, arithmetic and copies ran while one was open for 25% -> 26% of each run, Pallas kernels for 0% -> 0%
where the time goes in v14:
time: 61.6 us; the launch traced here: 61.2 us
  local copies, waits for them, and re-layouts  18.1 us (29%)
  other arithmetic  17.3 us (28%)
  Pallas kernels  14 us (23%)
  starting transfers between devices  7.91 us (13%)
  waiting for transfers between devices  3 us (5%)
    pallas_call x1, Pallas kernels, correlate(): pl.pallas_call(kernel, grid=(taps // steps,), in_specs=[pl.BlockSpec(grou...  14 us
    select_n x8, other arithmetic, place_moveout(): current = jnp.where(active[..., None], moved, current)  9.93 us
    reshape x2, local copies, waits for them, and re-layouts, correlate(): grouped = jnp.transpose(padded, (0, 2, 1)).reshape(count, n_groups, width)  8.94 us
    ppermute x3, starting transfers between devices, shards(): pieces.append(lax.ppermute(signal, 'chan', pairs))  6.12 us
    transpose x2, local copies, waits for them, and re-layouts, correlate(): grouped = jnp.transpose(padded, (0, 2, 1)).reshape(count, n_groups, width)  5.22 us
    ppermute x3, waiting for transfers between devices, shards(): stack = stack + lax.ppermute(outgoing, 'tmpl', pairs).astype(jnp.float32)  3 us
    ppermute x3, starting transfers between devices, shards(): stack = stack + lax.ppermute(outgoing, 'tmpl', pairs).astype(jnp.float32)  1.79 us
    reduce_sum x2, other arithmetic, normalize_rows(): scale = lax.rsqrt(jnp.mean(centred * centred, axis=-1, keepdims=True) + eps)  1.62 us
  transfers between devices with their start and end apart: 6, of which 2 were waited for; matrix products, arithmetic and copies ran while one was open for 26% of the time, Pallas kernels for 0%

profile of v14, /device:TPU:0, one launch (start us, length us, event | category | flops | bytes accessed | tf_op | source)
XLA Modules:
  0.0 61.2 jit_solution(2887579325792439640)
XLA Ops:
  0.0 0.0 copy-start
  0.0 1.1 %convert_reduce_fusion.1 = f32[32]{0:T(128)S(1)} fusion(bf16[32,1664]{1,0:T(8,128)(2,1)} %param.7), kind=kLoop, calls=%fused_computation.26 | loop fusion | flops 106464 | bytes 106624 | tf_op jit(solution)/shard_map/reduce_sum | solution.py:19
  1.1 1.1 %fusion.10 = f32[32]{0:T(128)S(1)} fusion(bf16[32,1664]{1,0:T(8,128)(2,1)} %param.7, f32[32]{0:T(128)S(1)} %broadcast_multiply_fusion.2), kind=kLoop, calls=%fused_computation.30 | loop fusion | flops 212960 | bytes 106752 | tf_op jit(solution)/shard_map/reduce_sum | solution.py:20
  2.2 1.0 %fusion.12 = bf16[1664,32]{0,1:T(8,128)(2,1)S(1)} fusion(bf16[32,1664]{1,0:T(8,128)(2,1)} %param.7, f32[32]{0:T(128)S(1)} %add_rsqrt_fusion.2, f32[32]{0:T(128)S(1)} %broadcast_multiply_fusion.2), kind=kLoop, calls=%fused_computation.32 | loop fusion | flops 212992 | bytes 213248 | tf_op jit(solution)/shard_map/transpose | solution.py:133
  3.2 0.3 copy.8
  3.5 0.0 copy-start.1
  3.5 0.3 reshape.182
  3.8 0.0 copy-done
  3.8 0.2 convert_reduce_fusion
  4.0 0.5 fusion.2
  4.6 0.0 copy-done.1
  4.6 0.5 convolution_convert_fusion
  5.1 0.0 copy-start.2
  5.2 0.1 pad_slice_fusion
  5.3 0.6 copy-done.2
  5.9 0.6 select_reduce_fusion
  6.5 1.3 %pad_select_fusion.7 = bf16[32,32,640]{2,1,0:T(8,128)(2,1)S(1)} fusion(bf16[32,32,639]{2,1,0:T(8,128)(2,1)S(1)} %pad_slice_fusion, pred[32,32]{1,0:T(8,128)(4,1)S(1)} %get-tuple-element.25, bf16[32,32,512]{2,1,0:T(8,128)(2,1)S(1)} %convolution_convert_fusion), kind=kLoop, calls=%fused_computation.18 | loop fusion | flops 655360 | bytes 3668992 | tf_op jit(solution)/shard_map/jit(_where)/select_n | solution.py:33
  7.8 1.3 %pad_select_fusion.6 = bf16[32,32,640]{2,1,0:T(8,128)(2,1)S(1)} fusion(bf16[32,32,640]{2,1,0:T(8,128)(2,1)S(1)} %pad_select_fusion.7, bf16[32,32,638]{2,1,0:T(8,128)(2,1)S(1)} %bitcast.38, pred[32,32]{1,0:T(8,128)(4,1)S(1)} %get-tuple-element.26), kind=kLoop, calls=%fused_computation.17 | loop fusion | flops 655360 | bytes 3929088 | tf_op jit(solution)/shard_map/jit(_where)/select_n | solution.py:33
  9.2 1.3 %pad_select_fusion.5 = bf16[32,32,640]{2,1,0:T(8,128)(2,1)S(1)} fusion(bf16[32,32,640]{2,1,0:T(8,128)(2,1)S(1)} %pad_select_fusion.6, bf16[32,32,636]{2,1,0:T(8,128)(2,1)S(1)} %bitcast.39, pred[32,32]{1,0:T(8,128)(4,1)S(1)} %get-tuple-element.27), kind=kLoop, calls=%fused_computation.16 | loop fusion | flops 655360 | bytes 3924992 | tf_op jit(solution)/shard_map/jit(_where)/select_n | solution.py:33
  10.5 1.3 %pad_select_fusion.4 = bf16[32,32,640]{2,1,0:T(8,128)(2,1)S(1)} fusion(bf16[32,32,640]{2,1,0:T(8,128)(2,1)S(1)} %pad_select_fusion.5, bf16[32,32,632]{2,1,0:T(8,128)(2,1)S(1)} %bitcast.40, pred[32,32]{1,0:T(8,128)(4,1)S(1)} %get-tuple-element.28), kind=kLoop, calls=%fused_computation.15 | loop fusion | flops 655360 | bytes 3916800 | tf_op jit(solution)/shard_map/jit(_where)/select_n | solution.py:33
  11.9 1.3 %pad_select_fusion.3 = bf16[32,32,640]{2,1,0:T(8,128)(2,1)S(1)} fusion(bf16[32,32,640]{2,1,0:T(8,128)(2,1)S(1)} %pad_select_fusion.4, bf16[32,32,624]{2,1,0:T(8,128)(2,1)S(1)} %bitcast.41, pred[32,32]{1,0:T(8,128)(4,1)S(1)} %get-tuple-element.29), kind=kLoop, calls=%fused_computation.14 | loop fusion | flops 655360 | bytes 3900416 | tf_op jit(solution)/shard_map/jit(_where)/select_n | solution.py:33
  13.2 1.3 %pad_select_fusion.2 = bf16[32,32,640]{2,1,0:T(8,128)(2,1)S(1)} fusion(bf16[32,32,640]{2,1,0:T(8,128)(2,1)S(1)} %pad_select_fusion.3, bf16[32,32,608]{2,1,0:T(8,128)(2,1)S(1)} %bitcast.42, pred[32,32]{1,0:T(8,128)(4,1)S(1)} %get-tuple-element.30), kind=kLoop, calls=%fused_computation.13 | loop fusion | flops 655360 | bytes 3867648 | tf_op jit(solution)/shard_map/jit(_where)/select_n | solution.py:33
  14.6 1.3 %pad_select_fusion.1 = bf16[32,32,640]{2,1,0:T(8,128)(2,1)S(1)} fusion(bf16[32,32,640]{2,1,0:T(8,128)(2,1)S(1)} %pad_select_fusion.2, bf16[32,32,576]{2,1,0:T(8,128)(2,1)S(1)} %bitcast.43, pred[32,32]{1,0:T(8,128)(4,1)S(1)} %get-tuple-element.31), kind=kLoop, calls=%fused_computation.12 | loop fusion | flops 655360 | bytes 3802112 | tf_op jit(solution)/shard_map/jit(_where)/select_n | solution.py:33
  15.9 0.1 slice.53
  16.1 0.6 pad_select_fusion
  16.6 5.1 %collective-permute-start.2 = (bf16[216,256]{1,0:T(8,128)(2,1)S(1)}, bf16[216,256]{1,0:T(8,128)(2,1)S(1)}, u32[]{:S(2)}, u32[]{:S(2)}) collective-permute-start(bf16[216,256]{1,0:T(8,128)(2,1)S(1)} %pad.17), channel_id=1, source_target_pairs={{0,12},{4,0},{8,4},{12,8},{1,13},{5,1},{9,5},{13,9},{2,14},{6,2},{... | collective-permute-start | bytes 331784 | tf_op jit(solution)/shard_map/ppermute | solution.py:201
  21.7 0.0 collective-permute-start.1
  21.7 1.0 %collective-permute-start = (bf16[216,256]{1,0:T(8,128)(2,1)S(1)}, bf16[216,256]{1,0:T(8,128)(2,1)S(1)}, u32[]{:S(2)}, u32[]{:S(2)}) collective-permute-start(bf16[216,256]{1,0:T(8,128)(2,1)S(1)} %pad.17), channel_id=1, source_target_pairs={{0,4},{4,8},{8,12},{12,0},{1,5},{5,9},{9,13},{13,1},{2,6},{6,10},{... | collective-permute-start | bytes 331784 | tf_op jit(solution)/shard_map/ppermute | solution.py:201
  22.8 0.1 slice_reduce_fusion
  22.9 0.7 %pad_bitcast_fusion = bf16[32,712,32]{1,2,0:T(8,128)(2,1)S(1)} fusion(bf16[32,32,640]{2,1,0:T(8,128)(2,1)S(1)} %pad_select_fusion), kind=kLoop, calls=%fused_computation.8 | loop fusion | bytes 2768896 | tf_op jit(solution)/shard_map/transpose | solution.py:147
  23.7 4.5 %copy.9 = bf16[32,712,32]{2,1,0:T(8,128)(2,1)} copy(bf16[32,712,32]{1,2,0:T(8,128)(2,1)S(1)} %pad_bitcast_fusion) | data formatting | bytes 2916352 | tf_op jit(solution)/shard_map/transpose | solution.py:147
  28.2 7.0 %reshape.183 = bf16[32,89,256]{2,1,0:T(8,128)(2,1)S(1)} reshape(bf16[32,712,32]{2,1,0:T(8,128)(2,1)} %copy.9) | data formatting | bytes 2916352 | tf_op jit(solution)/shard_map/reshape | solution.py:147
  35.2 0.0 copy-start.3
  35.2 1.9 %copy.15 = bf16[32,89,256]{2,0,1:T(8,128)(2,1)} copy(bf16[32,89,256]{2,1,0:T(8,128)(2,1)S(1)} %reshape.183) | data formatting | bytes 2916352 | tf_op jit(solution)/shard_map/reshape | solution.py:147
  37.1 0.0 copy-done.3
  37.1 0.7 %scatter_custom_fusion = s32[32]{0:T(128)S(1)} fusion(s32[32]{0:T(128)S(1)} %fusion.16, s32[32]{0:T(128)S(1)} %iota.14, s32[]{:T(128)} %constant.104.clone.1), kind=kCustom, calls=%fused_computation.70 | custom fusion | bytes 132 | tf_op jit(solution)/shard_map/scatter | solution.py:211
  37.8 0.7 %tile.9.mask_ref = f32[4,1,256]{2,1,0:T(1,128)} reshape(f32[4,8,32]{2,1,0:T(8,128)S(1)} %tile.8) | data formatting | bytes 8192 | tf_op jit(solution)/shard_map/tile | solution.py:151
  38.5 0.0 collective-permute-done.2
  38.5 0.0 collective-permute-done.1
  38.5 0.0 collective-permute-done
  38.5 1.0 %maximum_convert_fusion.signal_ref = f32[4,216,256]{2,1,0:T(8,128)} fusion(bf16[1,216,256]{2,1,0:T(8,128)(2,1)S(1)} %bitcast.51, bf16[1,216,256]{2,1,0:T(8,128)(2,1)S(1)} %bitcast.52, bf16[1,216,256]{2,1,0:T(8,128)(2,1)S(1)} %bitcast.53, bf16[1,216,256]{2,1,0:T(8,128)(2,1)S(1)} %bitcast.46), kind=kLoop, calls=%fused_computation.24 | loop fusion | flops 884736 | bytes 1327104 | tf_op jit(solution)/shard_map/convert_element_type | solution.py:149
  39.5 14.0 %shard_map.55 = f32[128,256]{1,0:T(8,128)} custom-call(bf16[89,32,256]{2,1,0:T(8,128)(2,1)} %bitcast.44, f32[4,216,256]{2,1,0:T(8,128)} %maximum_convert_fusion.signal_ref, f32[4,1,256]{2,1,0:T(1,128)} %tile.9.mask_ref), custom_call_target="tpu_custom_call" | custom-call | tf_op jit(solution)/shard_map/pallas_call | solution.py:155
  53.5 0.9 %convert_element_type.61 = bf16[128,256]{1,0:T(8,128)(2,1)S(1)} convert(f32[128,256]{1,0:T(8,128)} %shard_map.55) | non-fusion elementwise | flops 32768 | bytes 196608 | tf_op jit(solution)/shard_map/convert_element_type | solution.py:209
  54.4 0.1 copy.11
  54.5 0.2 copy.12
  54.7 0.1 copy.13
  54.9 0.6 %gather_fusion = bf16[32,1024]{1,0:T(8,128)(2,1)S(1)} fusion(bf16[32,1024]{1,0:T(8,128)(2,1)S(1)} %copy.13, s32[1024]{0:T(1024)S(1)} %pad_clamp_fusion), kind=kCustom, calls=%fused_computation | custom fusion | bytes 131200 | tf_op jit(solution)/shard_map/gather | solution.py:213
  55.5 0.1 collective-permute-start.5
  55.7 1.5 %collective-permute-start.4 = (bf16[8,1024]{1,0:T(8,128)(2,1)S(1)}, bf16[8,1024]{1,0:T(8,128)(2,1)S(1)}, u32[]{:S(2)}, u32[]{:S(2)}) collective-permute-start(bf16[8,1024]{1,0:T(8,128)(2,1)S(1)} %get-tuple-element.23), channel_id=1, source_target_pairs={{0,2},{1,3},{2,0},{3,1},{4,6},{5,7},{6,4},{7,5},{8,10},{9,11},{10,... | collective-permute-start | bytes 49160 | tf_op jit(solution)/shard_map/ppermute | solution.py:220
  57.2 0.2 collective-permute-start.3
  57.3 0.0 collective-permute-done.5
  57.3 2.1 %collective-permute-done.4 = bf16[8,1024]{1,0:T(8,128)(2,1)S(1)} collective-permute-done((bf16[8,1024]{1,0:T(8,128)(2,1)S(1)}, bf16[8,1024]{1,0:T(8,128)(2,1)S(1)}, u32[]{:S(2)}, u32[]{:S(2)}) %collective-permute-start.4) | collective-permute-done | bytes 16416 | tf_op jit(solution)/shard_map/ppermute | solution.py:220
  59.4 0.9 %collective-permute-done.3 = bf16[8,1024]{1,0:T(8,128)(2,1)S(1)} collective-permute-done((bf16[8,1024]{1,0:T(8,128)(2,1)S(1)}, bf16[8,1024]{1,0:T(8,128)(2,1)S(1)}, u32[]{:S(2)}, u32[]{:S(2)}) %collective-permute-start.3) | collective-permute-done | bytes 16416 | tf_op jit(solution)/shard_map/ppermute | solution.py:220
  60.3 0.1 multiply_reduce_fusion
  60.5 0.7 %broadcast_multiply_fusion = f32[8,1024]{1,0:T(8,128)} fusion(f32[8]{0:T(128)S(1)} %add_rsqrt_fusion.1, bf16[8,1024]{1,0:T(8,128)(2,1)S(1)} %collective-permute-done.5, bf16[8,1024]{1,0:T(8,128)(2,1)S(1)} %collective-permute-done.4, bf16[8,1024]{1,0:T(8,128)(2,1)S(1)} %collective-permute-done.3, bf16[4,8,1024]{2,1,0:T(8,128)(2,1)S(1)} %bitcast.49, ...), kind=kLoop, calls=%fused_computation.42 | loop fusion | flops 73728 | bytes 98341 | tf_op jit(solution)/shard_map/mul | solution.py:225
  (15 shorter events, 0.1 us)
Async XLA Ops:
  0.0 3.8 %copy-start = (bf16[32,32,512]{2,1,0:T(8,128)(2,1)S(1)}, bf16[32,32,512]{2,1,0:T(8,128)(2,1)}, u32[]{:S(2)}) copy-start(bf16[32,32,512]{2,1,0:T(8,128)(2,1)} %param.8) | copy-start | bytes 3145732
  3.5 1.1 %copy-start.1 = (s32[32,32]{1,0:T(8,128)S(1)}, s32[32,32]{1,0:T(8,128)}, u32[]{:S(2)}) copy-start(s32[32,32]{1,0:T(8,128)} %param.9) | copy-start | bytes 12292
  5.1 0.7 %copy-start.2 = (s32[32,32]{1,0:T(8,128)S(1)}, s32[32,32]{1,0:T(8,128)}, u32[]{:S(2)}) copy-start(s32[32,32]{1,0:T(8,128)} %param.10) | copy-start | bytes 12292
  16.6 21.9 %collective-permute-start.2 = (bf16[216,256]{1,0:T(8,128)(2,1)S(1)}, bf16[216,256]{1,0:T(8,128)(2,1)S(1)}, u32[]{:S(2)}, u32[]{:S(2)}) collective-permute-start(bf16[216,256]{1,0:T(8,128)(2,1)S(1)} %pad.17), channel_id=1, source_target_pairs={{0,12},{4,0},{8,4},{12,8},{1,13},{5,1},{9,5},{13,9},{2,14},{6,2},{... | collective-permute-start | bytes 331784 | tf_op jit(solution)/shard_map/ppermute | solution.py:201
  21.7 16.8 %collective-permute-start.1 = (bf16[216,256]{1,0:T(8,128)(2,1)S(1)}, bf16[216,256]{1,0:T(8,128)(2,1)S(1)}, u32[]{:S(2)}, u32[]{:S(2)}) collective-permute-start(bf16[216,256]{1,0:T(8,128)(2,1)S(1)} %pad.17), channel_id=1, source_target_pairs={{0,8},{4,12},{8,0},{12,4},{1,9},{5,13},{9,1},{13,5},{2,10},{6,14},... | collective-permute-start | bytes 331784 | tf_op jit(solution)/shard_map/ppermute | solution.py:201
  21.7 16.8 %collective-permute-start = (bf16[216,256]{1,0:T(8,128)(2,1)S(1)}, bf16[216,256]{1,0:T(8,128)(2,1)S(1)}, u32[]{:S(2)}, u32[]{:S(2)}) collective-permute-start(bf16[216,256]{1,0:T(8,128)(2,1)S(1)} %pad.17), channel_id=1, source_target_pairs={{0,4},{4,8},{8,12},{12,0},{1,5},{5,9},{9,13},{13,1},{2,6},{6,10},{... | collective-permute-start | bytes 331784 | tf_op jit(solution)/shard_map/ppermute | solution.py:201
  35.2 2.0 %copy-start.3 = (s32[1,32]{1,0:T(1,128)S(1)}, s32[1,32]{1,0:T(1,128)}, u32[]{:S(2)}) copy-start(s32[1,32]{1,0:T(1,128)} %param.11) | copy-start | bytes 388
  55.5 1.8 %collective-permute-start.5 = (bf16[8,1024]{1,0:T(8,128)(2,1)S(1)}, bf16[8,1024]{1,0:T(8,128)(2,1)S(1)}, u32[]{:S(2)}, u32[]{:S(2)}) collective-permute-start(bf16[8,1024]{1,0:T(8,128)(2,1)S(1)} %get-tuple-element.22), channel_id=1, source_target_pairs={{0,3},{1,0},{2,1},{3,2},{4,7},{5,4},{6,5},{7,6},{8,11},{9,8},{10,9... | collective-permute-start | bytes 49160 | tf_op jit(solution)/shard_map/ppermute | solution.py:220
  55.7 3.7 %collective-permute-start.4 = (bf16[8,1024]{1,0:T(8,128)(2,1)S(1)}, bf16[8,1024]{1,0:T(8,128)(2,1)S(1)}, u32[]{:S(2)}, u32[]{:S(2)}) collective-permute-start(bf16[8,1024]{1,0:T(8,128)(2,1)S(1)} %get-tuple-element.23), channel_id=1, source_target_pairs={{0,2},{1,3},{2,0},{3,1},{4,6},{5,7},{6,4},{7,5},{8,10},{9,11},{10,... | collective-permute-start | bytes 49160 | tf_op jit(solution)/shard_map/ppermute | solution.py:220
  57.2 3.2 %collective-permute-start.3 = (bf16[8,1024]{1,0:T(8,128)(2,1)S(1)}, bf16[8,1024]{1,0:T(8,128)(2,1)S(1)}, u32[]{:S(2)}, u32[]{:S(2)}) collective-permute-start(bf16[8,1024]{1,0:T(8,128)(2,1)S(1)} %get-tuple-element.21), channel_id=1, source_target_pairs={{0,1},{1,2},{2,3},{3,0},{4,5},{5,6},{6,7},{7,4},{8,9},{9,10},{10,1... | collective-permute-start | bytes 49160 | tf_op jit(solution)/shard_map/ppermute | solution.py:220

commit v15 on v13

--- a/solution.py
+++ b/solution.py
@@ -69,7 +69,7 @@
     )(grouped)
 
 
-def _corr_kernel(grouped_ref, signal_ref, out_ref, acc_ref, filt_ref, *, steps, count, chans, phases, rows):
+def _corr_kernel(grouped_ref, signal_ref, out_ref, acc_ref, filt_ref, *, steps, extra_taps, count, chans, phases, rows):
     width = phases * chans
     pid = pl.program_id(0)
 
@@ -113,6 +113,27 @@
 
     @pl.when(pid == pl.num_programs(0) - 1)
     def _():
+        for extra in range(extra_taps):
+            q = (pid + 1) * steps + extra
+            joined = jnp.concatenate([grouped_ref[q], grouped_ref[q + 1]], axis=-1)
+            joined = joined.astype(jnp.float32)
+            parts = []
+            for e in range(phases):
+                cut = (phases - 1 - e) * chans
+                moved = pltpu.roll(joined, 2 * width - cut, 1) if cut else joined
+                parts.append(moved[:, :width])
+            filt = jnp.transpose(jnp.concatenate(parts, axis=0)).astype(filt_ref.dtype)
+            start = pl.multiple_of((pid + 1) * steps, steps)
+
+            def tail(g, carry):
+                window = signal_ref[g, pl.ds(start, rows + steps), :][extra : extra + rows]
+                lo = pl.multiple_of(g * rows, rows)
+                acc_ref[pl.ds(lo, rows), :] += jnp.dot(
+                    window.astype(filt.dtype), filt, preferred_element_type=jnp.float32
+                )
+                return carry
+
+            lax.fori_loop(0, n_blocks, tail, 0)
         out_ref[...] = acc_ref[...].reshape(out_ref.shape)
 
 
@@ -121,7 +142,8 @@
 
 def corr_taps(padded_len, phases):
     taps = padded_len // phases + 1
-    return taps, -(-taps // CORR_STEPS) * CORR_STEPS
+    main = taps // CORR_STEPS * CORR_STEPS
+    return taps - main, main + CORR_STEPS
 
 
 def polyphase_rows(signal, phases, total_rows):
@@ -134,9 +156,10 @@
     count, chans, padded_len = placed.shape
     n_blocks = signal_rows.shape[0]
     steps = CORR_STEPS
-    _, taps = corr_taps(padded_len, phases)
+    extra_taps, span = corr_taps(padded_len, phases)
+    taps = span - steps
     front = phases - 1
-    n_groups = taps + 1
+    n_groups = taps + extra_taps + 1
     rows = lags // phases
     width = phases * chans
     padded = jnp.pad(placed, ((0, 0), (0, 0), (front, n_groups * phases - padded_len - front)))
@@ -144,7 +167,8 @@
     grouped = jnp.transpose(grouped, (1, 0, 2))
     signal = signal_rows.astype(jnp.float32)
     kernel = functools.partial(
-        _corr_kernel, steps=steps, count=count, chans=chans, phases=phases, rows=rows
+        _corr_kernel, steps=steps, extra_taps=extra_taps, count=count, chans=chans,
+        phases=phases, rows=rows,
     )
     return pl.pallas_call(
         kernel,
@@ -184,8 +208,8 @@
     ).astype(jnp.bfloat16)
     ordered_shift = jnp.sum(jnp.where(hit, offsets[:, :, None], 0), axis=1)
     placed = place_moveout(ordered, ordered_shift, padded_len)
-    _, taps = corr_taps(padded_len, phases)
-    signal = polyphase_rows(signal, phases, taps + lags // phases)
+    _, span = corr_taps(padded_len, phases)
+    signal = polyphase_rows(signal, phases, span + lags // phases)
     signal, placed = lax.optimization_barrier((signal, placed))
     if n_chan <= 8:
         pieces = [signal]

time: 61.2 us -> 60.1 us (0.982)
  local copies, waits for them, and re-layouts: 17.5 us -> 16.6 us
    reshape x2, local copies, waits for them, and re-layouts: 8.94 us -> 8.25 us  [correlate(): grouped = jnp.transpose(padded, (0, 2, 1)).reshape(count, n_groups, width)]
  transfers between devices with their start and end apart: 6 -> 6, of which waited for: 2 -> 2; matrix products, arithmetic and copies ran while one was open for 25% -> 24% of each run, Pallas kernels for 0% -> 0%
where the time goes in v15:
time: 60.1 us; the launch traced here: 59.7 us
  other arithmetic  17.6 us (29%)
  local copies, waits for them, and re-layouts  16.6 us (28%)
  Pallas kernels  13.8 us (23%)
  starting transfers between devices  7.89 us (13%)
  waiting for transfers between devices  3 us (5%)
    pallas_call x1, Pallas kernels, correlate(): pl.pallas_call(kernel, grid=(taps // steps,), in_specs=[pl.BlockSpec(grou...  13.8 us
    select_n x8, other arithmetic, place_moveout(): current = jnp.where(active[..., None], moved, current)  9.93 us
    reshape x2, local copies, waits for them, and re-layouts, correlate(): grouped = jnp.transpose(padded, (0, 2, 1)).reshape(count, n_groups, width)  8.25 us
    ppermute x3, starting transfers between devices, shards(): pieces.append(lax.ppermute(signal, 'chan', pairs))  6.12 us
    transpose x2, local copies, waits for them, and re-layouts, correlate(): grouped = jnp.transpose(padded, (0, 2, 1)).reshape(count, n_groups, width)  5.01 us
    ppermute x3, waiting for transfers between devices, shards(): stack = stack + lax.ppermute(outgoing, 'tmpl', pairs).astype(jnp.float32)  3 us
    ppermute x3, starting transfers between devices, shards(): stack = stack + lax.ppermute(outgoing, 'tmpl', pairs).astype(jnp.float32)  1.78 us
    reduce_sum x2, other arithmetic, normalize_rows(): scale = lax.rsqrt(jnp.mean(centred * centred, axis=-1, keepdims=True) + eps)  1.62 us
  transfers between devices with their start and end apart: 6, of which 2 were waited for; matrix products, arithmetic and copies ran while one was open for 24% of the time, Pallas kernels for 0%

profile of v15, /device:TPU:0, one launch (start us, length us, event | category | flops | bytes accessed | tf_op | source)
XLA Modules:
  0.0 59.7 jit_solution(2909862528608945782)
XLA Ops:
  0.0 0.0 copy-start
  0.0 1.1 %convert_reduce_fusion.1 = f32[32]{0:T(128)S(1)} fusion(bf16[32,1664]{1,0:T(8,128)(2,1)} %param.7), kind=kLoop, calls=%fused_computation.27 | loop fusion | flops 106464 | bytes 106624 | tf_op jit(solution)/shard_map/reduce_sum | solution.py:19
  1.1 1.1 %fusion.10 = f32[32]{0:T(128)S(1)} fusion(bf16[32,1664]{1,0:T(8,128)(2,1)} %param.7, f32[32]{0:T(128)S(1)} %broadcast_multiply_fusion.2), kind=kLoop, calls=%fused_computation.31 | loop fusion | flops 212960 | bytes 106752 | tf_op jit(solution)/shard_map/reduce_sum | solution.py:20
  2.2 1.0 %fusion.12 = bf16[1664,32]{0,1:T(8,128)(2,1)S(1)} fusion(bf16[32,1664]{1,0:T(8,128)(2,1)} %param.7, f32[32]{0:T(128)S(1)} %add_rsqrt_fusion.2, f32[32]{0:T(128)S(1)} %broadcast_multiply_fusion.2), kind=kLoop, calls=%fused_computation.33 | loop fusion | flops 212992 | bytes 213248 | tf_op jit(solution)/shard_map/transpose | solution.py:151
  3.2 0.3 copy.12
  3.5 0.0 copy-start.1
  3.5 0.3 reshape.175
  3.8 0.0 copy-done
  3.8 0.2 convert_reduce_fusion
  4.0 0.5 fusion.2
  4.6 0.0 copy-done.1
  4.6 0.5 convolution_convert_fusion
  5.1 0.0 copy-start.2
  5.2 0.1 pad_slice_fusion
  5.3 0.6 copy-done.2
  5.9 0.6 %select_reduce_fusion.1 = s32[32,32]{1,0:T(8,128)S(1)} fusion(s32[32,32]{1,0:T(8,128)S(1)} %copy-done.2, s32[32,32]{1,0:T(8,128)S(1)} %add_select_fusion), kind=kLoop, calls=%fused_computation.23 | loop fusion | flops 97280 | bytes 12288 | tf_op jit(solution)/shard_map/reduce_sum | solution.py:209
  6.5 1.3 %pad_select_fusion.7 = bf16[32,32,640]{2,1,0:T(8,128)(2,1)S(1)} fusion(bf16[32,32,639]{2,1,0:T(8,128)(2,1)S(1)} %pad_slice_fusion, pred[32,32]{1,0:T(8,128)(4,1)S(1)} %get-tuple-element.25, bf16[32,32,512]{2,1,0:T(8,128)(2,1)S(1)} %convolution_convert_fusion), kind=kLoop, calls=%fused_computation.18 | loop fusion | flops 655360 | bytes 3668992 | tf_op jit(solution)/shard_map/jit(_where)/select_n | solution.py:33
  7.8 1.3 %pad_select_fusion.6 = bf16[32,32,640]{2,1,0:T(8,128)(2,1)S(1)} fusion(bf16[32,32,640]{2,1,0:T(8,128)(2,1)S(1)} %pad_select_fusion.7, bf16[32,32,638]{2,1,0:T(8,128)(2,1)S(1)} %bitcast.38, pred[32,32]{1,0:T(8,128)(4,1)S(1)} %get-tuple-element.26), kind=kLoop, calls=%fused_computation.17 | loop fusion | flops 655360 | bytes 3929088 | tf_op jit(solution)/shard_map/jit(_where)/select_n | solution.py:33
  9.2 1.3 %pad_select_fusion.5 = bf16[32,32,640]{2,1,0:T(8,128)(2,1)S(1)} fusion(bf16[32,32,640]{2,1,0:T(8,128)(2,1)S(1)} %pad_select_fusion.6, bf16[32,32,636]{2,1,0:T(8,128)(2,1)S(1)} %bitcast.39, pred[32,32]{1,0:T(8,128)(4,1)S(1)} %get-tuple-element.27), kind=kLoop, calls=%fused_computation.16 | loop fusion | flops 655360 | bytes 3924992 | tf_op jit(solution)/shard_map/jit(_where)/select_n | solution.py:33
  10.5 1.3 %pad_select_fusion.4 = bf16[32,32,640]{2,1,0:T(8,128)(2,1)S(1)} fusion(bf16[32,32,640]{2,1,0:T(8,128)(2,1)S(1)} %pad_select_fusion.5, bf16[32,32,632]{2,1,0:T(8,128)(2,1)S(1)} %bitcast.40, pred[32,32]{1,0:T(8,128)(4,1)S(1)} %get-tuple-element.28), kind=kLoop, calls=%fused_computation.15 | loop fusion | flops 655360 | bytes 3916800 | tf_op jit(solution)/shard_map/jit(_where)/select_n | solution.py:33
  11.9 1.3 %pad_select_fusion.3 = bf16[32,32,640]{2,1,0:T(8,128)(2,1)S(1)} fusion(bf16[32,32,640]{2,1,0:T(8,128)(2,1)S(1)} %pad_select_fusion.4, bf16[32,32,624]{2,1,0:T(8,128)(2,1)S(1)} %bitcast.41, pred[32,32]{1,0:T(8,128)(4,1)S(1)} %get-tuple-element.29), kind=kLoop, calls=%fused_computation.14 | loop fusion | flops 655360 | bytes 3900416 | tf_op jit(solution)/shard_map/jit(_where)/select_n | solution.py:33
  13.2 1.3 %pad_select_fusion.2 = bf16[32,32,640]{2,1,0:T(8,128)(2,1)S(1)} fusion(bf16[32,32,640]{2,1,0:T(8,128)(2,1)S(1)} %pad_select_fusion.3, bf16[32,32,608]{2,1,0:T(8,128)(2,1)S(1)} %bitcast.42, pred[32,32]{1,0:T(8,128)(4,1)S(1)} %get-tuple-element.30), kind=kLoop, calls=%fused_computation.13 | loop fusion | flops 655360 | bytes 3867648 | tf_op jit(solution)/shard_map/jit(_where)/select_n | solution.py:33
  14.6 1.3 %pad_select_fusion.1 = bf16[32,32,640]{2,1,0:T(8,128)(2,1)S(1)} fusion(bf16[32,32,640]{2,1,0:T(8,128)(2,1)S(1)} %pad_select_fusion.2, bf16[32,32,576]{2,1,0:T(8,128)(2,1)S(1)} %bitcast.43, pred[32,32]{1,0:T(8,128)(4,1)S(1)} %get-tuple-element.31), kind=kLoop, calls=%fused_computation.12 | loop fusion | flops 655360 | bytes 3802112 | tf_op jit(solution)/shard_map/jit(_where)/select_n | solution.py:33
  15.9 0.1 slice.53
  16.1 0.6 pad_select_fusion
  16.6 5.1 %collective-permute-start.2 = (bf16[216,256]{1,0:T(8,128)(2,1)S(1)}, bf16[216,256]{1,0:T(8,128)(2,1)S(1)}, u32[]{:S(2)}, u32[]{:S(2)}) collective-permute-start(bf16[216,256]{1,0:T(8,128)(2,1)S(1)} %pad.17), channel_id=1, source_target_pairs={{0,12},{4,0},{8,4},{12,8},{1,13},{5,1},{9,5},{13,9},{2,14},{6,2},{... | collective-permute-start | bytes 331784 | tf_op jit(solution)/shard_map/ppermute | solution.py:218
  21.7 0.0 collective-permute-start.1
  21.7 1.0 %collective-permute-start = (bf16[216,256]{1,0:T(8,128)(2,1)S(1)}, bf16[216,256]{1,0:T(8,128)(2,1)S(1)}, u32[]{:S(2)}, u32[]{:S(2)}) collective-permute-start(bf16[216,256]{1,0:T(8,128)(2,1)S(1)} %pad.17), channel_id=1, source_target_pairs={{0,4},{4,8},{8,12},{12,0},{1,5},{5,9},{9,13},{13,1},{2,6},{6,10},{... | collective-permute-start | bytes 331784 | tf_op jit(solution)/shard_map/ppermute | solution.py:218
  22.8 0.1 slice_reduce_fusion
  22.9 0.7 %pad_bitcast_fusion = bf16[32,656,32]{1,2,0:T(8,128)(2,1)S(1)} fusion(bf16[32,32,640]{2,1,0:T(8,128)(2,1)S(1)} %pad_select_fusion), kind=kLoop, calls=%fused_computation.8 | loop fusion | bytes 2654208 | tf_op jit(solution)/shard_map/transpose | solution.py:166
  23.7 4.3 %copy.13 = bf16[32,656,32]{2,1,0:T(8,128)(2,1)} copy(bf16[32,656,32]{1,2,0:T(8,128)(2,1)S(1)} %pad_bitcast_fusion) | data formatting | bytes 2686976 | tf_op jit(solution)/shard_map/transpose | solution.py:166
  27.9 6.9 %reshape.176 = bf16[32,82,256]{2,1,0:T(8,128)(2,1)S(1)} reshape(bf16[32,656,32]{2,1,0:T(8,128)(2,1)} %copy.13) | data formatting | bytes 2686976 | tf_op jit(solution)/shard_map/reshape | solution.py:166
  34.8 0.0 copy-start.3
  34.8 1.4 %copy.19 = bf16[32,82,256]{2,0,1:T(8,128)(2,1)} copy(bf16[32,82,256]{2,1,0:T(8,128)(2,1)S(1)} %reshape.176) | data formatting | bytes 2686976 | tf_op jit(solution)/shard_map/reshape | solution.py:166
  36.2 0.0 copy-done.3
  36.2 0.7 %scatter_custom_fusion = s32[32]{0:T(128)S(1)} fusion(s32[32]{0:T(128)S(1)} %fusion.15, s32[32]{0:T(128)S(1)} %iota.14, s32[]{:T(128)} %constant.103.clone.1), kind=kCustom, calls=%fused_computation.71 | custom fusion | bytes 132 | tf_op jit(solution)/shard_map/scatter | solution.py:230
  36.9 0.1 broadcast_in_dim.111
  37.0 0.0 collective-permute-done.2
  37.1 0.0 collective-permute-done.1
  37.1 0.0 collective-permute-done
  37.1 1.0 %maximum_convert_fusion.signal_ref = f32[4,216,256]{2,1,0:T(8,128)} fusion(bf16[1,216,256]{2,1,0:T(8,128)(2,1)S(1)} %bitcast.51, bf16[1,216,256]{2,1,0:T(8,128)(2,1)S(1)} %bitcast.52, bf16[1,216,256]{2,1,0:T(8,128)(2,1)S(1)} %bitcast.53, bf16[1,216,256]{2,1,0:T(8,128)(2,1)S(1)} %bitcast.46), kind=kLoop, calls=%fused_computation.25 | loop fusion | flops 884736 | bytes 1327104 | tf_op jit(solution)/shard_map/convert_element_type | solution.py:168
  38.1 13.8 %shard_map.55 = f32[4,128,256]{2,1,0:T(8,128)} custom-call(bf16[82,32,256]{2,1,0:T(8,128)(2,1)} %bitcast.44, f32[4,216,256]{2,1,0:T(8,128)} %maximum_convert_fusion.signal_ref), custom_call_target="tpu_custom_call" | custom-call | tf_op jit(solution)/shard_map/pallas_call | solution.py:173
  51.9 1.1 %select_reduce_fusion = bf16[128,256]{1,0:T(8,128)(2,1)S(1)} fusion(f32[4,128,256]{2,1,0:T(8,128)} %shard_map.55, pred[4,256]{1,0:T(4,128)(4,1)S(1)} %broadcast_in_dim.111), kind=kLoop, calls=%fused_computation.22 | loop fusion | flops 229376 | bytes 590848 | tf_op jit(solution)/shard_map/reduce_sum | solution.py:226
  53.0 0.1 copy.15
  53.1 0.2 copy.16
  53.3 0.1 copy.17
  53.4 0.6 %gather_fusion = bf16[32,1024]{1,0:T(8,128)(2,1)S(1)} fusion(bf16[32,1024]{1,0:T(8,128)(2,1)S(1)} %copy.17, s32[1024]{0:T(1024)S(1)} %pad_clamp_fusion), kind=kCustom, calls=%fused_computation | custom fusion | bytes 131200 | tf_op jit(solution)/shard_map/gather | solution.py:232
  54.1 0.1 collective-permute-start.5
  54.2 1.5 %collective-permute-start.4 = (bf16[8,1024]{1,0:T(8,128)(2,1)S(1)}, bf16[8,1024]{1,0:T(8,128)(2,1)S(1)}, u32[]{:S(2)}, u32[]{:S(2)}) collective-permute-start(bf16[8,1024]{1,0:T(8,128)(2,1)S(1)} %get-tuple-element.23), channel_id=1, source_target_pairs={{0,2},{1,3},{2,0},{3,1},{4,6},{5,7},{6,4},{7,5},{8,10},{9,11},{10,... | collective-permute-start | bytes 49160 | tf_op jit(solution)/shard_map/ppermute | solution.py:239
  55.7 0.2 collective-permute-start.3
  55.9 0.0 collective-permute-done.5
  55.9 2.1 %collective-permute-done.4 = bf16[8,1024]{1,0:T(8,128)(2,1)S(1)} collective-permute-done((bf16[8,1024]{1,0:T(8,128)(2,1)S(1)}, bf16[8,1024]{1,0:T(8,128)(2,1)S(1)}, u32[]{:S(2)}, u32[]{:S(2)}) %collective-permute-start.4) | collective-permute-done | bytes 16416 | tf_op jit(solution)/shard_map/ppermute | solution.py:239
  58.0 0.9 %collective-permute-done.3 = bf16[8,1024]{1,0:T(8,128)(2,1)S(1)} collective-permute-done((bf16[8,1024]{1,0:T(8,128)(2,1)S(1)}, bf16[8,1024]{1,0:T(8,128)(2,1)S(1)}, u32[]{:S(2)}, u32[]{:S(2)}) %collective-permute-start.3) | collective-permute-done | bytes 16416 | tf_op jit(solution)/shard_map/ppermute | solution.py:239
  58.9 0.1 multiply_reduce_fusion
  59.0 0.7 %broadcast_multiply_fusion = f32[8,1024]{1,0:T(8,128)} fusion(f32[8]{0:T(128)S(1)} %add_rsqrt_fusion.1, bf16[8,1024]{1,0:T(8,128)(2,1)S(1)} %collective-permute-done.5, bf16[8,1024]{1,0:T(8,128)(2,1)S(1)} %collective-permute-done.4, bf16[8,1024]{1,0:T(8,128)(2,1)S(1)} %collective-permute-done.3, bf16[4,8,1024]{2,1,0:T(8,128)(2,1)S(1)} %bitcast.49, ...), kind=kLoop, calls=%fused_computation.43 | loop fusion | flops 73728 | bytes 98341 | tf_op jit(solution)/shard_map/mul | solution.py:244
  (15 shorter events, 0.2 us)
Async XLA Ops:
  0.0 3.8 %copy-start = (bf16[32,32,512]{2,1,0:T(8,128)(2,1)S(1)}, bf16[32,32,512]{2,1,0:T(8,128)(2,1)}, u32[]{:S(2)}) copy-start(bf16[32,32,512]{2,1,0:T(8,128)(2,1)} %param.8) | copy-start | bytes 3145732
  3.5 1.1 %copy-start.1 = (s32[32,32]{1,0:T(8,128)S(1)}, s32[32,32]{1,0:T(8,128)}, u32[]{:S(2)}) copy-start(s32[32,32]{1,0:T(8,128)} %param.9) | copy-start | bytes 12292
  5.1 0.7 %copy-start.2 = (s32[32,32]{1,0:T(8,128)S(1)}, s32[32,32]{1,0:T(8,128)}, u32[]{:S(2)}) copy-start(s32[32,32]{1,0:T(8,128)} %param.10) | copy-start | bytes 12292
  16.6 20.4 %collective-permute-start.2 = (bf16[216,256]{1,0:T(8,128)(2,1)S(1)}, bf16[216,256]{1,0:T(8,128)(2,1)S(1)}, u32[]{:S(2)}, u32[]{:S(2)}) collective-permute-start(bf16[216,256]{1,0:T(8,128)(2,1)S(1)} %pad.17), channel_id=1, source_target_pairs={{0,12},{4,0},{8,4},{12,8},{1,13},{5,1},{9,5},{13,9},{2,14},{6,2},{... | collective-permute-start | bytes 331784 | tf_op jit(solution)/shard_map/ppermute | solution.py:218
  21.7 15.3 %collective-permute-start.1 = (bf16[216,256]{1,0:T(8,128)(2,1)S(1)}, bf16[216,256]{1,0:T(8,128)(2,1)S(1)}, u32[]{:S(2)}, u32[]{:S(2)}) collective-permute-start(bf16[216,256]{1,0:T(8,128)(2,1)S(1)} %pad.17), channel_id=1, source_target_pairs={{0,8},{4,12},{8,0},{12,4},{1,9},{5,13},{9,1},{13,5},{2,10},{6,14},... | collective-permute-start | bytes 331784 | tf_op jit(solution)/shard_map/ppermute | solution.py:218
  21.7 15.3 %collective-permute-start = (bf16[216,256]{1,0:T(8,128)(2,1)S(1)}, bf16[216,256]{1,0:T(8,128)(2,1)S(1)}, u32[]{:S(2)}, u32[]{:S(2)}) collective-permute-start(bf16[216,256]{1,0:T(8,128)(2,1)S(1)} %pad.17), channel_id=1, source_target_pairs={{0,4},{4,8},{8,12},{12,0},{1,5},{5,9},{9,13},{13,1},{2,6},{6,10},{... | collective-permute-start | bytes 331784 | tf_op jit(solution)/shard_map/ppermute | solution.py:218
  34.8 1.4 %copy-start.3 = (s32[1,32]{1,0:T(1,128)S(1)}, s32[1,32]{1,0:T(1,128)}, u32[]{:S(2)}) copy-start(s32[1,32]{1,0:T(1,128)} %param.11) | copy-start | bytes 388
  54.1 1.8 %collective-permute-start.5 = (bf16[8,1024]{1,0:T(8,128)(2,1)S(1)}, bf16[8,1024]{1,0:T(8,128)(2,1)S(1)}, u32[]{:S(2)}, u32[]{:S(2)}) collective-permute-start(bf16[8,1024]{1,0:T(8,128)(2,1)S(1)} %get-tuple-element.22), channel_id=1, source_target_pairs={{0,3},{1,0},{2,1},{3,2},{4,7},{5,4},{6,5},{7,6},{8,11},{9,8},{10,9... | collective-permute-start | bytes 49160 | tf_op jit(solution)/shard_map/ppermute | solution.py:239
  54.2 3.7 %collective-permute-start.4 = (bf16[8,1024]{1,0:T(8,128)(2,1)S(1)}, bf16[8,1024]{1,0:T(8,128)(2,1)S(1)}, u32[]{:S(2)}, u32[]{:S(2)}) collective-permute-start(bf16[8,1024]{1,0:T(8,128)(2,1)S(1)} %get-tuple-element.23), channel_id=1, source_target_pairs={{0,2},{1,3},{2,0},{3,1},{4,6},{5,7},{6,4},{7,5},{8,10},{9,11},{10,... | collective-permute-start | bytes 49160 | tf_op jit(solution)/shard_map/ppermute | solution.py:239
  55.7 3.2 %collective-permute-start.3 = (bf16[8,1024]{1,0:T(8,128)(2,1)S(1)}, bf16[8,1024]{1,0:T(8,128)(2,1)S(1)}, u32[]{:S(2)}, u32[]{:S(2)}) collective-permute-start(bf16[8,1024]{1,0:T(8,128)(2,1)S(1)} %get-tuple-element.21), channel_id=1, source_target_pairs={{0,1},{1,2},{2,3},{3,0},{4,5},{5,6},{6,7},{7,4},{8,9},{9,10},{10,1... | collective-permute-start | bytes 49160 | tf_op jit(solution)/shard_map/ppermute | solution.py:239

commit v16 on v15

--- a/solution.py
+++ b/solution.py
@@ -137,7 +137,7 @@
         out_ref[...] = acc_ref[...].reshape(out_ref.shape)
 
 
-CORR_STEPS = 8
+CORR_STEPS = 16
 
 
 def corr_taps(padded_len, phases):

time: 60.1 us -> 58.6 us (0.975)
  Pallas kernels: 13.8 us -> 12.2 us
    pallas_call x1, Pallas kernels: 13.8 us -> 12.2 us  [correlate(): pl.pallas_call(kernel, grid=(taps // steps,), in_specs=[pl.BlockSpec(grou...]
where the time goes in v16:
time: 58.6 us; the launch traced here: 58.2 us
  other arithmetic  17.6 us (30%)
  local copies, waits for them, and re-layouts  16.6 us (28%)
  Pallas kernels  12.2 us (21%)
  starting transfers between devices  7.91 us (13%)
  waiting for transfers between devices  3 us (5%)
    pallas_call x1, Pallas kernels, correlate(): pl.pallas_call(kernel, grid=(taps // steps,), in_specs=[pl.BlockSpec(grou...  12.2 us
    select_n x8, other arithmetic, place_moveout(): current = jnp.where(active[..., None], moved, current)  9.93 us
    reshape x2, local copies, waits for them, and re-layouts, correlate(): grouped = jnp.transpose(padded, (0, 2, 1)).reshape(count, n_groups, width)  8.25 us
    ppermute x3, starting transfers between devices, shards(): pieces.append(lax.ppermute(signal, 'chan', pairs))  6.12 us
    transpose x2, local copies, waits for them, and re-layouts, correlate(): grouped = jnp.transpose(padded, (0, 2, 1)).reshape(count, n_groups, width)  5.01 us
    ppermute x3, waiting for transfers between devices, shards(): stack = stack + lax.ppermute(outgoing, 'tmpl', pairs).astype(jnp.float32)  3 us
    ppermute x3, starting transfers between devices, shards(): stack = stack + lax.ppermute(outgoing, 'tmpl', pairs).astype(jnp.float32)  1.79 us
    reduce_sum x2, other arithmetic, normalize_rows(): scale = lax.rsqrt(jnp.mean(centred * centred, axis=-1, keepdims=True) + eps)  1.62 us
  transfers between devices with their start and end apart: 6, of which 2 were waited for; matrix products, arithmetic and copies ran while one was open for 24% of the time, Pallas kernels for 0%

profile of v16, /device:TPU:0, one launch (start us, length us, event | category | flops | bytes accessed | tf_op | source)
XLA Modules:
  0.0 58.2 jit_solution(16129770061783157257)
XLA Ops:
  0.0 0.0 copy-start
  0.0 1.1 %convert_reduce_fusion.1 = f32[32]{0:T(128)S(1)} fusion(bf16[32,1664]{1,0:T(8,128)(2,1)} %param.7), kind=kLoop, calls=%fused_computation.27 | loop fusion | flops 106464 | bytes 106624 | tf_op jit(solution)/shard_map/reduce_sum | solution.py:19
  1.1 1.1 %fusion.10 = f32[32]{0:T(128)S(1)} fusion(bf16[32,1664]{1,0:T(8,128)(2,1)} %param.7, f32[32]{0:T(128)S(1)} %broadcast_multiply_fusion.2), kind=kLoop, calls=%fused_computation.31 | loop fusion | flops 212960 | bytes 106752 | tf_op jit(solution)/shard_map/reduce_sum | solution.py:20
  2.2 1.0 %fusion.12 = bf16[1664,32]{0,1:T(8,128)(2,1)S(1)} fusion(bf16[32,1664]{1,0:T(8,128)(2,1)} %param.7, f32[32]{0:T(128)S(1)} %add_rsqrt_fusion.2, f32[32]{0:T(128)S(1)} %broadcast_multiply_fusion.2), kind=kLoop, calls=%fused_computation.33 | loop fusion | flops 212992 | bytes 213248 | tf_op jit(solution)/shard_map/transpose | solution.py:151
  3.2 0.3 copy.12
  3.5 0.0 copy-start.1
  3.5 0.3 reshape.175
  3.8 0.0 copy-done
  3.8 0.2 convert_reduce_fusion
  4.0 0.5 fusion.2
  4.6 0.0 copy-done.1
  4.6 0.5 convolution_convert_fusion
  5.1 0.0 copy-start.2
  5.2 0.1 pad_slice_fusion
  5.3 0.6 %copy-done.2 = s32[32,32]{1,0:T(8,128)S(1)} copy-done((s32[32,32]{1,0:T(8,128)S(1)}, s32[32,32]{1,0:T(8,128)}, u32[]{:S(2)}) %copy-start.2) | copy-done | bytes 4120
  5.9 0.6 %select_reduce_fusion.1 = s32[32,32]{1,0:T(8,128)S(1)} fusion(s32[32,32]{1,0:T(8,128)S(1)} %copy-done.2, s32[32,32]{1,0:T(8,128)S(1)} %add_select_fusion), kind=kLoop, calls=%fused_computation.23 | loop fusion | flops 97280 | bytes 12288 | tf_op jit(solution)/shard_map/reduce_sum | solution.py:209
  6.5 1.3 %pad_select_fusion.7 = bf16[32,32,640]{2,1,0:T(8,128)(2,1)S(1)} fusion(bf16[32,32,639]{2,1,0:T(8,128)(2,1)S(1)} %pad_slice_fusion, pred[32,32]{1,0:T(8,128)(4,1)S(1)} %get-tuple-element.25, bf16[32,32,512]{2,1,0:T(8,128)(2,1)S(1)} %convolution_convert_fusion), kind=kLoop, calls=%fused_computation.18 | loop fusion | flops 655360 | bytes 3668992 | tf_op jit(solution)/shard_map/jit(_where)/select_n | solution.py:33
  7.8 1.3 %pad_select_fusion.6 = bf16[32,32,640]{2,1,0:T(8,128)(2,1)S(1)} fusion(bf16[32,32,640]{2,1,0:T(8,128)(2,1)S(1)} %pad_select_fusion.7, bf16[32,32,638]{2,1,0:T(8,128)(2,1)S(1)} %bitcast.38, pred[32,32]{1,0:T(8,128)(4,1)S(1)} %get-tuple-element.26), kind=kLoop, calls=%fused_computation.17 | loop fusion | flops 655360 | bytes 3929088 | tf_op jit(solution)/shard_map/jit(_where)/select_n | solution.py:33
  9.2 1.3 %pad_select_fusion.5 = bf16[32,32,640]{2,1,0:T(8,128)(2,1)S(1)} fusion(bf16[32,32,640]{2,1,0:T(8,128)(2,1)S(1)} %pad_select_fusion.6, bf16[32,32,636]{2,1,0:T(8,128)(2,1)S(1)} %bitcast.39, pred[32,32]{1,0:T(8,128)(4,1)S(1)} %get-tuple-element.27), kind=kLoop, calls=%fused_computation.16 | loop fusion | flops 655360 | bytes 3924992 | tf_op jit(solution)/shard_map/jit(_where)/select_n | solution.py:33
  10.5 1.3 %pad_select_fusion.4 = bf16[32,32,640]{2,1,0:T(8,128)(2,1)S(1)} fusion(bf16[32,32,640]{2,1,0:T(8,128)(2,1)S(1)} %pad_select_fusion.5, bf16[32,32,632]{2,1,0:T(8,128)(2,1)S(1)} %bitcast.40, pred[32,32]{1,0:T(8,128)(4,1)S(1)} %get-tuple-element.28), kind=kLoop, calls=%fused_computation.15 | loop fusion | flops 655360 | bytes 3916800 | tf_op jit(solution)/shard_map/jit(_where)/select_n | solution.py:33
  11.9 1.3 %pad_select_fusion.3 = bf16[32,32,640]{2,1,0:T(8,128)(2,1)S(1)} fusion(bf16[32,32,640]{2,1,0:T(8,128)(2,1)S(1)} %pad_select_fusion.4, bf16[32,32,624]{2,1,0:T(8,128)(2,1)S(1)} %bitcast.41, pred[32,32]{1,0:T(8,128)(4,1)S(1)} %get-tuple-element.29), kind=kLoop, calls=%fused_computation.14 | loop fusion | flops 655360 | bytes 3900416 | tf_op jit(solution)/shard_map/jit(_where)/select_n | solution.py:33
  13.2 1.3 %pad_select_fusion.2 = bf16[32,32,640]{2,1,0:T(8,128)(2,1)S(1)} fusion(bf16[32,32,640]{2,1,0:T(8,128)(2,1)S(1)} %pad_select_fusion.3, bf16[32,32,608]{2,1,0:T(8,128)(2,1)S(1)} %bitcast.42, pred[32,32]{1,0:T(8,128)(4,1)S(1)} %get-tuple-element.30), kind=kLoop, calls=%fused_computation.13 | loop fusion | flops 655360 | bytes 3867648 | tf_op jit(solution)/shard_map/jit(_where)/select_n | solution.py:33
  14.6 1.3 %pad_select_fusion.1 = bf16[32,32,640]{2,1,0:T(8,128)(2,1)S(1)} fusion(bf16[32,32,640]{2,1,0:T(8,128)(2,1)S(1)} %pad_select_fusion.2, bf16[32,32,576]{2,1,0:T(8,128)(2,1)S(1)} %bitcast.43, pred[32,32]{1,0:T(8,128)(4,1)S(1)} %get-tuple-element.31), kind=kLoop, calls=%fused_computation.12 | loop fusion | flops 655360 | bytes 3802112 | tf_op jit(solution)/shard_map/jit(_where)/select_n | solution.py:33
  15.9 0.1 slice.53
  16.1 0.6 pad_select_fusion
  16.6 5.1 %collective-permute-start.2 = (bf16[224,256]{1,0:T(8,128)(2,1)S(1)}, bf16[224,256]{1,0:T(8,128)(2,1)S(1)}, u32[]{:S(2)}, u32[]{:S(2)}) collective-permute-start(bf16[224,256]{1,0:T(8,128)(2,1)S(1)} %pad.17), channel_id=1, source_target_pairs={{0,12},{4,0},{8,4},{12,8},{1,13},{5,1},{9,5},{13,9},{2,14},{6,2},{... | collective-permute-start | bytes 344072 | tf_op jit(solution)/shard_map/ppermute | solution.py:218
  21.7 0.0 collective-permute-start.1
  21.7 1.0 %collective-permute-start = (bf16[224,256]{1,0:T(8,128)(2,1)S(1)}, bf16[224,256]{1,0:T(8,128)(2,1)S(1)}, u32[]{:S(2)}, u32[]{:S(2)}) collective-permute-start(bf16[224,256]{1,0:T(8,128)(2,1)S(1)} %pad.17), channel_id=1, source_target_pairs={{0,4},{4,8},{8,12},{12,0},{1,5},{5,9},{9,13},{13,1},{2,6},{6,10},{... | collective-permute-start | bytes 344072 | tf_op jit(solution)/shard_map/ppermute | solution.py:218
  22.8 0.1 slice_reduce_fusion
  22.9 0.0 copy-start.3
  22.9 0.7 %pad_bitcast_fusion = bf16[32,656,32]{1,2,0:T(8,128)(2,1)S(1)} fusion(bf16[32,32,640]{2,1,0:T(8,128)(2,1)S(1)} %pad_select_fusion), kind=kLoop, calls=%fused_computation.8 | loop fusion | bytes 2654208 | tf_op jit(solution)/shard_map/transpose | solution.py:166
  23.6 0.0 copy-done.3
  23.7 0.7 %scatter_custom_fusion = s32[32]{0:T(128)S(1)} fusion(s32[32]{0:T(128)S(1)} %fusion.15, s32[32]{0:T(128)S(1)} %iota.14, s32[]{:T(128)} %constant.103.clone.1), kind=kCustom, calls=%fused_computation.71 | custom fusion | bytes 132 | tf_op jit(solution)/shard_map/scatter | solution.py:230
  24.4 4.3 %copy.13 = bf16[32,656,32]{2,1,0:T(8,128)(2,1)} copy(bf16[32,656,32]{1,2,0:T(8,128)(2,1)S(1)} %pad_bitcast_fusion) | data formatting | bytes 2686976 | tf_op jit(solution)/shard_map/transpose | solution.py:166
  28.7 6.9 %reshape.176 = bf16[32,82,256]{2,1,0:T(8,128)(2,1)S(1)} reshape(bf16[32,656,32]{2,1,0:T(8,128)(2,1)} %copy.13) | data formatting | bytes 2686976 | tf_op jit(solution)/shard_map/reshape | solution.py:166
  35.6 1.4 %copy.19 = bf16[32,82,256]{2,0,1:T(8,128)(2,1)} copy(bf16[32,82,256]{2,1,0:T(8,128)(2,1)S(1)} %reshape.176) | data formatting | bytes 2686976 | tf_op jit(solution)/shard_map/reshape | solution.py:166
  37.0 0.1 broadcast_in_dim.111
  37.1 0.0 collective-permute-done.2
  37.1 0.0 collective-permute-done.1
  37.1 0.0 collective-permute-done
  37.1 1.0 %maximum_convert_fusion.signal_ref = f32[4,224,256]{2,1,0:T(8,128)} fusion(bf16[1,224,256]{2,1,0:T(8,128)(2,1)S(1)} %bitcast.51, bf16[1,224,256]{2,1,0:T(8,128)(2,1)S(1)} %bitcast.52, bf16[1,224,256]{2,1,0:T(8,128)(2,1)S(1)} %bitcast.53, bf16[1,224,256]{2,1,0:T(8,128)(2,1)S(1)} %bitcast.46), kind=kLoop, calls=%fused_computation.25 | loop fusion | flops 917504 | bytes 1376256 | tf_op jit(solution)/shard_map/convert_element_type | solution.py:168
  38.2 12.2 %shard_map.55 = f32[4,128,256]{2,1,0:T(8,128)} custom-call(bf16[82,32,256]{2,1,0:T(8,128)(2,1)} %bitcast.44, f32[4,224,256]{2,1,0:T(8,128)} %maximum_convert_fusion.signal_ref), custom_call_target="tpu_custom_call" | custom-call | tf_op jit(solution)/shard_map/pallas_call | solution.py:173
  50.4 1.1 %select_reduce_fusion = bf16[128,256]{1,0:T(8,128)(2,1)S(1)} fusion(f32[4,128,256]{2,1,0:T(8,128)} %shard_map.55, pred[4,256]{1,0:T(4,128)(4,1)S(1)} %broadcast_in_dim.111), kind=kLoop, calls=%fused_computation.22 | loop fusion | flops 229376 | bytes 590848 | tf_op jit(solution)/shard_map/reduce_sum | solution.py:226
  51.5 0.1 copy.15
  51.6 0.2 copy.16
  51.8 0.1 copy.17
  51.9 0.6 %gather_fusion = bf16[32,1024]{1,0:T(8,128)(2,1)S(1)} fusion(bf16[32,1024]{1,0:T(8,128)(2,1)S(1)} %copy.17, s32[1024]{0:T(1024)S(1)} %pad_clamp_fusion), kind=kCustom, calls=%fused_computation | custom fusion | bytes 131200 | tf_op jit(solution)/shard_map/gather | solution.py:232
  52.6 0.2 collective-permute-start.5
  52.7 1.5 %collective-permute-start.4 = (bf16[8,1024]{1,0:T(8,128)(2,1)S(1)}, bf16[8,1024]{1,0:T(8,128)(2,1)S(1)}, u32[]{:S(2)}, u32[]{:S(2)}) collective-permute-start(bf16[8,1024]{1,0:T(8,128)(2,1)S(1)} %get-tuple-element.23), channel_id=1, source_target_pairs={{0,2},{1,3},{2,0},{3,1},{4,6},{5,7},{6,4},{7,5},{8,10},{9,11},{10,... | collective-permute-start | bytes 49160 | tf_op jit(solution)/shard_map/ppermute | solution.py:239
  54.2 0.2 collective-permute-start.3
  54.4 0.0 collective-permute-done.5
  54.4 2.1 %collective-permute-done.4 = bf16[8,1024]{1,0:T(8,128)(2,1)S(1)} collective-permute-done((bf16[8,1024]{1,0:T(8,128)(2,1)S(1)}, bf16[8,1024]{1,0:T(8,128)(2,1)S(1)}, u32[]{:S(2)}, u32[]{:S(2)}) %collective-permute-start.4) | collective-permute-done | bytes 16416 | tf_op jit(solution)/shard_map/ppermute | solution.py:239
  56.5 0.9 %collective-permute-done.3 = bf16[8,1024]{1,0:T(8,128)(2,1)S(1)} collective-permute-done((bf16[8,1024]{1,0:T(8,128)(2,1)S(1)}, bf16[8,1024]{1,0:T(8,128)(2,1)S(1)}, u32[]{:S(2)}, u32[]{:S(2)}) %collective-permute-start.3) | collective-permute-done | bytes 16416 | tf_op jit(solution)/shard_map/ppermute | solution.py:239
  57.4 0.1 multiply_reduce_fusion
  57.5 0.7 %broadcast_multiply_fusion = f32[8,1024]{1,0:T(8,128)} fusion(f32[8]{0:T(128)S(1)} %add_rsqrt_fusion.1, bf16[8,1024]{1,0:T(8,128)(2,1)S(1)} %collective-permute-done.5, bf16[8,1024]{1,0:T(8,128)(2,1)S(1)} %collective-permute-done.4, bf16[8,1024]{1,0:T(8,128)(2,1)S(1)} %collective-permute-done.3, bf16[4,8,1024]{2,1,0:T(8,128)(2,1)S(1)} %bitcast.49, ...), kind=kLoop, calls=%fused_computation.43 | loop fusion | flops 73728 | bytes 98341 | tf_op jit(solution)/shard_map/mul | solution.py:244
  (15 shorter events, 0.2 us)
Async XLA Ops:
  0.0 3.8 %copy-start = (bf16[32,32,512]{2,1,0:T(8,128)(2,1)S(1)}, bf16[32,32,512]{2,1,0:T(8,128)(2,1)}, u32[]{:S(2)}) copy-start(bf16[32,32,512]{2,1,0:T(8,128)(2,1)} %param.8) | copy-start | bytes 3145732
  3.5 1.1 %copy-start.1 = (s32[32,32]{1,0:T(8,128)S(1)}, s32[32,32]{1,0:T(8,128)}, u32[]{:S(2)}) copy-start(s32[32,32]{1,0:T(8,128)} %param.9) | copy-start | bytes 12292
  5.1 0.7 %copy-start.2 = (s32[32,32]{1,0:T(8,128)S(1)}, s32[32,32]{1,0:T(8,128)}, u32[]{:S(2)}) copy-start(s32[32,32]{1,0:T(8,128)} %param.10) | copy-start | bytes 12292
  16.6 20.4 %collective-permute-start.2 = (bf16[224,256]{1,0:T(8,128)(2,1)S(1)}, bf16[224,256]{1,0:T(8,128)(2,1)S(1)}, u32[]{:S(2)}, u32[]{:S(2)}) collective-permute-start(bf16[224,256]{1,0:T(8,128)(2,1)S(1)} %pad.17), channel_id=1, source_target_pairs={{0,12},{4,0},{8,4},{12,8},{1,13},{5,1},{9,5},{13,9},{2,14},{6,2},{... | collective-permute-start | bytes 344072 | tf_op jit(solution)/shard_map/ppermute | solution.py:218
  21.7 15.4 %collective-permute-start.1 = (bf16[224,256]{1,0:T(8,128)(2,1)S(1)}, bf16[224,256]{1,0:T(8,128)(2,1)S(1)}, u32[]{:S(2)}, u32[]{:S(2)}) collective-permute-start(bf16[224,256]{1,0:T(8,128)(2,1)S(1)} %pad.17), channel_id=1, source_target_pairs={{0,8},{4,12},{8,0},{12,4},{1,9},{5,13},{9,1},{13,5},{2,10},{6,14},... | collective-permute-start | bytes 344072 | tf_op jit(solution)/shard_map/ppermute | solution.py:218
  21.7 15.4 %collective-permute-start = (bf16[224,256]{1,0:T(8,128)(2,1)S(1)}, bf16[224,256]{1,0:T(8,128)(2,1)S(1)}, u32[]{:S(2)}, u32[]{:S(2)}) collective-permute-start(bf16[224,256]{1,0:T(8,128)(2,1)S(1)} %pad.17), channel_id=1, source_target_pairs={{0,4},{4,8},{8,12},{12,0},{1,5},{5,9},{9,13},{13,1},{2,6},{6,10},{... | collective-permute-start | bytes 344072 | tf_op jit(solution)/shard_map/ppermute | solution.py:218
  22.9 0.8 %copy-start.3 = (s32[1,32]{1,0:T(1,128)S(1)}, s32[1,32]{1,0:T(1,128)}, u32[]{:S(2)}) copy-start(s32[1,32]{1,0:T(1,128)} %param.11) | copy-start | bytes 388
  52.6 1.8 %collective-permute-start.5 = (bf16[8,1024]{1,0:T(8,128)(2,1)S(1)}, bf16[8,1024]{1,0:T(8,128)(2,1)S(1)}, u32[]{:S(2)}, u32[]{:S(2)}) collective-permute-start(bf16[8,1024]{1,0:T(8,128)(2,1)S(1)} %get-tuple-element.22), channel_id=1, source_target_pairs={{0,3},{1,0},{2,1},{3,2},{4,7},{5,4},{6,5},{7,6},{8,11},{9,8},{10,9... | collective-permute-start | bytes 49160 | tf_op jit(solution)/shard_map/ppermute | solution.py:239
  52.7 3.7 %collective-permute-start.4 = (bf16[8,1024]{1,0:T(8,128)(2,1)S(1)}, bf16[8,1024]{1,0:T(8,128)(2,1)S(1)}, u32[]{:S(2)}, u32[]{:S(2)}) collective-permute-start(bf16[8,1024]{1,0:T(8,128)(2,1)S(1)} %get-tuple-element.23), channel_id=1, source_target_pairs={{0,2},{1,3},{2,0},{3,1},{4,6},{5,7},{6,4},{7,5},{8,10},{9,11},{10,... | collective-permute-start | bytes 49160 | tf_op jit(solution)/shard_map/ppermute | solution.py:239
  54.2 3.2 %collective-permute-start.3 = (bf16[8,1024]{1,0:T(8,128)(2,1)S(1)}, bf16[8,1024]{1,0:T(8,128)(2,1)S(1)}, u32[]{:S(2)}, u32[]{:S(2)}) collective-permute-start(bf16[8,1024]{1,0:T(8,128)(2,1)S(1)} %get-tuple-element.21), channel_id=1, source_target_pairs={{0,1},{1,2},{2,3},{3,0},{4,5},{5,6},{6,7},{7,4},{8,9},{9,10},{10,1... | collective-permute-start | bytes 49160 | tf_op jit(solution)/shard_map/ppermute | solution.py:239

commit v17 on v16

--- a/solution.py
+++ b/solution.py
@@ -137,7 +137,7 @@
         out_ref[...] = acc_ref[...].reshape(out_ref.shape)
 
 
-CORR_STEPS = 16
+CORR_STEPS = 40
 
 
 def corr_taps(padded_len, phases):

time: 58.6 us -> 57.7 us (0.985)
  Pallas kernels: 12.2 us -> 11.3 us
    pallas_call x1, Pallas kernels: 12.2 us -> 11.3 us  [correlate(): pl.pallas_call(kernel, grid=(taps // steps,), in_specs=[pl.BlockSpec(grou...]
  transfers between devices with their start and end apart: 6 -> 6, of which waited for: 2 -> 2; matrix products, arithmetic and copies ran while one was open for 24% -> 25% of each run, Pallas kernels for 0% -> 0%
where the time goes in v17:
time: 57.7 us; the launch traced here: 57.3 us
  other arithmetic  17.6 us (31%)
  local copies, waits for them, and re-layouts  16.6 us (29%)
  Pallas kernels  11.3 us (20%)
  starting transfers between devices  7.9 us (14%)
  waiting for transfers between devices  3 us (5%)
    pallas_call x1, Pallas kernels, correlate(): pl.pallas_call(kernel, grid=(taps // steps,), in_specs=[pl.BlockSpec(grou...  11.3 us
    select_n x8, other arithmetic, place_moveout(): current = jnp.where(active[..., None], moved, current)  9.93 us
    reshape x2, local copies, waits for them, and re-layouts, correlate(): grouped = jnp.transpose(padded, (0, 2, 1)).reshape(count, n_groups, width)  8.25 us
    ppermute x3, starting transfers between devices, shards(): pieces.append(lax.ppermute(signal, 'chan', pairs))  6.12 us
    transpose x2, local copies, waits for them, and re-layouts, correlate(): grouped = jnp.transpose(padded, (0, 2, 1)).reshape(count, n_groups, width)  5.01 us
    ppermute x3, waiting for transfers between devices, shards(): stack = stack + lax.ppermute(outgoing, 'tmpl', pairs).astype(jnp.float32)  3 us
    ppermute x3, starting transfers between devices, shards(): stack = stack + lax.ppermute(outgoing, 'tmpl', pairs).astype(jnp.float32)  1.78 us
    reduce_sum x2, other arithmetic, normalize_rows(): scale = lax.rsqrt(jnp.mean(centred * centred, axis=-1, keepdims=True) + eps)  1.62 us
  transfers between devices with their start and end apart: 6, of which 2 were waited for; matrix products, arithmetic and copies ran while one was open for 25% of the time, Pallas kernels for 0%

profile of v17, /device:TPU:0, one launch (start us, length us, event | category | flops | bytes accessed | tf_op | source)
XLA Modules:
  0.0 57.3 jit_solution(12263075278536515356)
XLA Ops:
  0.0 0.0 copy-start
  0.0 1.1 %convert_reduce_fusion.1 = f32[32]{0:T(128)S(1)} fusion(bf16[32,1664]{1,0:T(8,128)(2,1)} %param.7), kind=kLoop, calls=%fused_computation.27 | loop fusion | flops 106464 | bytes 106624 | tf_op jit(solution)/shard_map/reduce_sum | solution.py:19
  1.1 1.1 %fusion.10 = f32[32]{0:T(128)S(1)} fusion(bf16[32,1664]{1,0:T(8,128)(2,1)} %param.7, f32[32]{0:T(128)S(1)} %broadcast_multiply_fusion.2), kind=kLoop, calls=%fused_computation.31 | loop fusion | flops 212960 | bytes 106752 | tf_op jit(solution)/shard_map/reduce_sum | solution.py:20
  2.2 1.0 %fusion.12 = bf16[1664,32]{0,1:T(8,128)(2,1)S(1)} fusion(bf16[32,1664]{1,0:T(8,128)(2,1)} %param.7, f32[32]{0:T(128)S(1)} %add_rsqrt_fusion.2, f32[32]{0:T(128)S(1)} %broadcast_multiply_fusion.2), kind=kLoop, calls=%fused_computation.33 | loop fusion | flops 212992 | bytes 213248 | tf_op jit(solution)/shard_map/transpose | solution.py:151
  3.2 0.3 copy.12
  3.5 0.0 copy-start.1
  3.5 0.3 reshape.175
  3.8 0.0 copy-done
  3.8 0.2 convert_reduce_fusion
  4.0 0.5 fusion.2
  4.6 0.0 copy-done.1
  4.6 0.5 convolution_convert_fusion
  5.1 0.0 copy-start.2
  5.2 0.1 pad_slice_fusion
  5.3 0.6 %copy-done.2 = s32[32,32]{1,0:T(8,128)S(1)} copy-done((s32[32,32]{1,0:T(8,128)S(1)}, s32[32,32]{1,0:T(8,128)}, u32[]{:S(2)}) %copy-start.2) | copy-done | bytes 4120
  5.9 0.6 %select_reduce_fusion.1 = s32[32,32]{1,0:T(8,128)S(1)} fusion(s32[32,32]{1,0:T(8,128)S(1)} %copy-done.2, s32[32,32]{1,0:T(8,128)S(1)} %add_select_fusion), kind=kLoop, calls=%fused_computation.23 | loop fusion | flops 97280 | bytes 12288 | tf_op jit(solution)/shard_map/reduce_sum | solution.py:209
  6.5 1.3 %pad_select_fusion.7 = bf16[32,32,640]{2,1,0:T(8,128)(2,1)S(1)} fusion(bf16[32,32,639]{2,1,0:T(8,128)(2,1)S(1)} %pad_slice_fusion, pred[32,32]{1,0:T(8,128)(4,1)S(1)} %get-tuple-element.25, bf16[32,32,512]{2,1,0:T(8,128)(2,1)S(1)} %convolution_convert_fusion), kind=kLoop, calls=%fused_computation.18 | loop fusion | flops 655360 | bytes 3668992 | tf_op jit(solution)/shard_map/jit(_where)/select_n | solution.py:33
  7.8 1.3 %pad_select_fusion.6 = bf16[32,32,640]{2,1,0:T(8,128)(2,1)S(1)} fusion(bf16[32,32,640]{2,1,0:T(8,128)(2,1)S(1)} %pad_select_fusion.7, bf16[32,32,638]{2,1,0:T(8,128)(2,1)S(1)} %bitcast.38, pred[32,32]{1,0:T(8,128)(4,1)S(1)} %get-tuple-element.26), kind=kLoop, calls=%fused_computation.17 | loop fusion | flops 655360 | bytes 3929088 | tf_op jit(solution)/shard_map/jit(_where)/select_n | solution.py:33
  9.2 1.3 %pad_select_fusion.5 = bf16[32,32,640]{2,1,0:T(8,128)(2,1)S(1)} fusion(bf16[32,32,640]{2,1,0:T(8,128)(2,1)S(1)} %pad_select_fusion.6, bf16[32,32,636]{2,1,0:T(8,128)(2,1)S(1)} %bitcast.39, pred[32,32]{1,0:T(8,128)(4,1)S(1)} %get-tuple-element.27), kind=kLoop, calls=%fused_computation.16 | loop fusion | flops 655360 | bytes 3924992 | tf_op jit(solution)/shard_map/jit(_where)/select_n | solution.py:33
  10.5 1.3 %pad_select_fusion.4 = bf16[32,32,640]{2,1,0:T(8,128)(2,1)S(1)} fusion(bf16[32,32,640]{2,1,0:T(8,128)(2,1)S(1)} %pad_select_fusion.5, bf16[32,32,632]{2,1,0:T(8,128)(2,1)S(1)} %bitcast.40, pred[32,32]{1,0:T(8,128)(4,1)S(1)} %get-tuple-element.28), kind=kLoop, calls=%fused_computation.15 | loop fusion | flops 655360 | bytes 3916800 | tf_op jit(solution)/shard_map/jit(_where)/select_n | solution.py:33
  11.9 1.3 %pad_select_fusion.3 = bf16[32,32,640]{2,1,0:T(8,128)(2,1)S(1)} fusion(bf16[32,32,640]{2,1,0:T(8,128)(2,1)S(1)} %pad_select_fusion.4, bf16[32,32,624]{2,1,0:T(8,128)(2,1)S(1)} %bitcast.41, pred[32,32]{1,0:T(8,128)(4,1)S(1)} %get-tuple-element.29), kind=kLoop, calls=%fused_computation.14 | loop fusion | flops 655360 | bytes 3900416 | tf_op jit(solution)/shard_map/jit(_where)/select_n | solution.py:33
  13.2 1.3 %pad_select_fusion.2 = bf16[32,32,640]{2,1,0:T(8,128)(2,1)S(1)} fusion(bf16[32,32,640]{2,1,0:T(8,128)(2,1)S(1)} %pad_select_fusion.3, bf16[32,32,608]{2,1,0:T(8,128)(2,1)S(1)} %bitcast.42, pred[32,32]{1,0:T(8,128)(4,1)S(1)} %get-tuple-element.30), kind=kLoop, calls=%fused_computation.13 | loop fusion | flops 655360 | bytes 3867648 | tf_op jit(solution)/shard_map/jit(_where)/select_n | solution.py:33
  14.6 1.3 %pad_select_fusion.1 = bf16[32,32,640]{2,1,0:T(8,128)(2,1)S(1)} fusion(bf16[32,32,640]{2,1,0:T(8,128)(2,1)S(1)} %pad_select_fusion.2, bf16[32,32,576]{2,1,0:T(8,128)(2,1)S(1)} %bitcast.43, pred[32,32]{1,0:T(8,128)(4,1)S(1)} %get-tuple-element.31), kind=kLoop, calls=%fused_computation.12 | loop fusion | flops 655360 | bytes 3802112 | tf_op jit(solution)/shard_map/jit(_where)/select_n | solution.py:33
  15.9 0.1 slice.53
  16.1 0.0 copy-start.3
  16.1 0.6 pad_select_fusion
  16.7 5.1 %collective-permute-start.2 = (bf16[248,256]{1,0:T(8,128)(2,1)S(1)}, bf16[248,256]{1,0:T(8,128)(2,1)S(1)}, u32[]{:S(2)}, u32[]{:S(2)}) collective-permute-start(bf16[248,256]{1,0:T(8,128)(2,1)S(1)} %pad.17), channel_id=1, source_target_pairs={{0,12},{4,0},{8,4},{12,8},{1,13},{5,1},{9,5},{13,9},{2,14},{6,2},{... | collective-permute-start | bytes 380936 | tf_op jit(solution)/shard_map/ppermute | solution.py:218
  21.8 0.0 collective-permute-start.1
  21.8 1.0 %collective-permute-start = (bf16[248,256]{1,0:T(8,128)(2,1)S(1)}, bf16[248,256]{1,0:T(8,128)(2,1)S(1)}, u32[]{:S(2)}, u32[]{:S(2)}) collective-permute-start(bf16[248,256]{1,0:T(8,128)(2,1)S(1)} %pad.17), channel_id=1, source_target_pairs={{0,4},{4,8},{8,12},{12,0},{1,5},{5,9},{9,13},{13,1},{2,6},{6,10},{... | collective-permute-start | bytes 380936 | tf_op jit(solution)/shard_map/ppermute | solution.py:218
  22.8 0.1 slice_reduce_fusion
  22.9 0.0 copy-done.3
  22.9 0.7 %scatter_custom_fusion = s32[32]{0:T(128)S(1)} fusion(s32[32]{0:T(128)S(1)} %fusion.15, s32[32]{0:T(128)S(1)} %iota.14, s32[]{:T(128)} %constant.103.clone.1), kind=kCustom, calls=%fused_computation.71 | custom fusion | bytes 132 | tf_op jit(solution)/shard_map/scatter | solution.py:230
  23.6 0.7 %pad_bitcast_fusion = bf16[32,656,32]{1,2,0:T(8,128)(2,1)S(1)} fusion(bf16[32,32,640]{2,1,0:T(8,128)(2,1)S(1)} %pad_select_fusion), kind=kLoop, calls=%fused_computation.8 | loop fusion | bytes 2654208 | tf_op jit(solution)/shard_map/transpose | solution.py:166
  24.4 4.3 %copy.13 = bf16[32,656,32]{2,1,0:T(8,128)(2,1)} copy(bf16[32,656,32]{1,2,0:T(8,128)(2,1)S(1)} %pad_bitcast_fusion) | data formatting | bytes 2686976 | tf_op jit(solution)/shard_map/transpose | solution.py:166
  28.7 6.9 %reshape.176 = bf16[32,82,256]{2,1,0:T(8,128)(2,1)S(1)} reshape(bf16[32,656,32]{2,1,0:T(8,128)(2,1)} %copy.13) | data formatting | bytes 2686976 | tf_op jit(solution)/shard_map/reshape | solution.py:166
  35.6 1.4 %copy.19 = bf16[32,82,256]{2,0,1:T(8,128)(2,1)} copy(bf16[32,82,256]{2,1,0:T(8,128)(2,1)S(1)} %reshape.176) | data formatting | bytes 2686976 | tf_op jit(solution)/shard_map/reshape | solution.py:166
  37.0 0.1 broadcast_in_dim.111
  37.1 0.0 collective-permute-done.2
  37.1 0.0 collective-permute-done.1
  37.1 0.0 collective-permute-done
  37.1 1.1 %maximum_convert_fusion.signal_ref = f32[4,248,256]{2,1,0:T(8,128)} fusion(bf16[1,248,256]{2,1,0:T(8,128)(2,1)S(1)} %bitcast.51, bf16[1,248,256]{2,1,0:T(8,128)(2,1)S(1)} %bitcast.52, bf16[1,248,256]{2,1,0:T(8,128)(2,1)S(1)} %bitcast.53, bf16[1,248,256]{2,1,0:T(8,128)(2,1)S(1)} %bitcast.46), kind=kLoop, calls=%fused_computation.25 | loop fusion | flops 1015808 | bytes 1523712 | tf_op jit(solution)/shard_map/convert_element_type | solution.py:168
  38.2 11.3 %shard_map.55 = f32[4,128,256]{2,1,0:T(8,128)} custom-call(bf16[82,32,256]{2,1,0:T(8,128)(2,1)} %bitcast.44, f32[4,248,256]{2,1,0:T(8,128)} %maximum_convert_fusion.signal_ref), custom_call_target="tpu_custom_call" | custom-call | tf_op jit(solution)/shard_map/pallas_call | solution.py:173
  49.5 1.1 %select_reduce_fusion = bf16[128,256]{1,0:T(8,128)(2,1)S(1)} fusion(f32[4,128,256]{2,1,0:T(8,128)} %shard_map.55, pred[4,256]{1,0:T(4,128)(4,1)S(1)} %broadcast_in_dim.111), kind=kLoop, calls=%fused_computation.22 | loop fusion | flops 229376 | bytes 590848 | tf_op jit(solution)/shard_map/reduce_sum | solution.py:226
  50.6 0.1 copy.15
  50.7 0.2 copy.16
  50.9 0.1 copy.17
  51.0 0.6 %gather_fusion = bf16[32,1024]{1,0:T(8,128)(2,1)S(1)} fusion(bf16[32,1024]{1,0:T(8,128)(2,1)S(1)} %copy.17, s32[1024]{0:T(1024)S(1)} %pad_clamp_fusion), kind=kCustom, calls=%fused_computation | custom fusion | bytes 131200 | tf_op jit(solution)/shard_map/gather | solution.py:232
  51.7 0.1 collective-permute-start.5
  51.8 1.5 %collective-permute-start.4 = (bf16[8,1024]{1,0:T(8,128)(2,1)S(1)}, bf16[8,1024]{1,0:T(8,128)(2,1)S(1)}, u32[]{:S(2)}, u32[]{:S(2)}) collective-permute-start(bf16[8,1024]{1,0:T(8,128)(2,1)S(1)} %get-tuple-element.23), channel_id=1, source_target_pairs={{0,2},{1,3},{2,0},{3,1},{4,6},{5,7},{6,4},{7,5},{8,10},{9,11},{10,... | collective-permute-start | bytes 49160 | tf_op jit(solution)/shard_map/ppermute | solution.py:239
  53.3 0.2 collective-permute-start.3
  53.5 0.0 collective-permute-done.5
  53.5 2.1 %collective-permute-done.4 = bf16[8,1024]{1,0:T(8,128)(2,1)S(1)} collective-permute-done((bf16[8,1024]{1,0:T(8,128)(2,1)S(1)}, bf16[8,1024]{1,0:T(8,128)(2,1)S(1)}, u32[]{:S(2)}, u32[]{:S(2)}) %collective-permute-start.4) | collective-permute-done | bytes 16416 | tf_op jit(solution)/shard_map/ppermute | solution.py:239
  55.6 0.9 %collective-permute-done.3 = bf16[8,1024]{1,0:T(8,128)(2,1)S(1)} collective-permute-done((bf16[8,1024]{1,0:T(8,128)(2,1)S(1)}, bf16[8,1024]{1,0:T(8,128)(2,1)S(1)}, u32[]{:S(2)}, u32[]{:S(2)}) %collective-permute-start.3) | collective-permute-done | bytes 16416 | tf_op jit(solution)/shard_map/ppermute | solution.py:239
  56.5 0.1 multiply_reduce_fusion
  56.6 0.7 %broadcast_multiply_fusion = f32[8,1024]{1,0:T(8,128)} fusion(f32[8]{0:T(128)S(1)} %add_rsqrt_fusion.1, bf16[8,1024]{1,0:T(8,128)(2,1)S(1)} %collective-permute-done.5, bf16[8,1024]{1,0:T(8,128)(2,1)S(1)} %collective-permute-done.4, bf16[8,1024]{1,0:T(8,128)(2,1)S(1)} %collective-permute-done.3, bf16[4,8,1024]{2,1,0:T(8,128)(2,1)S(1)} %bitcast.49, ...), kind=kLoop, calls=%fused_computation.43 | loop fusion | flops 73728 | bytes 98341 | tf_op jit(solution)/shard_map/mul | solution.py:244
  (15 shorter events, 0.2 us)
Async XLA Ops:
  0.0 3.8 %copy-start = (bf16[32,32,512]{2,1,0:T(8,128)(2,1)S(1)}, bf16[32,32,512]{2,1,0:T(8,128)(2,1)}, u32[]{:S(2)}) copy-start(bf16[32,32,512]{2,1,0:T(8,128)(2,1)} %param.8) | copy-start | bytes 3145732
  3.5 1.1 %copy-start.1 = (s32[32,32]{1,0:T(8,128)S(1)}, s32[32,32]{1,0:T(8,128)}, u32[]{:S(2)}) copy-start(s32[32,32]{1,0:T(8,128)} %param.9) | copy-start | bytes 12292
  5.1 0.7 %copy-start.2 = (s32[32,32]{1,0:T(8,128)S(1)}, s32[32,32]{1,0:T(8,128)}, u32[]{:S(2)}) copy-start(s32[32,32]{1,0:T(8,128)} %param.10) | copy-start | bytes 12292
  16.1 6.8 %copy-start.3 = (s32[1,32]{1,0:T(1,128)S(1)}, s32[1,32]{1,0:T(1,128)}, u32[]{:S(2)}) copy-start(s32[1,32]{1,0:T(1,128)} %param.11) | copy-start | bytes 388
  16.7 20.4 %collective-permute-start.2 = (bf16[248,256]{1,0:T(8,128)(2,1)S(1)}, bf16[248,256]{1,0:T(8,128)(2,1)S(1)}, u32[]{:S(2)}, u32[]{:S(2)}) collective-permute-start(bf16[248,256]{1,0:T(8,128)(2,1)S(1)} %pad.17), channel_id=1, source_target_pairs={{0,12},{4,0},{8,4},{12,8},{1,13},{5,1},{9,5},{13,9},{2,14},{6,2},{... | collective-permute-start | bytes 380936 | tf_op jit(solution)/shard_map/ppermute | solution.py:218
  21.8 15.3 %collective-permute-start.1 = (bf16[248,256]{1,0:T(8,128)(2,1)S(1)}, bf16[248,256]{1,0:T(8,128)(2,1)S(1)}, u32[]{:S(2)}, u32[]{:S(2)}) collective-permute-start(bf16[248,256]{1,0:T(8,128)(2,1)S(1)} %pad.17), channel_id=1, source_target_pairs={{0,8},{4,12},{8,0},{12,4},{1,9},{5,13},{9,1},{13,5},{2,10},{6,14},... | collective-permute-start | bytes 380936 | tf_op jit(solution)/shard_map/ppermute | solution.py:218
  21.8 15.3 %collective-permute-start = (bf16[248,256]{1,0:T(8,128)(2,1)S(1)}, bf16[248,256]{1,0:T(8,128)(2,1)S(1)}, u32[]{:S(2)}, u32[]{:S(2)}) collective-permute-start(bf16[248,256]{1,0:T(8,128)(2,1)S(1)} %pad.17), channel_id=1, source_target_pairs={{0,4},{4,8},{8,12},{12,0},{1,5},{5,9},{9,13},{13,1},{2,6},{6,10},{... | collective-permute-start | bytes 380936 | tf_op jit(solution)/shard_map/ppermute | solution.py:218
  51.7 1.8 %collective-permute-start.5 = (bf16[8,1024]{1,0:T(8,128)(2,1)S(1)}, bf16[8,1024]{1,0:T(8,128)(2,1)S(1)}, u32[]{:S(2)}, u32[]{:S(2)}) collective-permute-start(bf16[8,1024]{1,0:T(8,128)(2,1)S(1)} %get-tuple-element.22), channel_id=1, source_target_pairs={{0,3},{1,0},{2,1},{3,2},{4,7},{5,4},{6,5},{7,6},{8,11},{9,8},{10,9... | collective-permute-start | bytes 49160 | tf_op jit(solution)/shard_map/ppermute | solution.py:239
  51.8 3.7 %collective-permute-start.4 = (bf16[8,1024]{1,0:T(8,128)(2,1)S(1)}, bf16[8,1024]{1,0:T(8,128)(2,1)S(1)}, u32[]{:S(2)}, u32[]{:S(2)}) collective-permute-start(bf16[8,1024]{1,0:T(8,128)(2,1)S(1)} %get-tuple-element.23), channel_id=1, source_target_pairs={{0,2},{1,3},{2,0},{3,1},{4,6},{5,7},{6,4},{7,5},{8,10},{9,11},{10,... | collective-permute-start | bytes 49160 | tf_op jit(solution)/shard_map/ppermute | solution.py:239
  53.3 3.2 %collective-permute-start.3 = (bf16[8,1024]{1,0:T(8,128)(2,1)S(1)}, bf16[8,1024]{1,0:T(8,128)(2,1)S(1)}, u32[]{:S(2)}, u32[]{:S(2)}) collective-permute-start(bf16[8,1024]{1,0:T(8,128)(2,1)S(1)} %get-tuple-element.21), channel_id=1, source_target_pairs={{0,1},{1,2},{2,3},{3,0},{4,5},{5,6},{6,7},{7,4},{8,9},{9,10},{10,1... | collective-permute-start | bytes 49160 | tf_op jit(solution)/shard_map/ppermute | solution.py:239

commit v18 on v17

--- a/solution.py
+++ b/solution.py
@@ -140,10 +140,17 @@
 CORR_STEPS = 40
 
 
-def corr_taps(padded_len, phases):
+def corr_steps(padded_len, phases, n_blocks):
     taps = padded_len // phases + 1
-    main = taps // CORR_STEPS * CORR_STEPS
-    return taps - main, main + CORR_STEPS
+    if n_blocks <= 8:
+        return max(8, taps // 8 * 8)
+    return CORR_STEPS
+
+
+def corr_taps(padded_len, phases, steps):
+    taps = padded_len // phases + 1
+    main = taps // steps * steps
+    return taps - main, main + steps
 
 
 def polyphase_rows(signal, phases, total_rows):
@@ -155,8 +162,8 @@
 def correlate(placed, signal_rows, phases, lags):
     count, chans, padded_len = placed.shape
     n_blocks = signal_rows.shape[0]
-    steps = CORR_STEPS
-    extra_taps, span = corr_taps(padded_len, phases)
+    steps = corr_steps(padded_len, phases, n_blocks)
+    extra_taps, span = corr_taps(padded_len, phases, steps)
     taps = span - steps
     front = phases - 1
     n_groups = taps + extra_taps + 1
@@ -208,7 +215,7 @@
     ).astype(jnp.bfloat16)
     ordered_shift = jnp.sum(jnp.where(hit, offsets[:, :, None], 0), axis=1)
     placed = place_moveout(ordered, ordered_shift, padded_len)
-    _, span = corr_taps(padded_len, phases)
+    _, span = corr_taps(padded_len, phases, corr_steps(padded_len, phases, n_chan))
     signal = polyphase_rows(signal, phases, span + lags // phases)
     signal, placed = lax.optimization_barrier((signal, placed))
     if n_chan <= 8:

time: 57.7 us -> 57.4 us (level)
  no operation moved by 1% of the time
where the time goes in v18:
time: 57.4 us; the launch traced here: 57 us
  other arithmetic  17.7 us (31%)
  local copies, waits for them, and re-layouts  16.6 us (29%)
  Pallas kernels  10.9 us (19%)
  starting transfers between devices  7.91 us (14%)
  waiting for transfers between devices  3 us (5%)
    pallas_call x1, Pallas kernels, correlate(): pl.pallas_call(kernel, grid=(taps // steps,), in_specs=[pl.BlockSpec(grou...  10.9 us
    select_n x8, other arithmetic, place_moveout(): current = jnp.where(active[..., None], moved, current)  9.93 us
    reshape x2, local copies, waits for them, and re-layouts, correlate(): grouped = jnp.transpose(padded, (0, 2, 1)).reshape(count, n_groups, width)  8.25 us
    ppermute x3, starting transfers between devices, shards(): pieces.append(lax.ppermute(signal, 'chan', pairs))  6.12 us
    transpose x2, local copies, waits for them, and re-layouts, correlate(): grouped = jnp.transpose(padded, (0, 2, 1)).reshape(count, n_groups, width)  5.01 us
    ppermute x3, waiting for transfers between devices, shards(): stack = stack + lax.ppermute(outgoing, 'tmpl', pairs).astype(jnp.float32)  3 us
    ppermute x3, starting transfers between devices, shards(): stack = stack + lax.ppermute(outgoing, 'tmpl', pairs).astype(jnp.float32)  1.79 us
    reduce_sum x2, other arithmetic, normalize_rows(): scale = lax.rsqrt(jnp.mean(centred * centred, axis=-1, keepdims=True) + eps)  1.62 us
  transfers between devices with their start and end apart: 6, of which 2 were waited for; matrix products, arithmetic and copies ran while one was open for 25% of the time, Pallas kernels for 0%

profile of v18, /device:TPU:0, one launch (start us, length us, event | category | flops | bytes accessed | tf_op | source)
XLA Modules:
  0.0 57.0 jit_solution(14428231456401419741)
XLA Ops:
  0.0 0.0 copy-start
  0.0 1.1 %convert_reduce_fusion.1 = f32[32]{0:T(128)S(1)} fusion(bf16[32,1664]{1,0:T(8,128)(2,1)} %param.7), kind=kLoop, calls=%fused_computation.27 | loop fusion | flops 106464 | bytes 106624 | tf_op jit(solution)/shard_map/reduce_sum | solution.py:19
  1.1 1.1 %fusion.10 = f32[32]{0:T(128)S(1)} fusion(bf16[32,1664]{1,0:T(8,128)(2,1)} %param.7, f32[32]{0:T(128)S(1)} %broadcast_multiply_fusion.2), kind=kLoop, calls=%fused_computation.31 | loop fusion | flops 212960 | bytes 106752 | tf_op jit(solution)/shard_map/reduce_sum | solution.py:20
  2.2 1.0 %fusion.12 = bf16[1664,32]{0,1:T(8,128)(2,1)S(1)} fusion(bf16[32,1664]{1,0:T(8,128)(2,1)} %param.7, f32[32]{0:T(128)S(1)} %add_rsqrt_fusion.2, f32[32]{0:T(128)S(1)} %broadcast_multiply_fusion.2), kind=kLoop, calls=%fused_computation.33 | loop fusion | flops 212992 | bytes 213248 | tf_op jit(solution)/shard_map/transpose | solution.py:158
  3.2 0.3 copy.12
  3.5 0.0 copy-start.1
  3.5 0.3 reshape.175
  3.8 0.0 copy-done
  3.8 0.2 convert_reduce_fusion
  4.0 0.5 fusion.2
  4.6 0.0 copy-done.1
  4.6 0.5 convolution_convert_fusion
  5.1 0.0 copy-start.2
  5.2 0.1 pad_slice_fusion
  5.3 0.6 %copy-done.2 = s32[32,32]{1,0:T(8,128)S(1)} copy-done((s32[32,32]{1,0:T(8,128)S(1)}, s32[32,32]{1,0:T(8,128)}, u32[]{:S(2)}) %copy-start.2) | copy-done | bytes 4120
  5.9 0.6 %select_reduce_fusion.1 = s32[32,32]{1,0:T(8,128)S(1)} fusion(s32[32,32]{1,0:T(8,128)S(1)} %copy-done.2, s32[32,32]{1,0:T(8,128)S(1)} %add_select_fusion), kind=kLoop, calls=%fused_computation.24 | loop fusion | flops 97280 | bytes 12288 | tf_op jit(solution)/shard_map/reduce_sum | solution.py:216
  6.5 1.3 %pad_select_fusion.7 = bf16[32,32,640]{2,1,0:T(8,128)(2,1)S(1)} fusion(bf16[32,32,639]{2,1,0:T(8,128)(2,1)S(1)} %pad_slice_fusion, pred[32,32]{1,0:T(8,128)(4,1)S(1)} %get-tuple-element.25, bf16[32,32,512]{2,1,0:T(8,128)(2,1)S(1)} %convolution_convert_fusion), kind=kLoop, calls=%fused_computation.18 | loop fusion | flops 655360 | bytes 3668992 | tf_op jit(solution)/shard_map/jit(_where)/select_n | solution.py:33
  7.8 1.3 %pad_select_fusion.6 = bf16[32,32,640]{2,1,0:T(8,128)(2,1)S(1)} fusion(bf16[32,32,640]{2,1,0:T(8,128)(2,1)S(1)} %pad_select_fusion.7, bf16[32,32,638]{2,1,0:T(8,128)(2,1)S(1)} %bitcast.38, pred[32,32]{1,0:T(8,128)(4,1)S(1)} %get-tuple-element.26), kind=kLoop, calls=%fused_computation.17 | loop fusion | flops 655360 | bytes 3929088 | tf_op jit(solution)/shard_map/jit(_where)/select_n | solution.py:33
  9.2 1.3 %pad_select_fusion.5 = bf16[32,32,640]{2,1,0:T(8,128)(2,1)S(1)} fusion(bf16[32,32,640]{2,1,0:T(8,128)(2,1)S(1)} %pad_select_fusion.6, bf16[32,32,636]{2,1,0:T(8,128)(2,1)S(1)} %bitcast.39, pred[32,32]{1,0:T(8,128)(4,1)S(1)} %get-tuple-element.27), kind=kLoop, calls=%fused_computation.16 | loop fusion | flops 655360 | bytes 3924992 | tf_op jit(solution)/shard_map/jit(_where)/select_n | solution.py:33
  10.5 1.3 %pad_select_fusion.4 = bf16[32,32,640]{2,1,0:T(8,128)(2,1)S(1)} fusion(bf16[32,32,640]{2,1,0:T(8,128)(2,1)S(1)} %pad_select_fusion.5, bf16[32,32,632]{2,1,0:T(8,128)(2,1)S(1)} %bitcast.40, pred[32,32]{1,0:T(8,128)(4,1)S(1)} %get-tuple-element.28), kind=kLoop, calls=%fused_computation.15 | loop fusion | flops 655360 | bytes 3916800 | tf_op jit(solution)/shard_map/jit(_where)/select_n | solution.py:33
  11.9 1.3 %pad_select_fusion.3 = bf16[32,32,640]{2,1,0:T(8,128)(2,1)S(1)} fusion(bf16[32,32,640]{2,1,0:T(8,128)(2,1)S(1)} %pad_select_fusion.4, bf16[32,32,624]{2,1,0:T(8,128)(2,1)S(1)} %bitcast.41, pred[32,32]{1,0:T(8,128)(4,1)S(1)} %get-tuple-element.29), kind=kLoop, calls=%fused_computation.14 | loop fusion | flops 655360 | bytes 3900416 | tf_op jit(solution)/shard_map/jit(_where)/select_n | solution.py:33
  13.2 1.3 %pad_select_fusion.2 = bf16[32,32,640]{2,1,0:T(8,128)(2,1)S(1)} fusion(bf16[32,32,640]{2,1,0:T(8,128)(2,1)S(1)} %pad_select_fusion.3, bf16[32,32,608]{2,1,0:T(8,128)(2,1)S(1)} %bitcast.42, pred[32,32]{1,0:T(8,128)(4,1)S(1)} %get-tuple-element.30), kind=kLoop, calls=%fused_computation.13 | loop fusion | flops 655360 | bytes 3867648 | tf_op jit(solution)/shard_map/jit(_where)/select_n | solution.py:33
  14.6 1.3 %pad_select_fusion.1 = bf16[32,32,640]{2,1,0:T(8,128)(2,1)S(1)} fusion(bf16[32,32,640]{2,1,0:T(8,128)(2,1)S(1)} %pad_select_fusion.2, bf16[32,32,576]{2,1,0:T(8,128)(2,1)S(1)} %bitcast.43, pred[32,32]{1,0:T(8,128)(4,1)S(1)} %get-tuple-element.31), kind=kLoop, calls=%fused_computation.12 | loop fusion | flops 655360 | bytes 3802112 | tf_op jit(solution)/shard_map/jit(_where)/select_n | solution.py:33
  15.9 0.1 slice.53
  16.1 0.0 copy-start.3
  16.1 0.6 pad_select_fusion
  16.7 5.1 %collective-permute-start.2 = (bf16[288,256]{1,0:T(8,128)(2,1)S(1)}, bf16[288,256]{1,0:T(8,128)(2,1)S(1)}, u32[]{:S(2)}, u32[]{:S(2)}) collective-permute-start(bf16[288,256]{1,0:T(8,128)(2,1)S(1)} %pad.17), channel_id=1, source_target_pairs={{0,12},{4,0},{8,4},{12,8},{1,13},{5,1},{9,5},{13,9},{2,14},{6,2},{... | collective-permute-start | bytes 442376 | tf_op jit(solution)/shard_map/ppermute | solution.py:225
  21.8 0.0 collective-permute-start.1
  21.8 1.0 %collective-permute-start = (bf16[288,256]{1,0:T(8,128)(2,1)S(1)}, bf16[288,256]{1,0:T(8,128)(2,1)S(1)}, u32[]{:S(2)}, u32[]{:S(2)}) collective-permute-start(bf16[288,256]{1,0:T(8,128)(2,1)S(1)} %pad.17), channel_id=1, source_target_pairs={{0,4},{4,8},{8,12},{12,0},{1,5},{5,9},{9,13},{13,1},{2,6},{6,10},{... | collective-permute-start | bytes 442376 | tf_op jit(solution)/shard_map/ppermute | solution.py:225
  22.8 0.1 slice_reduce_fusion
  22.9 0.0 copy-done.3
  22.9 0.7 %scatter_custom_fusion = s32[32]{0:T(128)S(1)} fusion(s32[32]{0:T(128)S(1)} %fusion.15, s32[32]{0:T(128)S(1)} %iota.14, s32[]{:T(128)} %constant.103.clone.1), kind=kCustom, calls=%fused_computation.71 | custom fusion | bytes 132 | tf_op jit(solution)/shard_map/scatter | solution.py:237
  23.6 0.7 %pad_bitcast_fusion = bf16[32,656,32]{1,2,0:T(8,128)(2,1)S(1)} fusion(bf16[32,32,640]{2,1,0:T(8,128)(2,1)S(1)} %pad_select_fusion), kind=kLoop, calls=%fused_computation.8 | loop fusion | bytes 2654208 | tf_op jit(solution)/shard_map/transpose | solution.py:173
  24.4 4.3 %copy.13 = bf16[32,656,32]{2,1,0:T(8,128)(2,1)} copy(bf16[32,656,32]{1,2,0:T(8,128)(2,1)S(1)} %pad_bitcast_fusion) | data formatting | bytes 2686976 | tf_op jit(solution)/shard_map/transpose | solution.py:173
  28.7 6.9 %reshape.176 = bf16[32,82,256]{2,1,0:T(8,128)(2,1)S(1)} reshape(bf16[32,656,32]{2,1,0:T(8,128)(2,1)} %copy.13) | data formatting | bytes 2686976 | tf_op jit(solution)/shard_map/reshape | solution.py:173
  35.6 1.4 %copy.19 = bf16[32,82,256]{2,0,1:T(8,128)(2,1)} copy(bf16[32,82,256]{2,1,0:T(8,128)(2,1)S(1)} %reshape.176) | data formatting | bytes 2686976 | tf_op jit(solution)/shard_map/reshape | solution.py:173
  37.0 0.1 broadcast_in_dim.111
  37.1 0.0 collective-permute-done.2
  37.1 0.0 collective-permute-done.1
  37.1 0.0 collective-permute-done
  37.1 1.1 %maximum_convert_fusion.signal_ref = f32[4,288,256]{2,1,0:T(8,128)} fusion(bf16[1,288,256]{2,1,0:T(8,128)(2,1)S(1)} %bitcast.51, bf16[1,288,256]{2,1,0:T(8,128)(2,1)S(1)} %bitcast.52, bf16[1,288,256]{2,1,0:T(8,128)(2,1)S(1)} %bitcast.53, bf16[1,288,256]{2,1,0:T(8,128)(2,1)S(1)} %bitcast.46), kind=kLoop, calls=%fused_computation.22 | loop fusion | flops 1179648 | bytes 1769472 | tf_op jit(solution)/shard_map/convert_element_type | solution.py:175
  38.2 10.9 %shard_map.55 = f32[4,128,256]{2,1,0:T(8,128)} custom-call(bf16[82,32,256]{2,1,0:T(8,128)(2,1)} %bitcast.44, f32[4,288,256]{2,1,0:T(8,128)} %maximum_convert_fusion.signal_ref), custom_call_target="tpu_custom_call" | custom-call | tf_op jit(solution)/shard_map/pallas_call | solution.py:180
  49.2 1.1 %select_reduce_fusion = bf16[128,256]{1,0:T(8,128)(2,1)S(1)} fusion(f32[4,128,256]{2,1,0:T(8,128)} %shard_map.55, pred[4,256]{1,0:T(4,128)(4,1)S(1)} %broadcast_in_dim.111), kind=kLoop, calls=%fused_computation.23 | loop fusion | flops 229376 | bytes 590848 | tf_op jit(solution)/shard_map/reduce_sum | solution.py:233
  50.2 0.1 copy.15
  50.4 0.2 copy.16
  50.6 0.1 copy.17
  50.7 0.6 %gather_fusion = bf16[32,1024]{1,0:T(8,128)(2,1)S(1)} fusion(bf16[32,1024]{1,0:T(8,128)(2,1)S(1)} %copy.17, s32[1024]{0:T(1024)S(1)} %pad_clamp_fusion), kind=kCustom, calls=%fused_computation | custom fusion | bytes 131200 | tf_op jit(solution)/shard_map/gather | solution.py:239
  51.3 0.2 collective-permute-start.5
  51.5 1.5 %collective-permute-start.4 = (bf16[8,1024]{1,0:T(8,128)(2,1)S(1)}, bf16[8,1024]{1,0:T(8,128)(2,1)S(1)}, u32[]{:S(2)}, u32[]{:S(2)}) collective-permute-start(bf16[8,1024]{1,0:T(8,128)(2,1)S(1)} %get-tuple-element.23), channel_id=1, source_target_pairs={{0,2},{1,3},{2,0},{3,1},{4,6},{5,7},{6,4},{7,5},{8,10},{9,11},{10,... | collective-permute-start | bytes 49160 | tf_op jit(solution)/shard_map/ppermute | solution.py:246
  53.0 0.2 collective-permute-start.3
  53.1 0.0 collective-permute-done.5
  53.1 2.1 %collective-permute-done.4 = bf16[8,1024]{1,0:T(8,128)(2,1)S(1)} collective-permute-done((bf16[8,1024]{1,0:T(8,128)(2,1)S(1)}, bf16[8,1024]{1,0:T(8,128)(2,1)S(1)}, u32[]{:S(2)}, u32[]{:S(2)}) %collective-permute-start.4) | collective-permute-done | bytes 16416 | tf_op jit(solution)/shard_map/ppermute | solution.py:246
  55.2 0.9 %collective-permute-done.3 = bf16[8,1024]{1,0:T(8,128)(2,1)S(1)} collective-permute-done((bf16[8,1024]{1,0:T(8,128)(2,1)S(1)}, bf16[8,1024]{1,0:T(8,128)(2,1)S(1)}, u32[]{:S(2)}, u32[]{:S(2)}) %collective-permute-start.3) | collective-permute-done | bytes 16416 | tf_op jit(solution)/shard_map/ppermute | solution.py:246
  56.1 0.1 multiply_reduce_fusion
  56.3 0.7 %broadcast_multiply_fusion = f32[8,1024]{1,0:T(8,128)} fusion(f32[8]{0:T(128)S(1)} %add_rsqrt_fusion.1, bf16[8,1024]{1,0:T(8,128)(2,1)S(1)} %collective-permute-done.5, bf16[8,1024]{1,0:T(8,128)(2,1)S(1)} %collective-permute-done.4, bf16[8,1024]{1,0:T(8,128)(2,1)S(1)} %collective-permute-done.3, bf16[4,8,1024]{2,1,0:T(8,128)(2,1)S(1)} %bitcast.49, ...), kind=kLoop, calls=%fused_computation.43 | loop fusion | flops 73728 | bytes 98341 | tf_op jit(solution)/shard_map/mul | solution.py:251
  (15 shorter events, 0.2 us)
Async XLA Ops:
  0.0 3.8 %copy-start = (bf16[32,32,512]{2,1,0:T(8,128)(2,1)S(1)}, bf16[32,32,512]{2,1,0:T(8,128)(2,1)}, u32[]{:S(2)}) copy-start(bf16[32,32,512]{2,1,0:T(8,128)(2,1)} %param.8) | copy-start | bytes 3145732
  3.5 1.1 %copy-start.1 = (s32[32,32]{1,0:T(8,128)S(1)}, s32[32,32]{1,0:T(8,128)}, u32[]{:S(2)}) copy-start(s32[32,32]{1,0:T(8,128)} %param.9) | copy-start | bytes 12292
  5.1 0.7 %copy-start.2 = (s32[32,32]{1,0:T(8,128)S(1)}, s32[32,32]{1,0:T(8,128)}, u32[]{:S(2)}) copy-start(s32[32,32]{1,0:T(8,128)} %param.10) | copy-start | bytes 12292
  16.1 6.8 %copy-start.3 = (s32[1,32]{1,0:T(1,128)S(1)}, s32[1,32]{1,0:T(1,128)}, u32[]{:S(2)}) copy-start(s32[1,32]{1,0:T(1,128)} %param.11) | copy-start | bytes 388
  16.7 20.4 %collective-permute-start.2 = (bf16[288,256]{1,0:T(8,128)(2,1)S(1)}, bf16[288,256]{1,0:T(8,128)(2,1)S(1)}, u32[]{:S(2)}, u32[]{:S(2)}) collective-permute-start(bf16[288,256]{1,0:T(8,128)(2,1)S(1)} %pad.17), channel_id=1, source_target_pairs={{0,12},{4,0},{8,4},{12,8},{1,13},{5,1},{9,5},{13,9},{2,14},{6,2},{... | collective-permute-start | bytes 442376 | tf_op jit(solution)/shard_map/ppermute | solution.py:225
  21.8 15.3 %collective-permute-start.1 = (bf16[288,256]{1,0:T(8,128)(2,1)S(1)}, bf16[288,256]{1,0:T(8,128)(2,1)S(1)}, u32[]{:S(2)}, u32[]{:S(2)}) collective-permute-start(bf16[288,256]{1,0:T(8,128)(2,1)S(1)} %pad.17), channel_id=1, source_target_pairs={{0,8},{4,12},{8,0},{12,4},{1,9},{5,13},{9,1},{13,5},{2,10},{6,14},... | collective-permute-start | bytes 442376 | tf_op jit(solution)/shard_map/ppermute | solution.py:225
  21.8 15.3 %collective-permute-start = (bf16[288,256]{1,0:T(8,128)(2,1)S(1)}, bf16[288,256]{1,0:T(8,128)(2,1)S(1)}, u32[]{:S(2)}, u32[]{:S(2)}) collective-permute-start(bf16[288,256]{1,0:T(8,128)(2,1)S(1)} %pad.17), channel_id=1, source_target_pairs={{0,4},{4,8},{8,12},{12,0},{1,5},{5,9},{9,13},{13,1},{2,6},{6,10},{... | collective-permute-start | bytes 442376 | tf_op jit(solution)/shard_map/ppermute | solution.py:225
  51.3 1.8 %collective-permute-start.5 = (bf16[8,1024]{1,0:T(8,128)(2,1)S(1)}, bf16[8,1024]{1,0:T(8,128)(2,1)S(1)}, u32[]{:S(2)}, u32[]{:S(2)}) collective-permute-start(bf16[8,1024]{1,0:T(8,128)(2,1)S(1)} %get-tuple-element.22), channel_id=1, source_target_pairs={{0,3},{1,0},{2,1},{3,2},{4,7},{5,4},{6,5},{7,6},{8,11},{9,8},{10,9... | collective-permute-start | bytes 49160 | tf_op jit(solution)/shard_map/ppermute | solution.py:246
  51.5 3.7 %collective-permute-start.4 = (bf16[8,1024]{1,0:T(8,128)(2,1)S(1)}, bf16[8,1024]{1,0:T(8,128)(2,1)S(1)}, u32[]{:S(2)}, u32[]{:S(2)}) collective-permute-start(bf16[8,1024]{1,0:T(8,128)(2,1)S(1)} %get-tuple-element.23), channel_id=1, source_target_pairs={{0,2},{1,3},{2,0},{3,1},{4,6},{5,7},{6,4},{7,5},{8,10},{9,11},{10,... | collective-permute-start | bytes 49160 | tf_op jit(solution)/shard_map/ppermute | solution.py:246
  53.0 3.2 %collective-permute-start.3 = (bf16[8,1024]{1,0:T(8,128)(2,1)S(1)}, bf16[8,1024]{1,0:T(8,128)(2,1)S(1)}, u32[]{:S(2)}, u32[]{:S(2)}) collective-permute-start(bf16[8,1024]{1,0:T(8,128)(2,1)S(1)} %get-tuple-element.21), channel_id=1, source_target_pairs={{0,1},{1,2},{2,3},{3,0},{4,5},{5,6},{6,7},{7,4},{8,9},{9,10},{10,1... | collective-permute-start | bytes 49160 | tf_op jit(solution)/shard_map/ppermute | solution.py:246

commit v19 on v18

--- a/solution.py
+++ b/solution.py
@@ -216,7 +216,7 @@
     ordered_shift = jnp.sum(jnp.where(hit, offsets[:, :, None], 0), axis=1)
     placed = place_moveout(ordered, ordered_shift, padded_len)
     _, span = corr_taps(padded_len, phases, corr_steps(padded_len, phases, n_chan))
-    signal = polyphase_rows(signal, phases, span + lags // phases)
+    signal = polyphase_rows(signal, phases, span + lags // phases).astype(jnp.float32)
     signal, placed = lax.optimization_barrier((signal, placed))
     if n_chan <= 8:
         pieces = [signal]

time: 57.4 us -> 68.3 us (1.19)
  waiting for transfers between devices: 3 us -> 12.9 us
  other arithmetic: 17.7 us -> 18.7 us
    ppermute x3, waiting for transfers between devices: 0.01 us -> 9.92 us  [shards(): pieces.append(lax.ppermute(signal, 'chan', pairs))]
    another operation x0 -> x1, other arithmetic: none -> 2.18 us  [shards(): blocks = jnp.stack(pieces)]
    convert_element_type x1, other arithmetic: 1.14 us -> 0.02 us  [shards(): polyphase_rows(signal, phases, span + lags // phases).astype(jnp.float32)]
  transfers between devices with their start and end apart: 6 -> 6, of which waited for: 2 -> 3; matrix products, arithmetic and copies ran while one was open for 25% -> 21% of each run, Pallas kernels for 0% -> 0%
where the time goes in v19:
time: 68.3 us; the launch traced here: 67.9 us
  other arithmetic  18.7 us (27%)
  local copies, waits for them, and re-layouts  16.6 us (24%)
  waiting for transfers between devices  12.9 us (19%)
  Pallas kernels  10.9 us (16%)
  starting transfers between devices  7.91 us (12%)
    pallas_call x1, Pallas kernels, correlate(): pl.pallas_call(kernel, grid=(taps // steps,), in_specs=[pl.BlockSpec(grou...  10.9 us
    select_n x8, other arithmetic, place_moveout(): current = jnp.where(active[..., None], moved, current)  9.93 us
    ppermute x3, waiting for transfers between devices, shards(): pieces.append(lax.ppermute(signal, 'chan', pairs))  9.92 us
    reshape x2, local copies, waits for them, and re-layouts, correlate(): grouped = jnp.transpose(padded, (0, 2, 1)).reshape(count, n_groups, width)  8.25 us
    ppermute x3, starting transfers between devices, shards(): pieces.append(lax.ppermute(signal, 'chan', pairs))  6.12 us
    transpose x2, local copies, waits for them, and re-layouts, correlate(): grouped = jnp.transpose(padded, (0, 2, 1)).reshape(count, n_groups, width)  5.01 us
    ppermute x3, waiting for transfers between devices, shards(): stack = stack + lax.ppermute(outgoing, 'tmpl', pairs).astype(jnp.float32)  3 us
    another operation x1, other arithmetic, shards(): blocks = jnp.stack(pieces)  2.18 us
  transfers between devices with their start and end apart: 6, of which 3 were waited for; matrix products, arithmetic and copies ran while one was open for 21% of the time, Pallas kernels for 0%

profile of v19, /device:TPU:0, one launch (start us, length us, event | category | flops | bytes accessed | tf_op | source)
XLA Modules:
  0.0 67.9 jit_solution(13354925135887198314)
XLA Ops:
  0.0 0.0 copy-start
  0.0 1.1 %convert_reduce_fusion.1 = f32[32]{0:T(128)S(1)} fusion(bf16[32,1664]{1,0:T(8,128)(2,1)} %param.7), kind=kLoop, calls=%fused_computation.27 | loop fusion | flops 106464 | bytes 106624 | tf_op jit(solution)/shard_map/reduce_sum | solution.py:19
  1.1 1.1 %fusion.10 = f32[32]{0:T(128)S(1)} fusion(bf16[32,1664]{1,0:T(8,128)(2,1)} %param.7, f32[32]{0:T(128)S(1)} %broadcast_multiply_fusion.2), kind=kLoop, calls=%fused_computation.31 | loop fusion | flops 212960 | bytes 106752 | tf_op jit(solution)/shard_map/reduce_sum | solution.py:20
  2.2 1.0 %fusion.12 = bf16[1664,32]{0,1:T(8,128)(2,1)S(1)} fusion(bf16[32,1664]{1,0:T(8,128)(2,1)} %param.7, f32[32]{0:T(128)S(1)} %add_rsqrt_fusion.2, f32[32]{0:T(128)S(1)} %broadcast_multiply_fusion.2), kind=kLoop, calls=%fused_computation.34 | loop fusion | flops 212992 | bytes 213248 | tf_op jit(solution)/shard_map/transpose | solution.py:158
  3.2 0.3 copy.12
  3.5 0.3 reshape.175
  3.8 0.0 copy-start.1
  3.8 0.0 copy-done
  3.8 0.2 convert_reduce_fusion
  4.1 0.5 fusion.2
  4.6 0.0 copy-done.1
  4.6 0.5 convolution_convert_fusion
  5.2 0.0 copy-start.2
  5.2 0.1 pad_slice_fusion
  5.3 0.6 copy-done.2
  5.9 0.6 select_reduce_fusion.1
  6.6 1.3 %pad_select_fusion.7 = bf16[32,32,640]{2,1,0:T(8,128)(2,1)S(1)} fusion(bf16[32,32,639]{2,1,0:T(8,128)(2,1)S(1)} %pad_slice_fusion, pred[32,32]{1,0:T(8,128)(4,1)S(1)} %get-tuple-element.25, bf16[32,32,512]{2,1,0:T(8,128)(2,1)S(1)} %convolution_convert_fusion), kind=kLoop, calls=%fused_computation.18 | loop fusion | flops 655360 | bytes 3668992 | tf_op jit(solution)/shard_map/jit(_where)/select_n | solution.py:33
  7.9 1.3 %pad_select_fusion.6 = bf16[32,32,640]{2,1,0:T(8,128)(2,1)S(1)} fusion(bf16[32,32,640]{2,1,0:T(8,128)(2,1)S(1)} %pad_select_fusion.7, bf16[32,32,638]{2,1,0:T(8,128)(2,1)S(1)} %bitcast.38, pred[32,32]{1,0:T(8,128)(4,1)S(1)} %get-tuple-element.26), kind=kLoop, calls=%fused_computation.17 | loop fusion | flops 655360 | bytes 3929088 | tf_op jit(solution)/shard_map/jit(_where)/select_n | solution.py:33
  9.2 1.3 %pad_select_fusion.5 = bf16[32,32,640]{2,1,0:T(8,128)(2,1)S(1)} fusion(bf16[32,32,640]{2,1,0:T(8,128)(2,1)S(1)} %pad_select_fusion.6, bf16[32,32,636]{2,1,0:T(8,128)(2,1)S(1)} %bitcast.39, pred[32,32]{1,0:T(8,128)(4,1)S(1)} %get-tuple-element.27), kind=kLoop, calls=%fused_computation.16 | loop fusion | flops 655360 | bytes 3924992 | tf_op jit(solution)/shard_map/jit(_where)/select_n | solution.py:33
  10.6 1.3 %pad_select_fusion.4 = bf16[32,32,640]{2,1,0:T(8,128)(2,1)S(1)} fusion(bf16[32,32,640]{2,1,0:T(8,128)(2,1)S(1)} %pad_select_fusion.5, bf16[32,32,632]{2,1,0:T(8,128)(2,1)S(1)} %bitcast.40, pred[32,32]{1,0:T(8,128)(4,1)S(1)} %get-tuple-element.28), kind=kLoop, calls=%fused_computation.15 | loop fusion | flops 655360 | bytes 3916800 | tf_op jit(solution)/shard_map/jit(_where)/select_n | solution.py:33
  11.9 1.3 %pad_select_fusion.3 = bf16[32,32,640]{2,1,0:T(8,128)(2,1)S(1)} fusion(bf16[32,32,640]{2,1,0:T(8,128)(2,1)S(1)} %pad_select_fusion.4, bf16[32,32,624]{2,1,0:T(8,128)(2,1)S(1)} %bitcast.41, pred[32,32]{1,0:T(8,128)(4,1)S(1)} %get-tuple-element.29), kind=kLoop, calls=%fused_computation.14 | loop fusion | flops 655360 | bytes 3900416 | tf_op jit(solution)/shard_map/jit(_where)/select_n | solution.py:33
  13.3 1.3 %pad_select_fusion.2 = bf16[32,32,640]{2,1,0:T(8,128)(2,1)S(1)} fusion(bf16[32,32,640]{2,1,0:T(8,128)(2,1)S(1)} %pad_select_fusion.3, bf16[32,32,608]{2,1,0:T(8,128)(2,1)S(1)} %bitcast.42, pred[32,32]{1,0:T(8,128)(4,1)S(1)} %get-tuple-element.30), kind=kLoop, calls=%fused_computation.13 | loop fusion | flops 655360 | bytes 3867648 | tf_op jit(solution)/shard_map/jit(_where)/select_n | solution.py:33
  14.6 1.3 %pad_select_fusion.1 = bf16[32,32,640]{2,1,0:T(8,128)(2,1)S(1)} fusion(bf16[32,32,640]{2,1,0:T(8,128)(2,1)S(1)} %pad_select_fusion.2, bf16[32,32,576]{2,1,0:T(8,128)(2,1)S(1)} %bitcast.43, pred[32,32]{1,0:T(8,128)(4,1)S(1)} %get-tuple-element.31), kind=kLoop, calls=%fused_computation.12 | loop fusion | flops 655360 | bytes 3802112 | tf_op jit(solution)/shard_map/jit(_where)/select_n | solution.py:33
  16.0 0.1 slice.53
  16.1 0.6 pad_select_fusion
  16.7 5.1 %collective-permute-start.2 = (f32[288,256]{1,0:T(8,128)S(1)}, f32[288,256]{1,0:T(8,128)S(1)}, u32[]{:S(2)}, u32[]{:S(2)}) collective-permute-start(f32[288,256]{1,0:T(8,128)S(1)} %pad_convert_fusion), channel_id=1, source_target_pairs={{0,12},{4,0},{8,4},{12,8},{1,13},{5,1},{9,5},{13,9},{2,14},{6,2},{... | collective-permute-start | bytes 884744 | tf_op jit(solution)/shard_map/ppermute | solution.py:225
  21.8 0.0 collective-permute-start.1
  21.8 1.0 %collective-permute-start = (f32[288,256]{1,0:T(8,128)S(1)}, f32[288,256]{1,0:T(8,128)}, u32[]{:S(2)}, u32[]{:S(2)}) collective-permute-start(f32[288,256]{1,0:T(8,128)S(1)} %pad_convert_fusion), channel_id=1, source_target_pairs={{0,4},{4,8},{8,12},{12,0},{1,5},{5,9},{9,13},{13,1},{2,6},{6,10},{... | collective-permute-start | bytes 884744 | tf_op jit(solution)/shard_map/ppermute | solution.py:225
  22.8 0.1 slice_reduce_fusion
  22.9 0.7 %pad_bitcast_fusion = bf16[32,656,32]{1,2,0:T(8,128)(2,1)S(1)} fusion(bf16[32,32,640]{2,1,0:T(8,128)(2,1)S(1)} %pad_select_fusion), kind=kLoop, calls=%fused_computation.8 | loop fusion | bytes 2654208 | tf_op jit(solution)/shard_map/transpose | solution.py:173
  23.7 4.3 %copy.13 = bf16[32,656,32]{2,1,0:T(8,128)(2,1)} copy(bf16[32,656,32]{1,2,0:T(8,128)(2,1)S(1)} %pad_bitcast_fusion) | data formatting | bytes 2686976 | tf_op jit(solution)/shard_map/transpose | solution.py:173
  28.0 6.9 %reshape.176 = bf16[32,82,256]{2,1,0:T(8,128)(2,1)S(1)} reshape(bf16[32,656,32]{2,1,0:T(8,128)(2,1)} %copy.13) | data formatting | bytes 2686976 | tf_op jit(solution)/shard_map/reshape | solution.py:173
  34.8 0.0 copy-start.3
  34.8 1.4 %copy.19 = bf16[32,82,256]{2,0,1:T(8,128)(2,1)} copy(bf16[32,82,256]{2,1,0:T(8,128)(2,1)S(1)} %reshape.176) | data formatting | bytes 2686976 | tf_op jit(solution)/shard_map/reshape | solution.py:173
  36.2 0.0 copy-done.3
  36.2 0.7 scatter_custom_fusion
  37.0 0.1 broadcast_in_dim.111
  37.1 0.0 collective-permute-done.2
  37.1 9.9 %collective-permute-done.1 = f32[288,256]{1,0:T(8,128)} collective-permute-done((f32[288,256]{1,0:T(8,128)S(1)}, f32[288,256]{1,0:T(8,128)}, u32[]{:S(2)}, u32[]{:S(2)}) %collective-permute-start.1) | collective-permute-done | bytes 294944 | tf_op jit(solution)/shard_map/ppermute | solution.py:225
  47.0 0.0 collective-permute-done
  47.0 2.2 %pad_maximum_fusion.signal_ref = f32[4,288,256]{2,1,0:T(8,128)} fusion(f32[1,288,256]{2,1,0:T(8,128)S(1)} %bitcast.50, f32[1,288,256]{2,1,0:T(8,128)} %bitcast.5, f32[1,288,256]{2,1,0:T(8,128)} %bitcast.4, f32[1,288,256]{2,1,0:T(8,128)S(1)} %bitcast.45), kind=kLoop, calls=%fused_computation.20 | loop fusion | flops 884736 | bytes 2359296 | tf_op jit(solution)/shard_map/stack | solution.py:226
  49.2 10.9 %shard_map.55 = f32[4,128,256]{2,1,0:T(8,128)} custom-call(bf16[82,32,256]{2,1,0:T(8,128)(2,1)} %bitcast.44, f32[4,288,256]{2,1,0:T(8,128)} %pad_maximum_fusion.signal_ref), custom_call_target="tpu_custom_call" | custom-call | tf_op jit(solution)/shard_map/pallas_call | solution.py:180
  60.1 1.1 %select_reduce_fusion = bf16[128,256]{1,0:T(8,128)(2,1)S(1)} fusion(f32[4,128,256]{2,1,0:T(8,128)} %shard_map.55, pred[4,256]{1,0:T(4,128)(4,1)S(1)} %broadcast_in_dim.111), kind=kLoop, calls=%fused_computation.23 | loop fusion | flops 229376 | bytes 590848 | tf_op jit(solution)/shard_map/reduce_sum | solution.py:233
  61.2 0.1 copy.15
  61.3 0.2 copy.16
  61.5 0.1 copy.17
  61.6 0.6 gather_fusion
  62.3 0.1 collective-permute-start.5
  62.4 1.5 %collective-permute-start.4 = (bf16[8,1024]{1,0:T(8,128)(2,1)S(1)}, bf16[8,1024]{1,0:T(8,128)(2,1)S(1)}, u32[]{:S(2)}, u32[]{:S(2)}) collective-permute-start(bf16[8,1024]{1,0:T(8,128)(2,1)S(1)} %get-tuple-element.23), channel_id=1, source_target_pairs={{0,2},{1,3},{2,0},{3,1},{4,6},{5,7},{6,4},{7,5},{8,10},{9,11},{10,... | collective-permute-start | bytes 49160 | tf_op jit(solution)/shard_map/ppermute | solution.py:246
  63.9 0.2 collective-permute-start.3
  64.1 0.0 collective-permute-done.5
  64.1 2.1 %collective-permute-done.4 = bf16[8,1024]{1,0:T(8,128)(2,1)S(1)} collective-permute-done((bf16[8,1024]{1,0:T(8,128)(2,1)S(1)}, bf16[8,1024]{1,0:T(8,128)(2,1)S(1)}, u32[]{:S(2)}, u32[]{:S(2)}) %collective-permute-start.4) | collective-permute-done | bytes 16416 | tf_op jit(solution)/shard_map/ppermute | solution.py:246
  66.1 0.9 %collective-permute-done.3 = bf16[8,1024]{1,0:T(8,128)(2,1)S(1)} collective-permute-done((bf16[8,1024]{1,0:T(8,128)(2,1)S(1)}, bf16[8,1024]{1,0:T(8,128)(2,1)S(1)}, u32[]{:S(2)}, u32[]{:S(2)}) %collective-permute-start.3) | collective-permute-done | bytes 16416 | tf_op jit(solution)/shard_map/ppermute | solution.py:246
  67.1 0.1 multiply_reduce_fusion
  67.2 0.7 %broadcast_multiply_fusion = f32[8,1024]{1,0:T(8,128)} fusion(f32[8]{0:T(128)S(1)} %add_rsqrt_fusion.1, bf16[8,1024]{1,0:T(8,128)(2,1)S(1)} %collective-permute-done.5, bf16[8,1024]{1,0:T(8,128)(2,1)S(1)} %collective-permute-done.4, bf16[8,1024]{1,0:T(8,128)(2,1)S(1)} %collective-permute-done.3, bf16[4,8,1024]{2,1,0:T(8,128)(2,1)S(1)} %bitcast.49, ...), kind=kLoop, calls=%fused_computation.44 | loop fusion | flops 73728 | bytes 98341 | tf_op jit(solution)/shard_map/mul | solution.py:251
  (15 shorter events, 0.2 us)
Async XLA Ops:
  0.0 3.8 %copy-start = (bf16[32,32,512]{2,1,0:T(8,128)(2,1)S(1)}, bf16[32,32,512]{2,1,0:T(8,128)(2,1)}, u32[]{:S(2)}) copy-start(bf16[32,32,512]{2,1,0:T(8,128)(2,1)} %param.8) | copy-start | bytes 3145732
  3.8 0.8 %copy-start.1 = (s32[32,32]{1,0:T(8,128)S(1)}, s32[32,32]{1,0:T(8,128)}, u32[]{:S(2)}) copy-start(s32[32,32]{1,0:T(8,128)} %param.9) | copy-start | bytes 12292
  5.2 0.7 %copy-start.2 = (s32[32,32]{1,0:T(8,128)S(1)}, s32[32,32]{1,0:T(8,128)}, u32[]{:S(2)}) copy-start(s32[32,32]{1,0:T(8,128)} %param.10) | copy-start | bytes 12292
  16.7 20.4 %collective-permute-start.2 = (f32[288,256]{1,0:T(8,128)S(1)}, f32[288,256]{1,0:T(8,128)S(1)}, u32[]{:S(2)}, u32[]{:S(2)}) collective-permute-start(f32[288,256]{1,0:T(8,128)S(1)} %pad_convert_fusion), channel_id=1, source_target_pairs={{0,12},{4,0},{8,4},{12,8},{1,13},{5,1},{9,5},{13,9},{2,14},{6,2},{... | collective-permute-start | bytes 884744 | tf_op jit(solution)/shard_map/ppermute | solution.py:225
  21.8 25.2 %collective-permute-start.1 = (f32[288,256]{1,0:T(8,128)S(1)}, f32[288,256]{1,0:T(8,128)}, u32[]{:S(2)}, u32[]{:S(2)}) collective-permute-start(f32[288,256]{1,0:T(8,128)S(1)} %pad_convert_fusion), channel_id=1, source_target_pairs={{0,8},{4,12},{8,0},{12,4},{1,9},{5,13},{9,1},{13,5},{2,10},{6,14},... | collective-permute-start | bytes 884744 | tf_op jit(solution)/shard_map/ppermute | solution.py:225
  21.8 25.2 %collective-permute-start = (f32[288,256]{1,0:T(8,128)S(1)}, f32[288,256]{1,0:T(8,128)}, u32[]{:S(2)}, u32[]{:S(2)}) collective-permute-start(f32[288,256]{1,0:T(8,128)S(1)} %pad_convert_fusion), channel_id=1, source_target_pairs={{0,4},{4,8},{8,12},{12,0},{1,5},{5,9},{9,13},{13,1},{2,6},{6,10},{... | collective-permute-start | bytes 884744 | tf_op jit(solution)/shard_map/ppermute | solution.py:225
  34.8 1.4 %copy-start.3 = (s32[1,32]{1,0:T(1,128)S(1)}, s32[1,32]{1,0:T(1,128)}, u32[]{:S(2)}) copy-start(s32[1,32]{1,0:T(1,128)} %param.11) | copy-start | bytes 388
  62.3 1.8 %collective-permute-start.5 = (bf16[8,1024]{1,0:T(8,128)(2,1)S(1)}, bf16[8,1024]{1,0:T(8,128)(2,1)S(1)}, u32[]{:S(2)}, u32[]{:S(2)}) collective-permute-start(bf16[8,1024]{1,0:T(8,128)(2,1)S(1)} %get-tuple-element.22), channel_id=1, source_target_pairs={{0,3},{1,0},{2,1},{3,2},{4,7},{5,4},{6,5},{7,6},{8,11},{9,8},{10,9... | collective-permute-start | bytes 49160 | tf_op jit(solution)/shard_map/ppermute | solution.py:246
  62.4 3.8 %collective-permute-start.4 = (bf16[8,1024]{1,0:T(8,128)(2,1)S(1)}, bf16[8,1024]{1,0:T(8,128)(2,1)S(1)}, u32[]{:S(2)}, u32[]{:S(2)}) collective-permute-start(bf16[8,1024]{1,0:T(8,128)(2,1)S(1)} %get-tuple-element.23), channel_id=1, source_target_pairs={{0,2},{1,3},{2,0},{3,1},{4,6},{5,7},{6,4},{7,5},{8,10},{9,11},{10,... | collective-permute-start | bytes 49160 | tf_op jit(solution)/shard_map/ppermute | solution.py:246
  63.9 3.2 %collective-permute-start.3 = (bf16[8,1024]{1,0:T(8,128)(2,1)S(1)}, bf16[8,1024]{1,0:T(8,128)(2,1)S(1)}, u32[]{:S(2)}, u32[]{:S(2)}) collective-permute-start(bf16[8,1024]{1,0:T(8,128)(2,1)S(1)} %get-tuple-element.21), channel_id=1, source_target_pairs={{0,1},{1,2},{2,3},{3,0},{4,5},{5,6},{6,7},{7,4},{8,9},{9,10},{10,1... | collective-permute-start | bytes 49160 | tf_op jit(solution)/shard_map/ppermute | solution.py:246

commit v20 on v19

--- a/solution.py
+++ b/solution.py
@@ -113,6 +113,7 @@
 
     @pl.when(pid == pl.num_programs(0) - 1)
     def _():
+        tail_rows = -(-extra_taps // 8) * 8
         for extra in range(extra_taps):
             q = (pid + 1) * steps + extra
             joined = jnp.concatenate([grouped_ref[q], grouped_ref[q + 1]], axis=-1)
@@ -126,7 +127,7 @@
             start = pl.multiple_of((pid + 1) * steps, steps)
 
             def tail(g, carry):
-                window = signal_ref[g, pl.ds(start, rows + steps), :][extra : extra + rows]
+                window = signal_ref[g, pl.ds(start, rows + tail_rows), :][extra : extra + rows]
                 lo = pl.multiple_of(g * rows, rows)
                 acc_ref[pl.ds(lo, rows), :] += jnp.dot(
                     window.astype(filt.dtype), filt, preferred_element_type=jnp.float32
@@ -215,8 +216,10 @@
     ).astype(jnp.bfloat16)
     ordered_shift = jnp.sum(jnp.where(hit, offsets[:, :, None], 0), axis=1)
     placed = place_moveout(ordered, ordered_shift, padded_len)
-    _, span = corr_taps(padded_len, phases, corr_steps(padded_len, phases, n_chan))
-    signal = polyphase_rows(signal, phases, span + lags // phases).astype(jnp.float32)
+    steps = corr_steps(padded_len, phases, n_chan)
+    extra, span = corr_taps(padded_len, phases, steps)
+    total_rows = span - steps + lags // phases + -(-extra // 8) * 8
+    signal = polyphase_rows(signal, phases, total_rows)
     signal, placed = lax.optimization_barrier((signal, placed))
     if n_chan <= 8:
         pieces = [signal]

time: 68.3 us -> 57.2 us (0.84)
  waiting for transfers between devices: 12.9 us -> 3 us
  other arithmetic: 18.7 us -> 17.6 us
    ppermute x3, waiting for transfers between devices: 9.92 us -> 0.01 us  [shards(): pieces.append(lax.ppermute(signal, 'chan', pairs))]
    another operation x1 -> x0, other arithmetic: 2.18 us -> none  [shards(): blocks = jnp.stack(pieces)]
    convert_element_type x1, other arithmetic: 0.02 us -> 1.05 us  [correlate(): signal = signal_rows.astype(jnp.float32)]
  transfers between devices with their start and end apart: 6 -> 6, of which waited for: 3 -> 2; matrix products, arithmetic and copies ran while one was open for 21% -> 25% of each run, Pallas kernels for 0% -> 0%
where the time goes in v20:
time: 57.2 us; the launch traced here: 56.7 us
  other arithmetic  17.6 us (31%)
  local copies, waits for them, and re-layouts  16.6 us (29%)
  Pallas kernels  10.8 us (19%)
  starting transfers between devices  7.9 us (14%)
  waiting for transfers between devices  3 us (5%)
    pallas_call x1, Pallas kernels, correlate(): pl.pallas_call(kernel, grid=(taps // steps,), in_specs=[pl.BlockSpec(grou...  10.8 us
    select_n x8, other arithmetic, place_moveout(): current = jnp.where(active[..., None], moved, current)  9.93 us
    reshape x2, local copies, waits for them, and re-layouts, correlate(): grouped = jnp.transpose(padded, (0, 2, 1)).reshape(count, n_groups, width)  8.25 us
    ppermute x3, starting transfers between devices, shards(): pieces.append(lax.ppermute(signal, 'chan', pairs))  6.12 us
    transpose x2, local copies, waits for them, and re-layouts, correlate(): grouped = jnp.transpose(padded, (0, 2, 1)).reshape(count, n_groups, width)  5.01 us
    ppermute x3, waiting for transfers between devices, shards(): stack = stack + lax.ppermute(outgoing, 'tmpl', pairs).astype(jnp.float32)  3 us
    ppermute x3, starting transfers between devices, shards(): stack = stack + lax.ppermute(outgoing, 'tmpl', pairs).astype(jnp.float32)  1.78 us
    reduce_sum x2, other arithmetic, normalize_rows(): scale = lax.rsqrt(jnp.mean(centred * centred, axis=-1, keepdims=True) + eps)  1.62 us
  transfers between devices with their start and end apart: 6, of which 2 were waited for; matrix products, arithmetic and copies ran while one was open for 25% of the time, Pallas kernels for 0%

profile of v20, /device:TPU:0, one launch (start us, length us, event | category | flops | bytes accessed | tf_op | source)
XLA Modules:
  0.0 56.7 jit_solution(2462511180814672233)
XLA Ops:
  0.0 0.0 copy-start
  0.0 1.1 %convert_reduce_fusion.1 = f32[32]{0:T(128)S(1)} fusion(bf16[32,1664]{1,0:T(8,128)(2,1)} %param.7), kind=kLoop, calls=%fused_computation.27 | loop fusion | flops 106464 | bytes 106624 | tf_op jit(solution)/shard_map/reduce_sum | solution.py:19
  1.1 1.1 %fusion.10 = f32[32]{0:T(128)S(1)} fusion(bf16[32,1664]{1,0:T(8,128)(2,1)} %param.7, f32[32]{0:T(128)S(1)} %broadcast_multiply_fusion.2), kind=kLoop, calls=%fused_computation.31 | loop fusion | flops 212960 | bytes 106752 | tf_op jit(solution)/shard_map/reduce_sum | solution.py:20
  2.2 1.0 %fusion.12 = bf16[1664,32]{0,1:T(8,128)(2,1)S(1)} fusion(bf16[32,1664]{1,0:T(8,128)(2,1)} %param.7, f32[32]{0:T(128)S(1)} %add_rsqrt_fusion.2, f32[32]{0:T(128)S(1)} %broadcast_multiply_fusion.2), kind=kLoop, calls=%fused_computation.33 | loop fusion | flops 212992 | bytes 213248 | tf_op jit(solution)/shard_map/transpose | solution.py:159
  3.2 0.3 copy.12
  3.5 0.0 copy-start.1
  3.5 0.3 reshape.175
  3.8 0.0 copy-done
  3.8 0.2 convert_reduce_fusion
  4.0 0.5 fusion.2
  4.6 0.0 copy-done.1
  4.6 0.5 convolution_convert_fusion
  5.1 0.0 copy-start.2
  5.2 0.1 pad_slice_fusion
  5.3 0.6 %copy-done.2 = s32[32,32]{1,0:T(8,128)S(1)} copy-done((s32[32,32]{1,0:T(8,128)S(1)}, s32[32,32]{1,0:T(8,128)}, u32[]{:S(2)}) %copy-start.2) | copy-done | bytes 4120
  5.9 0.6 %select_reduce_fusion.1 = s32[32,32]{1,0:T(8,128)S(1)} fusion(s32[32,32]{1,0:T(8,128)S(1)} %copy-done.2, s32[32,32]{1,0:T(8,128)S(1)} %add_select_fusion), kind=kLoop, calls=%fused_computation.23 | loop fusion | flops 97280 | bytes 12288 | tf_op jit(solution)/shard_map/reduce_sum | solution.py:217
  6.5 1.3 %pad_select_fusion.7 = bf16[32,32,640]{2,1,0:T(8,128)(2,1)S(1)} fusion(bf16[32,32,639]{2,1,0:T(8,128)(2,1)S(1)} %pad_slice_fusion, pred[32,32]{1,0:T(8,128)(4,1)S(1)} %get-tuple-element.25, bf16[32,32,512]{2,1,0:T(8,128)(2,1)S(1)} %convolution_convert_fusion), kind=kLoop, calls=%fused_computation.18 | loop fusion | flops 655360 | bytes 3668992 | tf_op jit(solution)/shard_map/jit(_where)/select_n | solution.py:33
  7.8 1.3 %pad_select_fusion.6 = bf16[32,32,640]{2,1,0:T(8,128)(2,1)S(1)} fusion(bf16[32,32,640]{2,1,0:T(8,128)(2,1)S(1)} %pad_select_fusion.7, bf16[32,32,638]{2,1,0:T(8,128)(2,1)S(1)} %bitcast.38, pred[32,32]{1,0:T(8,128)(4,1)S(1)} %get-tuple-element.26), kind=kLoop, calls=%fused_computation.17 | loop fusion | flops 655360 | bytes 3929088 | tf_op jit(solution)/shard_map/jit(_where)/select_n | solution.py:33
  9.2 1.3 %pad_select_fusion.5 = bf16[32,32,640]{2,1,0:T(8,128)(2,1)S(1)} fusion(bf16[32,32,640]{2,1,0:T(8,128)(2,1)S(1)} %pad_select_fusion.6, bf16[32,32,636]{2,1,0:T(8,128)(2,1)S(1)} %bitcast.39, pred[32,32]{1,0:T(8,128)(4,1)S(1)} %get-tuple-element.27), kind=kLoop, calls=%fused_computation.16 | loop fusion | flops 655360 | bytes 3924992 | tf_op jit(solution)/shard_map/jit(_where)/select_n | solution.py:33
  10.5 1.3 %pad_select_fusion.4 = bf16[32,32,640]{2,1,0:T(8,128)(2,1)S(1)} fusion(bf16[32,32,640]{2,1,0:T(8,128)(2,1)S(1)} %pad_select_fusion.5, bf16[32,32,632]{2,1,0:T(8,128)(2,1)S(1)} %bitcast.40, pred[32,32]{1,0:T(8,128)(4,1)S(1)} %get-tuple-element.28), kind=kLoop, calls=%fused_computation.15 | loop fusion | flops 655360 | bytes 3916800 | tf_op jit(solution)/shard_map/jit(_where)/select_n | solution.py:33
  11.9 1.3 %pad_select_fusion.3 = bf16[32,32,640]{2,1,0:T(8,128)(2,1)S(1)} fusion(bf16[32,32,640]{2,1,0:T(8,128)(2,1)S(1)} %pad_select_fusion.4, bf16[32,32,624]{2,1,0:T(8,128)(2,1)S(1)} %bitcast.41, pred[32,32]{1,0:T(8,128)(4,1)S(1)} %get-tuple-element.29), kind=kLoop, calls=%fused_computation.14 | loop fusion | flops 655360 | bytes 3900416 | tf_op jit(solution)/shard_map/jit(_where)/select_n | solution.py:33
  13.2 1.3 %pad_select_fusion.2 = bf16[32,32,640]{2,1,0:T(8,128)(2,1)S(1)} fusion(bf16[32,32,640]{2,1,0:T(8,128)(2,1)S(1)} %pad_select_fusion.3, bf16[32,32,608]{2,1,0:T(8,128)(2,1)S(1)} %bitcast.42, pred[32,32]{1,0:T(8,128)(4,1)S(1)} %get-tuple-element.30), kind=kLoop, calls=%fused_computation.13 | loop fusion | flops 655360 | bytes 3867648 | tf_op jit(solution)/shard_map/jit(_where)/select_n | solution.py:33
  14.6 1.3 %pad_select_fusion.1 = bf16[32,32,640]{2,1,0:T(8,128)(2,1)S(1)} fusion(bf16[32,32,640]{2,1,0:T(8,128)(2,1)S(1)} %pad_select_fusion.2, bf16[32,32,576]{2,1,0:T(8,128)(2,1)S(1)} %bitcast.43, pred[32,32]{1,0:T(8,128)(4,1)S(1)} %get-tuple-element.31), kind=kLoop, calls=%fused_computation.12 | loop fusion | flops 655360 | bytes 3802112 | tf_op jit(solution)/shard_map/jit(_where)/select_n | solution.py:33
  15.9 0.1 slice.53
  16.1 0.6 pad_select_fusion
  16.6 5.1 %collective-permute-start.2 = (bf16[216,256]{1,0:T(8,128)(2,1)S(1)}, bf16[216,256]{1,0:T(8,128)(2,1)S(1)}, u32[]{:S(2)}, u32[]{:S(2)}) collective-permute-start(bf16[216,256]{1,0:T(8,128)(2,1)S(1)} %pad.17), channel_id=1, source_target_pairs={{0,12},{4,0},{8,4},{12,8},{1,13},{5,1},{9,5},{13,9},{2,14},{6,2},{... | collective-permute-start | bytes 331784 | tf_op jit(solution)/shard_map/ppermute | solution.py:228
  21.7 0.0 collective-permute-start.1
  21.7 1.0 %collective-permute-start = (bf16[216,256]{1,0:T(8,128)(2,1)S(1)}, bf16[216,256]{1,0:T(8,128)(2,1)S(1)}, u32[]{:S(2)}, u32[]{:S(2)}) collective-permute-start(bf16[216,256]{1,0:T(8,128)(2,1)S(1)} %pad.17), channel_id=1, source_target_pairs={{0,4},{4,8},{8,12},{12,0},{1,5},{5,9},{9,13},{13,1},{2,6},{6,10},{... | collective-permute-start | bytes 331784 | tf_op jit(solution)/shard_map/ppermute | solution.py:228
  22.8 0.1 slice_reduce_fusion
  22.9 0.7 %pad_bitcast_fusion = bf16[32,656,32]{1,2,0:T(8,128)(2,1)S(1)} fusion(bf16[32,32,640]{2,1,0:T(8,128)(2,1)S(1)} %pad_select_fusion), kind=kLoop, calls=%fused_computation.8 | loop fusion | bytes 2654208 | tf_op jit(solution)/shard_map/transpose | solution.py:174
  23.7 4.3 %copy.13 = bf16[32,656,32]{2,1,0:T(8,128)(2,1)} copy(bf16[32,656,32]{1,2,0:T(8,128)(2,1)S(1)} %pad_bitcast_fusion) | data formatting | bytes 2686976 | tf_op jit(solution)/shard_map/transpose | solution.py:174
  27.9 6.9 %reshape.176 = bf16[32,82,256]{2,1,0:T(8,128)(2,1)S(1)} reshape(bf16[32,656,32]{2,1,0:T(8,128)(2,1)} %copy.13) | data formatting | bytes 2686976 | tf_op jit(solution)/shard_map/reshape | solution.py:174
  34.8 0.0 copy-start.3
  34.8 1.4 %copy.19 = bf16[32,82,256]{2,0,1:T(8,128)(2,1)} copy(bf16[32,82,256]{2,1,0:T(8,128)(2,1)S(1)} %reshape.176) | data formatting | bytes 2686976 | tf_op jit(solution)/shard_map/reshape | solution.py:174
  36.2 0.0 copy-done.3
  36.2 0.7 %scatter_custom_fusion = s32[32]{0:T(128)S(1)} fusion(s32[32]{0:T(128)S(1)} %fusion.15, s32[32]{0:T(128)S(1)} %iota.14, s32[]{:T(128)} %constant.103.clone.1), kind=kCustom, calls=%fused_computation.71 | custom fusion | bytes 132 | tf_op jit(solution)/shard_map/scatter | solution.py:240
  36.9 0.1 broadcast_in_dim.111
  37.0 0.0 collective-permute-done.2
  37.1 0.0 collective-permute-done.1
  37.1 0.0 collective-permute-done
  37.1 1.0 %maximum_convert_fusion.signal_ref = f32[4,216,256]{2,1,0:T(8,128)} fusion(bf16[1,216,256]{2,1,0:T(8,128)(2,1)S(1)} %bitcast.51, bf16[1,216,256]{2,1,0:T(8,128)(2,1)S(1)} %bitcast.52, bf16[1,216,256]{2,1,0:T(8,128)(2,1)S(1)} %bitcast.53, bf16[1,216,256]{2,1,0:T(8,128)(2,1)S(1)} %bitcast.46), kind=kLoop, calls=%fused_computation.25 | loop fusion | flops 884736 | bytes 1327104 | tf_op jit(solution)/shard_map/convert_element_type | solution.py:176
  38.1 10.8 %shard_map.55 = f32[4,128,256]{2,1,0:T(8,128)} custom-call(bf16[82,32,256]{2,1,0:T(8,128)(2,1)} %bitcast.44, f32[4,216,256]{2,1,0:T(8,128)} %maximum_convert_fusion.signal_ref), custom_call_target="tpu_custom_call" | custom-call | tf_op jit(solution)/shard_map/pallas_call | solution.py:181
  48.9 1.1 %select_reduce_fusion = bf16[128,256]{1,0:T(8,128)(2,1)S(1)} fusion(f32[4,128,256]{2,1,0:T(8,128)} %shard_map.55, pred[4,256]{1,0:T(4,128)(4,1)S(1)} %broadcast_in_dim.111), kind=kLoop, calls=%fused_computation.22 | loop fusion | flops 229376 | bytes 590848 | tf_op jit(solution)/shard_map/reduce_sum | solution.py:236
  50.0 0.1 copy.15
  50.1 0.2 copy.16
  50.3 0.1 copy.17
  50.5 0.6 %gather_fusion = bf16[32,1024]{1,0:T(8,128)(2,1)S(1)} fusion(bf16[32,1024]{1,0:T(8,128)(2,1)S(1)} %copy.17, s32[1024]{0:T(1024)S(1)} %pad_clamp_fusion), kind=kCustom, calls=%fused_computation | custom fusion | bytes 131200 | tf_op jit(solution)/shard_map/gather | solution.py:242
  51.1 0.1 collective-permute-start.5
  51.3 1.5 %collective-permute-start.4 = (bf16[8,1024]{1,0:T(8,128)(2,1)S(1)}, bf16[8,1024]{1,0:T(8,128)(2,1)S(1)}, u32[]{:S(2)}, u32[]{:S(2)}) collective-permute-start(bf16[8,1024]{1,0:T(8,128)(2,1)S(1)} %get-tuple-element.23), channel_id=1, source_target_pairs={{0,2},{1,3},{2,0},{3,1},{4,6},{5,7},{6,4},{7,5},{8,10},{9,11},{10,... | collective-permute-start | bytes 49160 | tf_op jit(solution)/shard_map/ppermute | solution.py:249
  52.7 0.2 collective-permute-start.3
  52.9 0.0 collective-permute-done.5
  52.9 2.1 %collective-permute-done.4 = bf16[8,1024]{1,0:T(8,128)(2,1)S(1)} collective-permute-done((bf16[8,1024]{1,0:T(8,128)(2,1)S(1)}, bf16[8,1024]{1,0:T(8,128)(2,1)S(1)}, u32[]{:S(2)}, u32[]{:S(2)}) %collective-permute-start.4) | collective-permute-done | bytes 16416 | tf_op jit(solution)/shard_map/ppermute | solution.py:249
  55.0 0.9 %collective-permute-done.3 = bf16[8,1024]{1,0:T(8,128)(2,1)S(1)} collective-permute-done((bf16[8,1024]{1,0:T(8,128)(2,1)S(1)}, bf16[8,1024]{1,0:T(8,128)(2,1)S(1)}, u32[]{:S(2)}, u32[]{:S(2)}) %collective-permute-start.3) | collective-permute-done | bytes 16416 | tf_op jit(solution)/shard_map/ppermute | solution.py:249
  55.9 0.1 multiply_reduce_fusion
  56.0 0.7 %broadcast_multiply_fusion = f32[8,1024]{1,0:T(8,128)} fusion(f32[8]{0:T(128)S(1)} %add_rsqrt_fusion.1, bf16[8,1024]{1,0:T(8,128)(2,1)S(1)} %collective-permute-done.5, bf16[8,1024]{1,0:T(8,128)(2,1)S(1)} %collective-permute-done.4, bf16[8,1024]{1,0:T(8,128)(2,1)S(1)} %collective-permute-done.3, bf16[4,8,1024]{2,1,0:T(8,128)(2,1)S(1)} %bitcast.49, ...), kind=kLoop, calls=%fused_computation.43 | loop fusion | flops 73728 | bytes 98341 | tf_op jit(solution)/shard_map/mul | solution.py:254
  (15 shorter events, 0.2 us)
Async XLA Ops:
  0.0 3.8 %copy-start = (bf16[32,32,512]{2,1,0:T(8,128)(2,1)S(1)}, bf16[32,32,512]{2,1,0:T(8,128)(2,1)}, u32[]{:S(2)}) copy-start(bf16[32,32,512]{2,1,0:T(8,128)(2,1)} %param.8) | copy-start | bytes 3145732
  3.5 1.1 %copy-start.1 = (s32[32,32]{1,0:T(8,128)S(1)}, s32[32,32]{1,0:T(8,128)}, u32[]{:S(2)}) copy-start(s32[32,32]{1,0:T(8,128)} %param.9) | copy-start | bytes 12292
  5.1 0.7 %copy-start.2 = (s32[32,32]{1,0:T(8,128)S(1)}, s32[32,32]{1,0:T(8,128)}, u32[]{:S(2)}) copy-start(s32[32,32]{1,0:T(8,128)} %param.10) | copy-start | bytes 12292
  16.6 20.4 %collective-permute-start.2 = (bf16[216,256]{1,0:T(8,128)(2,1)S(1)}, bf16[216,256]{1,0:T(8,128)(2,1)S(1)}, u32[]{:S(2)}, u32[]{:S(2)}) collective-permute-start(bf16[216,256]{1,0:T(8,128)(2,1)S(1)} %pad.17), channel_id=1, source_target_pairs={{0,12},{4,0},{8,4},{12,8},{1,13},{5,1},{9,5},{13,9},{2,14},{6,2},{... | collective-permute-start | bytes 331784 | tf_op jit(solution)/shard_map/ppermute | solution.py:228
  21.7 15.3 %collective-permute-start.1 = (bf16[216,256]{1,0:T(8,128)(2,1)S(1)}, bf16[216,256]{1,0:T(8,128)(2,1)S(1)}, u32[]{:S(2)}, u32[]{:S(2)}) collective-permute-start(bf16[216,256]{1,0:T(8,128)(2,1)S(1)} %pad.17), channel_id=1, source_target_pairs={{0,8},{4,12},{8,0},{12,4},{1,9},{5,13},{9,1},{13,5},{2,10},{6,14},... | collective-permute-start | bytes 331784 | tf_op jit(solution)/shard_map/ppermute | solution.py:228
  21.7 15.3 %collective-permute-start = (bf16[216,256]{1,0:T(8,128)(2,1)S(1)}, bf16[216,256]{1,0:T(8,128)(2,1)S(1)}, u32[]{:S(2)}, u32[]{:S(2)}) collective-permute-start(bf16[216,256]{1,0:T(8,128)(2,1)S(1)} %pad.17), channel_id=1, source_target_pairs={{0,4},{4,8},{8,12},{12,0},{1,5},{5,9},{9,13},{13,1},{2,6},{6,10},{... | collective-permute-start | bytes 331784 | tf_op jit(solution)/shard_map/ppermute | solution.py:228
  34.8 1.4 %copy-start.3 = (s32[1,32]{1,0:T(1,128)S(1)}, s32[1,32]{1,0:T(1,128)}, u32[]{:S(2)}) copy-start(s32[1,32]{1,0:T(1,128)} %param.11) | copy-start | bytes 388
  51.1 1.8 %collective-permute-start.5 = (bf16[8,1024]{1,0:T(8,128)(2,1)S(1)}, bf16[8,1024]{1,0:T(8,128)(2,1)S(1)}, u32[]{:S(2)}, u32[]{:S(2)}) collective-permute-start(bf16[8,1024]{1,0:T(8,128)(2,1)S(1)} %get-tuple-element.22), channel_id=1, source_target_pairs={{0,3},{1,0},{2,1},{3,2},{4,7},{5,4},{6,5},{7,6},{8,11},{9,8},{10,9... | collective-permute-start | bytes 49160 | tf_op jit(solution)/shard_map/ppermute | solution.py:249
  51.3 3.7 %collective-permute-start.4 = (bf16[8,1024]{1,0:T(8,128)(2,1)S(1)}, bf16[8,1024]{1,0:T(8,128)(2,1)S(1)}, u32[]{:S(2)}, u32[]{:S(2)}) collective-permute-start(bf16[8,1024]{1,0:T(8,128)(2,1)S(1)} %get-tuple-element.23), channel_id=1, source_target_pairs={{0,2},{1,3},{2,0},{3,1},{4,6},{5,7},{6,4},{7,5},{8,10},{9,11},{10,... | collective-permute-start | bytes 49160 | tf_op jit(solution)/shard_map/ppermute | solution.py:249
  52.7 3.2 %collective-permute-start.3 = (bf16[8,1024]{1,0:T(8,128)(2,1)S(1)}, bf16[8,1024]{1,0:T(8,128)(2,1)S(1)}, u32[]{:S(2)}, u32[]{:S(2)}) collective-permute-start(bf16[8,1024]{1,0:T(8,128)(2,1)S(1)} %get-tuple-element.21), channel_id=1, source_target_pairs={{0,1},{1,2},{2,3},{3,0},{4,5},{5,6},{6,7},{7,4},{8,9},{9,10},{10,1... | collective-permute-start | bytes 49160 | tf_op jit(solution)/shard_map/ppermute | solution.py:249

commit v21 on v20

--- a/solution.py
+++ b/solution.py
@@ -173,7 +173,7 @@
     padded = jnp.pad(placed, ((0, 0), (0, 0), (front, n_groups * phases - padded_len - front)))
     grouped = jnp.transpose(padded, (0, 2, 1)).reshape(count, n_groups, width)
     grouped = jnp.transpose(grouped, (1, 0, 2))
-    signal = signal_rows.astype(jnp.float32)
+    signal = signal_rows if n_blocks <= 8 else signal_rows.astype(jnp.float32)
     kernel = functools.partial(
         _corr_kernel, steps=steps, extra_taps=extra_taps, count=count, chans=chans,
         phases=phases, rows=rows,

time: 57.2 us -> 56.9 us (level)
    convert_element_type x1 -> x0, other arithmetic: 1.05 us -> none  [correlate(): signal = signal_rows.astype(jnp.float32)]
    another operation x0 -> x1, other arithmetic: none -> 0.84 us  [shards(): blocks = jnp.stack(pieces)]
where the time goes in v21:
time: 56.9 us; the launch traced here: 56.4 us
  other arithmetic  17.4 us (31%)
  local copies, waits for them, and re-layouts  16.6 us (29%)
  Pallas kernels  10.7 us (19%)
  starting transfers between devices  7.9 us (14%)
  waiting for transfers between devices  3 us (5%)
    pallas_call x1, Pallas kernels, correlate(): pl.pallas_call(kernel, grid=(taps // steps,), in_specs=[pl.BlockSpec(grou...  10.7 us
    select_n x8, other arithmetic, place_moveout(): current = jnp.where(active[..., None], moved, current)  9.93 us
    reshape x2, local copies, waits for them, and re-layouts, correlate(): grouped = jnp.transpose(padded, (0, 2, 1)).reshape(count, n_groups, width)  8.25 us
    ppermute x3, starting transfers between devices, shards(): pieces.append(lax.ppermute(signal, 'chan', pairs))  6.12 us
    transpose x2, local copies, waits for them, and re-layouts, correlate(): grouped = jnp.transpose(padded, (0, 2, 1)).reshape(count, n_groups, width)  5.01 us
    ppermute x3, waiting for transfers between devices, shards(): stack = stack + lax.ppermute(outgoing, 'tmpl', pairs).astype(jnp.float32)  3 us
    ppermute x3, starting transfers between devices, shards(): stack = stack + lax.ppermute(outgoing, 'tmpl', pairs).astype(jnp.float32)  1.78 us
    reduce_sum x2, other arithmetic, normalize_rows(): scale = lax.rsqrt(jnp.mean(centred * centred, axis=-1, keepdims=True) + eps)  1.62 us
  transfers between devices with their start and end apart: 6, of which 2 were waited for; matrix products, arithmetic and copies ran while one was open for 25% of the time, Pallas kernels for 0%

profile of v21, /device:TPU:0, one launch (start us, length us, event | category | flops | bytes accessed | tf_op | source)
XLA Modules:
  0.0 56.4 jit_solution(9323823787026254991)
XLA Ops:
  0.0 0.0 copy-start
  0.0 1.1 %convert_reduce_fusion.1 = f32[32]{0:T(128)S(1)} fusion(bf16[32,1664]{1,0:T(8,128)(2,1)} %param.7), kind=kLoop, calls=%fused_computation.27 | loop fusion | flops 106464 | bytes 106624 | tf_op jit(solution)/shard_map/reduce_sum | solution.py:19
  1.1 1.1 %fusion.10 = f32[32]{0:T(128)S(1)} fusion(bf16[32,1664]{1,0:T(8,128)(2,1)} %param.7, f32[32]{0:T(128)S(1)} %broadcast_multiply_fusion.2), kind=kLoop, calls=%fused_computation.31 | loop fusion | flops 212960 | bytes 106752 | tf_op jit(solution)/shard_map/reduce_sum | solution.py:20
  2.2 1.0 %fusion.12 = bf16[1664,32]{0,1:T(8,128)(2,1)S(1)} fusion(bf16[32,1664]{1,0:T(8,128)(2,1)} %param.7, f32[32]{0:T(128)S(1)} %add_rsqrt_fusion.2, f32[32]{0:T(128)S(1)} %broadcast_multiply_fusion.2), kind=kLoop, calls=%fused_computation.33 | loop fusion | flops 212992 | bytes 213248 | tf_op jit(solution)/shard_map/transpose | solution.py:159
  3.2 0.3 copy.12
  3.5 0.0 copy-start.1
  3.5 0.3 reshape.175
  3.8 0.0 copy-done
  3.8 0.2 convert_reduce_fusion
  4.0 0.5 fusion.2
  4.6 0.0 copy-done.1
  4.6 0.5 convolution_convert_fusion
  5.1 0.0 copy-start.2
  5.2 0.1 pad_slice_fusion
  5.3 0.6 %copy-done.2 = s32[32,32]{1,0:T(8,128)S(1)} copy-done((s32[32,32]{1,0:T(8,128)S(1)}, s32[32,32]{1,0:T(8,128)}, u32[]{:S(2)}) %copy-start.2) | copy-done | bytes 4120
  5.9 0.6 %select_reduce_fusion.1 = s32[32,32]{1,0:T(8,128)S(1)} fusion(s32[32,32]{1,0:T(8,128)S(1)} %copy-done.2, s32[32,32]{1,0:T(8,128)S(1)} %add_select_fusion), kind=kLoop, calls=%fused_computation.23 | loop fusion | flops 97280 | bytes 12288 | tf_op jit(solution)/shard_map/reduce_sum | solution.py:217
  6.5 1.3 %pad_select_fusion.7 = bf16[32,32,640]{2,1,0:T(8,128)(2,1)S(1)} fusion(bf16[32,32,639]{2,1,0:T(8,128)(2,1)S(1)} %pad_slice_fusion, pred[32,32]{1,0:T(8,128)(4,1)S(1)} %get-tuple-element.25, bf16[32,32,512]{2,1,0:T(8,128)(2,1)S(1)} %convolution_convert_fusion), kind=kLoop, calls=%fused_computation.18 | loop fusion | flops 655360 | bytes 3668992 | tf_op jit(solution)/shard_map/jit(_where)/select_n | solution.py:33
  7.8 1.3 %pad_select_fusion.6 = bf16[32,32,640]{2,1,0:T(8,128)(2,1)S(1)} fusion(bf16[32,32,640]{2,1,0:T(8,128)(2,1)S(1)} %pad_select_fusion.7, bf16[32,32,638]{2,1,0:T(8,128)(2,1)S(1)} %bitcast.38, pred[32,32]{1,0:T(8,128)(4,1)S(1)} %get-tuple-element.26), kind=kLoop, calls=%fused_computation.17 | loop fusion | flops 655360 | bytes 3929088 | tf_op jit(solution)/shard_map/jit(_where)/select_n | solution.py:33
  9.2 1.3 %pad_select_fusion.5 = bf16[32,32,640]{2,1,0:T(8,128)(2,1)S(1)} fusion(bf16[32,32,640]{2,1,0:T(8,128)(2,1)S(1)} %pad_select_fusion.6, bf16[32,32,636]{2,1,0:T(8,128)(2,1)S(1)} %bitcast.39, pred[32,32]{1,0:T(8,128)(4,1)S(1)} %get-tuple-element.27), kind=kLoop, calls=%fused_computation.16 | loop fusion | flops 655360 | bytes 3924992 | tf_op jit(solution)/shard_map/jit(_where)/select_n | solution.py:33
  10.5 1.3 %pad_select_fusion.4 = bf16[32,32,640]{2,1,0:T(8,128)(2,1)S(1)} fusion(bf16[32,32,640]{2,1,0:T(8,128)(2,1)S(1)} %pad_select_fusion.5, bf16[32,32,632]{2,1,0:T(8,128)(2,1)S(1)} %bitcast.40, pred[32,32]{1,0:T(8,128)(4,1)S(1)} %get-tuple-element.28), kind=kLoop, calls=%fused_computation.15 | loop fusion | flops 655360 | bytes 3916800 | tf_op jit(solution)/shard_map/jit(_where)/select_n | solution.py:33
  11.9 1.3 %pad_select_fusion.3 = bf16[32,32,640]{2,1,0:T(8,128)(2,1)S(1)} fusion(bf16[32,32,640]{2,1,0:T(8,128)(2,1)S(1)} %pad_select_fusion.4, bf16[32,32,624]{2,1,0:T(8,128)(2,1)S(1)} %bitcast.41, pred[32,32]{1,0:T(8,128)(4,1)S(1)} %get-tuple-element.29), kind=kLoop, calls=%fused_computation.14 | loop fusion | flops 655360 | bytes 3900416 | tf_op jit(solution)/shard_map/jit(_where)/select_n | solution.py:33
  13.2 1.3 %pad_select_fusion.2 = bf16[32,32,640]{2,1,0:T(8,128)(2,1)S(1)} fusion(bf16[32,32,640]{2,1,0:T(8,128)(2,1)S(1)} %pad_select_fusion.3, bf16[32,32,608]{2,1,0:T(8,128)(2,1)S(1)} %bitcast.42, pred[32,32]{1,0:T(8,128)(4,1)S(1)} %get-tuple-element.30), kind=kLoop, calls=%fused_computation.13 | loop fusion | flops 655360 | bytes 3867648 | tf_op jit(solution)/shard_map/jit(_where)/select_n | solution.py:33
  14.6 1.3 %pad_select_fusion.1 = bf16[32,32,640]{2,1,0:T(8,128)(2,1)S(1)} fusion(bf16[32,32,640]{2,1,0:T(8,128)(2,1)S(1)} %pad_select_fusion.2, bf16[32,32,576]{2,1,0:T(8,128)(2,1)S(1)} %bitcast.43, pred[32,32]{1,0:T(8,128)(4,1)S(1)} %get-tuple-element.31), kind=kLoop, calls=%fused_computation.12 | loop fusion | flops 655360 | bytes 3802112 | tf_op jit(solution)/shard_map/jit(_where)/select_n | solution.py:33
  15.9 0.1 slice.53
  16.1 0.6 %pad_select_fusion = bf16[32,32,640]{2,1,0:T(8,128)(2,1)S(1)} fusion(bf16[32,32,640]{2,1,0:T(8,128)(2,1)S(1)} %pad_select_fusion.1, bf16[32,32,512]{2,1,0:T(8,128)(2,1)S(1)} %slice.53, pred[32,32]{1,0:T(8,128)(4,1)S(1)} %get-tuple-element.24), kind=kLoop, calls=%fused_computation.11 | loop fusion | flops 655360 | bytes 3671040 | tf_op jit(solution)/shard_map/jit(_where)/select_n | solution.py:33
  16.6 5.1 %collective-permute-start.2 = (bf16[216,256]{1,0:T(8,128)(2,1)S(1)}, bf16[216,256]{1,0:T(8,128)(2,1)S(1)}, u32[]{:S(2)}, u32[]{:S(2)}) collective-permute-start(bf16[216,256]{1,0:T(8,128)(2,1)S(1)} %pad.17), channel_id=1, source_target_pairs={{0,12},{4,0},{8,4},{12,8},{1,13},{5,1},{9,5},{13,9},{2,14},{6,2},{... | collective-permute-start | bytes 331784 | tf_op jit(solution)/shard_map/ppermute | solution.py:228
  21.7 0.0 collective-permute-start.1
  21.7 1.0 %collective-permute-start = (bf16[216,256]{1,0:T(8,128)(2,1)S(1)}, bf16[216,256]{1,0:T(8,128)(2,1)S(1)}, u32[]{:S(2)}, u32[]{:S(2)}) collective-permute-start(bf16[216,256]{1,0:T(8,128)(2,1)S(1)} %pad.17), channel_id=1, source_target_pairs={{0,4},{4,8},{8,12},{12,0},{1,5},{5,9},{9,13},{13,1},{2,6},{6,10},{... | collective-permute-start | bytes 331784 | tf_op jit(solution)/shard_map/ppermute | solution.py:228
  22.8 0.1 slice_reduce_fusion
  22.9 0.7 %pad_bitcast_fusion = bf16[32,656,32]{1,2,0:T(8,128)(2,1)S(1)} fusion(bf16[32,32,640]{2,1,0:T(8,128)(2,1)S(1)} %pad_select_fusion), kind=kLoop, calls=%fused_computation.8 | loop fusion | bytes 2654208 | tf_op jit(solution)/shard_map/transpose | solution.py:174
  23.7 4.3 %copy.13 = bf16[32,656,32]{2,1,0:T(8,128)(2,1)} copy(bf16[32,656,32]{1,2,0:T(8,128)(2,1)S(1)} %pad_bitcast_fusion) | data formatting | bytes 2686976 | tf_op jit(solution)/shard_map/transpose | solution.py:174
  27.9 6.9 %reshape.176 = bf16[32,82,256]{2,1,0:T(8,128)(2,1)S(1)} reshape(bf16[32,656,32]{2,1,0:T(8,128)(2,1)} %copy.13) | data formatting | bytes 2686976 | tf_op jit(solution)/shard_map/reshape | solution.py:174
  34.8 0.0 copy-start.3
  34.8 1.4 %copy.19 = bf16[32,82,256]{2,0,1:T(8,128)(2,1)} copy(bf16[32,82,256]{2,1,0:T(8,128)(2,1)S(1)} %reshape.176) | data formatting | bytes 2686976 | tf_op jit(solution)/shard_map/reshape | solution.py:174
  36.2 0.0 copy-done.3
  36.2 0.7 %scatter_custom_fusion = s32[32]{0:T(128)S(1)} fusion(s32[32]{0:T(128)S(1)} %fusion.15, s32[32]{0:T(128)S(1)} %iota.14, s32[]{:T(128)} %constant.103.clone.1), kind=kCustom, calls=%fused_computation.71 | custom fusion | bytes 132 | tf_op jit(solution)/shard_map/scatter | solution.py:240
  36.9 0.1 broadcast_in_dim.111
  37.0 0.0 collective-permute-done.2
  37.1 0.0 collective-permute-done.1
  37.1 0.0 collective-permute-done
  37.1 0.8 %pad_maximum_fusion.signal_ref = bf16[4,216,256]{2,1,0:T(8,128)(2,1)} fusion(bf16[1,216,256]{2,1,0:T(8,128)(2,1)S(1)} %bitcast.51, bf16[1,216,256]{2,1,0:T(8,128)(2,1)S(1)} %bitcast.52, bf16[1,216,256]{2,1,0:T(8,128)(2,1)S(1)} %bitcast.53, bf16[1,216,256]{2,1,0:T(8,128)(2,1)S(1)} %bitcast.46), kind=kLoop, calls=%fused_computation.25 | loop fusion | flops 663552 | bytes 884736 | tf_op jit(solution)/shard_map/stack | solution.py:229
  37.9 10.7 %shard_map.55 = f32[4,128,256]{2,1,0:T(8,128)} custom-call(bf16[82,32,256]{2,1,0:T(8,128)(2,1)} %bitcast.44, bf16[4,216,256]{2,1,0:T(8,128)(2,1)} %pad_maximum_fusion.signal_ref), custom_call_target="tpu_custom_call" | custom-call | tf_op jit(solution)/shard_map/pallas_call | solution.py:181
  48.6 1.1 %select_reduce_fusion = bf16[128,256]{1,0:T(8,128)(2,1)S(1)} fusion(f32[4,128,256]{2,1,0:T(8,128)} %shard_map.55, pred[4,256]{1,0:T(4,128)(4,1)S(1)} %broadcast_in_dim.111), kind=kLoop, calls=%fused_computation.22 | loop fusion | flops 229376 | bytes 590848 | tf_op jit(solution)/shard_map/reduce_sum | solution.py:236
  49.7 0.1 copy.15
  49.8 0.2 copy.16
  50.0 0.1 copy.17
  50.1 0.6 %gather_fusion = bf16[32,1024]{1,0:T(8,128)(2,1)S(1)} fusion(bf16[32,1024]{1,0:T(8,128)(2,1)S(1)} %copy.17, s32[1024]{0:T(1024)S(1)} %pad_clamp_fusion), kind=kCustom, calls=%fused_computation | custom fusion | bytes 131200 | tf_op jit(solution)/shard_map/gather | solution.py:242
  50.8 0.1 collective-permute-start.5
  50.9 1.5 %collective-permute-start.4 = (bf16[8,1024]{1,0:T(8,128)(2,1)S(1)}, bf16[8,1024]{1,0:T(8,128)(2,1)S(1)}, u32[]{:S(2)}, u32[]{:S(2)}) collective-permute-start(bf16[8,1024]{1,0:T(8,128)(2,1)S(1)} %get-tuple-element.23), channel_id=1, source_target_pairs={{0,2},{1,3},{2,0},{3,1},{4,6},{5,7},{6,4},{7,5},{8,10},{9,11},{10,... | collective-permute-start | bytes 49160 | tf_op jit(solution)/shard_map/ppermute | solution.py:249
  52.4 0.2 collective-permute-start.3
  52.6 0.0 collective-permute-done.5
  52.6 2.1 %collective-permute-done.4 = bf16[8,1024]{1,0:T(8,128)(2,1)S(1)} collective-permute-done((bf16[8,1024]{1,0:T(8,128)(2,1)S(1)}, bf16[8,1024]{1,0:T(8,128)(2,1)S(1)}, u32[]{:S(2)}, u32[]{:S(2)}) %collective-permute-start.4) | collective-permute-done | bytes 16416 | tf_op jit(solution)/shard_map/ppermute | solution.py:249
  54.7 0.9 %collective-permute-done.3 = bf16[8,1024]{1,0:T(8,128)(2,1)S(1)} collective-permute-done((bf16[8,1024]{1,0:T(8,128)(2,1)S(1)}, bf16[8,1024]{1,0:T(8,128)(2,1)S(1)}, u32[]{:S(2)}, u32[]{:S(2)}) %collective-permute-start.3) | collective-permute-done | bytes 16416 | tf_op jit(solution)/shard_map/ppermute | solution.py:249
  55.6 0.1 multiply_reduce_fusion
  55.7 0.7 %broadcast_multiply_fusion = f32[8,1024]{1,0:T(8,128)} fusion(f32[8]{0:T(128)S(1)} %add_rsqrt_fusion.1, bf16[8,1024]{1,0:T(8,128)(2,1)S(1)} %collective-permute-done.5, bf16[8,1024]{1,0:T(8,128)(2,1)S(1)} %collective-permute-done.4, bf16[8,1024]{1,0:T(8,128)(2,1)S(1)} %collective-permute-done.3, bf16[4,8,1024]{2,1,0:T(8,128)(2,1)S(1)} %bitcast.49, ...), kind=kLoop, calls=%fused_computation.43 | loop fusion | flops 73728 | bytes 98341 | tf_op jit(solution)/shard_map/mul | solution.py:254
  (15 shorter events, 0.2 us)
Async XLA Ops:
  0.0 3.8 %copy-start = (bf16[32,32,512]{2,1,0:T(8,128)(2,1)S(1)}, bf16[32,32,512]{2,1,0:T(8,128)(2,1)}, u32[]{:S(2)}) copy-start(bf16[32,32,512]{2,1,0:T(8,128)(2,1)} %param.8) | copy-start | bytes 3145732
  3.5 1.1 %copy-start.1 = (s32[32,32]{1,0:T(8,128)S(1)}, s32[32,32]{1,0:T(8,128)}, u32[]{:S(2)}) copy-start(s32[32,32]{1,0:T(8,128)} %param.9) | copy-start | bytes 12292
  5.1 0.7 %copy-start.2 = (s32[32,32]{1,0:T(8,128)S(1)}, s32[32,32]{1,0:T(8,128)}, u32[]{:S(2)}) copy-start(s32[32,32]{1,0:T(8,128)} %param.10) | copy-start | bytes 12292
  16.6 20.4 %collective-permute-start.2 = (bf16[216,256]{1,0:T(8,128)(2,1)S(1)}, bf16[216,256]{1,0:T(8,128)(2,1)S(1)}, u32[]{:S(2)}, u32[]{:S(2)}) collective-permute-start(bf16[216,256]{1,0:T(8,128)(2,1)S(1)} %pad.17), channel_id=1, source_target_pairs={{0,12},{4,0},{8,4},{12,8},{1,13},{5,1},{9,5},{13,9},{2,14},{6,2},{... | collective-permute-start | bytes 331784 | tf_op jit(solution)/shard_map/ppermute | solution.py:228
  21.7 15.3 %collective-permute-start.1 = (bf16[216,256]{1,0:T(8,128)(2,1)S(1)}, bf16[216,256]{1,0:T(8,128)(2,1)S(1)}, u32[]{:S(2)}, u32[]{:S(2)}) collective-permute-start(bf16[216,256]{1,0:T(8,128)(2,1)S(1)} %pad.17), channel_id=1, source_target_pairs={{0,8},{4,12},{8,0},{12,4},{1,9},{5,13},{9,1},{13,5},{2,10},{6,14},... | collective-permute-start | bytes 331784 | tf_op jit(solution)/shard_map/ppermute | solution.py:228
  21.7 15.3 %collective-permute-start = (bf16[216,256]{1,0:T(8,128)(2,1)S(1)}, bf16[216,256]{1,0:T(8,128)(2,1)S(1)}, u32[]{:S(2)}, u32[]{:S(2)}) collective-permute-start(bf16[216,256]{1,0:T(8,128)(2,1)S(1)} %pad.17), channel_id=1, source_target_pairs={{0,4},{4,8},{8,12},{12,0},{1,5},{5,9},{9,13},{13,1},{2,6},{6,10},{... | collective-permute-start | bytes 331784 | tf_op jit(solution)/shard_map/ppermute | solution.py:228
  34.8 1.4 %copy-start.3 = (s32[1,32]{1,0:T(1,128)S(1)}, s32[1,32]{1,0:T(1,128)}, u32[]{:S(2)}) copy-start(s32[1,32]{1,0:T(1,128)} %param.11) | copy-start | bytes 388
  50.8 1.8 %collective-permute-start.5 = (bf16[8,1024]{1,0:T(8,128)(2,1)S(1)}, bf16[8,1024]{1,0:T(8,128)(2,1)S(1)}, u32[]{:S(2)}, u32[]{:S(2)}) collective-permute-start(bf16[8,1024]{1,0:T(8,128)(2,1)S(1)} %get-tuple-element.22), channel_id=1, source_target_pairs={{0,3},{1,0},{2,1},{3,2},{4,7},{5,4},{6,5},{7,6},{8,11},{9,8},{10,9... | collective-permute-start | bytes 49160 | tf_op jit(solution)/shard_map/ppermute | solution.py:249
  50.9 3.7 %collective-permute-start.4 = (bf16[8,1024]{1,0:T(8,128)(2,1)S(1)}, bf16[8,1024]{1,0:T(8,128)(2,1)S(1)}, u32[]{:S(2)}, u32[]{:S(2)}) collective-permute-start(bf16[8,1024]{1,0:T(8,128)(2,1)S(1)} %get-tuple-element.23), channel_id=1, source_target_pairs={{0,2},{1,3},{2,0},{3,1},{4,6},{5,7},{6,4},{7,5},{8,10},{9,11},{10,... | collective-permute-start | bytes 49160 | tf_op jit(solution)/shard_map/ppermute | solution.py:249
  52.4 3.2 %collective-permute-start.3 = (bf16[8,1024]{1,0:T(8,128)(2,1)S(1)}, bf16[8,1024]{1,0:T(8,128)(2,1)S(1)}, u32[]{:S(2)}, u32[]{:S(2)}) collective-permute-start(bf16[8,1024]{1,0:T(8,128)(2,1)S(1)} %get-tuple-element.21), channel_id=1, source_target_pairs={{0,1},{1,2},{2,3},{3,0},{4,5},{5,6},{6,7},{7,4},{8,9},{9,10},{10,1... | collective-permute-start | bytes 49160 | tf_op jit(solution)/shard_map/ppermute | solution.py:249

commit v22 on v21

--- a/solution.py
+++ b/solution.py
@@ -80,13 +80,13 @@
     base = pl.multiple_of(pid * steps, steps)
     for step in range(steps):
         joined = jnp.concatenate([grouped_ref[base + step], grouped_ref[base + step + 1]], axis=-1)
-        joined = joined.astype(jnp.float32)
         parts = []
         for e in range(phases):
             cut = (phases - 1 - e) * chans
             moved = pltpu.roll(joined, 2 * width - cut, 1) if cut else joined
             parts.append(moved[:, :width])
-        filt_ref[step] = jnp.transpose(jnp.concatenate(parts, axis=0)).astype(filt_ref.dtype)
+        slab = jnp.concatenate(parts, axis=0).astype(jnp.float32)
+        filt_ref[step] = jnp.transpose(slab).astype(filt_ref.dtype)
 
     n_blocks = signal_ref.shape[0]
     if n_blocks <= 8:

time: 56.9 us -> 57.2 us (level)
  no operation moved by 1% of the time
where the time goes in v22:
time: 57.2 us; the launch traced here: 56.7 us
  other arithmetic  17.4 us (30%)
  local copies, waits for them, and re-layouts  16.6 us (29%)
  Pallas kernels  11 us (19%)
  starting transfers between devices  7.9 us (14%)
  waiting for transfers between devices  3 us (5%)
    pallas_call x1, Pallas kernels, correlate(): pl.pallas_call(kernel, grid=(taps // steps,), in_specs=[pl.BlockSpec(grou...  11 us
    select_n x8, other arithmetic, place_moveout(): current = jnp.where(active[..., None], moved, current)  9.93 us
    reshape x2, local copies, waits for them, and re-layouts, correlate(): grouped = jnp.transpose(padded, (0, 2, 1)).reshape(count, n_groups, width)  8.25 us
    ppermute x3, starting transfers between devices, shards(): pieces.append(lax.ppermute(signal, 'chan', pairs))  6.12 us
    transpose x2, local copies, waits for them, and re-layouts, correlate(): grouped = jnp.transpose(padded, (0, 2, 1)).reshape(count, n_groups, width)  5.01 us
    ppermute x3, waiting for transfers between devices, shards(): stack = stack + lax.ppermute(outgoing, 'tmpl', pairs).astype(jnp.float32)  3 us
    ppermute x3, starting transfers between devices, shards(): stack = stack + lax.ppermute(outgoing, 'tmpl', pairs).astype(jnp.float32)  1.78 us
    reduce_sum x2, other arithmetic, normalize_rows(): scale = lax.rsqrt(jnp.mean(centred * centred, axis=-1, keepdims=True) + eps)  1.62 us
  transfers between devices with their start and end apart: 6, of which 2 were waited for; matrix products, arithmetic and copies ran while one was open for 25% of the time, Pallas kernels for 0%

profile of v22, /device:TPU:0, one launch (start us, length us, event | category | flops | bytes accessed | tf_op | source)
XLA Modules:
  0.0 56.7 jit_solution(13703060161591852517)
XLA Ops:
  0.0 0.0 copy-start
  0.0 1.1 %convert_reduce_fusion.1 = f32[32]{0:T(128)S(1)} fusion(bf16[32,1664]{1,0:T(8,128)(2,1)} %param.7), kind=kLoop, calls=%fused_computation.27 | loop fusion | flops 106464 | bytes 106624 | tf_op jit(solution)/shard_map/reduce_sum | solution.py:19
  1.1 1.1 %fusion.10 = f32[32]{0:T(128)S(1)} fusion(bf16[32,1664]{1,0:T(8,128)(2,1)} %param.7, f32[32]{0:T(128)S(1)} %broadcast_multiply_fusion.2), kind=kLoop, calls=%fused_computation.31 | loop fusion | flops 212960 | bytes 106752 | tf_op jit(solution)/shard_map/reduce_sum | solution.py:20
  2.2 1.0 %fusion.12 = bf16[1664,32]{0,1:T(8,128)(2,1)S(1)} fusion(bf16[32,1664]{1,0:T(8,128)(2,1)} %param.7, f32[32]{0:T(128)S(1)} %add_rsqrt_fusion.2, f32[32]{0:T(128)S(1)} %broadcast_multiply_fusion.2), kind=kLoop, calls=%fused_computation.33 | loop fusion | flops 212992 | bytes 213248 | tf_op jit(solution)/shard_map/transpose | solution.py:159
  3.2 0.3 copy.12
  3.5 0.0 copy-start.1
  3.5 0.3 reshape.175
  3.8 0.0 copy-done
  3.8 0.2 convert_reduce_fusion
  4.0 0.5 fusion.2
  4.6 0.0 copy-done.1
  4.6 0.5 convolution_convert_fusion
  5.1 0.0 copy-start.2
  5.2 0.1 pad_slice_fusion
  5.3 0.6 %copy-done.2 = s32[32,32]{1,0:T(8,128)S(1)} copy-done((s32[32,32]{1,0:T(8,128)S(1)}, s32[32,32]{1,0:T(8,128)}, u32[]{:S(2)}) %copy-start.2) | copy-done | bytes 4120
  5.9 0.6 %select_reduce_fusion.1 = s32[32,32]{1,0:T(8,128)S(1)} fusion(s32[32,32]{1,0:T(8,128)S(1)} %copy-done.2, s32[32,32]{1,0:T(8,128)S(1)} %add_select_fusion), kind=kLoop, calls=%fused_computation.23 | loop fusion | flops 97280 | bytes 12288 | tf_op jit(solution)/shard_map/reduce_sum | solution.py:217
  6.5 1.3 %pad_select_fusion.7 = bf16[32,32,640]{2,1,0:T(8,128)(2,1)S(1)} fusion(bf16[32,32,639]{2,1,0:T(8,128)(2,1)S(1)} %pad_slice_fusion, pred[32,32]{1,0:T(8,128)(4,1)S(1)} %get-tuple-element.25, bf16[32,32,512]{2,1,0:T(8,128)(2,1)S(1)} %convolution_convert_fusion), kind=kLoop, calls=%fused_computation.18 | loop fusion | flops 655360 | bytes 3668992 | tf_op jit(solution)/shard_map/jit(_where)/select_n | solution.py:33
  7.8 1.3 %pad_select_fusion.6 = bf16[32,32,640]{2,1,0:T(8,128)(2,1)S(1)} fusion(bf16[32,32,640]{2,1,0:T(8,128)(2,1)S(1)} %pad_select_fusion.7, bf16[32,32,638]{2,1,0:T(8,128)(2,1)S(1)} %bitcast.38, pred[32,32]{1,0:T(8,128)(4,1)S(1)} %get-tuple-element.26), kind=kLoop, calls=%fused_computation.17 | loop fusion | flops 655360 | bytes 3929088 | tf_op jit(solution)/shard_map/jit(_where)/select_n | solution.py:33
  9.2 1.3 %pad_select_fusion.5 = bf16[32,32,640]{2,1,0:T(8,128)(2,1)S(1)} fusion(bf16[32,32,640]{2,1,0:T(8,128)(2,1)S(1)} %pad_select_fusion.6, bf16[32,32,636]{2,1,0:T(8,128)(2,1)S(1)} %bitcast.39, pred[32,32]{1,0:T(8,128)(4,1)S(1)} %get-tuple-element.27), kind=kLoop, calls=%fused_computation.16 | loop fusion | flops 655360 | bytes 3924992 | tf_op jit(solution)/shard_map/jit(_where)/select_n | solution.py:33
  10.5 1.3 %pad_select_fusion.4 = bf16[32,32,640]{2,1,0:T(8,128)(2,1)S(1)} fusion(bf16[32,32,640]{2,1,0:T(8,128)(2,1)S(1)} %pad_select_fusion.5, bf16[32,32,632]{2,1,0:T(8,128)(2,1)S(1)} %bitcast.40, pred[32,32]{1,0:T(8,128)(4,1)S(1)} %get-tuple-element.28), kind=kLoop, calls=%fused_computation.15 | loop fusion | flops 655360 | bytes 3916800 | tf_op jit(solution)/shard_map/jit(_where)/select_n | solution.py:33
  11.9 1.3 %pad_select_fusion.3 = bf16[32,32,640]{2,1,0:T(8,128)(2,1)S(1)} fusion(bf16[32,32,640]{2,1,0:T(8,128)(2,1)S(1)} %pad_select_fusion.4, bf16[32,32,624]{2,1,0:T(8,128)(2,1)S(1)} %bitcast.41, pred[32,32]{1,0:T(8,128)(4,1)S(1)} %get-tuple-element.29), kind=kLoop, calls=%fused_computation.14 | loop fusion | flops 655360 | bytes 3900416 | tf_op jit(solution)/shard_map/jit(_where)/select_n | solution.py:33
  13.2 1.3 %pad_select_fusion.2 = bf16[32,32,640]{2,1,0:T(8,128)(2,1)S(1)} fusion(bf16[32,32,640]{2,1,0:T(8,128)(2,1)S(1)} %pad_select_fusion.3, bf16[32,32,608]{2,1,0:T(8,128)(2,1)S(1)} %bitcast.42, pred[32,32]{1,0:T(8,128)(4,1)S(1)} %get-tuple-element.30), kind=kLoop, calls=%fused_computation.13 | loop fusion | flops 655360 | bytes 3867648 | tf_op jit(solution)/shard_map/jit(_where)/select_n | solution.py:33
  14.6 1.3 %pad_select_fusion.1 = bf16[32,32,640]{2,1,0:T(8,128)(2,1)S(1)} fusion(bf16[32,32,640]{2,1,0:T(8,128)(2,1)S(1)} %pad_select_fusion.2, bf16[32,32,576]{2,1,0:T(8,128)(2,1)S(1)} %bitcast.43, pred[32,32]{1,0:T(8,128)(4,1)S(1)} %get-tuple-element.31), kind=kLoop, calls=%fused_computation.12 | loop fusion | flops 655360 | bytes 3802112 | tf_op jit(solution)/shard_map/jit(_where)/select_n | solution.py:33
  15.9 0.1 slice.53
  16.1 0.6 pad_select_fusion
  16.6 5.1 %collective-permute-start.2 = (bf16[216,256]{1,0:T(8,128)(2,1)S(1)}, bf16[216,256]{1,0:T(8,128)(2,1)S(1)}, u32[]{:S(2)}, u32[]{:S(2)}) collective-permute-start(bf16[216,256]{1,0:T(8,128)(2,1)S(1)} %pad.17), channel_id=1, source_target_pairs={{0,12},{4,0},{8,4},{12,8},{1,13},{5,1},{9,5},{13,9},{2,14},{6,2},{... | collective-permute-start | bytes 331784 | tf_op jit(solution)/shard_map/ppermute | solution.py:228
  21.7 0.0 collective-permute-start.1
  21.7 1.0 %collective-permute-start = (bf16[216,256]{1,0:T(8,128)(2,1)S(1)}, bf16[216,256]{1,0:T(8,128)(2,1)S(1)}, u32[]{:S(2)}, u32[]{:S(2)}) collective-permute-start(bf16[216,256]{1,0:T(8,128)(2,1)S(1)} %pad.17), channel_id=1, source_target_pairs={{0,4},{4,8},{8,12},{12,0},{1,5},{5,9},{9,13},{13,1},{2,6},{6,10},{... | collective-permute-start | bytes 331784 | tf_op jit(solution)/shard_map/ppermute | solution.py:228
  22.8 0.1 slice_reduce_fusion
  22.9 0.7 %pad_bitcast_fusion = bf16[32,656,32]{1,2,0:T(8,128)(2,1)S(1)} fusion(bf16[32,32,640]{2,1,0:T(8,128)(2,1)S(1)} %pad_select_fusion), kind=kLoop, calls=%fused_computation.8 | loop fusion | bytes 2654208 | tf_op jit(solution)/shard_map/transpose | solution.py:174
  23.7 4.3 %copy.13 = bf16[32,656,32]{2,1,0:T(8,128)(2,1)} copy(bf16[32,656,32]{1,2,0:T(8,128)(2,1)S(1)} %pad_bitcast_fusion) | data formatting | bytes 2686976 | tf_op jit(solution)/shard_map/transpose | solution.py:174
  27.9 6.9 %reshape.176 = bf16[32,82,256]{2,1,0:T(8,128)(2,1)S(1)} reshape(bf16[32,656,32]{2,1,0:T(8,128)(2,1)} %copy.13) | data formatting | bytes 2686976 | tf_op jit(solution)/shard_map/reshape | solution.py:174
  34.8 0.0 copy-start.3
  34.8 1.4 %copy.19 = bf16[32,82,256]{2,0,1:T(8,128)(2,1)} copy(bf16[32,82,256]{2,1,0:T(8,128)(2,1)S(1)} %reshape.176) | data formatting | bytes 2686976 | tf_op jit(solution)/shard_map/reshape | solution.py:174
  36.2 0.0 copy-done.3
  36.2 0.7 %scatter_custom_fusion = s32[32]{0:T(128)S(1)} fusion(s32[32]{0:T(128)S(1)} %fusion.15, s32[32]{0:T(128)S(1)} %iota.14, s32[]{:T(128)} %constant.103.clone.1), kind=kCustom, calls=%fused_computation.71 | custom fusion | bytes 132 | tf_op jit(solution)/shard_map/scatter | solution.py:240
  36.9 0.1 broadcast_in_dim.111
  37.0 0.0 collective-permute-done.2
  37.1 0.0 collective-permute-done.1
  37.1 0.0 collective-permute-done
  37.1 0.8 %pad_maximum_fusion.signal_ref = bf16[4,216,256]{2,1,0:T(8,128)(2,1)} fusion(bf16[1,216,256]{2,1,0:T(8,128)(2,1)S(1)} %bitcast.51, bf16[1,216,256]{2,1,0:T(8,128)(2,1)S(1)} %bitcast.52, bf16[1,216,256]{2,1,0:T(8,128)(2,1)S(1)} %bitcast.53, bf16[1,216,256]{2,1,0:T(8,128)(2,1)S(1)} %bitcast.46), kind=kLoop, calls=%fused_computation.25 | loop fusion | flops 663552 | bytes 884736 | tf_op jit(solution)/shard_map/stack | solution.py:229
  37.9 11.0 %shard_map.55 = f32[4,128,256]{2,1,0:T(8,128)} custom-call(bf16[82,32,256]{2,1,0:T(8,128)(2,1)} %bitcast.44, bf16[4,216,256]{2,1,0:T(8,128)(2,1)} %pad_maximum_fusion.signal_ref), custom_call_target="tpu_custom_call" | custom-call | tf_op jit(solution)/shard_map/pallas_call | solution.py:181
  48.9 1.1 %select_reduce_fusion = bf16[128,256]{1,0:T(8,128)(2,1)S(1)} fusion(f32[4,128,256]{2,1,0:T(8,128)} %shard_map.55, pred[4,256]{1,0:T(4,128)(4,1)S(1)} %broadcast_in_dim.111), kind=kLoop, calls=%fused_computation.22 | loop fusion | flops 229376 | bytes 590848 | tf_op jit(solution)/shard_map/reduce_sum | solution.py:236
  50.0 0.1 copy.15
  50.1 0.2 copy.16
  50.3 0.1 copy.17
  50.5 0.6 %gather_fusion = bf16[32,1024]{1,0:T(8,128)(2,1)S(1)} fusion(bf16[32,1024]{1,0:T(8,128)(2,1)S(1)} %copy.17, s32[1024]{0:T(1024)S(1)} %pad_clamp_fusion), kind=kCustom, calls=%fused_computation | custom fusion | bytes 131200 | tf_op jit(solution)/shard_map/gather | solution.py:242
  51.1 0.1 collective-permute-start.5
  51.3 1.5 %collective-permute-start.4 = (bf16[8,1024]{1,0:T(8,128)(2,1)S(1)}, bf16[8,1024]{1,0:T(8,128)(2,1)S(1)}, u32[]{:S(2)}, u32[]{:S(2)}) collective-permute-start(bf16[8,1024]{1,0:T(8,128)(2,1)S(1)} %get-tuple-element.23), channel_id=1, source_target_pairs={{0,2},{1,3},{2,0},{3,1},{4,6},{5,7},{6,4},{7,5},{8,10},{9,11},{10,... | collective-permute-start | bytes 49160 | tf_op jit(solution)/shard_map/ppermute | solution.py:249
  52.7 0.2 collective-permute-start.3
  52.9 0.0 collective-permute-done.5
  52.9 2.1 %collective-permute-done.4 = bf16[8,1024]{1,0:T(8,128)(2,1)S(1)} collective-permute-done((bf16[8,1024]{1,0:T(8,128)(2,1)S(1)}, bf16[8,1024]{1,0:T(8,128)(2,1)S(1)}, u32[]{:S(2)}, u32[]{:S(2)}) %collective-permute-start.4) | collective-permute-done | bytes 16416 | tf_op jit(solution)/shard_map/ppermute | solution.py:249
  55.0 0.9 %collective-permute-done.3 = bf16[8,1024]{1,0:T(8,128)(2,1)S(1)} collective-permute-done((bf16[8,1024]{1,0:T(8,128)(2,1)S(1)}, bf16[8,1024]{1,0:T(8,128)(2,1)S(1)}, u32[]{:S(2)}, u32[]{:S(2)}) %collective-permute-start.3) | collective-permute-done | bytes 16416 | tf_op jit(solution)/shard_map/ppermute | solution.py:249
  55.9 0.1 multiply_reduce_fusion
  56.0 0.7 %broadcast_multiply_fusion = f32[8,1024]{1,0:T(8,128)} fusion(f32[8]{0:T(128)S(1)} %add_rsqrt_fusion.1, bf16[8,1024]{1,0:T(8,128)(2,1)S(1)} %collective-permute-done.5, bf16[8,1024]{1,0:T(8,128)(2,1)S(1)} %collective-permute-done.4, bf16[8,1024]{1,0:T(8,128)(2,1)S(1)} %collective-permute-done.3, bf16[4,8,1024]{2,1,0:T(8,128)(2,1)S(1)} %bitcast.49, ...), kind=kLoop, calls=%fused_computation.43 | loop fusion | flops 73728 | bytes 98341 | tf_op jit(solution)/shard_map/mul | solution.py:254
  (15 shorter events, 0.2 us)
Async XLA Ops:
  0.0 3.8 %copy-start = (bf16[32,32,512]{2,1,0:T(8,128)(2,1)S(1)}, bf16[32,32,512]{2,1,0:T(8,128)(2,1)}, u32[]{:S(2)}) copy-start(bf16[32,32,512]{2,1,0:T(8,128)(2,1)} %param.8) | copy-start | bytes 3145732
  3.5 1.1 %copy-start.1 = (s32[32,32]{1,0:T(8,128)S(1)}, s32[32,32]{1,0:T(8,128)}, u32[]{:S(2)}) copy-start(s32[32,32]{1,0:T(8,128)} %param.9) | copy-start | bytes 12292
  5.1 0.7 %copy-start.2 = (s32[32,32]{1,0:T(8,128)S(1)}, s32[32,32]{1,0:T(8,128)}, u32[]{:S(2)}) copy-start(s32[32,32]{1,0:T(8,128)} %param.10) | copy-start | bytes 12292
  16.6 20.4 %collective-permute-start.2 = (bf16[216,256]{1,0:T(8,128)(2,1)S(1)}, bf16[216,256]{1,0:T(8,128)(2,1)S(1)}, u32[]{:S(2)}, u32[]{:S(2)}) collective-permute-start(bf16[216,256]{1,0:T(8,128)(2,1)S(1)} %pad.17), channel_id=1, source_target_pairs={{0,12},{4,0},{8,4},{12,8},{1,13},{5,1},{9,5},{13,9},{2,14},{6,2},{... | collective-permute-start | bytes 331784 | tf_op jit(solution)/shard_map/ppermute | solution.py:228
  21.7 15.3 %collective-permute-start.1 = (bf16[216,256]{1,0:T(8,128)(2,1)S(1)}, bf16[216,256]{1,0:T(8,128)(2,1)S(1)}, u32[]{:S(2)}, u32[]{:S(2)}) collective-permute-start(bf16[216,256]{1,0:T(8,128)(2,1)S(1)} %pad.17), channel_id=1, source_target_pairs={{0,8},{4,12},{8,0},{12,4},{1,9},{5,13},{9,1},{13,5},{2,10},{6,14},... | collective-permute-start | bytes 331784 | tf_op jit(solution)/shard_map/ppermute | solution.py:228
  21.7 15.3 %collective-permute-start = (bf16[216,256]{1,0:T(8,128)(2,1)S(1)}, bf16[216,256]{1,0:T(8,128)(2,1)S(1)}, u32[]{:S(2)}, u32[]{:S(2)}) collective-permute-start(bf16[216,256]{1,0:T(8,128)(2,1)S(1)} %pad.17), channel_id=1, source_target_pairs={{0,4},{4,8},{8,12},{12,0},{1,5},{5,9},{9,13},{13,1},{2,6},{6,10},{... | collective-permute-start | bytes 331784 | tf_op jit(solution)/shard_map/ppermute | solution.py:228
  34.8 1.4 %copy-start.3 = (s32[1,32]{1,0:T(1,128)S(1)}, s32[1,32]{1,0:T(1,128)}, u32[]{:S(2)}) copy-start(s32[1,32]{1,0:T(1,128)} %param.11) | copy-start | bytes 388
  51.1 1.8 %collective-permute-start.5 = (bf16[8,1024]{1,0:T(8,128)(2,1)S(1)}, bf16[8,1024]{1,0:T(8,128)(2,1)S(1)}, u32[]{:S(2)}, u32[]{:S(2)}) collective-permute-start(bf16[8,1024]{1,0:T(8,128)(2,1)S(1)} %get-tuple-element.22), channel_id=1, source_target_pairs={{0,3},{1,0},{2,1},{3,2},{4,7},{5,4},{6,5},{7,6},{8,11},{9,8},{10,9... | collective-permute-start | bytes 49160 | tf_op jit(solution)/shard_map/ppermute | solution.py:249
  51.3 3.7 %collective-permute-start.4 = (bf16[8,1024]{1,0:T(8,128)(2,1)S(1)}, bf16[8,1024]{1,0:T(8,128)(2,1)S(1)}, u32[]{:S(2)}, u32[]{:S(2)}) collective-permute-start(bf16[8,1024]{1,0:T(8,128)(2,1)S(1)} %get-tuple-element.23), channel_id=1, source_target_pairs={{0,2},{1,3},{2,0},{3,1},{4,6},{5,7},{6,4},{7,5},{8,10},{9,11},{10,... | collective-permute-start | bytes 49160 | tf_op jit(solution)/shard_map/ppermute | solution.py:249
  52.7 3.2 %collective-permute-start.3 = (bf16[8,1024]{1,0:T(8,128)(2,1)S(1)}, bf16[8,1024]{1,0:T(8,128)(2,1)S(1)}, u32[]{:S(2)}, u32[]{:S(2)}) collective-permute-start(bf16[8,1024]{1,0:T(8,128)(2,1)S(1)} %get-tuple-element.21), channel_id=1, source_target_pairs={{0,1},{1,2},{2,3},{3,0},{4,5},{5,6},{6,7},{7,4},{8,9},{9,10},{10,1... | collective-permute-start | bytes 49160 | tf_op jit(solution)/shard_map/ppermute | solution.py:249
